TPU v7x, 256 devices: a whole 4x4x8 slice. The times are simulated.
256 devices in a mesh: row: 8 (over z), gx: 2 (over y_hi), gy: 16 (over y_lo, x, core).
Axes of the slice: x: 4, y: 4 (y_hi: 2, y_lo: 2; y = y_hi * 2 + y_lo), z: 8, core: 2. Of those that a mesh axis runs over, the one named last changes fastest.
Arguments:
- flow_pops: float32 [19, 64, 48, 256], P(None, 'gy', 'row', 'gx'), may hold values from 0 to 0.5, as said below
- concentration: float32 [64, 64, 48, 256], P('row', 'gy', None, 'gx'), may hold values from 0.2 to 2
- solid_mask: int32 [64, 48, 256], P('gy', None, 'gx'), may hold values from 0 to 1
- source_cell: int32 [96], replicated, may hold values from 0 to 786431
- source_scalar: int32 [96], replicated, may hold values from 0 to 63
- source_rate: float32 [96], replicated, may hold values from 0.5 to 2
Outputs:
- final_flow: float32 [19, 64, 48, 256], P(None, 'gy', 'row', 'gx')
- final_concentration: float32 [64, 64, 48, 256], P('row', 'gy', None, 'gx')
Inputs may be any that keep to these rules, and one draw needn't show every extreme that they name: `flow_pops`: populations are positive, near the equilibrium of a light wind.
All inputs are finite; a program needn't handle non-finite values.
Results may differ from a plain program's by a relative error of at most 0.0003.
Values sent between devices are 32-bit elements; how exact they have to be, the bound alone decides.
No kernel may reach another device: no remote copies, remote signals or barrier semaphores. Data moves between devices by JAX's collectives and lax.ppermute only.
A program may use at most 64 MiB of HBM per device.

v0:
```python
import math

import jax
import jax.numpy as jnp
from jax import lax
from jax.sharding import PartitionSpec as P

STEPS = 3


flow_vectors = (
    (0, 0, 0),
    (1, 0, 0),
    (-1, 0, 0),
    (0, 1, 0),
    (0, -1, 0),
    (0, 0, 1),
    (0, 0, -1),
    (1, 1, 0),
    (-1, -1, 0),
    (1, -1, 0),
    (-1, 1, 0),
    (1, 0, 1),
    (-1, 0, -1),
    (1, 0, -1),
    (-1, 0, 1),
    (0, 1, 1),
    (0, -1, -1),
    (0, 1, -1),
    (0, -1, 1),
)
scalar_vectors = flow_vectors[:7]
flow_weights = (1.0 / 3.0,) + (1.0 / 18.0,) * 6 + (1.0 / 36.0,) * 12
flow_mirror = (0, 2, 1, 4, 3, 6, 5, 8, 7, 10, 9, 12, 11, 14, 13, 16, 15, 18, 17)
scalar_weights = (0.25,) + (0.125,) * 6
tau_base = 0.52
smag_const = 0.17
tau_scalar_base = 0.55
schmidt_turb = 0.7
inflow_speed = 0.08


def passed_along(block, axis, distance):
    devices = range(lax.axis_size(axis))
    route = [(i - distance, i) for i in devices if i - distance in devices]
    return lax.ppermute(block, axis, route)


def from_behind(value, axis, steps):
    count = lax.axis_size(axis)
    pairs = [(source, (source + steps) % count) for source in range(count)]
    return lax.ppermute(value, axis, pairs)


def in_order(tiles, dim):
    tiles = jnp.moveaxis(tiles, 0, dim)
    shape = tiles.shape
    return tiles.reshape(*shape[:dim], shape[dim] * shape[dim + 1], *shape[dim + 2 :])


def copy_for_each(x, axis):
    copies = jnp.broadcast_to(x, (lax.axis_size(axis), *x.shape))
    return lax.all_to_all(copies, axis, split_axis=0, concat_axis=0, tiled=True)


def gathered_copies(x, axis, dim):
    return in_order(copy_for_each(x, axis), dim)


def far_field(member):
    along = flow_vectors[member][0] * inflow_speed
    return flow_weights[member] * (
        1.0 + 3.0 * along + 4.5 * along * along - 1.5 * inflow_speed * inflow_speed
    )


def flow_collide(populations, solid):
    density = populations[0]
    for member in range(1, 19):
        density = density + populations[member]
    speeds = []
    for component in range(3):
        moment = jnp.zeros_like(density)
        for member in range(19):
            factor = flow_vectors[member][component]
            if factor != 0:
                moment = moment + factor * populations[member]
        speeds.append(moment / density)
    square = speeds[0] * speeds[0] + speeds[1] * speeds[1] + speeds[2] * speeds[2]
    equilibria = []
    for member in range(19):
        vector = flow_vectors[member]
        project = vector[0] * speeds[0] + vector[1] * speeds[1] + vector[2] * speeds[2]
        equilibria.append(
            flow_weights[member]
            * density
            * (1.0 + 3.0 * project + 4.5 * project * project - 1.5 * square)
        )
    stress = jnp.zeros_like(density)
    for first_axis in range(3):
        for second_axis in range(3):
            tensor = jnp.zeros_like(density)
            for member in range(19):
                factor = flow_vectors[member][first_axis] * flow_vectors[member][second_axis]
                if factor != 0:
                    tensor = tensor + factor * (populations[member] - equilibria[member])
            stress = stress + tensor * tensor
    relaxation = 0.5 * (
        tau_base
        + jnp.sqrt(
            tau_base * tau_base
            + 18.0 * math.sqrt(2.0) * smag_const * smag_const * jnp.sqrt(stress) / density
        )
    )
    eddy = (relaxation - tau_base) / 3.0
    fluid_part = jnp.where(solid, jnp.zeros_like(density), jnp.ones_like(density))
    updated = []
    for member in range(19):
        relaxed = populations[member] - (populations[member] - equilibria[member]) / relaxation
        updated.append(jnp.where(solid, populations[flow_mirror[member]], relaxed))
    motion = jnp.stack(
        [speeds[0] * fluid_part, speeds[1] * fluid_part, speeds[2] * fluid_part, eddy * fluid_part]
    )
    return (updated, motion)


def scalar_collide(scalar, motion, solid, source):
    amount = scalar[0]
    for member in range(1, 7):
        amount = amount + scalar[member]
    relaxation = tau_scalar_base + 4.0 * motion[3] / schmidt_turb
    updated = []
    for member in range(7):
        vector = flow_vectors[member]
        project = vector[0] * motion[0] + vector[1] * motion[1] + vector[2] * motion[2]
        equilibrium = scalar_weights[member] * amount * (1.0 + 4.0 * project)
        relaxed = (
            scalar[member]
            - (scalar[member] - equilibrium) / relaxation
            + scalar_weights[member] * source
        )
        updated.append(jnp.where(solid, scalar[flow_mirror[member]], relaxed))
    return updated


def edge_planes(pieces, vectors, component, dimension, heading):
    planes = []
    for member in range(len(pieces)):
        if vectors[member][component] == heading:
            length = pieces[member].shape[dimension]
            position = length - 1 if heading == 1 else 0
            planes.append(lax.index_in_dim(pieces[member], position, dimension, keepdims=False))
    return jnp.stack(planes)


def displace(pieces, vectors, component, dimension, from_low, from_high):
    result = []
    low_count = 0
    high_count = 0
    for member in range(len(pieces)):
        piece = pieces[member]
        length = piece.shape[dimension]
        heading = vectors[member][component]
        if heading == 1:
            entering = jnp.expand_dims(from_low[low_count], dimension)
            low_count = low_count + 1
            result.append(
                jnp.concatenate(
                    [entering, lax.slice_in_dim(piece, 0, length - 1, axis=dimension)], dimension
                )
            )
        elif heading == -1:
            entering = jnp.expand_dims(from_high[high_count], dimension)
            high_count = high_count + 1
            result.append(
                jnp.concatenate(
                    [lax.slice_in_dim(piece, 1, length, axis=dimension), entering], dimension
                )
            )
        else:
            result.append(piece)
    return result


def local_vertical(pieces, vectors, dimension):
    from_low = jnp.zeros_like(edge_planes(pieces, vectors, 2, dimension, 1))
    from_high = jnp.zeros_like(edge_planes(pieces, vectors, 2, dimension, -1))
    return displace(pieces, vectors, 2, dimension, from_low, from_high)


def send_vertical(planes, offset):
    return passed_along(planes, "row", offset)


def send_spanwise(packed, offset):
    return from_behind(packed, "gy", offset)


def send_streamwise(packed, offset):
    return passed_along(packed, "gx", offset)


def keep_spanwise(flow_in, heading):
    return flow_in


def inflow_fill(flow_in, heading):
    boundary = 0 if heading == 1 else lax.axis_size("gx") - 1
    members = [member for member in range(19) if flow_vectors[member][0] == heading]
    values = jnp.array([far_field(member) for member in members], jnp.float32).reshape(-1, 1, 1)
    return jnp.where(lax.axis_index("gx") == boundary, values + jnp.zeros_like(flow_in), flow_in)


def cross_section(flow, scalar, component, flow_dim, sender, edge_fill, keep_rows):
    arrived_flow = {}
    arrived_scalar = {}
    for heading in (1, -1):
        flow_planes = edge_planes(flow, flow_vectors, component, flow_dim, heading)
        scalar_planes = edge_planes(scalar, scalar_vectors, component, flow_dim + 1, heading)
        if keep_rows:
            width = flow_planes.shape[-1]
            packed = jnp.concatenate(
                [flow_planes.reshape(-1, width), scalar_planes.reshape(-1, width)], 0
            )
            split_at = flow_planes.size // width
        else:
            packed = jnp.concatenate([flow_planes.reshape(-1), scalar_planes.reshape(-1)], 0)
            split_at = flow_planes.size
        arrived = sender(packed, heading)
        arrived_flow[heading] = edge_fill(arrived[:split_at].reshape(flow_planes.shape), heading)
        arrived_scalar[heading] = arrived[split_at:].reshape(scalar_planes.shape)
    flow = displace(flow, flow_vectors, component, flow_dim, arrived_flow[1], arrived_flow[-1])
    scalar = displace(
        scalar, scalar_vectors, component, flow_dim + 1, arrived_scalar[1], arrived_scalar[-1]
    )
    return (flow, scalar)


def on_device(flow_pops, concentration, solid_mask, source_cell, source_scalar, source_rate):
    row_index = lax.axis_index("row")
    slab_depth = flow_pops.shape[2]
    scalars_here, span_y, depth, span_x = concentration.shape
    height = lax.broadcasted_iota(jnp.int32, solid_mask.shape, 1)
    solid = (solid_mask == 1) | (height == 0) | (height == depth - 1)
    total_x = span_x * lax.axis_size("gx")
    cell_y = source_cell // (depth * total_x)
    cell_z = source_cell // total_x % depth
    cell_x = source_cell % total_x
    local_y = cell_y - lax.axis_index("gy") * span_y
    local_x = cell_x - lax.axis_index("gx") * span_x
    local_scalar = source_scalar - row_index * scalars_here
    inside = (
        (local_y >= 0)
        & (local_y < span_y)
        & (local_x >= 0)
        & (local_x < span_x)
        & (local_scalar >= 0)
        & (local_scalar < scalars_here)
    )
    target = jnp.where(inside, local_scalar, scalars_here)
    source = (
        jnp.zeros(concentration.shape, jnp.float32)
        .at[target, local_y, cell_z, local_x]
        .add(source_rate, mode="drop")
    )
    flow_solid = lax.dynamic_slice_in_dim(solid, row_index * slab_depth, slab_depth, 1)
    flow = [flow_pops[member] for member in range(19)]
    scalar = [scalar_weights[member] * concentration for member in range(7)]
    for time_step in range(STEPS):
        flow, motion = flow_collide(flow, flow_solid)
        column = gathered_copies(motion, "row", 2)
        scalar = scalar_collide(
            scalar, [column[component] for component in range(4)], solid, source
        )
        from_below = send_vertical(edge_planes(flow, flow_vectors, 2, 1, 1), 1)
        from_above = send_vertical(edge_planes(flow, flow_vectors, 2, 1, -1), -1)
        flow = displace(flow, flow_vectors, 2, 1, from_below, from_above)
        scalar = local_vertical(scalar, scalar_vectors, 2)
        flow, scalar = cross_section(flow, scalar, 1, 0, send_spanwise, keep_spanwise, True)
        flow, scalar = cross_section(flow, scalar, 0, 2, send_streamwise, inflow_fill, False)
    amount = scalar[0]
    for member in range(1, 7):
        amount = amount + scalar[member]
    stacked = jnp.stack(flow)
    return (stacked, amount)


def solution(mesh):
    in_specs = (
        P(None, "gy", "row", "gx"),
        P("row", "gy", None, "gx"),
        P("gy", None, "gx"),
        P(),
        P(),
        P(),
    )
    out_specs = (P(None, "gy", "row", "gx"), P("row", "gy", None, "gx"))
    return jax.shard_map(
        on_device, mesh=mesh, in_specs=in_specs, out_specs=out_specs, check_vma=False
    )
```

profile of v0, /device:TPU:96, one launch (start us, length us, event | category | flops | bytes accessed | tf_op | source)
XLA Modules:
  0.0 297.6 jit_solution(11551863990136799372)
XLA Ops:
  3.5 7.7 %all-to-all-start = ((f32[8,4,4,6,128]{4,2,3,1,0:T(4,128)}), f32[8,4,4,6,128]{4,2,3,1,0:T(4,128)S(1)}, u32[]{:S(2)}, u32[]{:S(2)}) async-start(f32[8,4,4,6,128]{4,2,3,1,0:T(4,128)} %broadcast_in_dim.43), calls=%async_computation | async-start | bytes 786432 | tf_op jit(solution)/shard_map/all_to_all | solution.py:63
  11.3 4.6 %collective-permute-start = (f32[5,4,128]{2,1,0:T(4,128)S(1)}, f32[5,4,128]{2,1,0:T(4,128)S(1)}, u32[]{:S(2)}, u32[]{:S(2)}) collective-permute-start(f32[5,4,128]{2,1,0:T(4,128)S(1)} %constant_dynamic-update-slice_fusion), channel_id=1, source_target_pairs={{0,32},{32,64},{64,96},{96,128},{128,160},{160,192},{192,224},{1,3... | collective-permute-start | bytes 30728 | tf_op jit(solution)/shard_map/ppermute | solution.py:46
  16.0 1.9 collective-permute-start.1
  25.2 7.8 %scatter_fusion = f32[8,4,48,128]{3,2,1,0:T(8,128)S(1)} fusion(f32[8,4,48,128]{3,2,1,0:T(8,128)S(1)} %broadcast_in_dim.44, s32[96]{0:T(128)S(1)} %fusion.365, f32[96]{0:T(128)S(1)} %copy-done.211), kind=kCustom, calls=%fused_computation | custom fusion | flops 96 | bytes 2688 | tf_op jit(solution)/shard_map/scatter-add | solution.py:264
  40.6 2.0 add_select_fusion.10
  48.5 3.8 %collective-permute-start.3 = (f32[414,128]{1,0:T(8,128)}, f32[414,128]{1,0:T(8,128)}, u32[]{:S(2)}, u32[]{:S(2)}) collective-permute-start(f32[414,128]{1,0:T(8,128)} %pad_maximum_fusion.9), channel_id=1, source_target_pairs={{0,15},{1,0},{2,1},{3,2},{4,3},{5,4},{6,5},{7,6},{8,7},{9,8},{10,9... | collective-permute-start | bytes 635912 | tf_op jit(solution)/shard_map/ppermute | solution.py:52
  52.4 1.4 reshape_stack_squeeze.39
  55.7 3.9 %fusion.25 = (f32[8,4,47,128]{3,2,1,0:T(8,128)}, f32[8,4,47,128]{3,2,1,0:T(8,128)}) fusion(f32[8,4,48,128]{3,2,1,0:T(8,128)} %get-tuple-element.132, f32[8,4,48,128]{3,2,1,0:T(8,128)} %get-tuple-element.131, f32[8,4,48,128]{3,2,1,0:T(8,128)S(1)} %get-tuple-element.130, f32[4,47,128]{2,1,0:T(8,128)} %get-tuple-element.217, f32[4,47,128]{2,1,0:T(8,128)} %bitcast.910, ...), kind=kLoop, calls=%fused_computation.41 | loop fusion | flops 2310144 | bytes 6593536 | tf_op jit(solution)/shard_map/jit(_where)/select_n | solution.py:142
  68.6 6.0 %collective-permute-start.4 = (f32[1656]{0:T(1024)S(1)}, f32[1656]{0:T(1024)S(1)}, u32[]{:S(2)}, u32[]{:S(2)}) collective-permute-start(f32[1656]{0:T(1024)S(1)} %pad_maximum_fusion.65), channel_id=1, source_target_pairs={{0,16},{1,17},{2,18},{3,19},{4,20},{5,21},{6,22},{7,23},{8,24},{9,... | collective-permute-start | bytes 19880 | tf_op jit(solution)/shard_map/ppermute | solution.py:46
  74.7 1.7 slice.1728
  76.4 1.6 slice.1727
  85.4 7.8 %all-to-all-start.1 = ((f32[8,4,4,6,128]{4,2,3,1,0:T(4,128)}), f32[8,4,4,6,128]{4,2,3,1,0:T(4,128)S(1)}, u32[]{:S(2)}, u32[]{:S(2)}) async-start(f32[8,4,4,6,128]{4,2,3,1,0:T(4,128)} %broadcast_in_dim.49), calls=%async_computation.1 | async-start | bytes 786432 | tf_op jit(solution)/shard_map/all_to_all | solution.py:63
  93.2 4.6 %collective-permute-start.6 = (f32[5,4,128]{2,1,0:T(4,128)S(1)}, f32[5,4,128]{2,1,0:T(4,128)S(1)}, u32[]{:S(2)}, u32[]{:S(2)}) collective-permute-start(f32[5,4,128]{2,1,0:T(4,128)S(1)} %constant_dynamic-update-slice_fusion.20), channel_id=1, source_target_pairs={{0,32},{32,64},{64,96},{96,128},{128,160},{160,192},{192,224},{1,3... | collective-permute-start | bytes 30728 | tf_op jit(solution)/shard_map/ppermute | solution.py:46
  101.3 1.5 broadcast_in_dim_squeeze_reshape.49
  102.9 1.5 broadcast_in_dim_squeeze_reshape.48
  104.4 2.1 collective-permute-start.7
  107.7 3.4 %collective-permute-done.7 = f32[5,4,128]{2,1,0:T(4,128)S(1)} collective-permute-done((f32[5,4,128]{2,1,0:T(4,128)S(1)}, f32[5,4,128]{2,1,0:T(4,128)S(1)}, u32[]{:S(2)}, u32[]{:S(2)}) %collective-permute-start.7) | collective-permute-done | bytes 10272 | tf_op jit(solution)/shard_map/ppermute | solution.py:46
  117.8 4.2 %add_select_fusion.6 = (f32[8,4,48,128]{3,2,1,0:T(8,128)}, f32[8,4,48,128]{3,2,1,0:T(8,128)S(1)}) fusion(f32[4,48,128]{2,1,0:T(8,128)S(1)} %get-tuple-element.154, f32[4,48,128]{2,1,0:T(8,128)S(1)} %copy.645, pred[4,48,128]{2,1,0:T(8,128)(4,1)S(1)} %or_or_fusion, f32[8,4,48,1]{3,2,1,0:T(8,128)} %broadcast_in_dim_squeeze_reshape.49, ...), kind=kLoop, calls=%fused_computation.65 | loop fusion | flops 6291456 | bytes 8249344 | tf_op jit(solution)/shard_map/jit(_where)/select_n | solution.py:142
  128.2 3.9 %collective-permute-start.9 = (f32[414,128]{1,0:T(8,128)}, f32[414,128]{1,0:T(8,128)}, u32[]{:S(2)}, u32[]{:S(2)}) collective-permute-start(f32[414,128]{1,0:T(8,128)} %pad_maximum_fusion.11), channel_id=1, source_target_pairs={{0,15},{1,0},{2,1},{3,2},{4,3},{5,4},{6,5},{7,6},{8,7},{9,8},{10,9... | collective-permute-start | bytes 635912 | tf_op jit(solution)/shard_map/ppermute | solution.py:52
  133.4 3.8 %pad_select_fusion.3 = (f32[8,4,47,128]{3,2,1,0:T(8,128)}, f32[8,4,47,128]{3,2,1,0:T(8,128)}) fusion(f32[8,4,47,128]{3,2,1,0:T(8,128)} %get-tuple-element.123, f32[8,4,48,128]{3,2,1,0:T(8,128)S(1)} %get-tuple-element.67, f32[8,4,47,128]{3,2,1,0:T(8,128)} %get-tuple-element.122, f32[8,4,48,128]{3,2,1,0:T(8,128)S(1)} %get-tuple-element.130, ...), kind=kLoop, calls=%fused_computation.22 | loop fusion | flops 2310144 | bytes 6593536 | tf_op jit(solution)/shard_map/jit(_where)/select_n | solution.py:142
  145.6 6.0 %collective-permute-start.10 = (f32[1656]{0:T(1024)S(1)}, f32[1656]{0:T(1024)S(1)}, u32[]{:S(2)}, u32[]{:S(2)}) collective-permute-start(f32[1656]{0:T(1024)S(1)} %pad_maximum_fusion.67), channel_id=1, source_target_pairs={{0,16},{1,17},{2,18},{3,19},{4,20},{5,21},{6,22},{7,23},{8,24},{9,... | collective-permute-start | bytes 19880 | tf_op jit(solution)/shard_map/ppermute | solution.py:46
  151.8 1.6 slice.1840
  153.6 1.7 slice.1839
  161.3 5.2 %all-to-all-start.2 = ((f32[8,4,4,6,128]{4,2,3,1,0:T(4,128)}), f32[8,4,4,6,128]{4,2,3,1,0:T(4,128)S(1)}, u32[]{:S(2)}, u32[]{:S(2)}) async-start(f32[8,4,4,6,128]{4,2,3,1,0:T(4,128)} %broadcast_in_dim.50), calls=%async_computation.2 | async-start | bytes 786432 | tf_op jit(solution)/shard_map/all_to_all | solution.py:63
  168.1 4.6 %collective-permute-start.12 = (f32[5,4,128]{2,1,0:T(4,128)S(1)}, f32[5,4,128]{2,1,0:T(4,128)S(1)}, u32[]{:S(2)}, u32[]{:S(2)}) collective-permute-start(f32[5,4,128]{2,1,0:T(4,128)S(1)} %constant_dynamic-update-slice_fusion.40), channel_id=1, source_target_pairs={{0,32},{32,64},{64,96},{96,128},{128,160},{160,192},{192,224},{1,3... | collective-permute-start | bytes 30728 | tf_op jit(solution)/shard_map/ppermute | solution.py:46
  178.3 1.5 broadcast_in_dim_squeeze_reshape.51
  179.8 1.5 broadcast_in_dim_squeeze_reshape.50
  181.3 2.1 collective-permute-start.13
  184.2 3.9 %collective-permute-done.13 = f32[5,4,128]{2,1,0:T(4,128)S(1)} collective-permute-done((f32[5,4,128]{2,1,0:T(4,128)S(1)}, f32[5,4,128]{2,1,0:T(4,128)S(1)}, u32[]{:S(2)}, u32[]{:S(2)}) %collective-permute-start.13) | collective-permute-done | bytes 10272 | tf_op jit(solution)/shard_map/ppermute | solution.py:46
  195.8 3.8 %add_select_fusion = (f32[8,4,48,128]{3,2,1,0:T(8,128)S(1)}, f32[8,4,48,128]{3,2,1,0:T(8,128)S(1)}) fusion(f32[4,48,128]{2,1,0:T(8,128)S(1)} %get-tuple-element.148, f32[4,48,128]{2,1,0:T(8,128)S(1)} %copy.708, pred[4,48,128]{2,1,0:T(8,128)(4,1)S(1)} %or_or_fusion, f32[8,4,48,1]{3,2,1,0:T(8,128)} %broadcast_in_dim_squeeze_reshape.51, ...), kind=kLoop, calls=%fused_computation.58 | loop fusion | flops 7471104 | bytes 9232384 | tf_op jit(solution)/shard_map/jit(_where)/select_n | solution.py:142
  199.7 1.7 add_select_fusion.2
  206.8 3.8 %collective-permute-start.15 = (f32[414,128]{1,0:T(8,128)}, f32[414,128]{1,0:T(8,128)}, u32[]{:S(2)}, u32[]{:S(2)}) collective-permute-start(f32[414,128]{1,0:T(8,128)} %pad_maximum_fusion.13), channel_id=1, source_target_pairs={{0,15},{1,0},{2,1},{3,2},{4,3},{5,4},{6,5},{7,6},{8,7},{9,8},{10,9... | collective-permute-start | bytes 635912 | tf_op jit(solution)/shard_map/ppermute | solution.py:52
  211.3 2.3 slice_reduce_fusion.1
  213.6 1.4 reshape_stack_squeeze.46
  215.0 3.8 %pad_select_fusion.1 = (f32[8,4,47,128]{3,2,1,0:T(8,128)}, f32[8,4,47,128]{3,2,1,0:T(8,128)}) fusion(f32[8,4,47,128]{3,2,1,0:T(8,128)} %get-tuple-element.121, f32[8,4,48,128]{3,2,1,0:T(8,128)S(1)} %get-tuple-element.26, f32[8,4,47,128]{3,2,1,0:T(8,128)} %get-tuple-element.120, f32[8,4,48,128]{3,2,1,0:T(8,128)S(1)} %get-tuple-element.130, ...), kind=kLoop, calls=%fused_computation.8 | loop fusion | flops 2310144 | bytes 6593536 | tf_op jit(solution)/shard_map/jit(_where)/select_n | solution.py:142
  219.7 1.4 slice_bitcast_fusion
  229.3 6.0 %collective-permute-start.16 = (f32[1656]{0:T(1024)S(1)}, f32[1656]{0:T(1024)S(1)}, u32[]{:S(2)}, u32[]{:S(2)}) collective-permute-start(f32[1656]{0:T(1024)S(1)} %pad_maximum_fusion.69), channel_id=1, source_target_pairs={{0,16},{1,17},{2,18},{3,19},{4,20},{5,21},{6,22},{7,23},{8,24},{9,... | collective-permute-start | bytes 19880 | tf_op jit(solution)/shard_map/ppermute | solution.py:46
  239.9 1.6 slice.1937
  241.5 1.6 slice.1934
  243.2 1.5 broadcast_in_dim_squeeze_reshape.53
  244.8 1.5 broadcast_in_dim_squeeze_reshape.52
  249.8 1.4 copy.746
  251.3 1.4 fusion.291
  252.7 1.3 copy.745
  254.0 1.4 fusion.293
  255.4 1.4 copy.744
  256.8 1.4 fusion.295
  258.2 1.4 copy.743
  259.5 1.4 fusion.297
  261.7 1.4 fusion.299
  266.7 1.3 copy.727
  269.5 1.4 constant_dynamic-update-slice_fusion.81
  272.2 1.3 constant_dynamic-update-slice_fusion.79
  273.5 1.3 constant_dynamic-update-slice_fusion.78
  274.8 1.3 constant_dynamic-update-slice_fusion.77
  276.7 1.3 constant_dynamic-update-slice_fusion.75
  278.0 1.3 constant_dynamic-update-slice_fusion.74
  279.4 1.3 constant_dynamic-update-slice_fusion.73
  280.7 1.3 constant_dynamic-update-slice_fusion.72
  282.0 1.3 constant_dynamic-update-slice_fusion.71
  283.3 1.3 constant_dynamic-update-slice_fusion.70
  288.5 1.3 constant_dynamic-update-slice_fusion.66
  291.1 1.7 copy.771
  292.8 4.8 %fusion.30 = f32[8,4,48,128]{3,2,1,0:T(8,128)} fusion(f32[8,4,48,127]{3,2,1,0:T(8,128)S(1)} %bitcast.874, f32[8,4,48,1]{3,2,1,0:T(8,128)} %broadcast_in_dim_squeeze_reshape.52, f32[8,4,48,1]{3,2,1,0:T(8,128)} %broadcast_in_dim_squeeze_reshape.53, f32[8,4,48,127]{3,2,1,0:T(8,128)} %slice.1932, f32[8,3,48,128]{3,2,1,0:T(8,128)} %slice.1935, ...), kind=kLoop, calls=%fused_computation.57 | loop fusion | flops 7274496 | bytes 9232384 | tf_op jit(solution)/shard_map/add | solution.py:283
  (872 shorter events, 125.6 us)
Async XLA Ops:
  2.5 8.7 %copy-start.27 = (f32[4,6,128]{2,0,1:T(4,128)}, f32[4,6,128]{2,0,1:T(4,128)S(1)}, u32[]{:S(2)}) copy-start(f32[4,6,128]{2,0,1:T(4,128)S(1)} %get-tuple-element.89) | copy-start | bytes 36868
  2.5 16.6 %copy-start.83 = (f32[4,6,128]{2,0,1:T(4,128)}, f32[4,6,128]{2,0,1:T(4,128)S(1)}, u32[]{:S(2)}) copy-start(f32[4,6,128]{2,0,1:T(4,128)S(1)} %get-tuple-element.88) | copy-start | bytes 36868
  2.7 21.8 %copy-start.65 = (f32[4,6,128]{2,0,1:T(4,128)}, f32[4,6,128]{2,0,1:T(4,128)S(1)}, u32[]{:S(2)}) copy-start(f32[4,6,128]{2,0,1:T(4,128)S(1)} %get-tuple-element.171) | copy-start | bytes 36868
  3.5 35.5 %all-to-all-start = ((f32[8,4,4,6,128]{4,2,3,1,0:T(4,128)}), f32[8,4,4,6,128]{4,2,3,1,0:T(4,128)S(1)}, u32[]{:S(2)}, u32[]{:S(2)}) async-start(f32[8,4,4,6,128]{4,2,3,1,0:T(4,128)} %broadcast_in_dim.43), calls=%async_computation | async-start | bytes 786432 | tf_op jit(solution)/shard_map/all_to_all | solution.py:63
  11.2 13.3 %copy-start.35 = (f32[4,6,128]{2,0,1:T(4,128)}, f32[4,6,128]{2,0,1:T(4,128)S(1)}, u32[]{:S(2)}) copy-start(f32[4,6,128]{2,0,1:T(4,128)S(1)} %get-tuple-element.181) | copy-start | bytes 36868
  11.3 13.2 %copy-start.67 = (f32[4,6,128]{2,0,1:T(4,128)}, f32[4,6,128]{2,0,1:T(4,128)S(1)}, u32[]{:S(2)}) copy-start(f32[4,6,128]{2,0,1:T(4,128)S(1)} %get-tuple-element.176) | copy-start | bytes 36868
  11.3 21.6 %collective-permute-start = (f32[5,4,128]{2,1,0:T(4,128)S(1)}, f32[5,4,128]{2,1,0:T(4,128)S(1)}, u32[]{:S(2)}, u32[]{:S(2)}) collective-permute-start(f32[5,4,128]{2,1,0:T(4,128)S(1)} %constant_dynamic-update-slice_fusion), channel_id=1, source_target_pairs={{0,32},{32,64},{64,96},{96,128},{128,160},{160,192},{192,224},{1,3... | collective-permute-start | bytes 30728 | tf_op jit(solution)/shard_map/ppermute | solution.py:46
  16.0 18.1 %collective-permute-start.1 = (f32[5,4,128]{2,1,0:T(4,128)S(1)}, f32[5,4,128]{2,1,0:T(4,128)S(1)}, u32[]{:S(2)}, u32[]{:S(2)}) collective-permute-start(f32[5,4,128]{2,1,0:T(4,128)S(1)} %constant_dynamic-update-slice_fusion.5), channel_id=1, source_target_pairs={{32,0},{64,32},{96,64},{128,96},{160,128},{192,160},{224,192},{33,... | collective-permute-start | bytes 30728 | tf_op jit(solution)/shard_map/ppermute | solution.py:46
  20.7 12.8 %copy-start.115 = (f32[4,5,128]{2,0,1:T(4,128)}, f32[4,5,128]{2,0,1:T(4,128)S(1)}, u32[]{:S(2)}) copy-start(f32[4,5,128]{2,0,1:T(4,128)S(1)} %slice.1682) | copy-start | bytes 30724
  21.3 15.4 %copy-start.121 = (f32[4,5,128]{2,0,1:T(4,128)}, f32[4,5,128]{2,0,1:T(4,128)S(1)}, u32[]{:S(2)}) copy-start(f32[4,5,128]{2,0,1:T(4,128)S(1)} %slice.1677) | copy-start | bytes 30724
  21.3 16.1 %copy-start.123 = (f32[4,5,128]{2,0,1:T(4,128)}, f32[4,5,128]{2,0,1:T(4,128)S(1)}, u32[]{:S(2)}) copy-start(f32[4,5,128]{2,0,1:T(4,128)S(1)} %slice.1656) | copy-start | bytes 30724
  22.0 16.3 %copy-start.127 = (f32[4,5,128]{2,0,1:T(4,128)}, f32[4,5,128]{2,0,1:T(4,128)S(1)}, u32[]{:S(2)}) copy-start(f32[4,5,128]{2,0,1:T(4,128)S(1)} %slice.1659) | copy-start | bytes 30724
  42.6 11.2 %copy-start.5 = (f32[8,4,48,128]{3,2,1,0:T(8,128)}, f32[8,4,48,128]{3,2,1,0:T(8,128)S(1)}, u32[]{:S(2)}) copy-start(f32[8,4,48,128]{3,2,1,0:T(8,128)S(1)} %get-tuple-element.128) | copy-start | bytes 2359300
  47.8 11.8 %collective-permute-start.2 = (f32[414,128]{1,0:T(8,128)}, f32[414,128]{1,0:T(8,128)}, u32[]{:S(2)}, u32[]{:S(2)}) collective-permute-start(f32[414,128]{1,0:T(8,128)} %pad_maximum_fusion.8), channel_id=1, source_target_pairs={{0,1},{1,2},{2,3},{3,4},{4,5},{5,6},{6,7},{7,8},{8,9},{9,10},{10,1... | collective-permute-start | bytes 635912 | tf_op jit(solution)/shard_map/ppermute | solution.py:52
  48.5 12.0 %collective-permute-start.3 = (f32[414,128]{1,0:T(8,128)}, f32[414,128]{1,0:T(8,128)}, u32[]{:S(2)}, u32[]{:S(2)}) collective-permute-start(f32[414,128]{1,0:T(8,128)} %pad_maximum_fusion.9), channel_id=1, source_target_pairs={{0,15},{1,0},{2,1},{3,2},{4,3},{5,4},{6,5},{7,6},{8,7},{9,8},{10,9... | collective-permute-start | bytes 635912 | tf_op jit(solution)/shard_map/ppermute | solution.py:52
  64.2 13.9 %collective-permute-start.5 = (f32[1656]{0:T(1024)S(1)}, f32[1656]{0:T(1024)S(1)}, u32[]{:S(2)}, u32[]{:S(2)}) collective-permute-start(f32[1656]{0:T(1024)S(1)} %pad_maximum_fusion.66), channel_id=1, source_target_pairs={{16,0},{17,1},{18,2},{19,3},{20,4},{21,5},{22,6},{23,7},{24,8},{25... | collective-permute-start | bytes 19880 | tf_op jit(solution)/shard_map/ppermute | solution.py:46
  68.6 10.8 %collective-permute-start.4 = (f32[1656]{0:T(1024)S(1)}, f32[1656]{0:T(1024)S(1)}, u32[]{:S(2)}, u32[]{:S(2)}) collective-permute-start(f32[1656]{0:T(1024)S(1)} %pad_maximum_fusion.65), channel_id=1, source_target_pairs={{0,16},{1,17},{2,18},{3,19},{4,20},{5,21},{6,22},{7,23},{8,24},{9,... | collective-permute-start | bytes 19880 | tf_op jit(solution)/shard_map/ppermute | solution.py:46
  82.6 16.6 %copy-start.81 = (f32[4,6,128]{2,0,1:T(4,128)}, f32[4,6,128]{2,0,1:T(4,128)S(1)}, u32[]{:S(2)}) copy-start(f32[4,6,128]{2,0,1:T(4,128)S(1)} %get-tuple-element.47) | copy-start | bytes 36868
  82.6 23.8 %copy-start.63 = (f32[8,3,128]{2,0,1:T(8,128)}, f32[8,3,128]{2,0,1:T(8,128)S(1)}, u32[]{:S(2)}) copy-start(f32[8,3,128]{2,0,1:T(8,128)S(1)} %get-tuple-element.345) | copy-start | bytes 36868
  82.6 23.8 %copy-start.61 = (f32[8,3,128]{2,0,1:T(8,128)}, f32[8,3,128]{2,0,1:T(8,128)S(1)}, u32[]{:S(2)}) copy-start(f32[8,3,128]{2,0,1:T(8,128)S(1)} %get-tuple-element.338) | copy-start | bytes 36868
  85.4 30.7 %all-to-all-start.1 = ((f32[8,4,4,6,128]{4,2,3,1,0:T(4,128)}), f32[8,4,4,6,128]{4,2,3,1,0:T(4,128)S(1)}, u32[]{:S(2)}, u32[]{:S(2)}) async-start(f32[8,4,4,6,128]{4,2,3,1,0:T(4,128)} %broadcast_in_dim.49), calls=%async_computation.1 | async-start | bytes 786432 | tf_op jit(solution)/shard_map/all_to_all | solution.py:63
  93.1 22.2 %copy-start.113 = (f32[4,5,128]{2,0,1:T(4,128)}, f32[4,5,128]{2,0,1:T(4,128)S(1)}, u32[]{:S(2)}) copy-start(f32[4,5,128]{2,0,1:T(4,128)S(1)} %slice.1768) | copy-start | bytes 30724
  93.2 13.3 %collective-permute-start.6 = (f32[5,4,128]{2,1,0:T(4,128)S(1)}, f32[5,4,128]{2,1,0:T(4,128)S(1)}, u32[]{:S(2)}, u32[]{:S(2)}) collective-permute-start(f32[5,4,128]{2,1,0:T(4,128)S(1)} %constant_dynamic-update-slice_fusion.20), channel_id=1, source_target_pairs={{0,32},{32,64},{64,96},{96,128},{128,160},{160,192},{192,224},{1,3... | collective-permute-start | bytes 30728 | tf_op jit(solution)/shard_map/ppermute | solution.py:46
  99.4 7.1 %copy-start.37 = (f32[4,6,128]{2,0,1:T(4,128)}, f32[4,6,128]{2,0,1:T(4,128)S(1)}, u32[]{:S(2)}) copy-start(f32[4,6,128]{2,0,1:T(4,128)S(1)} %get-tuple-element.225) | copy-start | bytes 36868
  100.0 7.1 %copy-start.117 = (f32[4,5,128]{2,0,1:T(4,128)}, f32[4,5,128]{2,0,1:T(4,128)S(1)}, u32[]{:S(2)}) copy-start(f32[4,5,128]{2,0,1:T(4,128)S(1)} %slice.1794) | copy-start | bytes 30724
  100.0 11.7 %copy-start.119 = (f32[4,5,128]{2,0,1:T(4,128)}, f32[4,5,128]{2,0,1:T(4,128)S(1)}, u32[]{:S(2)}) copy-start(f32[4,5,128]{2,0,1:T(4,128)S(1)} %slice.1789) | copy-start | bytes 30724
  101.2 13.3 %copy-start.125 = (f32[4,5,128]{2,0,1:T(4,128)}, f32[4,5,128]{2,0,1:T(4,128)S(1)}, u32[]{:S(2)}) copy-start(f32[4,5,128]{2,0,1:T(4,128)S(1)} %slice.1771) | copy-start | bytes 30724
  104.4 6.8 %collective-permute-start.7 = (f32[5,4,128]{2,1,0:T(4,128)S(1)}, f32[5,4,128]{2,1,0:T(4,128)S(1)}, u32[]{:S(2)}, u32[]{:S(2)}) collective-permute-start(f32[5,4,128]{2,1,0:T(4,128)S(1)} %constant_dynamic-update-slice_fusion.25), channel_id=1, source_target_pairs={{32,0},{64,32},{96,64},{128,96},{160,128},{192,160},{224,192},{33,... | collective-permute-start | bytes 30728 | tf_op jit(solution)/shard_map/ppermute | solution.py:46
  107.1 6.6 %copy-start.91 = (f32[4,1,128]{2,0,1:T(4,128)}, f32[4,1,128]{2,0,1:T(4,128)S(1)}, u32[]{:S(2)}) copy-start(f32[4,1,128]{2,0,1:T(4,128)S(1)} %get-tuple-element.307) | copy-start | bytes 6148
  107.1 6.7 %copy-start.99 = (f32[4,1,128]{2,0,1:T(4,128)}, f32[4,1,128]{2,0,1:T(4,128)S(1)}, u32[]{:S(2)}) copy-start(f32[4,1,128]{2,0,1:T(4,128)S(1)} %get-tuple-element.306) | copy-start | bytes 6148
  107.1 8.2 %copy-start.158 = (f32[4,1,128]{2,0,1:T(4,128)}, f32[4,1,128]{2,0,1:T(4,128)S(1)}, u32[]{:S(2)}) copy-start(f32[4,1,128]{2,0,1:T(4,128)S(1)} %get-tuple-element.305) | copy-start | bytes 6148
  126.1 6.0 %copy-start.3 = (f32[8,4,48,128]{3,2,1,0:T(8,128)S(1)}, f32[8,4,48,128]{3,2,1,0:T(8,128)}, u32[]{:S(2)}) copy-start(f32[8,4,48,128]{3,2,1,0:T(8,128)} %get-tuple-element.66) | copy-start | bytes 2359300
  127.5 9.7 %collective-permute-start.8 = (f32[414,128]{1,0:T(8,128)}, f32[414,128]{1,0:T(8,128)}, u32[]{:S(2)}, u32[]{:S(2)}) collective-permute-start(f32[414,128]{1,0:T(8,128)} %pad_maximum_fusion.10), channel_id=1, source_target_pairs={{0,1},{1,2},{2,3},{3,4},{4,5},{5,6},{6,7},{7,8},{8,9},{9,10},{10,1... | collective-permute-start | bytes 635912 | tf_op jit(solution)/shard_map/ppermute | solution.py:52
  128.2 9.9 %collective-permute-start.9 = (f32[414,128]{1,0:T(8,128)}, f32[414,128]{1,0:T(8,128)}, u32[]{:S(2)}, u32[]{:S(2)}) collective-permute-start(f32[414,128]{1,0:T(8,128)} %pad_maximum_fusion.11), channel_id=1, source_target_pairs={{0,15},{1,0},{2,1},{3,2},{4,3},{5,4},{6,5},{7,6},{8,7},{9,8},{10,9... | collective-permute-start | bytes 635912 | tf_op jit(solution)/shard_map/ppermute | solution.py:52
  141.2 14.0 %collective-permute-start.11 = (f32[1656]{0:T(1024)S(1)}, f32[1656]{0:T(1024)S(1)}, u32[]{:S(2)}, u32[]{:S(2)}) collective-permute-start(f32[1656]{0:T(1024)S(1)} %pad_maximum_fusion.68), channel_id=1, source_target_pairs={{16,0},{17,1},{18,2},{19,3},{20,4},{21,5},{22,6},{23,7},{24,8},{25... | collective-permute-start | bytes 19880 | tf_op jit(solution)/shard_map/ppermute | solution.py:46
  145.6 10.9 %collective-permute-start.10 = (f32[1656]{0:T(1024)S(1)}, f32[1656]{0:T(1024)S(1)}, u32[]{:S(2)}, u32[]{:S(2)}) collective-permute-start(f32[1656]{0:T(1024)S(1)} %pad_maximum_fusion.67), channel_id=1, source_target_pairs={{0,16},{1,17},{2,18},{3,19},{4,20},{5,21},{6,22},{7,23},{8,24},{9,... | collective-permute-start | bytes 19880 | tf_op jit(solution)/shard_map/ppermute | solution.py:46
  153.4 4.5 %copy-start.82 = (f32[4,6,128]{2,0,1:T(4,128)S(1)}, f32[4,6,128]{2,0,1:T(4,128)}, u32[]{:S(2)}) copy-start(f32[4,6,128]{2,0,1:T(4,128)} %copy-done.81) | copy-start | bytes 36868
  160.4 23.1 %copy-start.57 = (f32[4,6,128]{2,0,1:T(4,128)}, f32[4,6,128]{2,0,1:T(4,128)S(1)}, u32[]{:S(2)}) copy-start(f32[4,6,128]{2,0,1:T(4,128)S(1)} %get-tuple-element.254) | copy-start | bytes 36868
  160.4 23.1 %copy-start.59 = (f32[4,6,128]{2,0,1:T(4,128)}, f32[4,6,128]{2,0,1:T(4,128)S(1)}, u32[]{:S(2)}) copy-start(f32[4,6,128]{2,0,1:T(4,128)S(1)} %get-tuple-element.232) | copy-start | bytes 36868
  161.3 5.2 %copy-start.148 = (f32[4,6,128]{2,0,1:T(4,128)S(1)}, f32[4,6,128]{2,0,1:T(4,128)}, u32[]{:S(2)}) copy-start(f32[4,6,128]{2,0,1:T(4,128)} %get-tuple-element.40) | copy-start | bytes 36868
  161.3 5.2 %copy-start.149 = (f32[4,6,128]{2,0,1:T(4,128)S(1)}, f32[4,6,128]{2,0,1:T(4,128)}, u32[]{:S(2)}) copy-start(f32[4,6,128]{2,0,1:T(4,128)} %get-tuple-element.15) | copy-start | bytes 36868
  161.3 5.2 %copy-start.150 = (f32[4,6,128]{2,0,1:T(4,128)S(1)}, f32[4,6,128]{2,0,1:T(4,128)}, u32[]{:S(2)}) copy-start(f32[4,6,128]{2,0,1:T(4,128)} %get-tuple-element.16) | copy-start | bytes 36868
  161.3 32.7 %all-to-all-start.2 = ((f32[8,4,4,6,128]{4,2,3,1,0:T(4,128)}), f32[8,4,4,6,128]{4,2,3,1,0:T(4,128)S(1)}, u32[]{:S(2)}, u32[]{:S(2)}) async-start(f32[8,4,4,6,128]{4,2,3,1,0:T(4,128)} %broadcast_in_dim.50), calls=%async_computation.2 | async-start | bytes 786432 | tf_op jit(solution)/shard_map/all_to_all | solution.py:63
  168.1 15.5 %collective-permute-start.12 = (f32[5,4,128]{2,1,0:T(4,128)S(1)}, f32[5,4,128]{2,1,0:T(4,128)S(1)}, u32[]{:S(2)}, u32[]{:S(2)}) collective-permute-start(f32[5,4,128]{2,1,0:T(4,128)S(1)} %constant_dynamic-update-slice_fusion.40), channel_id=1, source_target_pairs={{0,32},{32,64},{64,96},{96,128},{128,160},{160,192},{192,224},{1,3... | collective-permute-start | bytes 30728 | tf_op jit(solution)/shard_map/ppermute | solution.py:46
  172.7 10.8 %copy-start.134 = (f32[4,6,128]{2,0,1:T(4,128)}, f32[4,6,128]{2,0,1:T(4,128)S(1)}, u32[]{:S(2)}) copy-start(f32[4,6,128]{2,0,1:T(4,128)S(1)} %get-tuple-element.220) | copy-start | bytes 36868
  175.6 8.1 %copy-start.107 = (f32[4,5,128]{2,0,1:T(4,128)}, f32[4,5,128]{2,0,1:T(4,128)S(1)}, u32[]{:S(2)}) copy-start(f32[4,5,128]{2,0,1:T(4,128)S(1)} %slice.1904) | copy-start | bytes 30724
  175.6 12.5 %copy-start.104 = (f32[4,5,128]{2,0,1:T(4,128)}, f32[4,5,128]{2,0,1:T(4,128)S(1)}, u32[]{:S(2)}) copy-start(f32[4,5,128]{2,0,1:T(4,128)S(1)} %slice.1899) | copy-start | bytes 30724
  175.6 13.1 %copy-start.111 = (f32[4,5,128]{2,0,1:T(4,128)}, f32[4,5,128]{2,0,1:T(4,128)S(1)}, u32[]{:S(2)}) copy-start(f32[4,5,128]{2,0,1:T(4,128)S(1)} %slice.1831) | copy-start | bytes 30724
  175.6 13.1 %copy-start.109 = (f32[4,5,128]{2,0,1:T(4,128)}, f32[4,5,128]{2,0,1:T(4,128)S(1)}, u32[]{:S(2)}) copy-start(f32[4,5,128]{2,0,1:T(4,128)S(1)} %slice.1830) | copy-start | bytes 30724
  176.3 15.1 %copy-start.106 = (f32[4,5,128]{2,0,1:T(4,128)}, f32[4,5,128]{2,0,1:T(4,128)S(1)}, u32[]{:S(2)}) copy-start(f32[4,5,128]{2,0,1:T(4,128)S(1)} %slice.1881) | copy-start | bytes 30724
  176.3 15.8 %copy-start.105 = (f32[4,5,128]{2,0,1:T(4,128)}, f32[4,5,128]{2,0,1:T(4,128)S(1)}, u32[]{:S(2)}) copy-start(f32[4,5,128]{2,0,1:T(4,128)S(1)} %slice.1878) | copy-start | bytes 30724
  181.3 6.8 %collective-permute-start.13 = (f32[5,4,128]{2,1,0:T(4,128)S(1)}, f32[5,4,128]{2,1,0:T(4,128)S(1)}, u32[]{:S(2)}, u32[]{:S(2)}) collective-permute-start(f32[5,4,128]{2,1,0:T(4,128)S(1)} %constant_dynamic-update-slice_fusion.45), channel_id=1, source_target_pairs={{32,0},{64,32},{96,64},{128,96},{160,128},{192,160},{224,192},{33,... | collective-permute-start | bytes 30728 | tf_op jit(solution)/shard_map/ppermute | solution.py:46
  183.6 5.1 %copy-start.177 = (f32[4,1,128]{2,0,1:T(4,128)}, f32[4,1,128]{2,0,1:T(4,128)S(1)}, u32[]{:S(2)}) copy-start(f32[4,1,128]{2,0,1:T(4,128)S(1)} %get-tuple-element.292) | copy-start | bytes 6148
  183.6 7.1 %copy-start.181 = (f32[1,4,128]{2,1,0:T(4,128)}, f32[1,4,128]{2,1,0:T(4,128)S(1)}, u32[]{:S(2)}) copy-start(f32[1,4,128]{2,1,0:T(4,128)S(1)} %get-tuple-element.291) | copy-start | bytes 6148
  183.6 8.5 %copy-start.172 = (f32[4,1,128]{2,0,1:T(4,128)}, f32[4,1,128]{2,0,1:T(4,128)S(1)}, u32[]{:S(2)}) copy-start(f32[4,1,128]{2,0,1:T(4,128)S(1)} %get-tuple-element.290) | copy-start | bytes 6148
  206.1 12.6 %collective-permute-start.14 = (f32[414,128]{1,0:T(8,128)}, f32[414,128]{1,0:T(8,128)}, u32[]{:S(2)}, u32[]{:S(2)}) collective-permute-start(f32[414,128]{1,0:T(8,128)} %pad_maximum_fusion.12), channel_id=1, source_target_pairs={{0,1},{1,2},{2,3},{3,4},{4,5},{5,6},{6,7},{7,8},{8,9},{9,10},{10,1... | collective-permute-start | bytes 635912 | tf_op jit(solution)/shard_map/ppermute | solution.py:52
  206.8 12.9 %collective-permute-start.15 = (f32[414,128]{1,0:T(8,128)}, f32[414,128]{1,0:T(8,128)}, u32[]{:S(2)}, u32[]{:S(2)}) collective-permute-start(f32[414,128]{1,0:T(8,128)} %pad_maximum_fusion.13), channel_id=1, source_target_pairs={{0,15},{1,0},{2,1},{3,2},{4,3},{5,4},{6,5},{7,6},{8,7},{9,8},{10,9... | collective-permute-start | bytes 635912 | tf_op jit(solution)/shard_map/ppermute | solution.py:52
  223.9 19.3 %collective-permute-start.17 = (f32[1656]{0:T(1024)S(1)}, f32[1656]{0:T(1024)S(1)}, u32[]{:S(2)}, u32[]{:S(2)}) collective-permute-start(f32[1656]{0:T(1024)S(1)} %pad_maximum_fusion.70), channel_id=1, source_target_pairs={{16,0},{17,1},{18,2},{19,3},{20,4},{21,5},{22,6},{23,7},{24,8},{25... | collective-permute-start | bytes 19880 | tf_op jit(solution)/shard_map/ppermute | solution.py:46
  229.3 6.1 %copy-start.112 = (f32[4,5,128]{2,0,1:T(4,128)S(1)}, f32[4,5,128]{2,0,1:T(4,128)}, u32[]{:S(2)}) copy-start(f32[4,5,128]{2,0,1:T(4,128)} %copy-done.111) | copy-start | bytes 30724
  229.3 15.4 %collective-permute-start.16 = (f32[1656]{0:T(1024)S(1)}, f32[1656]{0:T(1024)S(1)}, u32[]{:S(2)}, u32[]{:S(2)}) collective-permute-start(f32[1656]{0:T(1024)S(1)} %pad_maximum_fusion.69), channel_id=1, source_target_pairs={{0,16},{1,17},{2,18},{3,19},{4,20},{5,21},{6,22},{7,23},{8,24},{9,... | collective-permute-start | bytes 19880 | tf_op jit(solution)/shard_map/ppermute | solution.py:46
  243.2 5.9 %copy-start.207 = (f32[5]{0:T(128)S(1)}, f32[5]{0:T(128)}, u32[]{:S(2)}) copy-start(f32[5]{0:T(128)} %constant.133.clone) | copy-start | bytes 64
  249.1 19.0 %copy-start.70 = (f32[4,6,128]{2,0,1:T(4,128)S(1)}, f32[4,6,128]{2,0,1:T(4,128)}, u32[]{:S(2)}) copy-start(f32[4,6,128]{2,0,1:T(4,128)} %copy-done.69) | copy-start | bytes 36868
  249.8 43.0 %copy-start.2 = (f32[8,4,48,128]{3,2,1,0:T(8,128)S(1)}, f32[8,4,48,128]{3,2,1,0:T(8,128)}, u32[]{:S(2)}) copy-start(f32[8,4,48,128]{3,2,1,0:T(8,128)} %param.13) | copy-start | bytes 2359300
  268.0 24.8 %copy-start.9 = (f32[8,4,48,128]{3,2,1,0:T(8,128)S(1)}, f32[8,4,48,128]{3,2,1,0:T(8,128)}, u32[]{:S(2)}) copy-start(f32[8,4,48,128]{3,2,1,0:T(8,128)} %get-tuple-element.124) | copy-start | bytes 2359300
  (171 other events, 299.3 us)
where the time goes:
time: 303 us; the launch traced here: 298 us
  local copies, waits for them, and re-layouts  145 us (48%)
  starting transfers between devices  74 us (24%)
  other arithmetic  67.7 us (22%)
  waiting for transfers between devices  7.4 us (2%)
  between operations  3.53 us (1%)
    unnamed x496, local copies, waits for them, and re-layouts  53.9 us
    ppermute x12, starting transfers between devices, passed_along(): return lax.ppermute(block, axis, route)  41.8 us
    select_n x8, other arithmetic, scalar_collide(): updated.append(jnp.where(solid, scalar[flow_mirror[member]], relaxed))  23.9 us
    all_to_all x3, starting transfers between devices, copy_for_each(): return lax.all_to_all(copies, axis, split_axis=0, concat_axis=0, tiled=True)  20.6 us
    slice x37, local copies, waits for them, and re-layouts, displace(): lax.slice_in_dim(piece, 1, length, axis=dimension)  16.8 us
    slice x63, local copies, waits for them, and re-layouts, edge_planes(): lax.index_in_dim(pieces[member], position, dimension, keepdims=False)  16 us
    another operation x16, other arithmetic, on_device(): stacked = jnp.stack(flow)  14.9 us
    another operation x24, local copies, waits for them, and re-layouts, displace(): entering = jnp.expand_dims(from_low[low_count], dimension)  12.9 us
  transfers between devices with their start and end apart: 21, of which 2 were waited for; matrix products, arithmetic and copies ran while one was open for 29% of the time, Pallas kernels for 0%

commit v1 on v0

--- a/solution.py
+++ b/solution.py
@@ -249,39 +249,38 @@
     local_y = cell_y - lax.axis_index("gy") * span_y
     local_x = cell_x - lax.axis_index("gx") * span_x
     local_scalar = source_scalar - row_index * scalars_here
-    inside = (
-        (local_y >= 0)
-        & (local_y < span_y)
-        & (local_x >= 0)
-        & (local_x < span_x)
-        & (local_scalar >= 0)
-        & (local_scalar < scalars_here)
-    )
-    target = jnp.where(inside, local_scalar, scalars_here)
-    source = (
-        jnp.zeros(concentration.shape, jnp.float32)
-        .at[target, local_y, cell_z, local_x]
-        .add(source_rate, mode="drop")
-    )
-    flow_solid = lax.dynamic_slice_in_dim(solid, row_index * slab_depth, slab_depth, 1)
-    flow = [flow_pops[member] for member in range(19)]
+    count = source_cell.shape[0]
+    plane_shape = (scalars_here, span_y, depth, count)
+    hit = (
+        (lax.broadcasted_iota(jnp.int32, plane_shape, 0) == local_scalar)
+        & (lax.broadcasted_iota(jnp.int32, plane_shape, 1) == local_y)
+        & (lax.broadcasted_iota(jnp.int32, plane_shape, 2) == cell_z)
+    )
+    weights = jnp.where(hit, source_rate, 0.0).reshape(-1, count)
+    columns = (
+        lax.broadcasted_iota(jnp.int32, (count, span_x), 1) == local_x[:, None]
+    ).astype(jnp.float32)
+    source = jnp.dot(
+        weights, columns, precision=lax.Precision.HIGHEST, preferred_element_type=jnp.float32
+    ).reshape(concentration.shape)
+    whole = lax.all_gather(flow_pops, "row", axis=2, tiled=True)
+    flow = [whole[member] for member in range(19)]
     scalar = [scalar_weights[member] * concentration for member in range(7)]
-    for time_step in range(STEPS):
-        flow, motion = flow_collide(flow, flow_solid)
-        column = gathered_copies(motion, "row", 2)
-        scalar = scalar_collide(
-            scalar, [column[component] for component in range(4)], solid, source
-        )
-        from_below = send_vertical(edge_planes(flow, flow_vectors, 2, 1, 1), 1)
-        from_above = send_vertical(edge_planes(flow, flow_vectors, 2, 1, -1), -1)
-        flow = displace(flow, flow_vectors, 2, 1, from_below, from_above)
+    def one_step(time_step, state):
+        flow, scalar = state
+        flow, motion = flow_collide(list(flow), solid)
+        scalar = scalar_collide(list(scalar), [motion[component] for component in range(4)], solid, source)
+        flow = local_vertical(flow, flow_vectors, 1)
         scalar = local_vertical(scalar, scalar_vectors, 2)
         flow, scalar = cross_section(flow, scalar, 1, 0, send_spanwise, keep_spanwise, True)
         flow, scalar = cross_section(flow, scalar, 0, 2, send_streamwise, inflow_fill, False)
+        return (tuple(flow), tuple(scalar))
+
+    flow, scalar = lax.fori_loop(0, STEPS, one_step, (tuple(flow), tuple(scalar)))
     amount = scalar[0]
     for member in range(1, 7):
         amount = amount + scalar[member]
-    stacked = jnp.stack(flow)
+    stacked = lax.dynamic_slice_in_dim(jnp.stack(flow), row_index * slab_depth, slab_depth, 2)
     return (stacked, amount)
 
 

time: 303 us -> 346 us (1.14)
  the two profiles are of different devices: /device:TPU:96 before, /device:TPU:7 now
where the time goes in v1:
time: 346 us; the launch traced here: 342 us
  local copies, waits for them, and re-layouts  132 us (38%)
  other arithmetic  122 us (35%)
  starting transfers between devices  35.8 us (10%)
  waiting for transfers between devices  34.1 us (10%)
  between operations  14.3 us (4%)
    all_gather x1, waiting for transfers between devices, on_device(): whole = lax.all_gather(flow_pops, 'row', axis=2, tiled=True)  34.1 us
    concatenate x30, other arithmetic, displace(): jnp.concatenate([lax.slice_in_dim(piece, 1, length, axis=dimension), ente...  33.5 us
    select_n x24, other arithmetic, flow_collide(): updated.append(jnp.where(solid, populations[flow_mirror[member]], relaxed))  29.2 us
    slice x39, local copies, waits for them, and re-layouts, displace(): lax.slice_in_dim(piece, 1, length, axis=dimension)  27.2 us
    concatenate x30, other arithmetic, displace(): jnp.concatenate([entering, lax.slice_in_dim(piece, 0, length - 1, axis=di...  23.2 us
    ppermute x6, starting transfers between devices, passed_along(): return lax.ppermute(block, axis, route)  22.1 us
    while x489, local copies, waits for them, and re-layouts  18.4 us
    unnamed x61, local copies, waits for them, and re-layouts  17 us
  transfers between devices with their start and end apart: 13, of which 1 were waited for; matrix products, arithmetic and copies ran while one was open for 36% of the time, Pallas kernels for 0%

profile of v1, /device:TPU:7, one launch (start us, length us, event | category | flops | bytes accessed | tf_op | source)
XLA Modules:
  0.0 342.2 jit_solution(17500929286192354240)
XLA Ops:
  7.2 1.7 copy.3655
  8.9 2.1 copy_multiply_fusion
  14.0 1.5 fusion.89
  15.5 34.1 %all-gather.2.cloned.1.call-done = f32[19,4,48,128]{3,1,0,2:T(4,128)} async-done(((f32[19,4,6,128]{3,1,0,2:T(4,128)}), f32[19,4,48,128]{3,1,0,2:T(4,128)}) %all-gather.2.cloned.1.call-update) | async-done | bytes 1867792 | tf_op jit(solution)/shard_map/all_gather | solution.py:266
  49.5 1.7 slice_bitcast_fusion.20
  56.6 269.4 %while.63 = (s32[]{:T(128)}, f32[4,48,128]{2,1,0:T(8,128)}, f32[4,48,128]{2,1,0:T(8,128)}, f32[4,48,128]{2,1,0:T(8,128)S(1)}, f32[4,48,128]{2,1,0:T(8,128)}, /*i...) while((s32[]{:T(128)}, f32[4,48,128]{2,1,0:T(8,128)}, ...), condition=%wide.region_1.2_spmd.clone, body=%wide.region_0.1_spmd.sunk.clone.sunk | while | flops 21975552 | bytes 121011608 | solution.py:279
  56.7 2.5 add_multiply_fusion.12
  59.4 2.5 subtract_select_fusion.12
  65.7 1.8 add_select_fusion.8
  70.5 4.9 %collective-permute-start.1 = (f32[624,128]{1,0:T(8,128)}, f32[624,128]{1,0:T(8,128)}, u32[]{:S(2)}, u32[]{:S(2)}) collective-permute-start(f32[624,128]{1,0:T(8,128)} %pad_maximum_fusion.45), channel_id=1, source_target_pairs={{0,15},{1,0},{2,1},{3,2},{4,3},{5,4},{6,5},{7,6},{8,7},{9,8},{10,9... | collective-permute-start | bytes 958472 | tf_op jit(solution)/shard_map/while/body/eval_jaxpr/ppermute | solution.py:52
  91.1 1.2 slice_select_fusion.22
  94.4 1.7 slice_select_fusion.23
  97.2 1.2 slice.1358
  100.2 1.5 slice_bitcast_fusion.43
  101.9 1.5 slice_bitcast_fusion.42
  110.3 1.3 collective-permute-start.3
  111.6 6.1 %collective-permute-start.2 = (f32[2496]{0:T(1024)S(1)}, f32[2496]{0:T(1024)}, u32[]{:S(2)}, u32[]{:S(2)}) collective-permute-start(f32[2496]{0:T(1024)S(1)} %pad_maximum_fusion.46), channel_id=1, source_target_pairs={{0,16},{1,17},{2,18},{3,19},{4,20},{5,21},{6,22},{7,23},{8,24},{9,... | collective-permute-start | bytes 29960 | tf_op jit(solution)/shard_map/while/body/eval_jaxpr/ppermute | solution.py:46
  118.7 2.1 pad_maximum_fusion.63
  126.9 1.7 fusion.129
  128.7 1.5 fusion.131
  131.5 1.2 copy.3776
  138.4 1.2 copy.3775
  139.7 1.8 pad_maximum_fusion.53
  141.5 1.6 pad_maximum_fusion.55
  144.6 1.6 pad_maximum_fusion.54
  148.0 2.5 add_multiply_fusion.12
  150.6 2.5 subtract_select_fusion.12
  156.9 1.8 add_select_fusion.8
  162.5 3.9 %collective-permute-start = (f32[624,128]{1,0:T(8,128)}, f32[624,128]{1,0:T(8,128)}, u32[]{:S(2)}, u32[]{:S(2)}) collective-permute-start(f32[624,128]{1,0:T(8,128)} %pad_maximum_fusion.44), channel_id=1, source_target_pairs={{0,1},{1,2},{2,3},{3,4},{4,5},{5,6},{6,7},{7,8},{8,9},{9,10},{10,1... | collective-permute-start | bytes 958472 | tf_op jit(solution)/shard_map/while/body/eval_jaxpr/ppermute | solution.py:52
  180.2 1.2 slice_select_fusion.22
  183.5 1.7 slice_select_fusion.23
  186.3 1.2 slice.1358
  189.3 1.5 slice_bitcast_fusion.43
  191.0 1.5 slice_bitcast_fusion.42
  199.4 1.3 collective-permute-start.3
  200.7 6.1 %collective-permute-start.2 = (f32[2496]{0:T(1024)S(1)}, f32[2496]{0:T(1024)}, u32[]{:S(2)}, u32[]{:S(2)}) collective-permute-start(f32[2496]{0:T(1024)S(1)} %pad_maximum_fusion.46), channel_id=1, source_target_pairs={{0,16},{1,17},{2,18},{3,19},{4,20},{5,21},{6,22},{7,23},{8,24},{9,... | collective-permute-start | bytes 29960 | tf_op jit(solution)/shard_map/while/body/eval_jaxpr/ppermute | solution.py:46
  207.8 2.1 pad_maximum_fusion.63
  216.0 1.7 fusion.129
  217.8 1.5 fusion.131
  220.5 1.2 copy.3776
  227.5 1.2 copy.3775
  228.8 1.8 pad_maximum_fusion.53
  230.6 1.6 pad_maximum_fusion.55
  233.7 1.6 pad_maximum_fusion.54
  237.1 2.5 add_multiply_fusion.12
  239.7 2.5 subtract_select_fusion.12
  246.0 1.8 add_select_fusion.8
  251.6 3.9 %collective-permute-start = (f32[624,128]{1,0:T(8,128)}, f32[624,128]{1,0:T(8,128)}, u32[]{:S(2)}, u32[]{:S(2)}) collective-permute-start(f32[624,128]{1,0:T(8,128)} %pad_maximum_fusion.44), channel_id=1, source_target_pairs={{0,1},{1,2},{2,3},{3,4},{4,5},{5,6},{6,7},{7,8},{8,9},{9,10},{10,1... | collective-permute-start | bytes 958472 | tf_op jit(solution)/shard_map/while/body/eval_jaxpr/ppermute | solution.py:52
  269.3 1.2 slice_select_fusion.22
  272.6 1.7 slice_select_fusion.23
  275.4 1.2 slice.1358
  278.4 1.5 slice_bitcast_fusion.43
  280.1 1.5 slice_bitcast_fusion.42
  288.5 1.3 collective-permute-start.3
  289.8 6.1 %collective-permute-start.2 = (f32[2496]{0:T(1024)S(1)}, f32[2496]{0:T(1024)}, u32[]{:S(2)}, u32[]{:S(2)}) collective-permute-start(f32[2496]{0:T(1024)S(1)} %pad_maximum_fusion.46), channel_id=1, source_target_pairs={{0,16},{1,17},{2,18},{3,19},{4,20},{5,21},{6,22},{7,23},{8,24},{9,... | collective-permute-start | bytes 29960 | tf_op jit(solution)/shard_map/while/body/eval_jaxpr/ppermute | solution.py:46
  296.9 2.1 pad_maximum_fusion.63
  305.1 1.7 fusion.129
  306.9 1.5 fusion.131
  309.6 1.2 copy.3776
  316.6 1.2 copy.3775
  317.9 1.8 pad_maximum_fusion.53
  319.7 1.6 pad_maximum_fusion.55
  322.8 1.6 pad_maximum_fusion.54
  334.2 1.2 copy_add_fusion
  (844 shorter events, 168.5 us)
Async XLA Ops:
  7.2 42.4 %all-gather.2.cloned.1.call-start = ((), (), s32[]{:S(2)}) async-start(), calls=%async_computation | async-start | bytes 2101248 | tf_op jit(solution)/shard_map/all_gather | solution.py:266
  70.5 29.7 %collective-permute-start.1 = (f32[624,128]{1,0:T(8,128)}, f32[624,128]{1,0:T(8,128)}, u32[]{:S(2)}, u32[]{:S(2)}) collective-permute-start(f32[624,128]{1,0:T(8,128)} %pad_maximum_fusion.45), channel_id=1, source_target_pairs={{0,15},{1,0},{2,1},{3,2},{4,3},{5,4},{6,5},{7,6},{8,7},{9,8},{10,9... | collective-permute-start | bytes 958472 | tf_op jit(solution)/shard_map/while/body/eval_jaxpr/ppermute | solution.py:52
  76.2 25.7 %collective-permute-start = (f32[624,128]{1,0:T(8,128)}, f32[624,128]{1,0:T(8,128)}, u32[]{:S(2)}, u32[]{:S(2)}) collective-permute-start(f32[624,128]{1,0:T(8,128)} %pad_maximum_fusion.44), channel_id=1, source_target_pairs={{0,1},{1,2},{2,3},{3,4},{4,5},{5,6},{6,7},{7,8},{8,9},{9,10},{10,1... | collective-permute-start | bytes 958472 | tf_op jit(solution)/shard_map/while/body/eval_jaxpr/ppermute | solution.py:52
  85.9 15.7 %copy-start.49 = (f32[3,48,128]{2,1,0:T(8,128)}, f32[3,48,128]{2,1,0:T(8,128)S(1)}, u32[]{:S(2)}) copy-start(f32[3,48,128]{2,1,0:T(8,128)S(1)} %slice.1348) | copy-start | bytes 221188 | tf_op jit(solution)/shard_map/while
  100.2 20.6 %copy-start.57 = (f32[3,48,128]{2,1,0:T(8,128)S(1)}, f32[3,48,128]{2,1,0:T(8,128)}, u32[]{:S(2)}) copy-start(f32[3,48,128]{2,1,0:T(8,128)} %slice.1355) | copy-start | bytes 221188 | tf_op jit(solution)/shard_map/while
  101.7 17.0 %copy-start.66 = (f32[1,48,128]{2,1,0:T(8,128)}, f32[1,48,128]{2,1,0:T(8,128)S(1)}, u32[]{:S(2)}) copy-start(f32[1,48,128]{2,1,0:T(8,128)S(1)} %get-tuple-element.1598) | copy-start | bytes 73732 | tf_op jit(solution)/shard_map/while
  101.7 20.4 %copy-start.62 = (f32[1,48,128]{2,1,0:T(8,128)}, f32[1,48,128]{2,1,0:T(8,128)S(1)}, u32[]{:S(2)}) copy-start(f32[1,48,128]{2,1,0:T(8,128)S(1)} %get-tuple-element.1584) | copy-start | bytes 73732 | tf_op jit(solution)/shard_map/while
  101.7 21.4 %copy-start.13 = (f32[8,3,48,128]{3,2,0,1:T(8,128)S(1)}, f32[8,3,48,128]{3,2,0,1:T(8,128)}, u32[]{:S(2)}) copy-start(f32[8,3,48,128]{3,2,0,1:T(8,128)} %slice.1359) | copy-start | bytes 1769476 | tf_op jit(solution)/shard_map/while
  101.9 19.6 %copy-start.59 = (f32[3,48,128]{2,1,0:T(8,128)S(1)}, f32[3,48,128]{2,1,0:T(8,128)}, u32[]{:S(2)}) copy-start(f32[3,48,128]{2,1,0:T(8,128)} %get-tuple-element.1624) | copy-start | bytes 221188 | tf_op jit(solution)/shard_map/while
  103.4 18.7 %copy-start.64 = (f32[1,48,128]{2,1,0:T(8,128)}, f32[1,48,128]{2,1,0:T(8,128)S(1)}, u32[]{:S(2)}) copy-start(f32[1,48,128]{2,1,0:T(8,128)S(1)} %get-tuple-element.1577) | copy-start | bytes 73732 | tf_op jit(solution)/shard_map/while
  103.4 18.7 %copy-start.68 = (f32[1,48,128]{2,1,0:T(8,128)}, f32[1,48,128]{2,1,0:T(8,128)S(1)}, u32[]{:S(2)}) copy-start(f32[1,48,128]{2,1,0:T(8,128)S(1)} %get-tuple-element.1599) | copy-start | bytes 73732 | tf_op jit(solution)/shard_map/while
  110.2 11.3 %copy-start.73 = (f32[1,48,128]{2,1,0:T(8,128)S(1)}, f32[1,48,128]{2,1,0:T(8,128)}, u32[]{:S(2)}) copy-start(f32[1,48,128]{2,1,0:T(8,128)} %get-tuple-element.1623) | copy-start | bytes 73732 | tf_op jit(solution)/shard_map/while
  110.2 11.9 %copy-start.61 = (f32[3,48,128]{2,1,0:T(8,128)S(1)}, f32[3,48,128]{2,1,0:T(8,128)}, u32[]{:S(2)}) copy-start(f32[3,48,128]{2,1,0:T(8,128)} %get-tuple-element.1628) | copy-start | bytes 221188 | tf_op jit(solution)/shard_map/while
  110.2 11.9 %copy-start.71 = (f32[1,48,128]{2,1,0:T(8,128)S(1)}, f32[1,48,128]{2,1,0:T(8,128)}, u32[]{:S(2)}) copy-start(f32[1,48,128]{2,1,0:T(8,128)} %get-tuple-element.1627) | copy-start | bytes 73732 | tf_op jit(solution)/shard_map/while
  110.3 15.8 %collective-permute-start.3 = (f32[2496]{0:T(1024)S(1)}, f32[2496]{0:T(1024)S(1)}, u32[]{:S(2)}, u32[]{:S(2)}) collective-permute-start(f32[2496]{0:T(1024)S(1)} %pad_maximum_fusion.48), channel_id=1, source_target_pairs={{16,0},{17,1},{18,2},{19,3},{20,4},{21,5},{22,6},{23,7},{24,8},{25... | collective-permute-start | bytes 29960 | tf_op jit(solution)/shard_map/while/body/eval_jaxpr/ppermute | solution.py:46
  111.6 21.1 %collective-permute-start.2 = (f32[2496]{0:T(1024)S(1)}, f32[2496]{0:T(1024)}, u32[]{:S(2)}, u32[]{:S(2)}) collective-permute-start(f32[2496]{0:T(1024)S(1)} %pad_maximum_fusion.46), channel_id=1, source_target_pairs={{0,16},{1,17},{2,18},{3,19},{4,20},{5,21},{6,22},{7,23},{8,24},{9,... | collective-permute-start | bytes 29960 | tf_op jit(solution)/shard_map/while/body/eval_jaxpr/ppermute | solution.py:46
  124.1 11.2 %copy-start.65 = (f32[1,48,128]{2,1,0:T(8,128)S(1)}, f32[1,48,128]{2,1,0:T(8,128)}, u32[]{:S(2)}) copy-start(f32[1,48,128]{2,1,0:T(8,128)} %copy-done.64) | copy-start | bytes 73732 | tf_op jit(solution)/shard_map/while
  124.1 12.0 %copy-start.50 = (f32[3,48,128]{2,1,0:T(8,128)S(1)}, f32[3,48,128]{2,1,0:T(8,128)}, u32[]{:S(2)}) copy-start(f32[3,48,128]{2,1,0:T(8,128)} %copy-done.49) | copy-start | bytes 221188 | tf_op jit(solution)/shard_map/while
  124.1 12.0 %copy-start.63 = (f32[1,48,128]{2,1,0:T(8,128)S(1)}, f32[1,48,128]{2,1,0:T(8,128)}, u32[]{:S(2)}) copy-start(f32[1,48,128]{2,1,0:T(8,128)} %copy-done.62) | copy-start | bytes 73732 | tf_op jit(solution)/shard_map/while
  126.9 12.7 %copy-start.54 = (f32[4,48,127]{2,1,0:T(8,128)S(1)}, f32[4,48,127]{2,1,0:T(8,128)}, u32[]{:S(2)}) copy-start(f32[4,48,127]{2,1,0:T(8,128)} %slice.1353) | copy-start | bytes 292612 | tf_op jit(solution)/shard_map/while
  131.4 11.7 %copy-start.44 = (f32[4,48,128]{2,1,0:T(8,128)S(1)}, f32[4,48,128]{2,1,0:T(8,128)}, u32[]{:S(2)}) copy-start(f32[4,48,128]{2,1,0:T(8,128)} %get-tuple-element.1556) | copy-start | bytes 294916 | tf_op jit(solution)/shard_map/while
  131.4 12.4 %copy-start.55 = (f32[4,48,127]{2,1,0:T(8,128)S(1)}, f32[4,48,127]{2,1,0:T(8,128)}, u32[]{:S(2)}) copy-start(f32[4,48,127]{2,1,0:T(8,128)} %get-tuple-element.1613) | copy-start | bytes 292612 | tf_op jit(solution)/shard_map/while
  161.7 27.6 %collective-permute-start.1 = (f32[624,128]{1,0:T(8,128)}, f32[624,128]{1,0:T(8,128)}, u32[]{:S(2)}, u32[]{:S(2)}) collective-permute-start(f32[624,128]{1,0:T(8,128)} %pad_maximum_fusion.45), channel_id=1, source_target_pairs={{0,15},{1,0},{2,1},{3,2},{4,3},{5,4},{6,5},{7,6},{8,7},{9,8},{10,9... | collective-permute-start | bytes 958472 | tf_op jit(solution)/shard_map/while/body/eval_jaxpr/ppermute | solution.py:52
  162.5 28.5 %collective-permute-start = (f32[624,128]{1,0:T(8,128)}, f32[624,128]{1,0:T(8,128)}, u32[]{:S(2)}, u32[]{:S(2)}) collective-permute-start(f32[624,128]{1,0:T(8,128)} %pad_maximum_fusion.44), channel_id=1, source_target_pairs={{0,1},{1,2},{2,3},{3,4},{4,5},{5,6},{6,7},{7,8},{8,9},{9,10},{10,1... | collective-permute-start | bytes 958472 | tf_op jit(solution)/shard_map/while/body/eval_jaxpr/ppermute | solution.py:52
  175.0 15.7 %copy-start.49 = (f32[3,48,128]{2,1,0:T(8,128)}, f32[3,48,128]{2,1,0:T(8,128)S(1)}, u32[]{:S(2)}) copy-start(f32[3,48,128]{2,1,0:T(8,128)S(1)} %slice.1348) | copy-start | bytes 221188 | tf_op jit(solution)/shard_map/while
  189.3 20.6 %copy-start.57 = (f32[3,48,128]{2,1,0:T(8,128)S(1)}, f32[3,48,128]{2,1,0:T(8,128)}, u32[]{:S(2)}) copy-start(f32[3,48,128]{2,1,0:T(8,128)} %slice.1355) | copy-start | bytes 221188 | tf_op jit(solution)/shard_map/while
  190.8 17.0 %copy-start.66 = (f32[1,48,128]{2,1,0:T(8,128)}, f32[1,48,128]{2,1,0:T(8,128)S(1)}, u32[]{:S(2)}) copy-start(f32[1,48,128]{2,1,0:T(8,128)S(1)} %get-tuple-element.1598) | copy-start | bytes 73732 | tf_op jit(solution)/shard_map/while
  190.8 20.4 %copy-start.62 = (f32[1,48,128]{2,1,0:T(8,128)}, f32[1,48,128]{2,1,0:T(8,128)S(1)}, u32[]{:S(2)}) copy-start(f32[1,48,128]{2,1,0:T(8,128)S(1)} %get-tuple-element.1584) | copy-start | bytes 73732 | tf_op jit(solution)/shard_map/while
  190.8 21.4 %copy-start.13 = (f32[8,3,48,128]{3,2,0,1:T(8,128)S(1)}, f32[8,3,48,128]{3,2,0,1:T(8,128)}, u32[]{:S(2)}) copy-start(f32[8,3,48,128]{3,2,0,1:T(8,128)} %slice.1359) | copy-start | bytes 1769476 | tf_op jit(solution)/shard_map/while
  191.0 19.6 %copy-start.59 = (f32[3,48,128]{2,1,0:T(8,128)S(1)}, f32[3,48,128]{2,1,0:T(8,128)}, u32[]{:S(2)}) copy-start(f32[3,48,128]{2,1,0:T(8,128)} %get-tuple-element.1624) | copy-start | bytes 221188 | tf_op jit(solution)/shard_map/while
  192.5 18.7 %copy-start.64 = (f32[1,48,128]{2,1,0:T(8,128)}, f32[1,48,128]{2,1,0:T(8,128)S(1)}, u32[]{:S(2)}) copy-start(f32[1,48,128]{2,1,0:T(8,128)S(1)} %get-tuple-element.1577) | copy-start | bytes 73732 | tf_op jit(solution)/shard_map/while
  192.5 18.7 %copy-start.68 = (f32[1,48,128]{2,1,0:T(8,128)}, f32[1,48,128]{2,1,0:T(8,128)S(1)}, u32[]{:S(2)}) copy-start(f32[1,48,128]{2,1,0:T(8,128)S(1)} %get-tuple-element.1599) | copy-start | bytes 73732 | tf_op jit(solution)/shard_map/while
  199.3 11.3 %copy-start.73 = (f32[1,48,128]{2,1,0:T(8,128)S(1)}, f32[1,48,128]{2,1,0:T(8,128)}, u32[]{:S(2)}) copy-start(f32[1,48,128]{2,1,0:T(8,128)} %get-tuple-element.1623) | copy-start | bytes 73732 | tf_op jit(solution)/shard_map/while
  199.3 11.9 %copy-start.61 = (f32[3,48,128]{2,1,0:T(8,128)S(1)}, f32[3,48,128]{2,1,0:T(8,128)}, u32[]{:S(2)}) copy-start(f32[3,48,128]{2,1,0:T(8,128)} %get-tuple-element.1628) | copy-start | bytes 221188 | tf_op jit(solution)/shard_map/while
  199.3 11.9 %copy-start.71 = (f32[1,48,128]{2,1,0:T(8,128)S(1)}, f32[1,48,128]{2,1,0:T(8,128)}, u32[]{:S(2)}) copy-start(f32[1,48,128]{2,1,0:T(8,128)} %get-tuple-element.1627) | copy-start | bytes 73732 | tf_op jit(solution)/shard_map/while
  199.4 15.8 %collective-permute-start.3 = (f32[2496]{0:T(1024)S(1)}, f32[2496]{0:T(1024)S(1)}, u32[]{:S(2)}, u32[]{:S(2)}) collective-permute-start(f32[2496]{0:T(1024)S(1)} %pad_maximum_fusion.48), channel_id=1, source_target_pairs={{16,0},{17,1},{18,2},{19,3},{20,4},{21,5},{22,6},{23,7},{24,8},{25... | collective-permute-start | bytes 29960 | tf_op jit(solution)/shard_map/while/body/eval_jaxpr/ppermute | solution.py:46
  200.7 21.1 %collective-permute-start.2 = (f32[2496]{0:T(1024)S(1)}, f32[2496]{0:T(1024)}, u32[]{:S(2)}, u32[]{:S(2)}) collective-permute-start(f32[2496]{0:T(1024)S(1)} %pad_maximum_fusion.46), channel_id=1, source_target_pairs={{0,16},{1,17},{2,18},{3,19},{4,20},{5,21},{6,22},{7,23},{8,24},{9,... | collective-permute-start | bytes 29960 | tf_op jit(solution)/shard_map/while/body/eval_jaxpr/ppermute | solution.py:46
  213.2 11.2 %copy-start.65 = (f32[1,48,128]{2,1,0:T(8,128)S(1)}, f32[1,48,128]{2,1,0:T(8,128)}, u32[]{:S(2)}) copy-start(f32[1,48,128]{2,1,0:T(8,128)} %copy-done.64) | copy-start | bytes 73732 | tf_op jit(solution)/shard_map/while
  213.2 12.0 %copy-start.50 = (f32[3,48,128]{2,1,0:T(8,128)S(1)}, f32[3,48,128]{2,1,0:T(8,128)}, u32[]{:S(2)}) copy-start(f32[3,48,128]{2,1,0:T(8,128)} %copy-done.49) | copy-start | bytes 221188 | tf_op jit(solution)/shard_map/while
  213.2 12.0 %copy-start.63 = (f32[1,48,128]{2,1,0:T(8,128)S(1)}, f32[1,48,128]{2,1,0:T(8,128)}, u32[]{:S(2)}) copy-start(f32[1,48,128]{2,1,0:T(8,128)} %copy-done.62) | copy-start | bytes 73732 | tf_op jit(solution)/shard_map/while
  216.0 12.7 %copy-start.54 = (f32[4,48,127]{2,1,0:T(8,128)S(1)}, f32[4,48,127]{2,1,0:T(8,128)}, u32[]{:S(2)}) copy-start(f32[4,48,127]{2,1,0:T(8,128)} %slice.1353) | copy-start | bytes 292612 | tf_op jit(solution)/shard_map/while
  220.5 11.7 %copy-start.44 = (f32[4,48,128]{2,1,0:T(8,128)S(1)}, f32[4,48,128]{2,1,0:T(8,128)}, u32[]{:S(2)}) copy-start(f32[4,48,128]{2,1,0:T(8,128)} %get-tuple-element.1556) | copy-start | bytes 294916 | tf_op jit(solution)/shard_map/while
  220.5 12.4 %copy-start.55 = (f32[4,48,127]{2,1,0:T(8,128)S(1)}, f32[4,48,127]{2,1,0:T(8,128)}, u32[]{:S(2)}) copy-start(f32[4,48,127]{2,1,0:T(8,128)} %get-tuple-element.1613) | copy-start | bytes 292612 | tf_op jit(solution)/shard_map/while
  250.8 27.6 %collective-permute-start.1 = (f32[624,128]{1,0:T(8,128)}, f32[624,128]{1,0:T(8,128)}, u32[]{:S(2)}, u32[]{:S(2)}) collective-permute-start(f32[624,128]{1,0:T(8,128)} %pad_maximum_fusion.45), channel_id=1, source_target_pairs={{0,15},{1,0},{2,1},{3,2},{4,3},{5,4},{6,5},{7,6},{8,7},{9,8},{10,9... | collective-permute-start | bytes 958472 | tf_op jit(solution)/shard_map/while/body/eval_jaxpr/ppermute | solution.py:52
  251.6 28.5 %collective-permute-start = (f32[624,128]{1,0:T(8,128)}, f32[624,128]{1,0:T(8,128)}, u32[]{:S(2)}, u32[]{:S(2)}) collective-permute-start(f32[624,128]{1,0:T(8,128)} %pad_maximum_fusion.44), channel_id=1, source_target_pairs={{0,1},{1,2},{2,3},{3,4},{4,5},{5,6},{6,7},{7,8},{8,9},{9,10},{10,1... | collective-permute-start | bytes 958472 | tf_op jit(solution)/shard_map/while/body/eval_jaxpr/ppermute | solution.py:52
  264.1 15.7 %copy-start.49 = (f32[3,48,128]{2,1,0:T(8,128)}, f32[3,48,128]{2,1,0:T(8,128)S(1)}, u32[]{:S(2)}) copy-start(f32[3,48,128]{2,1,0:T(8,128)S(1)} %slice.1348) | copy-start | bytes 221188 | tf_op jit(solution)/shard_map/while
  278.4 20.6 %copy-start.57 = (f32[3,48,128]{2,1,0:T(8,128)S(1)}, f32[3,48,128]{2,1,0:T(8,128)}, u32[]{:S(2)}) copy-start(f32[3,48,128]{2,1,0:T(8,128)} %slice.1355) | copy-start | bytes 221188 | tf_op jit(solution)/shard_map/while
  279.9 17.0 %copy-start.66 = (f32[1,48,128]{2,1,0:T(8,128)}, f32[1,48,128]{2,1,0:T(8,128)S(1)}, u32[]{:S(2)}) copy-start(f32[1,48,128]{2,1,0:T(8,128)S(1)} %get-tuple-element.1598) | copy-start | bytes 73732 | tf_op jit(solution)/shard_map/while
  279.9 20.4 %copy-start.62 = (f32[1,48,128]{2,1,0:T(8,128)}, f32[1,48,128]{2,1,0:T(8,128)S(1)}, u32[]{:S(2)}) copy-start(f32[1,48,128]{2,1,0:T(8,128)S(1)} %get-tuple-element.1584) | copy-start | bytes 73732 | tf_op jit(solution)/shard_map/while
  279.9 21.4 %copy-start.13 = (f32[8,3,48,128]{3,2,0,1:T(8,128)S(1)}, f32[8,3,48,128]{3,2,0,1:T(8,128)}, u32[]{:S(2)}) copy-start(f32[8,3,48,128]{3,2,0,1:T(8,128)} %slice.1359) | copy-start | bytes 1769476 | tf_op jit(solution)/shard_map/while
  280.1 19.6 %copy-start.59 = (f32[3,48,128]{2,1,0:T(8,128)S(1)}, f32[3,48,128]{2,1,0:T(8,128)}, u32[]{:S(2)}) copy-start(f32[3,48,128]{2,1,0:T(8,128)} %get-tuple-element.1624) | copy-start | bytes 221188 | tf_op jit(solution)/shard_map/while
  281.6 18.7 %copy-start.64 = (f32[1,48,128]{2,1,0:T(8,128)}, f32[1,48,128]{2,1,0:T(8,128)S(1)}, u32[]{:S(2)}) copy-start(f32[1,48,128]{2,1,0:T(8,128)S(1)} %get-tuple-element.1577) | copy-start | bytes 73732 | tf_op jit(solution)/shard_map/while
  281.6 18.7 %copy-start.68 = (f32[1,48,128]{2,1,0:T(8,128)}, f32[1,48,128]{2,1,0:T(8,128)S(1)}, u32[]{:S(2)}) copy-start(f32[1,48,128]{2,1,0:T(8,128)S(1)} %get-tuple-element.1599) | copy-start | bytes 73732 | tf_op jit(solution)/shard_map/while
  288.4 11.3 %copy-start.73 = (f32[1,48,128]{2,1,0:T(8,128)S(1)}, f32[1,48,128]{2,1,0:T(8,128)}, u32[]{:S(2)}) copy-start(f32[1,48,128]{2,1,0:T(8,128)} %get-tuple-element.1623) | copy-start | bytes 73732 | tf_op jit(solution)/shard_map/while
  288.4 11.9 %copy-start.61 = (f32[3,48,128]{2,1,0:T(8,128)S(1)}, f32[3,48,128]{2,1,0:T(8,128)}, u32[]{:S(2)}) copy-start(f32[3,48,128]{2,1,0:T(8,128)} %get-tuple-element.1628) | copy-start | bytes 221188 | tf_op jit(solution)/shard_map/while
  288.4 11.9 %copy-start.71 = (f32[1,48,128]{2,1,0:T(8,128)S(1)}, f32[1,48,128]{2,1,0:T(8,128)}, u32[]{:S(2)}) copy-start(f32[1,48,128]{2,1,0:T(8,128)} %get-tuple-element.1627) | copy-start | bytes 73732 | tf_op jit(solution)/shard_map/while
  288.5 15.8 %collective-permute-start.3 = (f32[2496]{0:T(1024)S(1)}, f32[2496]{0:T(1024)S(1)}, u32[]{:S(2)}, u32[]{:S(2)}) collective-permute-start(f32[2496]{0:T(1024)S(1)} %pad_maximum_fusion.48), channel_id=1, source_target_pairs={{16,0},{17,1},{18,2},{19,3},{20,4},{21,5},{22,6},{23,7},{24,8},{25... | collective-permute-start | bytes 29960 | tf_op jit(solution)/shard_map/while/body/eval_jaxpr/ppermute | solution.py:46
  289.8 21.1 %collective-permute-start.2 = (f32[2496]{0:T(1024)S(1)}, f32[2496]{0:T(1024)}, u32[]{:S(2)}, u32[]{:S(2)}) collective-permute-start(f32[2496]{0:T(1024)S(1)} %pad_maximum_fusion.46), channel_id=1, source_target_pairs={{0,16},{1,17},{2,18},{3,19},{4,20},{5,21},{6,22},{7,23},{8,24},{9,... | collective-permute-start | bytes 29960 | tf_op jit(solution)/shard_map/while/body/eval_jaxpr/ppermute | solution.py:46
  302.3 11.2 %copy-start.65 = (f32[1,48,128]{2,1,0:T(8,128)S(1)}, f32[1,48,128]{2,1,0:T(8,128)}, u32[]{:S(2)}) copy-start(f32[1,48,128]{2,1,0:T(8,128)} %copy-done.64) | copy-start | bytes 73732 | tf_op jit(solution)/shard_map/while
  302.3 12.0 %copy-start.50 = (f32[3,48,128]{2,1,0:T(8,128)S(1)}, f32[3,48,128]{2,1,0:T(8,128)}, u32[]{:S(2)}) copy-start(f32[3,48,128]{2,1,0:T(8,128)} %copy-done.49) | copy-start | bytes 221188 | tf_op jit(solution)/shard_map/while
  302.3 12.0 %copy-start.63 = (f32[1,48,128]{2,1,0:T(8,128)S(1)}, f32[1,48,128]{2,1,0:T(8,128)}, u32[]{:S(2)}) copy-start(f32[1,48,128]{2,1,0:T(8,128)} %copy-done.62) | copy-start | bytes 73732 | tf_op jit(solution)/shard_map/while
  305.1 12.7 %copy-start.54 = (f32[4,48,127]{2,1,0:T(8,128)S(1)}, f32[4,48,127]{2,1,0:T(8,128)}, u32[]{:S(2)}) copy-start(f32[4,48,127]{2,1,0:T(8,128)} %slice.1353) | copy-start | bytes 292612 | tf_op jit(solution)/shard_map/while
  309.6 11.7 %copy-start.44 = (f32[4,48,128]{2,1,0:T(8,128)S(1)}, f32[4,48,128]{2,1,0:T(8,128)}, u32[]{:S(2)}) copy-start(f32[4,48,128]{2,1,0:T(8,128)} %get-tuple-element.1556) | copy-start | bytes 294916 | tf_op jit(solution)/shard_map/while
  309.6 12.4 %copy-start.55 = (f32[4,48,127]{2,1,0:T(8,128)S(1)}, f32[4,48,127]{2,1,0:T(8,128)}, u32[]{:S(2)}) copy-start(f32[4,48,127]{2,1,0:T(8,128)} %get-tuple-element.1613) | copy-start | bytes 292612 | tf_op jit(solution)/shard_map/while
  (180 other events, 702.1 us)
Sparse Core Ops, SparseCore 0:
  10.3 39.1 all-gather.1

commit v2 on v1

--- a/solution.py
+++ b/solution.py
@@ -4,6 +4,8 @@
 import jax.numpy as jnp
 from jax import lax
 from jax.sharding import PartitionSpec as P
+from jax.experimental import pallas as pl
+from jax.experimental.pallas import tpu as pltpu
 
 STEPS = 3
 
@@ -236,6 +238,107 @@
     return (flow, scalar)
 
 
+def scalar_kernel(mode, span_y, depth, span_x):
+    def body(*refs):
+        if mode == "first":
+            conc_ref, motion_ref, solid_ref, source_ref, out_ref = refs
+        elif mode == "middle":
+            (g_ref, lo_x_ref, hi_x_ref, lo_y_ref, hi_y_ref,
+             motion_ref, solid_ref, source_ref, out_ref) = refs
+        else:
+            g_ref, lo_x_ref, hi_x_ref, lo_y_ref, hi_y_ref, out_ref = refs
+        lane = lax.broadcasted_iota(jnp.int32, (depth, span_x), 1)
+        level = lax.broadcasted_iota(jnp.int32, (depth, span_x), 0)
+        for y in range(span_y):
+            if mode == "first":
+                block = conc_ref[0, y]
+                scalar = [scalar_weights[member] * block for member in range(7)]
+            else:
+                moved_x = pltpu.roll(g_ref[1, 0, y], 1, 1)
+                back_x = pltpu.roll(g_ref[2, 0, y], span_x - 1, 1)
+                moved_z = pltpu.roll(g_ref[5, 0, y], 1, 0)
+                back_z = pltpu.roll(g_ref[6, 0, y], depth - 1, 0)
+                scalar = [
+                    g_ref[0, 0, y],
+                    jnp.where(lane == 0, lo_x_ref[0, y], moved_x),
+                    jnp.where(lane == span_x - 1, hi_x_ref[0, y], back_x),
+                    g_ref[3, 0, y - 1] if y > 0 else lo_y_ref[0],
+                    g_ref[4, 0, y + 1] if y < span_y - 1 else hi_y_ref[0],
+                    jnp.where(level == 0, 0.0, moved_z),
+                    jnp.where(level == depth - 1, 0.0, back_z),
+                ]
+            amount = scalar[0]
+            for member in range(1, 7):
+                amount = amount + scalar[member]
+            if mode == "final":
+                out_ref[0, y] = amount
+                continue
+            speeds = [motion_ref[component, y] for component in range(3)]
+            relaxation = tau_scalar_base + 4.0 * motion_ref[3, y] / schmidt_turb
+            solid = solid_ref[y] != 0
+            source = source_ref[0, y]
+            for member in range(7):
+                vector = flow_vectors[member]
+                project = vector[0] * speeds[0] + vector[1] * speeds[1] + vector[2] * speeds[2]
+                equilibrium = scalar_weights[member] * amount * (1.0 + 4.0 * project)
+                relaxed = (
+                    scalar[member]
+                    - (scalar[member] - equilibrium) / relaxation
+                    + scalar_weights[member] * source
+                )
+                out_ref[member, 0, y] = jnp.where(solid, scalar[flow_mirror[member]], relaxed)
+
+    return body
+
+
+def scalar_stage(mode, scalars, halos, motion, solid, source):
+    count, span_y, depth, span_x = source.shape if source is not None else scalars.shape[1:]
+    whole = lambda shape: pl.BlockSpec(shape, lambda s: (0,) * len(shape))
+    one = lambda shape: pl.BlockSpec(shape, lambda s: (s,) + (0,) * (len(shape) - 1))
+    stacked = pl.BlockSpec((7, 1, span_y, depth, span_x), lambda s: (0, s, 0, 0, 0))
+    cells = (span_y, depth, span_x)
+    edge_specs = [one((1, span_y, depth, 1))] * 2 + [one((1, depth, span_x))] * 2
+    if mode == "first":
+        operands = [scalars, motion, solid, source]
+        specs = [one((1,) + cells), whole((4,) + cells), whole(cells), one((1,) + cells)]
+    elif mode == "middle":
+        operands = [scalars, *halos, motion, solid, source]
+        specs = [stacked] + edge_specs + [whole((4,) + cells), whole(cells), one((1,) + cells)]
+    else:
+        operands = [scalars, *halos]
+        specs = [stacked] + edge_specs
+    if mode == "final":
+        out_spec = one((1,) + cells)
+        out_shape = jax.ShapeDtypeStruct((count,) + cells, jnp.float32)
+    else:
+        out_spec = stacked
+        out_shape = jax.ShapeDtypeStruct((7, count) + cells, jnp.float32)
+    return pl.pallas_call(
+        scalar_kernel(mode, span_y, depth, span_x),
+        grid=(count,),
+        in_specs=specs,
+        out_specs=out_spec,
+        out_shape=out_shape,
+    )(*operands)
+
+
+def scalar_edges(post):
+    span_y, span_x = post.shape[2], post.shape[4]
+    lo_x = passed_along(post[1, :, :, :, span_x - 1 : span_x], "gx", 1)
+    hi_x = passed_along(post[2, :, :, :, 0:1], "gx", -1)
+    lo_y = from_behind(post[3, :, span_y - 1], "gy", 1)
+    hi_y = from_behind(post[4, :, 0], "gy", -1)
+    return (lo_x, hi_x, lo_y, hi_y)
+
+
+def flow_section(flow, component, flow_dim, sender, edge_fill):
+    arrived = {}
+    for heading in (1, -1):
+        planes = edge_planes(flow, flow_vectors, component, flow_dim, heading)
+        arrived[heading] = edge_fill(sender(planes, heading), heading)
+    return displace(flow, flow_vectors, component, flow_dim, arrived[1], arrived[-1])
+
+
 def on_device(flow_pops, concentration, solid_mask, source_cell, source_scalar, source_rate):
     row_index = lax.axis_index("row")
     slab_depth = flow_pops.shape[2]
@@ -263,23 +366,20 @@
     source = jnp.dot(
         weights, columns, precision=lax.Precision.HIGHEST, preferred_element_type=jnp.float32
     ).reshape(concentration.shape)
-    whole = lax.all_gather(flow_pops, "row", axis=2, tiled=True)
+    solid_flag = solid.astype(jnp.int32)
+    whole = gathered_copies(flow_pops, "row", 2)
     flow = [whole[member] for member in range(19)]
-    scalar = [scalar_weights[member] * concentration for member in range(7)]
-    def one_step(time_step, state):
-        flow, scalar = state
-        flow, motion = flow_collide(list(flow), solid)
-        scalar = scalar_collide(list(scalar), [motion[component] for component in range(4)], solid, source)
+    scalars = concentration
+    halos = None
+    for time_step in range(STEPS):
+        flow, motion = flow_collide(flow, solid)
+        mode = "first" if time_step == 0 else "middle"
+        scalars = scalar_stage(mode, scalars, halos, motion, solid_flag, source)
+        halos = scalar_edges(scalars)
         flow = local_vertical(flow, flow_vectors, 1)
-        scalar = local_vertical(scalar, scalar_vectors, 2)
-        flow, scalar = cross_section(flow, scalar, 1, 0, send_spanwise, keep_spanwise, True)
-        flow, scalar = cross_section(flow, scalar, 0, 2, send_streamwise, inflow_fill, False)
-        return (tuple(flow), tuple(scalar))
-
-    flow, scalar = lax.fori_loop(0, STEPS, one_step, (tuple(flow), tuple(scalar)))
-    amount = scalar[0]
-    for member in range(1, 7):
-        amount = amount + scalar[member]
+        flow = flow_section(flow, 1, 0, send_spanwise, keep_spanwise)
+        flow = flow_section(flow, 0, 2, send_streamwise, inflow_fill)
+    amount = scalar_stage("final", scalars, halos, None, None, None)
     stacked = lax.dynamic_slice_in_dim(jnp.stack(flow), row_index * slab_depth, slab_depth, 2)
     return (stacked, amount)
 

time: 346 us -> 255 us (0.74)
  other arithmetic: 122 us -> 29.9 us
  local copies, waits for them, and re-layouts: 132 us -> 64.1 us
  waiting for transfers between devices: 34.1 us -> 70.2 us
  Pallas kernels: 0 us -> 33.3 us
  starting transfers between devices: 35.8 us -> 52.2 us
  between operations: 14.3 us -> 2.06 us
    concatenate x72 -> x0, other arithmetic: 61.5 us -> none  [the longest x30 33.5 us: displace(): jnp.concatenate([lax.slice_in_dim(piece, 1, length, axis=dimension), ente...]
    all_to_all x0 -> x1, waiting for transfers between devices: none -> 44.5 us  [copy_for_each(): return lax.all_to_all(copies, axis, split_axis=0, concat_axis=0, tiled=True)]
    all_gather x1 -> x0, waiting for transfers between devices: 34.1 us -> none  [on_device(): whole = lax.all_gather(flow_pops, 'row', axis=2, tiled=True)]
    pallas_call x0 -> x4, Pallas kernels: none -> 33.3 us  [scalar_stage(): pl.pallas_call(scalar_kernel(mode, span_y, depth, span_x), grid=(count,),...]
    select_n x24 -> x20, other arithmetic: 29.2 us -> 3.68 us  [flow_collide(): updated.append(jnp.where(solid, populations[flow_mirror[member]], relaxed))]
    slice x39 -> x24, local copies, waits for them, and re-layouts: 27.2 us -> 5.25 us  [displace(): lax.slice_in_dim(piece, 1, length, axis=dimension)]
    ppermute x6 -> x12, waiting for transfers between devices: 0.02 us -> 20.1 us  [passed_along(): return lax.ppermute(block, axis, route)]
    while x489 -> x0, local copies, waits for them, and re-layouts: 18.4 us -> none
  transfers between devices with their start and end apart: 13 -> 25, of which waited for: 1 -> 8; matrix products, arithmetic and copies ran while one was open for 36% -> 28% of each run, Pallas kernels for 0% -> 4%
where the time goes in v2:
time: 255 us; the launch traced here: 253 us
  waiting for transfers between devices  70.2 us (28%)
  local copies, waits for them, and re-layouts  64.1 us (25%)
  starting transfers between devices  52.2 us (20%)
  Pallas kernels  33.3 us (13%)
  other arithmetic  29.9 us (12%)
    all_to_all x1, waiting for transfers between devices, copy_for_each(): return lax.all_to_all(copies, axis, split_axis=0, concat_axis=0, tiled=True)  44.5 us
    pallas_call x4, Pallas kernels, scalar_stage(): pl.pallas_call(scalar_kernel(mode, span_y, depth, span_x), grid=(count,),...  33.3 us
    ppermute x12, starting transfers between devices, passed_along(): return lax.ppermute(block, axis, route)  26.5 us
    ppermute x12, waiting for transfers between devices, passed_along(): return lax.ppermute(block, axis, route)  20.1 us
    ppermute x12, starting transfers between devices, from_behind(): return lax.ppermute(value, axis, pairs)  17.4 us
    unnamed x139, local copies, waits for them, and re-layouts  16.7 us
    another operation x14, other arithmetic, flow_collide(): jnp.stack([speeds[0] * fluid_part, speeds[1] * fluid_part, speeds[2] * fl...  11.5 us
    unnamed x16, other arithmetic  11.3 us
  transfers between devices with their start and end apart: 25, of which 8 were waited for; matrix products, arithmetic and copies ran while one was open for 28% of the time, Pallas kernels for 4%

profile of v2, /device:TPU:7, one launch (start us, length us, event | category | flops | bytes accessed | tf_op | source)
XLA Modules:
  0.0 253.2 jit_solution(9990310898313612264)
XLA Ops:
  0.6 2.4 broadcast_in_dim.15
  3.1 8.3 %all-to-all-start = ((f32[8,19,4,6,128]{4,2,3,1,0:T(4,128)}), f32[8,19,4,6,128]{4,2,3,1,0:T(4,128)S(1)}, u32[]{:S(2)}, u32[]{:S(2)}) async-start(f32[8,19,4,6,128]{4,2,3,1,0:T(4,128)} %broadcast_in_dim.15), calls=%async_computation | async-start | bytes 3735552 | tf_op jit(solution)/shard_map/all_to_all | solution.py:65
  12.2 1.4 fusion.refs_3_.refs_7_
  13.6 44.5 %all-to-all-done = f32[8,19,4,6,128]{4,2,3,1,0:T(4,128)S(1)} async-done(((f32[8,19,4,6,128]{4,2,3,1,0:T(4,128)}), f32[8,19,4,6,128]{4,2,3,1,0:T(4,128)S(1)}, u32[]{:S(2)}, u32[]{:S(2)}) %all-to-all-start) | async-done | bytes 1867808 | tf_op jit(solution)/shard_map/all_to_all | solution.py:65
  59.0 1.9 fusion.276
  60.8 0.8 subtract_select_fusion.19
  63.7 0.8 pad_maximum_fusion.refs_1_
  64.5 7.9 %shard_map.131.refs_0_ = f32[7,8,4,48,128]{4,3,2,1,0:T(8,128)} custom-call(f32[8,4,48,128]{3,2,1,0:T(8,128)} %refs_0_.1, f32[4,4,48,128]{3,2,1,0:T(8,128)} %pad_maximum_fusion.refs_1_, s32[4,48,128]{2,1,0:T(8,128)} %get-tuple-element.146.refs_2_.refs_6_, f32[8,4,48,128]{3,2,1,0:T(8,128)} %fusion.refs_3_.refs_7_), custom_call_target="tpu_custom_call" | custom-call | tf_op jit(solution)/shard_map/pallas_call | solution.py:316
  72.4 1.9 slice_bitcast_fusion.4
  74.2 1.7 fusion.372
  79.3 1.3 constant_dynamic-update-slice_fusion.8
  80.6 1.3 constant_dynamic-update-slice_fusion.7
  85.1 1.6 collective-permute-start
  87.0 4.5 %collective-permute-start.12 = (f32[8,4,48,1]{2,0,3,1:T(8,128)S(1)}, f32[8,4,48,1]{2,0,3,1:T(8,128)S(1)}, u32[]{:S(2)}, u32[]{:S(2)}) collective-permute-start(f32[8,4,48,1]{2,0,3,1:T(8,128)S(1)} %bitcast.326), channel_id=1, source_target_pairs={{0,16},{1,17},{2,18},{3,19},{4,20},{5,21},{6,22},{7,23},{8,24},{9,... | collective-permute-start | bytes 18440 | tf_op jit(solution)/shard_map/ppermute | solution.py:48
  91.5 1.0 slice_select_fusion.1
  93.5 1.4 collective-permute-start.13
  95.0 0.9 slice.1051
  95.9 0.9 slice.1020
  96.8 1.2 collective-permute-start.1
  98.6 1.0 collective-permute-done.13
  99.6 4.7 %collective-permute-start.14 = (f32[8,48,128]{2,1,0:T(8,128)}, f32[8,48,128]{2,1,0:T(8,128)}, u32[]{:S(2)}, u32[]{:S(2)}) collective-permute-start(f32[8,48,128]{2,1,0:T(8,128)} %get-tuple-element.185), channel_id=1, source_target_pairs={{0,1},{1,2},{2,3},{3,4},{4,5},{5,6},{6,7},{7,8},{8,9},{9,10},{10,1... | collective-permute-start | bytes 589832 | tf_op jit(solution)/shard_map/ppermute | solution.py:54
  104.3 1.3 copy.15205.refs_2_
  105.5 1.2 copy.15204.refs_1_
  106.8 0.8 fusion.378
  108.0 3.1 %collective-permute-start.2 = (f32[5,4,48]{2,1,0:T(4,128)S(1)}, f32[5,4,48]{2,1,0:T(4,128)S(1)}, u32[]{:S(2)}, u32[]{:S(2)}) collective-permute-start(f32[5,4,48]{2,1,0:T(4,128)S(1)} %constant_dynamic-update-slice_fusion.10), channel_id=1, source_target_pairs={{0,16},{1,17},{2,18},{3,19},{4,20},{5,21},{6,22},{7,23},{8,24},{9,... | collective-permute-start | bytes 11528 | tf_op jit(solution)/shard_map/ppermute | solution.py:48
  111.4 1.5 collective-permute-start.3
  113.0 4.3 %collective-permute-done.3 = f32[5,4,48]{2,1,0:T(4,128)S(1)} collective-permute-done((f32[5,4,48]{2,1,0:T(4,128)S(1)}, f32[5,4,48]{2,1,0:T(4,128)S(1)}, u32[]{:S(2)}, u32[]{:S(2)}) %collective-permute-start.3) | collective-permute-done | bytes 3872 | tf_op jit(solution)/shard_map/ppermute | solution.py:48
  122.4 2.4 fusion.277
  125.0 1.5 fusion.280
  135.8 3.9 %collective-permute-start.4 = (f32[5,48,128]{2,1,0:T(8,128)}, f32[5,48,128]{2,1,0:T(8,128)}, u32[]{:S(2)}, u32[]{:S(2)}) collective-permute-start(f32[5,48,128]{2,1,0:T(8,128)} %constant_dynamic-update-slice_fusion.20), channel_id=1, source_target_pairs={{0,1},{1,2},{2,3},{3,4},{4,5},{5,6},{6,7},{7,8},{8,9},{9,10},{10,1... | collective-permute-start | bytes 368648 | tf_op jit(solution)/shard_map/ppermute | solution.py:54
  139.8 0.8 pad_maximum_fusion.1.refs_5_
  141.1 9.3 %shard_map.132.refs_0_ = f32[7,8,4,48,128]{4,3,2,1,0:T(8,128)} custom-call(f32[7,8,4,48,128]{4,3,2,1,0:T(8,128)} %shard_map.131.refs_0_, f32[8,4,48,1]{3,2,1,0:T(8,128)} %copy.15204.refs_1_, f32[8,4,48,1]{3,2,1,0:T(8,128)} %copy.15205.refs_2_, f32[8,48,128]{2,1,0:T(8,128)} %collective-permute-done.14.refs_3_, f32[8,48,128]{2,1,0:T(8,128)} %collective-permute-done.15.refs_4_, ...), custom_call_target="tpu_custom_call" | custom-call | tf_op jit(solution)/shard_map/pallas_call | solution.py:316
  150.4 1.6 fusion.371
  152.7 1.8 collective-permute-start.16
  154.5 1.3 collective-permute-start.17
  155.8 1.8 slice_bitcast_fusion.2
  157.6 2.9 %collective-permute-done.17 = f32[8,4,48,1]{2,0,3,1:T(8,128)S(1)} collective-permute-done((f32[8,4,48,1]{2,0,3,1:T(8,128)S(1)}, f32[8,4,48,1]{2,0,3,1:T(8,128)S(1)}, u32[]{:S(2)}, u32[]{:S(2)}) %collective-permute-start.17) | collective-permute-done | bytes 6176 | tf_op jit(solution)/shard_map/ppermute | solution.py:48
  160.5 1.0 collective-permute-start.18
  161.4 1.2 copy.15209.refs_2_
  162.7 1.2 copy.15208.refs_1_
  163.9 0.8 fusion.377
  164.9 0.8 fusion.376
  166.0 5.5 %collective-permute-start.6 = (f32[5,4,48]{2,1,0:T(4,128)S(1)}, f32[5,4,48]{2,1,0:T(4,128)S(1)}, u32[]{:S(2)}, u32[]{:S(2)}) collective-permute-start(f32[5,4,48]{2,1,0:T(4,128)S(1)} %constant_dynamic-update-slice_fusion.30), channel_id=1, source_target_pairs={{0,16},{1,17},{2,18},{3,19},{4,20},{5,21},{6,22},{7,23},{8,24},{9,... | collective-permute-start | bytes 11528 | tf_op jit(solution)/shard_map/ppermute | solution.py:48
  171.7 1.3 collective-permute-start.7
  173.1 4.5 %collective-permute-done.7 = f32[5,4,48]{2,1,0:T(4,128)S(1)} collective-permute-done((f32[5,4,48]{2,1,0:T(4,128)S(1)}, f32[5,4,48]{2,1,0:T(4,128)S(1)}, u32[]{:S(2)}, u32[]{:S(2)}) %collective-permute-start.7) | collective-permute-done | bytes 3872 | tf_op jit(solution)/shard_map/ppermute | solution.py:48
  182.7 1.7 fusion.281
  184.6 0.9 fusion.284
  187.4 1.1 collective-permute-start.8
  189.8 0.8 pad_maximum_fusion.2.refs_5_
  190.8 5.5 %collective-permute-done.9 = f32[5,48,128]{2,1,0:T(8,128)S(1)} collective-permute-done((f32[5,48,128]{2,1,0:T(8,128)S(1)}, f32[5,48,128]{2,1,0:T(8,128)S(1)}, u32[]{:S(2)}, u32[]{:S(2)}) %collective-permute-start.9) | collective-permute-done | bytes 122912 | tf_op jit(solution)/shard_map/ppermute | solution.py:54
  196.5 1.9 collective-permute-start.10
  198.6 1.3 collective-permute-start.11
  200.0 4.5 %collective-permute-done.11 = f32[5,4,48]{2,1,0:T(4,128)S(1)} collective-permute-done((f32[5,4,48]{2,1,0:T(4,128)S(1)}, f32[5,4,48]{2,1,0:T(4,128)S(1)}, u32[]{:S(2)}, u32[]{:S(2)}) %collective-permute-start.11) | collective-permute-done | bytes 3872 | tf_op jit(solution)/shard_map/ppermute | solution.py:48
  218.3 9.3 %shard_map.133.refs_0_ = f32[7,8,4,48,128]{4,3,2,1,0:T(8,128)} custom-call(f32[7,8,4,48,128]{4,3,2,1,0:T(8,128)} %shard_map.132.refs_0_, f32[8,4,48,1]{3,2,1,0:T(8,128)} %copy.15208.refs_1_, f32[8,4,48,1]{3,2,1,0:T(8,128)} %copy.15209.refs_2_, f32[8,48,128]{2,1,0:T(8,128)} %collective-permute-done.18.refs_3_, f32[8,48,128]{2,1,0:T(8,128)} %collective-permute-done.19.refs_4_, ...), custom_call_target="tpu_custom_call" | custom-call | tf_op jit(solution)/shard_map/pallas_call | solution.py:316
  227.6 1.0 slice_bitcast_fusion
  228.7 3.8 %collective-permute-start.22 = (f32[8,48,128]{2,1,0:T(8,128)S(1)}, f32[8,48,128]{2,1,0:T(8,128)S(1)}, u32[]{:S(2)}, u32[]{:S(2)}) collective-permute-start(f32[8,48,128]{2,1,0:T(8,128)S(1)} %get-tuple-element.177), channel_id=1, source_target_pairs={{0,1},{1,2},{2,3},{3,4},{4,5},{5,6},{6,7},{7,8},{8,9},{9,10},{10,1... | collective-permute-start | bytes 589832 | tf_op jit(solution)/shard_map/ppermute | solution.py:54
  232.6 1.6 fusion.370
  234.8 1.7 collective-permute-start.20
  236.5 1.3 collective-permute-start.21
  237.8 1.1 constant_dynamic-slice_fusion
  239.7 2.8 %collective-permute-done.21 = f32[8,4,48,1]{2,0,3,1:T(8,128)S(1)} collective-permute-done((f32[8,4,48,1]{2,0,3,1:T(8,128)S(1)}, f32[8,4,48,1]{2,0,3,1:T(8,128)S(1)}, u32[]{:S(2)}, u32[]{:S(2)}) %collective-permute-start.21) | collective-permute-done | bytes 6176 | tf_op jit(solution)/shard_map/ppermute | solution.py:48
  242.5 1.2 copy.15213.refs_2_
  243.7 1.3 copy.15212.refs_1_
  246.3 6.9 %shard_map.134 = f32[8,4,48,128]{3,2,1,0:T(8,128)} custom-call(f32[7,8,4,48,128]{4,3,2,1,0:T(8,128)} %shard_map.133.refs_0_, f32[8,4,48,1]{3,2,1,0:T(8,128)} %copy.15212.refs_1_, f32[8,4,48,1]{3,2,1,0:T(8,128)} %copy.15213.refs_2_, f32[8,48,128]{2,1,0:T(8,128)} %copy-done.30, f32[8,48,128]{2,1,0:T(8,128)} %copy-done.29), custom_call_target="tpu_custom_call" | custom-call | tf_op jit(solution)/shard_map/pallas_call | solution.py:316
  (340 shorter events, 54.0 us)
Async XLA Ops:
  3.1 8.3 %copy-start.38 = (s32[96]{0:T(128)S(1)}, s32[96]{0:T(128)}, u32[]{:S(2)}) copy-start(s32[96]{0:T(128)} %param.15) | copy-start | bytes 1156
  3.1 8.4 %copy-start.39 = (s32[96]{0:T(128)S(1)}, s32[96]{0:T(128)}, u32[]{:S(2)}) copy-start(s32[96]{0:T(128)} %param.16) | copy-start | bytes 1156
  3.1 8.4 %copy-start.31 = (s32[4,48,128]{2,1,0:T(8,128)S(1)}, s32[4,48,128]{2,1,0:T(8,128)}, u32[]{:S(2)}) copy-start(s32[4,48,128]{2,1,0:T(8,128)} %param.14) | copy-start | bytes 294916
  3.1 9.1 %copy-start.43 = (f32[96]{0:T(128)S(1)}, f32[96]{0:T(128)}, u32[]{:S(2)}) copy-start(f32[96]{0:T(128)} %param.17) | copy-start | bytes 1156
  3.1 55.1 %all-to-all-start = ((f32[8,19,4,6,128]{4,2,3,1,0:T(4,128)}), f32[8,19,4,6,128]{4,2,3,1,0:T(4,128)S(1)}, u32[]{:S(2)}, u32[]{:S(2)}) async-start(f32[8,19,4,6,128]{4,2,3,1,0:T(4,128)} %broadcast_in_dim.15), calls=%async_computation | async-start | bytes 3735552 | tf_op jit(solution)/shard_map/all_to_all | solution.py:65
  72.4 3.6 %copy-start.23 = (f32[4,48,128]{2,1,0:T(8,128)S(1)}, f32[4,48,128]{2,1,0:T(8,128)}, u32[]{:S(2)}) copy-start(f32[4,48,128]{2,1,0:T(8,128)} %get-tuple-element.169) | copy-start | bytes 294916
  72.4 3.6 %copy-start.24 = (f32[4,48,128]{2,1,0:T(8,128)S(1)}, f32[4,48,128]{2,1,0:T(8,128)}, u32[]{:S(2)}) copy-start(f32[4,48,128]{2,1,0:T(8,128)} %get-tuple-element.170) | copy-start | bytes 294916
  74.2 3.2 %copy-start.21 = (f32[4,48,128]{2,1,0:T(8,128)S(1)}, f32[4,48,128]{2,1,0:T(8,128)}, u32[]{:S(2)}) copy-start(f32[4,48,128]{2,1,0:T(8,128)} %get-tuple-element.167) | copy-start | bytes 294916
  74.2 3.2 %copy-start.22 = (f32[4,48,128]{2,1,0:T(8,128)S(1)}, f32[4,48,128]{2,1,0:T(8,128)}, u32[]{:S(2)}) copy-start(f32[4,48,128]{2,1,0:T(8,128)} %get-tuple-element.168) | copy-start | bytes 294916
  75.9 3.1 %copy-start.19 = (f32[4,48,128]{2,1,0:T(8,128)S(1)}, f32[4,48,128]{2,1,0:T(8,128)}, u32[]{:S(2)}) copy-start(f32[4,48,128]{2,1,0:T(8,128)} %get-tuple-element.173) | copy-start | bytes 294916
  75.9 3.1 %copy-start.20 = (f32[4,48,128]{2,1,0:T(8,128)S(1)}, f32[4,48,128]{2,1,0:T(8,128)}, u32[]{:S(2)}) copy-start(f32[4,48,128]{2,1,0:T(8,128)} %get-tuple-element.174) | copy-start | bytes 294916
  75.9 3.2 %copy-start.17 = (f32[4,48,128]{2,1,0:T(8,128)S(1)}, f32[4,48,128]{2,1,0:T(8,128)}, u32[]{:S(2)}) copy-start(f32[4,48,128]{2,1,0:T(8,128)} %get-tuple-element.171) | copy-start | bytes 294916
  76.0 3.2 %copy-start.18 = (f32[4,48,128]{2,1,0:T(8,128)S(1)}, f32[4,48,128]{2,1,0:T(8,128)}, u32[]{:S(2)}) copy-start(f32[4,48,128]{2,1,0:T(8,128)} %get-tuple-element.172) | copy-start | bytes 294916
  76.0 3.1 %copy-start.4 = (f32[4,47,128]{2,1,0:T(8,128)}, f32[4,47,128]{2,1,0:T(8,128)S(1)}, u32[]{:S(2)}) copy-start(f32[4,47,128]{2,1,0:T(8,128)S(1)} %get-tuple-element.245) | copy-start | bytes 288772
  77.5 5.1 %copy-start.14 = (f32[4,48,128]{2,1,0:T(8,128)S(1)}, f32[4,48,128]{2,1,0:T(8,128)}, u32[]{:S(2)}) copy-start(f32[4,48,128]{2,1,0:T(8,128)} %get-tuple-element.304) | copy-start | bytes 294916
  77.5 5.7 %copy-start.13 = (f32[4,48,128]{2,1,0:T(8,128)S(1)}, f32[4,48,128]{2,1,0:T(8,128)}, u32[]{:S(2)}) copy-start(f32[4,48,128]{2,1,0:T(8,128)} %get-tuple-element.302) | copy-start | bytes 294916
  82.0 12.9 %copy-start.5 = (f32[4,47,128]{2,1,0:T(8,128)S(1)}, f32[4,47,128]{2,1,0:T(8,128)}, u32[]{:S(2)}) copy-start(f32[4,47,128]{2,1,0:T(8,128)} %copy-done.4) | copy-start | bytes 288772
  83.2 27.9 %copy-start.12 = (f32[3,48,128]{2,1,0:T(8,128)}, f32[3,48,128]{2,1,0:T(8,128)S(1)}, u32[]{:S(2)}) copy-start(f32[3,48,128]{2,1,0:T(8,128)S(1)} %slice.1056) | copy-start | bytes 221188
  85.1 21.7 %collective-permute-start = (f32[5,48,128]{2,1,0:T(8,128)}, f32[5,48,128]{2,1,0:T(8,128)}, u32[]{:S(2)}, u32[]{:S(2)}) collective-permute-start(f32[5,48,128]{2,1,0:T(8,128)} %constant_dynamic-update-slice_fusion), channel_id=1, source_target_pairs={{0,1},{1,2},{2,3},{3,4},{4,5},{5,6},{6,7},{7,8},{8,9},{9,10},{10,1... | collective-permute-start | bytes 368648 | tf_op jit(solution)/shard_map/ppermute | solution.py:54
  86.7 54.4 %collective-permute-start.15 = (f32[8,48,128]{2,1,0:T(8,128)}, f32[8,48,128]{2,1,0:T(8,128)}, u32[]{:S(2)}, u32[]{:S(2)}) collective-permute-start(f32[8,48,128]{2,1,0:T(8,128)} %get-tuple-element.184), channel_id=1, source_target_pairs={{0,15},{1,0},{2,1},{3,2},{4,3},{5,4},{6,5},{7,6},{8,7},{9,8},{10,9... | collective-permute-start | bytes 589832 | tf_op jit(solution)/shard_map/ppermute | solution.py:54
  87.0 18.5 %collective-permute-start.12 = (f32[8,4,48,1]{2,0,3,1:T(8,128)S(1)}, f32[8,4,48,1]{2,0,3,1:T(8,128)S(1)}, u32[]{:S(2)}, u32[]{:S(2)}) collective-permute-start(f32[8,4,48,1]{2,0,3,1:T(8,128)S(1)} %bitcast.326), channel_id=1, source_target_pairs={{0,16},{1,17},{2,18},{3,19},{4,20},{5,21},{6,22},{7,23},{8,24},{9,... | collective-permute-start | bytes 18440 | tf_op jit(solution)/shard_map/ppermute | solution.py:48
  92.5 15.2 %copy-start.41 = (f32[5,4,48]{2,1,0:T(4,128)S(1)}, f32[5,4,48]{2,1,0:T(4,128)}, u32[]{:S(2)}) copy-start(f32[5,4,48]{2,1,0:T(4,128)} %constant_dynamic-update-slice_fusion.14) | copy-start | bytes 11524
  93.4 19.4 %copy-start.35 = (f32[5]{0:T(128)S(1)}, f32[5]{0:T(128)}, u32[]{:S(2)}) copy-start(f32[5]{0:T(128)} %constant.109.clone) | copy-start | bytes 64
  93.5 23.8 %copy-start.32 = (f32[5]{0:T(128)S(1)}, f32[5]{0:T(128)}, u32[]{:S(2)}) copy-start(f32[5]{0:T(128)} %constant.110.clone) | copy-start | bytes 64
  93.5 6.1 %collective-permute-start.13 = (f32[8,4,48,1]{2,0,3,1:T(8,128)S(1)}, f32[8,4,48,1]{2,0,3,1:T(8,128)S(1)}, u32[]{:S(2)}, u32[]{:S(2)}) collective-permute-start(f32[8,4,48,1]{2,0,3,1:T(8,128)S(1)} %bitcast.328), channel_id=1, source_target_pairs={{16,0},{17,1},{18,2},{19,3},{20,4},{21,5},{22,6},{23,7},{24,8},{25... | collective-permute-start | bytes 18440 | tf_op jit(solution)/shard_map/ppermute | solution.py:48
  96.8 11.0 %collective-permute-start.1 = (f32[5,48,128]{2,1,0:T(8,128)}, f32[5,48,128]{2,1,0:T(8,128)S(1)}, u32[]{:S(2)}, u32[]{:S(2)}) collective-permute-start(f32[5,48,128]{2,1,0:T(8,128)} %constant_dynamic-update-slice_fusion.5), channel_id=1, source_target_pairs={{0,15},{1,0},{2,1},{3,2},{4,3},{5,4},{6,5},{7,6},{8,7},{9,8},{10,9... | collective-permute-start | bytes 368648 | tf_op jit(solution)/shard_map/ppermute | solution.py:54
  98.3 24.0 %copy-start.1 = (f32[4,48,128]{2,1,0:T(8,128)S(1)}, f32[4,48,128]{2,1,0:T(8,128)}, u32[]{:S(2)}) copy-start(f32[4,48,128]{2,1,0:T(8,128)} %copy-done) | copy-start | bytes 294916
  98.3 24.0 %copy-start.3 = (f32[4,48,128]{2,1,0:T(8,128)S(1)}, f32[4,48,128]{2,1,0:T(8,128)}, u32[]{:S(2)}) copy-start(f32[4,48,128]{2,1,0:T(8,128)} %copy-done.2) | copy-start | bytes 294916
  98.3 24.0 %copy-start.6 = (f32[4,48,127]{2,1,0:T(8,128)S(1)}, f32[4,48,127]{2,1,0:T(8,128)}, u32[]{:S(2)}) copy-start(f32[4,48,127]{2,1,0:T(8,128)} %pad_slice_fusion.56) | copy-start | bytes 292612
  98.3 24.0 %copy-start.7 = (f32[4,48,127]{2,1,0:T(8,128)S(1)}, f32[4,48,127]{2,1,0:T(8,128)}, u32[]{:S(2)}) copy-start(f32[4,48,127]{2,1,0:T(8,128)} %pad_slice_fusion.58) | copy-start | bytes 292612
  98.4 24.0 %copy-start.8 = (f32[4,48,127]{2,1,0:T(8,128)S(1)}, f32[4,48,127]{2,1,0:T(8,128)}, u32[]{:S(2)}) copy-start(f32[4,48,127]{2,1,0:T(8,128)} %pad_slice_fusion.57) | copy-start | bytes 292612
  98.4 24.0 %copy-start.16 = (f32[4,48,127]{2,1,0:T(8,128)S(1)}, f32[4,48,127]{2,1,0:T(8,128)}, u32[]{:S(2)}) copy-start(f32[4,48,127]{2,1,0:T(8,128)} %slice.1049) | copy-start | bytes 292612
  99.6 41.5 %collective-permute-start.14 = (f32[8,48,128]{2,1,0:T(8,128)}, f32[8,48,128]{2,1,0:T(8,128)}, u32[]{:S(2)}, u32[]{:S(2)}) collective-permute-start(f32[8,48,128]{2,1,0:T(8,128)} %get-tuple-element.185), channel_id=1, source_target_pairs={{0,1},{1,2},{2,3},{3,4},{4,5},{5,6},{6,7},{7,8},{8,9},{9,10},{10,1... | collective-permute-start | bytes 589832 | tf_op jit(solution)/shard_map/ppermute | solution.py:54
  107.8 14.5 %copy-start.27 = (f32[1,48,128]{2,1,0:T(8,128)}, f32[1,48,128]{2,1,0:T(8,128)S(1)}, u32[]{:S(2)}) copy-start(f32[1,48,128]{2,1,0:T(8,128)S(1)} %get-tuple-element.296) | copy-start | bytes 73732
  107.8 14.5 %copy-start.28 = (f32[1,48,128]{2,1,0:T(8,128)}, f32[1,48,128]{2,1,0:T(8,128)S(1)}, u32[]{:S(2)}) copy-start(f32[1,48,128]{2,1,0:T(8,128)S(1)} %get-tuple-element.300) | copy-start | bytes 73732
  108.0 4.8 %collective-permute-start.2 = (f32[5,4,48]{2,1,0:T(4,128)S(1)}, f32[5,4,48]{2,1,0:T(4,128)S(1)}, u32[]{:S(2)}, u32[]{:S(2)}) collective-permute-start(f32[5,4,48]{2,1,0:T(4,128)S(1)} %constant_dynamic-update-slice_fusion.10), channel_id=1, source_target_pairs={{0,16},{1,17},{2,18},{3,19},{4,20},{5,21},{6,22},{7,23},{8,24},{9,... | collective-permute-start | bytes 11528 | tf_op jit(solution)/shard_map/ppermute | solution.py:48
  111.4 5.9 %collective-permute-start.3 = (f32[5,4,48]{2,1,0:T(4,128)S(1)}, f32[5,4,48]{2,1,0:T(4,128)S(1)}, u32[]{:S(2)}, u32[]{:S(2)}) collective-permute-start(f32[5,4,48]{2,1,0:T(4,128)S(1)} %constant_dynamic-update-slice_fusion.15), channel_id=1, source_target_pairs={{16,0},{17,1},{18,2},{19,3},{20,4},{21,5},{22,6},{23,7},{24,8},{25... | collective-permute-start | bytes 11528 | tf_op jit(solution)/shard_map/ppermute | solution.py:48
  134.0 30.7 %copy-start.11 = (f32[3,48,128]{2,1,0:T(8,128)}, f32[3,48,128]{2,1,0:T(8,128)S(1)}, u32[]{:S(2)}) copy-start(f32[3,48,128]{2,1,0:T(8,128)S(1)} %slice.1118) | copy-start | bytes 221188
  135.8 28.1 %collective-permute-start.5 = (f32[5,48,128]{2,1,0:T(8,128)}, f32[5,48,128]{2,1,0:T(8,128)}, u32[]{:S(2)}, u32[]{:S(2)}) collective-permute-start(f32[5,48,128]{2,1,0:T(8,128)} %constant_dynamic-update-slice_fusion.25), channel_id=1, source_target_pairs={{0,15},{1,0},{2,1},{3,2},{4,3},{5,4},{6,5},{7,6},{8,7},{9,8},{10,9... | collective-permute-start | bytes 368648 | tf_op jit(solution)/shard_map/ppermute | solution.py:54
  135.8 29.1 %collective-permute-start.4 = (f32[5,48,128]{2,1,0:T(8,128)}, f32[5,48,128]{2,1,0:T(8,128)}, u32[]{:S(2)}, u32[]{:S(2)}) collective-permute-start(f32[5,48,128]{2,1,0:T(8,128)} %constant_dynamic-update-slice_fusion.20), channel_id=1, source_target_pairs={{0,1},{1,2},{2,3},{3,4},{4,5},{5,6},{6,7},{7,8},{8,9},{9,10},{10,1... | collective-permute-start | bytes 368648 | tf_op jit(solution)/shard_map/ppermute | solution.py:54
  152.3 13.6 %copy-start.40 = (f32[5,4,48]{2,1,0:T(4,128)S(1)}, f32[5,4,48]{2,1,0:T(4,128)}, u32[]{:S(2)}) copy-start(f32[5,4,48]{2,1,0:T(4,128)} %constant_dynamic-update-slice_fusion.34) | copy-start | bytes 11524
  152.3 19.2 %copy-start.42 = (f32[5,4,48]{2,1,0:T(4,128)S(1)}, f32[5,4,48]{2,1,0:T(4,128)}, u32[]{:S(2)}) copy-start(f32[5,4,48]{2,1,0:T(4,128)} %constant_dynamic-update-slice_fusion.39) | copy-start | bytes 11524
  152.4 20.7 %copy-start.36 = (f32[5]{0:T(128)S(1)}, f32[5]{0:T(128)}, u32[]{:S(2)}) copy-start(f32[5]{0:T(128)} %constant.109.clone) | copy-start | bytes 64
  152.7 25.0 %copy-start.33 = (f32[5]{0:T(128)S(1)}, f32[5]{0:T(128)}, u32[]{:S(2)}) copy-start(f32[5]{0:T(128)} %constant.110.clone) | copy-start | bytes 64
  152.7 10.0 %collective-permute-start.16 = (f32[8,4,48,1]{2,0,3,1:T(8,128)S(1)}, f32[8,4,48,1]{2,0,3,1:T(8,128)S(1)}, u32[]{:S(2)}, u32[]{:S(2)}) collective-permute-start(f32[8,4,48,1]{2,0,3,1:T(8,128)S(1)} %bitcast.327), channel_id=1, source_target_pairs={{0,16},{1,17},{2,18},{3,19},{4,20},{5,21},{6,22},{7,23},{8,24},{9,... | collective-permute-start | bytes 18440 | tf_op jit(solution)/shard_map/ppermute | solution.py:48
  154.5 6.0 %collective-permute-start.17 = (f32[8,4,48,1]{2,0,3,1:T(8,128)S(1)}, f32[8,4,48,1]{2,0,3,1:T(8,128)S(1)}, u32[]{:S(2)}, u32[]{:S(2)}) collective-permute-start(f32[8,4,48,1]{2,0,3,1:T(8,128)S(1)} %bitcast.330), channel_id=1, source_target_pairs={{16,0},{17,1},{18,2},{19,3},{20,4},{21,5},{22,6},{23,7},{24,8},{25... | collective-permute-start | bytes 18440 | tf_op jit(solution)/shard_map/ppermute | solution.py:48
  157.6 25.1 %copy-start.10 = (f32[4,48,128]{2,1,0:T(8,128)S(1)}, f32[4,48,128]{2,1,0:T(8,128)}, u32[]{:S(2)}) copy-start(f32[4,48,128]{2,1,0:T(8,128)} %copy-done.9) | copy-start | bytes 294916
  157.6 25.1 %copy-start.15 = (f32[4,48,127]{2,1,0:T(8,128)S(1)}, f32[4,48,127]{2,1,0:T(8,128)}, u32[]{:S(2)}) copy-start(f32[4,48,127]{2,1,0:T(8,128)} %slice.1155) | copy-start | bytes 292612
  157.6 60.7 %collective-permute-start.19 = (f32[8,48,128]{2,1,0:T(8,128)}, f32[8,48,128]{2,1,0:T(8,128)}, u32[]{:S(2)}, u32[]{:S(2)}) collective-permute-start(f32[8,48,128]{2,1,0:T(8,128)} %get-tuple-element.180), channel_id=1, source_target_pairs={{0,15},{1,0},{2,1},{3,2},{4,3},{5,4},{6,5},{7,6},{8,7},{9,8},{10,9... | collective-permute-start | bytes 589832 | tf_op jit(solution)/shard_map/ppermute | solution.py:54
  160.5 57.9 %collective-permute-start.18 = (f32[8,48,128]{2,1,0:T(8,128)}, f32[8,48,128]{2,1,0:T(8,128)}, u32[]{:S(2)}, u32[]{:S(2)}) collective-permute-start(f32[8,48,128]{2,1,0:T(8,128)} %get-tuple-element.181), channel_id=1, source_target_pairs={{0,1},{1,2},{2,3},{3,4},{4,5},{5,6},{6,7},{7,8},{8,9},{9,10},{10,1... | collective-permute-start | bytes 589832 | tf_op jit(solution)/shard_map/ppermute | solution.py:54
  165.7 12.0 %copy-start.25 = (f32[1,48,128]{2,1,0:T(8,128)}, f32[1,48,128]{2,1,0:T(8,128)S(1)}, u32[]{:S(2)}) copy-start(f32[1,48,128]{2,1,0:T(8,128)S(1)} %get-tuple-element.277) | copy-start | bytes 73732
  165.7 12.0 %copy-start.26 = (f32[1,48,128]{2,1,0:T(8,128)}, f32[1,48,128]{2,1,0:T(8,128)S(1)}, u32[]{:S(2)}) copy-start(f32[1,48,128]{2,1,0:T(8,128)S(1)} %get-tuple-element.281) | copy-start | bytes 73732
  166.0 7.1 %collective-permute-start.6 = (f32[5,4,48]{2,1,0:T(4,128)S(1)}, f32[5,4,48]{2,1,0:T(4,128)S(1)}, u32[]{:S(2)}, u32[]{:S(2)}) collective-permute-start(f32[5,4,48]{2,1,0:T(4,128)S(1)} %constant_dynamic-update-slice_fusion.30), channel_id=1, source_target_pairs={{0,16},{1,17},{2,18},{3,19},{4,20},{5,21},{6,22},{7,23},{8,24},{9,... | collective-permute-start | bytes 11528 | tf_op jit(solution)/shard_map/ppermute | solution.py:48
  171.7 5.9 %collective-permute-start.7 = (f32[5,4,48]{2,1,0:T(4,128)S(1)}, f32[5,4,48]{2,1,0:T(4,128)S(1)}, u32[]{:S(2)}, u32[]{:S(2)}) collective-permute-start(f32[5,4,48]{2,1,0:T(4,128)S(1)} %constant_dynamic-update-slice_fusion.35), channel_id=1, source_target_pairs={{16,0},{17,1},{18,2},{19,3},{20,4},{21,5},{22,6},{23,7},{24,8},{25... | collective-permute-start | bytes 11528 | tf_op jit(solution)/shard_map/ppermute | solution.py:48
  187.4 3.2 %collective-permute-start.8 = (f32[5,48,128]{2,1,0:T(8,128)S(1)}, f32[5,48,128]{2,1,0:T(8,128)S(1)}, u32[]{:S(2)}, u32[]{:S(2)}) collective-permute-start(f32[5,48,128]{2,1,0:T(8,128)S(1)} %constant_dynamic-update-slice_fusion.40), channel_id=1, source_target_pairs={{0,1},{1,2},{2,3},{3,4},{4,5},{5,6},{6,7},{7,8},{8,9},{9,10},{10,1... | collective-permute-start | bytes 368648 | tf_op jit(solution)/shard_map/ppermute | solution.py:54
  188.6 11.4 %copy-start.37 = (f32[5]{0:T(128)S(1)}, f32[5]{0:T(128)}, u32[]{:S(2)}) copy-start(f32[5]{0:T(128)} %constant.109.clone) | copy-start | bytes 64
  188.6 16.0 %copy-start.34 = (f32[5]{0:T(128)S(1)}, f32[5]{0:T(128)}, u32[]{:S(2)}) copy-start(f32[5]{0:T(128)} %constant.110.clone) | copy-start | bytes 64
  189.7 6.6 %collective-permute-start.9 = (f32[5,48,128]{2,1,0:T(8,128)S(1)}, f32[5,48,128]{2,1,0:T(8,128)S(1)}, u32[]{:S(2)}, u32[]{:S(2)}) collective-permute-start(f32[5,48,128]{2,1,0:T(8,128)S(1)} %constant_dynamic-update-slice_fusion.45), channel_id=1, source_target_pairs={{0,15},{1,0},{2,1},{3,2},{4,3},{5,4},{6,5},{7,6},{8,7},{9,8},{10,9... | collective-permute-start | bytes 368648 | tf_op jit(solution)/shard_map/ppermute | solution.py:54
  196.5 3.4 %collective-permute-start.10 = (f32[5,4,48]{2,1,0:T(4,128)S(1)}, f32[5,4,48]{2,1,0:T(4,128)S(1)}, u32[]{:S(2)}, u32[]{:S(2)}) collective-permute-start(f32[5,4,48]{2,1,0:T(4,128)S(1)} %constant_dynamic-update-slice_fusion.50), channel_id=1, source_target_pairs={{0,16},{1,17},{2,18},{3,19},{4,20},{5,21},{6,22},{7,23},{8,24},{9,... | collective-permute-start | bytes 11528 | tf_op jit(solution)/shard_map/ppermute | solution.py:48
  198.6 5.9 %collective-permute-start.11 = (f32[5,4,48]{2,1,0:T(4,128)S(1)}, f32[5,4,48]{2,1,0:T(4,128)S(1)}, u32[]{:S(2)}, u32[]{:S(2)}) collective-permute-start(f32[5,4,48]{2,1,0:T(4,128)S(1)} %constant_dynamic-update-slice_fusion.55), channel_id=1, source_target_pairs={{16,0},{17,1},{18,2},{19,3},{20,4},{21,5},{22,6},{23,7},{24,8},{25... | collective-permute-start | bytes 11528 | tf_op jit(solution)/shard_map/ppermute | solution.py:48
  228.6 16.4 %collective-permute-start.23 = (f32[8,48,128]{2,1,0:T(8,128)S(1)}, f32[8,48,128]{2,1,0:T(8,128)S(1)}, u32[]{:S(2)}, u32[]{:S(2)}) collective-permute-start(f32[8,48,128]{2,1,0:T(8,128)S(1)} %get-tuple-element.176), channel_id=1, source_target_pairs={{0,15},{1,0},{2,1},{3,2},{4,3},{5,4},{6,5},{7,6},{8,7},{9,8},{10,9... | collective-permute-start | bytes 589832 | tf_op jit(solution)/shard_map/ppermute | solution.py:54
  228.7 16.3 %collective-permute-start.22 = (f32[8,48,128]{2,1,0:T(8,128)S(1)}, f32[8,48,128]{2,1,0:T(8,128)S(1)}, u32[]{:S(2)}, u32[]{:S(2)}) collective-permute-start(f32[8,48,128]{2,1,0:T(8,128)S(1)} %get-tuple-element.177), channel_id=1, source_target_pairs={{0,1},{1,2},{2,3},{3,4},{4,5},{5,6},{6,7},{7,8},{8,9},{9,10},{10,1... | collective-permute-start | bytes 589832 | tf_op jit(solution)/shard_map/ppermute | solution.py:54
  234.8 8.9 %collective-permute-start.20 = (f32[8,4,48,1]{2,0,3,1:T(8,128)S(1)}, f32[8,4,48,1]{2,0,3,1:T(8,128)S(1)}, u32[]{:S(2)}, u32[]{:S(2)}) collective-permute-start(f32[8,4,48,1]{2,0,3,1:T(8,128)S(1)} %bitcast.329), channel_id=1, source_target_pairs={{0,16},{1,17},{2,18},{3,19},{4,20},{5,21},{6,22},{7,23},{8,24},{9,... | collective-permute-start | bytes 18440 | tf_op jit(solution)/shard_map/ppermute | solution.py:48
  236.5 6.0 %collective-permute-start.21 = (f32[8,4,48,1]{2,0,3,1:T(8,128)S(1)}, f32[8,4,48,1]{2,0,3,1:T(8,128)S(1)}, u32[]{:S(2)}, u32[]{:S(2)}) collective-permute-start(f32[8,4,48,1]{2,0,3,1:T(8,128)S(1)} %bitcast.331), channel_id=1, source_target_pairs={{16,0},{17,1},{18,2},{19,3},{20,4},{21,5},{22,6},{23,7},{24,8},{25... | collective-permute-start | bytes 18440 | tf_op jit(solution)/shard_map/ppermute | solution.py:48
  (5 other events, 6.9 us)

commit v3 on v2

--- a/solution.py
+++ b/solution.py
@@ -367,20 +367,23 @@
         weights, columns, precision=lax.Precision.HIGHEST, preferred_element_type=jnp.float32
     ).reshape(concentration.shape)
     solid_flag = solid.astype(jnp.int32)
-    whole = gathered_copies(flow_pops, "row", 2)
-    flow = [whole[member] for member in range(19)]
+    flow_solid = lax.dynamic_slice_in_dim(solid, row_index * slab_depth, slab_depth, 1)
+    flow = [flow_pops[member] for member in range(19)]
     scalars = concentration
     halos = None
     for time_step in range(STEPS):
-        flow, motion = flow_collide(flow, solid)
+        flow, motion = flow_collide(flow, flow_solid)
+        column = gathered_copies(motion, "row", 2)
         mode = "first" if time_step == 0 else "middle"
-        scalars = scalar_stage(mode, scalars, halos, motion, solid_flag, source)
+        scalars = scalar_stage(mode, scalars, halos, column, solid_flag, source)
         halos = scalar_edges(scalars)
-        flow = local_vertical(flow, flow_vectors, 1)
+        from_below = send_vertical(edge_planes(flow, flow_vectors, 2, 1, 1), 1)
+        from_above = send_vertical(edge_planes(flow, flow_vectors, 2, 1, -1), -1)
+        flow = displace(flow, flow_vectors, 2, 1, from_below, from_above)
         flow = flow_section(flow, 1, 0, send_spanwise, keep_spanwise)
         flow = flow_section(flow, 0, 2, send_streamwise, inflow_fill)
     amount = scalar_stage("final", scalars, halos, None, None, None)
-    stacked = lax.dynamic_slice_in_dim(jnp.stack(flow), row_index * slab_depth, slab_depth, 2)
+    stacked = jnp.stack(flow)
     return (stacked, amount)
 
 

time: 255 us -> 214 us (0.84)
  the two profiles are of different devices: /device:TPU:7 before, /device:TPU:32 now
where the time goes in v3:
time: 214 us; the launch traced here: 211 us
  starting transfers between devices  93.3 us (44%)
  local copies, waits for them, and re-layouts  35.2 us (16%)
  Pallas kernels  33.3 us (16%)
  waiting for transfers between devices  31.1 us (15%)
  other arithmetic  14.1 us (7%)
  between operations  2.23 us (1%)
    ppermute x18, starting transfers between devices, passed_along(): return lax.ppermute(block, axis, route)  47.9 us
    pallas_call x4, Pallas kernels, scalar_stage(): pl.pallas_call(scalar_kernel(mode, span_y, depth, span_x), grid=(count,),...  33.3 us
    all_to_all x3, starting transfers between devices, copy_for_each(): return lax.all_to_all(copies, axis, split_axis=0, concat_axis=0, tiled=True)  26 us
    ppermute x18, waiting for transfers between devices, passed_along(): return lax.ppermute(block, axis, route)  21.3 us
    ppermute x12, starting transfers between devices, from_behind(): return lax.ppermute(value, axis, pairs)  19.4 us
    ppermute x12, waiting for transfers between devices, from_behind(): return lax.ppermute(value, axis, pairs)  9.83 us
    ppermute x6, local copies, waits for them, and re-layouts, passed_along(): return lax.ppermute(block, axis, route)  7.46 us
    slice x6, local copies, waits for them, and re-layouts, scalar_edges(): hi_x = passed_along(post[2, :, :, :, 0:1], 'gx', -1)  5.83 us
  transfers between devices with their start and end apart: 33, of which 8 were waited for; matrix products, arithmetic and copies ran while one was open for 16% of the time, Pallas kernels for 8%

profile of v3, /device:TPU:32, one launch (start us, length us, event | category | flops | bytes accessed | tf_op | source)
XLA Modules:
  0.0 211.4 jit_solution(9107477331508345777)
XLA Ops:
  0.7 1.0 fusion.25
  1.7 1.6 fusion.340
  3.3 1.1 bitcast_select_fusion.8
  4.4 0.9 fusion.306
  5.3 0.9 fusion.316
  6.3 3.7 %collective-permute-start.1 = (f32[5,4,128]{2,1,0:T(4,128)S(1)}, f32[5,4,128]{2,1,0:T(4,128)S(1)}, u32[]{:S(2)}, u32[]{:S(2)}) collective-permute-start(f32[5,4,128]{2,1,0:T(4,128)S(1)} %constant_dynamic-update-slice_fusion.5), channel_id=1, source_target_pairs={{32,0},{64,32},{96,64},{128,96},{160,128},{192,160},{224,192},{33,... | collective-permute-start | bytes 30728 | tf_op jit(solution)/shard_map/ppermute | solution.py:48
  10.0 0.8 bitcast_select_fusion.7
  10.8 0.9 bitcast_select_fusion.5
  11.7 2.1 %collective-permute-start = (f32[5,4,128]{2,1,0:T(4,128)S(1)}, f32[5,4,128]{2,1,0:T(4,128)S(1)}, u32[]{:S(2)}, u32[]{:S(2)}) collective-permute-start(f32[5,4,128]{2,1,0:T(4,128)S(1)} %constant_dynamic-update-slice_fusion), channel_id=1, source_target_pairs={{0,32},{32,64},{64,96},{96,128},{128,160},{160,192},{192,224},{1,3... | collective-permute-start | bytes 30728 | tf_op jit(solution)/shard_map/ppermute | solution.py:48
  14.8 2.1 fusion.refs_3_.refs_7_
  17.3 2.9 %collective-permute-start.3 = (f32[5,6,128]{2,0,1:T(8,128)S(1)}, f32[5,6,128]{2,0,1:T(8,128)S(1)}, u32[]{:S(2)}, u32[]{:S(2)}) collective-permute-start(f32[5,6,128]{2,0,1:T(8,128)S(1)} %stack.162), channel_id=1, source_target_pairs={{0,15},{1,0},{2,1},{3,2},{4,3},{5,4},{6,5},{7,6},{8,7},{9,8},{10,9... | collective-permute-start | bytes 46088 | tf_op jit(solution)/shard_map/ppermute | solution.py:54
  21.0 4.7 %collective-permute-done.2 = f32[5,6,128]{2,0,1:T(8,128)S(1)} collective-permute-done((f32[5,6,128]{2,0,1:T(8,128)S(1)}, f32[5,6,128]{2,0,1:T(8,128)S(1)}, u32[]{:S(2)}, u32[]{:S(2)}) %collective-permute-start.2) | collective-permute-done | bytes 15392 | tf_op jit(solution)/shard_map/ppermute | solution.py:54
  26.2 4.8 %collective-permute-start.4 = (f32[5,4,6]{2,1,0:T(4,128)S(1)}, f32[5,4,6]{2,1,0:T(4,128)S(1)}, u32[]{:S(2)}, u32[]{:S(2)}) collective-permute-start(f32[5,4,6]{2,1,0:T(4,128)S(1)} %constant_dynamic-update-slice_fusion.10), channel_id=1, source_target_pairs={{0,16},{1,17},{2,18},{3,19},{4,20},{5,21},{6,22},{7,23},{8,24},{9,... | collective-permute-start | bytes 1448 | tf_op jit(solution)/shard_map/ppermute | solution.py:48
  31.3 1.3 collective-permute-start.5
  33.5 4.9 %collective-permute-done.5 = f32[5,4,6]{2,1,0:T(4,128)S(1)} collective-permute-done((f32[5,4,6]{2,1,0:T(4,128)S(1)}, f32[5,4,6]{2,1,0:T(4,128)S(1)}, u32[]{:S(2)}, u32[]{:S(2)}) %collective-permute-start.5) | collective-permute-done | bytes 512 | tf_op jit(solution)/shard_map/ppermute | solution.py:48
  40.1 1.0 fusion.102
  41.6 2.0 collective-permute-start.7
  44.3 3.8 %collective-permute-start.6 = (f32[5,4,128]{2,1,0:T(4,128)S(1)}, f32[5,4,128]{2,1,0:T(4,128)S(1)}, u32[]{:S(2)}, u32[]{:S(2)}) collective-permute-start(f32[5,4,128]{2,1,0:T(4,128)S(1)} %constant_dynamic-update-slice_fusion.20), channel_id=1, source_target_pairs={{0,32},{32,64},{64,96},{96,128},{128,160},{160,192},{192,224},{1,3... | collective-permute-start | bytes 30728 | tf_op jit(solution)/shard_map/ppermute | solution.py:48
  48.2 1.7 collective-permute-done.6
  51.3 4.2 %collective-permute-done.8 = f32[5,6,128]{2,0,1:T(8,128)S(1)} collective-permute-done((f32[5,6,128]{2,0,1:T(8,128)S(1)}, f32[5,6,128]{2,0,1:T(8,128)S(1)}, u32[]{:S(2)}, u32[]{:S(2)}) %collective-permute-start.8) | collective-permute-done | bytes 15392 | tf_op jit(solution)/shard_map/ppermute | solution.py:54
  56.0 1.6 collective-permute-start.10
  57.9 1.3 collective-permute-start.11
  59.4 5.6 %collective-permute-done.11 = f32[5,4,6]{2,1,0:T(4,128)S(1)} collective-permute-done((f32[5,4,6]{2,1,0:T(4,128)S(1)}, f32[5,4,6]{2,1,0:T(4,128)S(1)}, u32[]{:S(2)}, u32[]{:S(2)}) %collective-permute-start.11) | collective-permute-done | bytes 512 | tf_op jit(solution)/shard_map/ppermute | solution.py:48
  67.6 4.6 %collective-permute-start.12 = (f32[5,4,128]{2,1,0:T(4,128)S(1)}, f32[5,4,128]{2,1,0:T(4,128)S(1)}, u32[]{:S(2)}, u32[]{:S(2)}) collective-permute-start(f32[5,4,128]{2,1,0:T(4,128)S(1)} %constant_dynamic-update-slice_fusion.40), channel_id=1, source_target_pairs={{0,32},{32,64},{64,96},{96,128},{128,160},{160,192},{192,224},{1,3... | collective-permute-start | bytes 30728 | tf_op jit(solution)/shard_map/ppermute | solution.py:48
  72.2 1.9 collective-permute-start.13
  74.4 0.8 broadcast_in_dim.21
  75.2 11.6 %all-to-all-start = ((f32[8,4,4,6,128]{4,2,3,1,0:T(4,128)}), f32[8,4,4,6,128]{4,2,3,1,0:T(4,128)S(1)}, u32[]{:S(2)}, u32[]{:S(2)}) async-start(f32[8,4,4,6,128]{4,2,3,1,0:T(4,128)} %broadcast_in_dim.21), calls=%async_computation | async-start | bytes 786432 | tf_op jit(solution)/shard_map/all_to_all | solution.py:65
  87.1 3.9 %collective-permute-start.15 = (f32[5,6,128]{2,1,0:T(8,128)S(1)}, f32[5,6,128]{2,1,0:T(8,128)S(1)}, u32[]{:S(2)}, u32[]{:S(2)}) collective-permute-start(f32[5,6,128]{2,1,0:T(8,128)S(1)} %constant_dynamic-update-slice_fusion.50), channel_id=1, source_target_pairs={{0,15},{1,0},{2,1},{3,2},{4,3},{5,4},{6,5},{7,6},{8,7},{9,8},{10,9... | collective-permute-start | bytes 46088 | tf_op jit(solution)/shard_map/ppermute | solution.py:54
  91.6 0.8 collective-permute-done.14
  92.8 1.6 collective-permute-start.16
  94.8 1.5 collective-permute-start.17
  96.6 5.3 %collective-permute-done.17 = f32[5,4,6]{2,1,0:T(4,128)S(1)} collective-permute-done((f32[5,4,6]{2,1,0:T(4,128)S(1)}, f32[5,4,6]{2,1,0:T(4,128)S(1)}, u32[]{:S(2)}, u32[]{:S(2)}) %collective-permute-start.17) | collective-permute-done | bytes 512 | tf_op jit(solution)/shard_map/ppermute | solution.py:48
  104.0 0.8 broadcast_in_dim.24
  104.7 7.2 %all-to-all-start.1 = ((f32[8,4,4,6,128]{4,2,3,1,0:T(4,128)}), f32[8,4,4,6,128]{4,2,3,1,0:T(4,128)S(1)}, u32[]{:S(2)}, u32[]{:S(2)}) async-start(f32[8,4,4,6,128]{4,2,3,1,0:T(4,128)} %broadcast_in_dim.24), calls=%async_computation.1 | async-start | bytes 786432 | tf_op jit(solution)/shard_map/all_to_all | solution.py:65
  112.0 0.8 copy.590.refs_1_
  112.8 7.9 %shard_map.131.refs_0_ = f32[7,8,4,48,128]{4,3,2,1,0:T(8,128)} custom-call(f32[8,4,48,128]{3,2,1,0:T(8,128)} %refs_0_.1, f32[4,4,48,128]{3,2,1,0:T(8,128)} %copy.590.refs_1_, s32[4,48,128]{2,1,0:T(8,128)} %get-tuple-element.30.refs_2_.refs_6_, f32[8,4,48,128]{3,2,1,0:T(8,128)} %fusion.refs_3_.refs_7_), custom_call_target="tpu_custom_call" | custom-call | tf_op jit(solution)/shard_map/pallas_call | solution.py:316
  120.7 1.6 fusion.388
  122.7 1.6 collective-permute-start.18
  124.6 1.3 collective-permute-start.19
  125.9 1.1 slice_bitcast_fusion.4
  127.1 3.8 %collective-permute-start.21 = (f32[8,48,128]{2,1,0:T(8,128)S(1)}, f32[8,48,128]{2,1,0:T(8,128)S(1)}, u32[]{:S(2)}, u32[]{:S(2)}) collective-permute-start(f32[8,48,128]{2,1,0:T(8,128)S(1)} %get-tuple-element.106), channel_id=1, source_target_pairs={{0,15},{1,0},{2,1},{3,2},{4,3},{5,4},{6,5},{7,6},{8,7},{9,8},{10,9... | collective-permute-start | bytes 589832 | tf_op jit(solution)/shard_map/ppermute | solution.py:54
  130.9 0.8 broadcast_in_dim.25
  131.7 7.2 %all-to-all-start.2 = ((f32[8,4,4,6,128]{4,2,3,1,0:T(4,128)}), f32[8,4,4,6,128]{4,2,3,1,0:T(4,128)S(1)}, u32[]{:S(2)}, u32[]{:S(2)}) async-start(f32[8,4,4,6,128]{4,2,3,1,0:T(4,128)} %broadcast_in_dim.25), calls=%async_computation.2 | async-start | bytes 786432 | tf_op jit(solution)/shard_map/all_to_all | solution.py:65
  139.0 0.8 copy.602.refs_5_
  139.7 1.3 copy.600.refs_1_
  141.0 1.2 copy.601.refs_2_
  143.6 9.3 %shard_map.132.refs_0_ = f32[7,8,4,48,128]{4,3,2,1,0:T(8,128)} custom-call(f32[7,8,4,48,128]{4,3,2,1,0:T(8,128)} %shard_map.131.refs_0_, f32[8,4,48,1]{3,2,1,0:T(8,128)} %copy.600.refs_1_, f32[8,4,48,1]{3,2,1,0:T(8,128)} %copy.601.refs_2_, f32[8,48,128]{2,1,0:T(8,128)} %copy-done, f32[8,48,128]{2,1,0:T(8,128)} %copy-done.1, ...), custom_call_target="tpu_custom_call" | custom-call | tf_op jit(solution)/shard_map/pallas_call | solution.py:316
  152.9 1.6 fusion.387
  154.8 6.1 %collective-permute-start.22 = (f32[8,4,48,1]{2,0,3,1:T(8,128)S(1)}, f32[8,4,48,1]{2,0,3,1:T(8,128)S(1)}, u32[]{:S(2)}, u32[]{:S(2)}) collective-permute-start(f32[8,4,48,1]{2,0,3,1:T(8,128)S(1)} %bitcast.860), channel_id=1, source_target_pairs={{0,16},{1,17},{2,18},{3,19},{4,20},{5,21},{6,22},{7,23},{8,24},{9,... | collective-permute-start | bytes 18440 | tf_op jit(solution)/shard_map/ppermute | solution.py:48
  161.2 1.3 collective-permute-start.23
  162.5 1.1 slice_bitcast_fusion.2
  163.6 3.8 %collective-permute-start.25 = (f32[8,48,128]{2,1,0:T(8,128)S(1)}, f32[8,48,128]{2,1,0:T(8,128)S(1)}, u32[]{:S(2)}, u32[]{:S(2)}) collective-permute-start(f32[8,48,128]{2,1,0:T(8,128)S(1)} %get-tuple-element.102), channel_id=1, source_target_pairs={{0,15},{1,0},{2,1},{3,2},{4,3},{5,4},{6,5},{7,6},{8,7},{9,8},{10,9... | collective-permute-start | bytes 589832 | tf_op jit(solution)/shard_map/ppermute | solution.py:54
  168.3 1.3 copy.614.refs_1_
  169.6 1.2 copy.615.refs_2_
  172.2 9.3 %shard_map.133.refs_0_ = f32[7,8,4,48,128]{4,3,2,1,0:T(8,128)} custom-call(f32[7,8,4,48,128]{4,3,2,1,0:T(8,128)} %shard_map.132.refs_0_, f32[8,4,48,1]{3,2,1,0:T(8,128)} %copy.614.refs_1_, f32[8,4,48,1]{3,2,1,0:T(8,128)} %copy.615.refs_2_, f32[8,48,128]{2,1,0:T(8,128)} %copy-done.2, f32[8,48,128]{2,1,0:T(8,128)} %copy-done.3, ...), custom_call_target="tpu_custom_call" | custom-call | tf_op jit(solution)/shard_map/pallas_call | solution.py:316
  181.4 1.0 slice_bitcast_fusion
  182.6 3.8 %collective-permute-start.29 = (f32[8,48,128]{2,1,0:T(8,128)S(1)}, f32[8,48,128]{2,1,0:T(8,128)S(1)}, u32[]{:S(2)}, u32[]{:S(2)}) collective-permute-start(f32[8,48,128]{2,1,0:T(8,128)S(1)} %get-tuple-element.98), channel_id=1, source_target_pairs={{0,15},{1,0},{2,1},{3,2},{4,3},{5,4},{6,5},{7,6},{8,7},{9,8},{10,9... | collective-permute-start | bytes 589832 | tf_op jit(solution)/shard_map/ppermute | solution.py:54
  186.4 1.6 fusion.386
  188.4 6.1 %collective-permute-start.26 = (f32[8,4,48,1]{2,0,3,1:T(8,128)S(1)}, f32[8,4,48,1]{2,0,3,1:T(8,128)S(1)}, u32[]{:S(2)}, u32[]{:S(2)}) collective-permute-start(f32[8,4,48,1]{2,0,3,1:T(8,128)S(1)} %bitcast.862), channel_id=1, source_target_pairs={{0,16},{1,17},{2,18},{3,19},{4,20},{5,21},{6,22},{7,23},{8,24},{9,... | collective-permute-start | bytes 18440 | tf_op jit(solution)/shard_map/ppermute | solution.py:48
  194.7 1.3 collective-permute-start.27
  196.8 1.2 copy.621.refs_1_
  198.0 3.8 %collective-permute-done.27 = f32[8,4,48,1]{2,0,3,1:T(8,128)S(1)} collective-permute-done((f32[8,4,48,1]{2,0,3,1:T(8,128)S(1)}, f32[8,4,48,1]{2,0,3,1:T(8,128)S(1)}, u32[]{:S(2)}, u32[]{:S(2)}) %collective-permute-start.27) | collective-permute-done | bytes 6176 | tf_op jit(solution)/shard_map/ppermute | solution.py:48
  201.9 1.2 copy.622.refs_2_
  204.5 6.9 %shard_map.134 = f32[8,4,48,128]{3,2,1,0:T(8,128)} custom-call(f32[7,8,4,48,128]{4,3,2,1,0:T(8,128)} %shard_map.133.refs_0_, f32[8,4,48,1]{3,2,1,0:T(8,128)} %copy.621.refs_1_, f32[8,4,48,1]{3,2,1,0:T(8,128)} %copy.622.refs_2_, f32[8,48,128]{2,1,0:T(8,128)} %copy-done.4, f32[8,48,128]{2,1,0:T(8,128)} %copy-done.5), custom_call_target="tpu_custom_call" | custom-call | tf_op jit(solution)/shard_map/pallas_call | solution.py:316
  (383 shorter events, 22.9 us)
Async XLA Ops:
  0.6 58.6 %copy-start.7 = (f32[5]{0:T(128)S(1)}, f32[5]{0:T(128)}, u32[]{:S(2)}) copy-start(f32[5]{0:T(128)} %constant.108.clone) | copy-start | bytes 64
  0.6 64.3 %copy-start.6 = (f32[5]{0:T(128)S(1)}, f32[5]{0:T(128)}, u32[]{:S(2)}) copy-start(f32[5]{0:T(128)} %constant.109.clone) | copy-start | bytes 64
  6.3 11.0 %collective-permute-start.1 = (f32[5,4,128]{2,1,0:T(4,128)S(1)}, f32[5,4,128]{2,1,0:T(4,128)S(1)}, u32[]{:S(2)}, u32[]{:S(2)}) collective-permute-start(f32[5,4,128]{2,1,0:T(4,128)S(1)} %constant_dynamic-update-slice_fusion.5), channel_id=1, source_target_pairs={{32,0},{64,32},{96,64},{128,96},{160,128},{192,160},{224,192},{33,... | collective-permute-start | bytes 30728 | tf_op jit(solution)/shard_map/ppermute | solution.py:48
  11.7 5.6 %collective-permute-start = (f32[5,4,128]{2,1,0:T(4,128)S(1)}, f32[5,4,128]{2,1,0:T(4,128)S(1)}, u32[]{:S(2)}, u32[]{:S(2)}) collective-permute-start(f32[5,4,128]{2,1,0:T(4,128)S(1)} %constant_dynamic-update-slice_fusion), channel_id=1, source_target_pairs={{0,32},{32,64},{64,96},{96,128},{128,160},{160,192},{192,224},{1,3... | collective-permute-start | bytes 30728 | tf_op jit(solution)/shard_map/ppermute | solution.py:48
  17.3 8.6 %collective-permute-start.3 = (f32[5,6,128]{2,0,1:T(8,128)S(1)}, f32[5,6,128]{2,0,1:T(8,128)S(1)}, u32[]{:S(2)}, u32[]{:S(2)}) collective-permute-start(f32[5,6,128]{2,0,1:T(8,128)S(1)} %stack.162), channel_id=1, source_target_pairs={{0,15},{1,0},{2,1},{3,2},{4,3},{5,4},{6,5},{7,6},{8,7},{9,8},{10,9... | collective-permute-start | bytes 46088 | tf_op jit(solution)/shard_map/ppermute | solution.py:54
  20.3 5.4 %collective-permute-start.2 = (f32[5,6,128]{2,0,1:T(8,128)S(1)}, f32[5,6,128]{2,0,1:T(8,128)S(1)}, u32[]{:S(2)}, u32[]{:S(2)}) collective-permute-start(f32[5,6,128]{2,0,1:T(8,128)S(1)} %stack.161), channel_id=1, source_target_pairs={{0,1},{1,2},{2,3},{3,4},{4,5},{5,6},{6,7},{7,8},{8,9},{9,10},{10,1... | collective-permute-start | bytes 46088 | tf_op jit(solution)/shard_map/ppermute | solution.py:54
  26.2 6.4 %collective-permute-start.4 = (f32[5,4,6]{2,1,0:T(4,128)S(1)}, f32[5,4,6]{2,1,0:T(4,128)S(1)}, u32[]{:S(2)}, u32[]{:S(2)}) collective-permute-start(f32[5,4,6]{2,1,0:T(4,128)S(1)} %constant_dynamic-update-slice_fusion.10), channel_id=1, source_target_pairs={{0,16},{1,17},{2,18},{3,19},{4,20},{5,21},{6,22},{7,23},{8,24},{9,... | collective-permute-start | bytes 1448 | tf_op jit(solution)/shard_map/ppermute | solution.py:48
  31.3 7.1 %collective-permute-start.5 = (f32[5,4,6]{2,1,0:T(4,128)S(1)}, f32[5,4,6]{2,1,0:T(4,128)S(1)}, u32[]{:S(2)}, u32[]{:S(2)}) collective-permute-start(f32[5,4,6]{2,1,0:T(4,128)S(1)} %constant_dynamic-update-slice_fusion.15), channel_id=1, source_target_pairs={{16,0},{17,1},{18,2},{19,3},{20,4},{21,5},{22,6},{23,7},{24,8},{25... | collective-permute-start | bytes 1448 | tf_op jit(solution)/shard_map/ppermute | solution.py:48
  41.6 6.6 %collective-permute-start.7 = (f32[5,4,128]{2,1,0:T(4,128)S(1)}, f32[5,4,128]{2,1,0:T(4,128)S(1)}, u32[]{:S(2)}, u32[]{:S(2)}) collective-permute-start(f32[5,4,128]{2,1,0:T(4,128)S(1)} %constant_dynamic-update-slice_fusion.25), channel_id=1, source_target_pairs={{32,0},{64,32},{96,64},{128,96},{160,128},{192,160},{224,192},{33,... | collective-permute-start | bytes 30728 | tf_op jit(solution)/shard_map/ppermute | solution.py:48
  44.3 5.6 %collective-permute-start.6 = (f32[5,4,128]{2,1,0:T(4,128)S(1)}, f32[5,4,128]{2,1,0:T(4,128)S(1)}, u32[]{:S(2)}, u32[]{:S(2)}) collective-permute-start(f32[5,4,128]{2,1,0:T(4,128)S(1)} %constant_dynamic-update-slice_fusion.20), channel_id=1, source_target_pairs={{0,32},{32,64},{64,96},{96,128},{128,160},{160,192},{192,224},{1,3... | collective-permute-start | bytes 30728 | tf_op jit(solution)/shard_map/ppermute | solution.py:48
  49.9 5.8 %collective-permute-start.9 = (f32[5,6,128]{2,0,1:T(8,128)S(1)}, f32[5,6,128]{2,0,1:T(8,128)S(1)}, u32[]{:S(2)}, u32[]{:S(2)}) collective-permute-start(f32[5,6,128]{2,0,1:T(8,128)S(1)} %stack.168), channel_id=1, source_target_pairs={{0,15},{1,0},{2,1},{3,2},{4,3},{5,4},{6,5},{7,6},{8,7},{9,8},{10,9... | collective-permute-start | bytes 46088 | tf_op jit(solution)/shard_map/ppermute | solution.py:54
  50.0 5.4 %collective-permute-start.8 = (f32[5,6,128]{2,0,1:T(8,128)S(1)}, f32[5,6,128]{2,0,1:T(8,128)S(1)}, u32[]{:S(2)}, u32[]{:S(2)}) collective-permute-start(f32[5,6,128]{2,0,1:T(8,128)S(1)} %stack.167), channel_id=1, source_target_pairs={{0,1},{1,2},{2,3},{3,4},{4,5},{5,6},{6,7},{7,8},{8,9},{9,10},{10,1... | collective-permute-start | bytes 46088 | tf_op jit(solution)/shard_map/ppermute | solution.py:54
  56.0 3.2 %collective-permute-start.10 = (f32[5,4,6]{2,1,0:T(4,128)S(1)}, f32[5,4,6]{2,1,0:T(4,128)S(1)}, u32[]{:S(2)}, u32[]{:S(2)}) collective-permute-start(f32[5,4,6]{2,1,0:T(4,128)S(1)} %constant_dynamic-update-slice_fusion.30), channel_id=1, source_target_pairs={{0,16},{1,17},{2,18},{3,19},{4,20},{5,21},{6,22},{7,23},{8,24},{9,... | collective-permute-start | bytes 1448 | tf_op jit(solution)/shard_map/ppermute | solution.py:48
  57.9 7.1 %collective-permute-start.11 = (f32[5,4,6]{2,1,0:T(4,128)S(1)}, f32[5,4,6]{2,1,0:T(4,128)S(1)}, u32[]{:S(2)}, u32[]{:S(2)}) collective-permute-start(f32[5,4,6]{2,1,0:T(4,128)S(1)} %constant_dynamic-update-slice_fusion.35), channel_id=1, source_target_pairs={{16,0},{17,1},{18,2},{19,3},{20,4},{21,5},{22,6},{23,7},{24,8},{25... | collective-permute-start | bytes 1448 | tf_op jit(solution)/shard_map/ppermute | solution.py:48
  67.6 19.3 %collective-permute-start.12 = (f32[5,4,128]{2,1,0:T(4,128)S(1)}, f32[5,4,128]{2,1,0:T(4,128)S(1)}, u32[]{:S(2)}, u32[]{:S(2)}) collective-permute-start(f32[5,4,128]{2,1,0:T(4,128)S(1)} %constant_dynamic-update-slice_fusion.40), channel_id=1, source_target_pairs={{0,32},{32,64},{64,96},{96,128},{128,160},{160,192},{192,224},{1,3... | collective-permute-start | bytes 30728 | tf_op jit(solution)/shard_map/ppermute | solution.py:48
  72.2 14.6 %collective-permute-start.13 = (f32[5,4,128]{2,1,0:T(4,128)S(1)}, f32[5,4,128]{2,1,0:T(4,128)S(1)}, u32[]{:S(2)}, u32[]{:S(2)}) collective-permute-start(f32[5,4,128]{2,1,0:T(4,128)S(1)} %constant_dynamic-update-slice_fusion.45), channel_id=1, source_target_pairs={{32,0},{64,32},{96,64},{128,96},{160,128},{192,160},{224,192},{33,... | collective-permute-start | bytes 30728 | tf_op jit(solution)/shard_map/ppermute | solution.py:48
  75.2 28.8 %all-to-all-start = ((f32[8,4,4,6,128]{4,2,3,1,0:T(4,128)}), f32[8,4,4,6,128]{4,2,3,1,0:T(4,128)S(1)}, u32[]{:S(2)}, u32[]{:S(2)}) async-start(f32[8,4,4,6,128]{4,2,3,1,0:T(4,128)} %broadcast_in_dim.21), calls=%async_computation | async-start | bytes 786432 | tf_op jit(solution)/shard_map/all_to_all | solution.py:65
  86.9 5.4 %collective-permute-start.14 = (f32[5,6,128]{2,0,1:T(8,128)S(1)}, f32[5,6,128]{2,0,1:T(8,128)S(1)}, u32[]{:S(2)}, u32[]{:S(2)}) collective-permute-start(f32[5,6,128]{2,0,1:T(8,128)S(1)} %stack.174), channel_id=1, source_target_pairs={{0,1},{1,2},{2,3},{3,4},{4,5},{5,6},{6,7},{7,8},{8,9},{9,10},{10,1... | collective-permute-start | bytes 46088 | tf_op jit(solution)/shard_map/ppermute | solution.py:54
  87.1 5.5 %collective-permute-start.15 = (f32[5,6,128]{2,1,0:T(8,128)S(1)}, f32[5,6,128]{2,1,0:T(8,128)S(1)}, u32[]{:S(2)}, u32[]{:S(2)}) collective-permute-start(f32[5,6,128]{2,1,0:T(8,128)S(1)} %constant_dynamic-update-slice_fusion.50), channel_id=1, source_target_pairs={{0,15},{1,0},{2,1},{3,2},{4,3},{5,4},{6,5},{7,6},{8,7},{9,8},{10,9... | collective-permute-start | bytes 46088 | tf_op jit(solution)/shard_map/ppermute | solution.py:54
  92.8 3.5 %collective-permute-start.16 = (f32[5,4,6]{2,1,0:T(4,128)S(1)}, f32[5,4,6]{2,1,0:T(4,128)S(1)}, u32[]{:S(2)}, u32[]{:S(2)}) collective-permute-start(f32[5,4,6]{2,1,0:T(4,128)S(1)} %constant_dynamic-update-slice_fusion.55), channel_id=1, source_target_pairs={{0,16},{1,17},{2,18},{3,19},{4,20},{5,21},{6,22},{7,23},{8,24},{9,... | collective-permute-start | bytes 1448 | tf_op jit(solution)/shard_map/ppermute | solution.py:48
  94.8 7.1 %collective-permute-start.17 = (f32[5,4,6]{2,1,0:T(4,128)S(1)}, f32[5,4,6]{2,1,0:T(4,128)S(1)}, u32[]{:S(2)}, u32[]{:S(2)}) collective-permute-start(f32[5,4,6]{2,1,0:T(4,128)S(1)} %constant_dynamic-update-slice_fusion.60), channel_id=1, source_target_pairs={{16,0},{17,1},{18,2},{19,3},{20,4},{21,5},{22,6},{23,7},{24,8},{25... | collective-permute-start | bytes 1448 | tf_op jit(solution)/shard_map/ppermute | solution.py:48
  104.7 26.2 %all-to-all-start.1 = ((f32[8,4,4,6,128]{4,2,3,1,0:T(4,128)}), f32[8,4,4,6,128]{4,2,3,1,0:T(4,128)S(1)}, u32[]{:S(2)}, u32[]{:S(2)}) async-start(f32[8,4,4,6,128]{4,2,3,1,0:T(4,128)} %broadcast_in_dim.24), calls=%async_computation.1 | async-start | bytes 786432 | tf_op jit(solution)/shard_map/all_to_all | solution.py:65
  122.7 17.1 %collective-permute-start.18 = (f32[8,4,48,1]{2,0,3,1:T(8,128)S(1)}, f32[8,4,48,1]{2,0,3,1:T(8,128)S(1)}, u32[]{:S(2)}, u32[]{:S(2)}) collective-permute-start(f32[8,4,48,1]{2,0,3,1:T(8,128)S(1)} %bitcast.858), channel_id=1, source_target_pairs={{0,16},{1,17},{2,18},{3,19},{4,20},{5,21},{6,22},{7,23},{8,24},{9,... | collective-permute-start | bytes 18440 | tf_op jit(solution)/shard_map/ppermute | solution.py:48
  124.6 16.4 %collective-permute-start.19 = (f32[8,4,48,1]{2,0,3,1:T(8,128)S(1)}, f32[8,4,48,1]{2,0,3,1:T(8,128)S(1)}, u32[]{:S(2)}, u32[]{:S(2)}) collective-permute-start(f32[8,4,48,1]{2,0,3,1:T(8,128)S(1)} %bitcast.859), channel_id=1, source_target_pairs={{16,0},{17,1},{18,2},{19,3},{20,4},{21,5},{22,6},{23,7},{24,8},{25... | collective-permute-start | bytes 18440 | tf_op jit(solution)/shard_map/ppermute | solution.py:48
  127.0 15.2 %collective-permute-start.20 = (f32[8,48,128]{2,1,0:T(8,128)S(1)}, f32[8,48,128]{2,1,0:T(8,128)S(1)}, u32[]{:S(2)}, u32[]{:S(2)}) collective-permute-start(f32[8,48,128]{2,1,0:T(8,128)S(1)} %get-tuple-element.107), channel_id=1, source_target_pairs={{0,1},{1,2},{2,3},{3,4},{4,5},{5,6},{6,7},{7,8},{8,9},{9,10},{10,1... | collective-permute-start | bytes 589832 | tf_op jit(solution)/shard_map/ppermute | solution.py:54
  127.1 15.2 %collective-permute-start.21 = (f32[8,48,128]{2,1,0:T(8,128)S(1)}, f32[8,48,128]{2,1,0:T(8,128)S(1)}, u32[]{:S(2)}, u32[]{:S(2)}) collective-permute-start(f32[8,48,128]{2,1,0:T(8,128)S(1)} %get-tuple-element.106), channel_id=1, source_target_pairs={{0,15},{1,0},{2,1},{3,2},{4,3},{5,4},{6,5},{7,6},{8,7},{9,8},{10,9... | collective-permute-start | bytes 589832 | tf_op jit(solution)/shard_map/ppermute | solution.py:54
  131.7 35.8 %all-to-all-start.2 = ((f32[8,4,4,6,128]{4,2,3,1,0:T(4,128)}), f32[8,4,4,6,128]{4,2,3,1,0:T(4,128)S(1)}, u32[]{:S(2)}, u32[]{:S(2)}) async-start(f32[8,4,4,6,128]{4,2,3,1,0:T(4,128)} %broadcast_in_dim.25), calls=%async_computation.2 | async-start | bytes 786432 | tf_op jit(solution)/shard_map/all_to_all | solution.py:65
  142.2 0.7 copy-start
  142.9 0.7 copy-start.1
  154.8 13.5 %collective-permute-start.22 = (f32[8,4,48,1]{2,0,3,1:T(8,128)S(1)}, f32[8,4,48,1]{2,0,3,1:T(8,128)S(1)}, u32[]{:S(2)}, u32[]{:S(2)}) collective-permute-start(f32[8,4,48,1]{2,0,3,1:T(8,128)S(1)} %bitcast.860), channel_id=1, source_target_pairs={{0,16},{1,17},{2,18},{3,19},{4,20},{5,21},{6,22},{7,23},{8,24},{9,... | collective-permute-start | bytes 18440 | tf_op jit(solution)/shard_map/ppermute | solution.py:48
  161.2 8.4 %collective-permute-start.23 = (f32[8,4,48,1]{2,0,3,1:T(8,128)S(1)}, f32[8,4,48,1]{2,0,3,1:T(8,128)S(1)}, u32[]{:S(2)}, u32[]{:S(2)}) collective-permute-start(f32[8,4,48,1]{2,0,3,1:T(8,128)S(1)} %bitcast.861), channel_id=1, source_target_pairs={{16,0},{17,1},{18,2},{19,3},{20,4},{21,5},{22,6},{23,7},{24,8},{25... | collective-permute-start | bytes 18440 | tf_op jit(solution)/shard_map/ppermute | solution.py:48
  163.6 7.3 %collective-permute-start.24 = (f32[8,48,128]{2,1,0:T(8,128)S(1)}, f32[8,48,128]{2,1,0:T(8,128)S(1)}, u32[]{:S(2)}, u32[]{:S(2)}) collective-permute-start(f32[8,48,128]{2,1,0:T(8,128)S(1)} %get-tuple-element.103), channel_id=1, source_target_pairs={{0,1},{1,2},{2,3},{3,4},{4,5},{5,6},{6,7},{7,8},{8,9},{9,10},{10,1... | collective-permute-start | bytes 589832 | tf_op jit(solution)/shard_map/ppermute | solution.py:54
  163.6 7.2 %collective-permute-start.25 = (f32[8,48,128]{2,1,0:T(8,128)S(1)}, f32[8,48,128]{2,1,0:T(8,128)S(1)}, u32[]{:S(2)}, u32[]{:S(2)}) collective-permute-start(f32[8,48,128]{2,1,0:T(8,128)S(1)} %get-tuple-element.102), channel_id=1, source_target_pairs={{0,15},{1,0},{2,1},{3,2},{4,3},{5,4},{6,5},{7,6},{8,7},{9,8},{10,9... | collective-permute-start | bytes 589832 | tf_op jit(solution)/shard_map/ppermute | solution.py:54
  170.8 0.7 copy-start.2
  171.5 0.7 copy-start.3
  182.5 20.6 %collective-permute-start.28 = (f32[8,48,128]{2,1,0:T(8,128)S(1)}, f32[8,48,128]{2,1,0:T(8,128)S(1)}, u32[]{:S(2)}, u32[]{:S(2)}) collective-permute-start(f32[8,48,128]{2,1,0:T(8,128)S(1)} %get-tuple-element.99), channel_id=1, source_target_pairs={{0,1},{1,2},{2,3},{3,4},{4,5},{5,6},{6,7},{7,8},{8,9},{9,10},{10,1... | collective-permute-start | bytes 589832 | tf_op jit(solution)/shard_map/ppermute | solution.py:54
  182.6 20.5 %collective-permute-start.29 = (f32[8,48,128]{2,1,0:T(8,128)S(1)}, f32[8,48,128]{2,1,0:T(8,128)S(1)}, u32[]{:S(2)}, u32[]{:S(2)}) collective-permute-start(f32[8,48,128]{2,1,0:T(8,128)S(1)} %get-tuple-element.98), channel_id=1, source_target_pairs={{0,15},{1,0},{2,1},{3,2},{4,3},{5,4},{6,5},{7,6},{8,7},{9,8},{10,9... | collective-permute-start | bytes 589832 | tf_op jit(solution)/shard_map/ppermute | solution.py:54
  188.4 8.4 %collective-permute-start.26 = (f32[8,4,48,1]{2,0,3,1:T(8,128)S(1)}, f32[8,4,48,1]{2,0,3,1:T(8,128)S(1)}, u32[]{:S(2)}, u32[]{:S(2)}) collective-permute-start(f32[8,4,48,1]{2,0,3,1:T(8,128)S(1)} %bitcast.862), channel_id=1, source_target_pairs={{0,16},{1,17},{2,18},{3,19},{4,20},{5,21},{6,22},{7,23},{8,24},{9,... | collective-permute-start | bytes 18440 | tf_op jit(solution)/shard_map/ppermute | solution.py:48
  194.7 7.1 %collective-permute-start.27 = (f32[8,4,48,1]{2,0,3,1:T(8,128)S(1)}, f32[8,4,48,1]{2,0,3,1:T(8,128)S(1)}, u32[]{:S(2)}, u32[]{:S(2)}) collective-permute-start(f32[8,4,48,1]{2,0,3,1:T(8,128)S(1)} %bitcast.863), channel_id=1, source_target_pairs={{16,0},{17,1},{18,2},{19,3},{20,4},{21,5},{22,6},{23,7},{24,8},{25... | collective-permute-start | bytes 18440 | tf_op jit(solution)/shard_map/ppermute | solution.py:48
  203.1 0.7 copy-start.4
  203.8 0.7 copy-start.5

commit v4 on v3

--- a/solution.py
+++ b/solution.py
@@ -322,13 +322,26 @@
     )(*operands)
 
 
-def scalar_edges(post):
-    span_y, span_x = post.shape[2], post.shape[4]
-    lo_x = passed_along(post[1, :, :, :, span_x - 1 : span_x], "gx", 1)
-    hi_x = passed_along(post[2, :, :, :, 0:1], "gx", -1)
-    lo_y = from_behind(post[3, :, span_y - 1], "gy", 1)
-    hi_y = from_behind(post[4, :, 0], "gy", -1)
-    return (lo_x, hi_x, lo_y, hi_y)
+def packed_section(flow, scalar_out, component, flow_dim, sender, edge_fill, keep_rows):
+    arrived_flow = {}
+    arrived_scalar = {}
+    for heading in (1, -1):
+        flow_planes = edge_planes(flow, flow_vectors, component, flow_dim, heading)
+        scalar_planes = scalar_out[heading]
+        if keep_rows:
+            width = flow_planes.shape[-1]
+            packed = jnp.concatenate(
+                [flow_planes.reshape(-1, width), scalar_planes.reshape(-1, width)], 0
+            )
+            split_at = flow_planes.size // width
+        else:
+            packed = jnp.concatenate([flow_planes.reshape(-1), scalar_planes.reshape(-1)], 0)
+            split_at = flow_planes.size
+        arrived = sender(packed, heading)
+        arrived_flow[heading] = edge_fill(arrived[:split_at].reshape(flow_planes.shape), heading)
+        arrived_scalar[heading] = arrived[split_at:].reshape(scalar_planes.shape)
+    flow = displace(flow, flow_vectors, component, flow_dim, arrived_flow[1], arrived_flow[-1])
+    return (flow, arrived_scalar)
 
 
 def flow_section(flow, component, flow_dim, sender, edge_fill):
@@ -376,12 +389,14 @@
         column = gathered_copies(motion, "row", 2)
         mode = "first" if time_step == 0 else "middle"
         scalars = scalar_stage(mode, scalars, halos, column, solid_flag, source)
-        halos = scalar_edges(scalars)
         from_below = send_vertical(edge_planes(flow, flow_vectors, 2, 1, 1), 1)
         from_above = send_vertical(edge_planes(flow, flow_vectors, 2, 1, -1), -1)
         flow = displace(flow, flow_vectors, 2, 1, from_below, from_above)
-        flow = flow_section(flow, 1, 0, send_spanwise, keep_spanwise)
-        flow = flow_section(flow, 0, 2, send_streamwise, inflow_fill)
+        leaving_y = {1: scalars[3, :, span_y - 1], -1: scalars[4, :, 0]}
+        flow, arrived_y = packed_section(flow, leaving_y, 1, 0, send_spanwise, keep_spanwise, True)
+        leaving_x = {1: scalars[1, :, :, :, span_x - 1 :], -1: scalars[2, :, :, :, :1]}
+        flow, arrived_x = packed_section(flow, leaving_x, 0, 2, send_streamwise, inflow_fill, False)
+        halos = (arrived_x[1], arrived_x[-1], arrived_y[1], arrived_y[-1])
     amount = scalar_stage("final", scalars, halos, None, None, None)
     stacked = jnp.stack(flow)
     return (stacked, amount)

time: 214 us -> 188 us (0.88)
  the two profiles are of different devices: /device:TPU:32 before, /device:TPU:7 now
where the time goes in v4:
time: 188 us; the launch traced here: 186 us
  starting transfers between devices  58.3 us (31%)
  local copies, waits for them, and re-layouts  38.8 us (21%)
  waiting for transfers between devices  38.1 us (20%)
  Pallas kernels  33.3 us (18%)
  other arithmetic  13.3 us (7%)
  between operations  2.36 us (1%)
  matrix products  2.09 us (1%)
    pallas_call x4, Pallas kernels, scalar_stage(): pl.pallas_call(scalar_kernel(mode, span_y, depth, span_x), grid=(count,),...  33.3 us
    ppermute x12, starting transfers between devices, passed_along(): return lax.ppermute(block, axis, route)  32.3 us
    all_to_all x3, waiting for transfers between devices, copy_for_each(): return lax.all_to_all(copies, axis, split_axis=0, concat_axis=0, tiled=True)  20.5 us
    all_to_all x3, starting transfers between devices, copy_for_each(): return lax.all_to_all(copies, axis, split_axis=0, concat_axis=0, tiled=True)  17.9 us
    ppermute x6, waiting for transfers between devices, from_behind(): return lax.ppermute(value, axis, pairs)  14.9 us
    reshape x6, local copies, waits for them, and re-layouts, packed_section(): arrived_scalar[heading] = arrived[split_at:].reshape(scalar_planes.shape)  9.15 us
    ppermute x6, starting transfers between devices, from_behind(): return lax.ppermute(value, axis, pairs)  8.15 us
    select_n x17, other arithmetic, flow_collide(): updated.append(jnp.where(solid, populations[flow_mirror[member]], relaxed))  5.17 us
  transfers between devices with their start and end apart: 21, of which 10 were waited for; matrix products, arithmetic and copies ran while one was open for 18% of the time, Pallas kernels for 0%

profile of v4, /device:TPU:7, one launch (start us, length us, event | category | flops | bytes accessed | tf_op | source)
XLA Modules:
  0.0 186.3 jit_solution(16629847441128276870)
XLA Ops:
  0.6 1.0 fusion.25
  1.6 1.6 fusion.402
  3.3 1.1 bitcast_select_fusion.8
  4.4 0.9 fusion.314
  5.3 0.9 bitcast_select_fusion
  6.2 3.5 %collective-permute-start = (f32[5,4,128]{2,1,0:T(4,128)S(1)}, f32[5,4,128]{2,1,0:T(4,128)S(1)}, u32[]{:S(2)}, u32[]{:S(2)}) collective-permute-start(f32[5,4,128]{2,1,0:T(4,128)S(1)} %constant_dynamic-update-slice_fusion), channel_id=1, source_target_pairs={{0,32},{32,64},{64,96},{96,128},{128,160},{160,192},{192,224},{1,3... | collective-permute-start | bytes 30728 | tf_op jit(solution)/shard_map/ppermute | solution.py:48
  9.8 0.9 fusion.330
  10.7 1.3 collective-permute-start.1
  12.0 0.8 broadcast_in_dim.21
  12.8 9.8 %all-to-all-start = ((f32[8,4,4,6,128]{4,2,3,1,0:T(4,128)}), f32[8,4,4,6,128]{4,2,3,1,0:T(4,128)S(1)}, u32[]{:S(2)}, u32[]{:S(2)}) async-start(f32[8,4,4,6,128]{4,2,3,1,0:T(4,128)} %broadcast_in_dim.21), calls=%async_computation | async-start | bytes 786432 | tf_op jit(solution)/shard_map/all_to_all | solution.py:65
  23.0 0.8 bitcast_select_fusion.7
  23.8 0.7 fusion.332
  24.5 2.1 %fusion.refs_3_.refs_7_ = f32[8,4,48,128]{3,2,1,0:T(8,128)} fusion(f32[96]{0:T(128)} %param.17, s32[96]{0:T(128)S(1)} %get-tuple-element.290, s32[96]{0:T(128)S(1)} %get-tuple-element.289, s32[96]{0:T(128)S(1)} %get-tuple-element.293, s32[96]{0:T(128)S(1)} %get-tuple-element.288), kind=kOutput, calls=%fused_computation.6 | convolution fusion | flops 227389440 | bytes 788352 | tf_op jit(solution)/shard_map/dot_general | solution.py:379
  27.7 8.0 %all-to-all-done = f32[8,4,4,6,128]{4,2,3,1,0:T(4,128)S(1)} async-done(((f32[8,4,4,6,128]{4,2,3,1,0:T(4,128)}), f32[8,4,4,6,128]{4,2,3,1,0:T(4,128)S(1)}, u32[]{:S(2)}, u32[]{:S(2)}) %all-to-all-start) | async-done | bytes 393248 | tf_op jit(solution)/shard_map/all_to_all | solution.py:65
  35.7 0.8 copy.380.refs_1_
  36.5 7.9 %shard_map.131.refs_0_ = f32[7,8,4,48,128]{4,3,2,1,0:T(8,128)} custom-call(f32[8,4,48,128]{3,2,1,0:T(8,128)} %refs_0_.1, f32[4,4,48,128]{3,2,1,0:T(8,128)} %copy.380.refs_1_, s32[4,48,128]{2,1,0:T(8,128)} %get-tuple-element.112.refs_2_.refs_6_, f32[8,4,48,128]{3,2,1,0:T(8,128)} %fusion.refs_3_.refs_7_), custom_call_target="tpu_custom_call" | custom-call | tf_op jit(solution)/shard_map/pallas_call | solution.py:316
  44.4 1.0 fusion.408
  45.5 3.8 %collective-permute-start.2 = (f32[414,128]{1,0:T(8,128)S(1)}, f32[414,128]{1,0:T(8,128)S(1)}, u32[]{:S(2)}, u32[]{:S(2)}) collective-permute-start(f32[414,128]{1,0:T(8,128)S(1)} %pad_maximum_fusion), channel_id=1, source_target_pairs={{0,1},{1,2},{2,3},{3,4},{4,5},{5,6},{6,7},{7,8},{8,9},{9,10},{10,1... | collective-permute-start | bytes 635912 | tf_op jit(solution)/shard_map/ppermute | solution.py:54
  49.4 2.1 %slice_reduce_fusion.5 = (f32[8,4,48]{2,1,0:T(4,128)S(1)}, f32[8,4,48]{2,1,0:T(4,128)S(1)}) fusion(f32[7,8,4,48,128]{4,3,2,1,0:T(8,128)} %shard_map.131.refs_0_), kind=kLoop, calls=%fused_computation.5 | loop fusion | bytes 24576 | tf_op jit(solution)/shard_map/slice | solution.py:397
  52.3 4.5 %collective-permute-done.3 = f32[414,128]{1,0:T(8,128)S(1)} collective-permute-done((f32[414,128]{1,0:T(8,128)S(1)}, f32[414,128]{1,0:T(8,128)S(1)}, u32[]{:S(2)}, u32[]{:S(2)}) %collective-permute-start.3) | collective-permute-done | bytes 212000 | tf_op jit(solution)/shard_map/ppermute | solution.py:54
  57.2 1.3 collective-permute-start.5
  59.1 5.5 %collective-permute-start.4 = (f32[1656]{0:T(1024)S(1)}, f32[1656]{0:T(1024)S(1)}, u32[]{:S(2)}, u32[]{:S(2)}) collective-permute-start(f32[1656]{0:T(1024)S(1)} %pad_maximum_fusion.57), channel_id=1, source_target_pairs={{0,16},{1,17},{2,18},{3,19},{4,20},{5,21},{6,22},{7,23},{8,24},{9,... | collective-permute-start | bytes 19880 | tf_op jit(solution)/shard_map/ppermute | solution.py:48
  64.6 0.7 slice.1589
  65.3 0.7 slice.1588
  67.5 1.0 fusion.252
  69.2 2.2 %collective-permute-start.6 = (f32[5,4,128]{2,1,0:T(4,128)S(1)}, f32[5,4,128]{2,1,0:T(4,128)S(1)}, u32[]{:S(2)}, u32[]{:S(2)}) collective-permute-start(f32[5,4,128]{2,1,0:T(4,128)S(1)} %constant_dynamic-update-slice_fusion.20), channel_id=1, source_target_pairs={{0,32},{32,64},{64,96},{96,128},{128,160},{160,192},{192,224},{1,3... | collective-permute-start | bytes 30728 | tf_op jit(solution)/shard_map/ppermute | solution.py:48
  71.5 1.3 collective-permute-start.7
  72.8 0.8 broadcast_in_dim.24
  73.6 4.6 %all-to-all-start.1 = ((f32[8,4,4,6,128]{4,2,3,1,0:T(4,128)}), f32[8,4,4,6,128]{4,2,3,1,0:T(4,128)S(1)}, u32[]{:S(2)}, u32[]{:S(2)}) async-start(f32[8,4,4,6,128]{4,2,3,1,0:T(4,128)} %broadcast_in_dim.24), calls=%async_computation.1 | async-start | bytes 786432 | tf_op jit(solution)/shard_map/all_to_all | solution.py:65
  78.8 1.6 reshape.278.refs_2_
  80.5 1.5 reshape.277.refs_1_
  82.8 9.0 %all-to-all-done.1 = f32[8,4,4,6,128]{4,2,3,1,0:T(4,128)S(1)} async-done(((f32[8,4,4,6,128]{4,2,3,1,0:T(4,128)}), f32[8,4,4,6,128]{4,2,3,1,0:T(4,128)S(1)}, u32[]{:S(2)}, u32[]{:S(2)}) %all-to-all-start.1) | async-done | bytes 393248 | tf_op jit(solution)/shard_map/all_to_all | solution.py:65
  91.9 0.8 copy.433.refs_5_
  92.7 9.3 %shard_map.132.refs_0_ = f32[7,8,4,48,128]{4,3,2,1,0:T(8,128)} custom-call(f32[7,8,4,48,128]{4,3,2,1,0:T(8,128)} %shard_map.131.refs_0_, f32[8,4,48,1]{3,2,1,0:T(8,128)} %reshape.277.refs_1_, f32[8,4,48,1]{3,2,1,0:T(8,128)} %reshape.278.refs_2_, f32[8,48,128]{2,1,0:T(8,128)} %bitcast.832, f32[8,48,128]{2,1,0:T(8,128)} %bitcast.831, ...), custom_call_target="tpu_custom_call" | custom-call | tf_op jit(solution)/shard_map/pallas_call | solution.py:316
  101.9 1.0 fusion.407
  103.0 1.3 collective-permute-start.8
  104.5 2.1 %slice_reduce_fusion.3 = (f32[8,4,48]{2,1,0:T(4,128)S(1)}, f32[8,4,48]{2,1,0:T(4,128)S(1)}) fusion(f32[7,8,4,48,128]{4,3,2,1,0:T(8,128)} %shard_map.132.refs_0_), kind=kLoop, calls=%fused_computation.3 | loop fusion | bytes 24576 | tf_op jit(solution)/shard_map/slice | solution.py:397
  107.3 4.5 %collective-permute-done.9 = f32[414,128]{1,0:T(8,128)S(1)} collective-permute-done((f32[414,128]{1,0:T(8,128)S(1)}, f32[414,128]{1,0:T(8,128)S(1)}, u32[]{:S(2)}, u32[]{:S(2)}) %collective-permute-start.9) | collective-permute-done | bytes 212000 | tf_op jit(solution)/shard_map/ppermute | solution.py:54
  112.2 1.5 collective-permute-start.11
  114.3 5.5 %collective-permute-start.10 = (f32[1656]{0:T(1024)S(1)}, f32[1656]{0:T(1024)S(1)}, u32[]{:S(2)}, u32[]{:S(2)}) collective-permute-start(f32[1656]{0:T(1024)S(1)} %pad_maximum_fusion.59), channel_id=1, source_target_pairs={{0,16},{1,17},{2,18},{3,19},{4,20},{5,21},{6,22},{7,23},{8,24},{9,... | collective-permute-start | bytes 19880 | tf_op jit(solution)/shard_map/ppermute | solution.py:48
  119.9 0.7 slice.1680
  120.6 0.7 slice.1681
  123.9 2.2 %collective-permute-start.12 = (f32[5,4,128]{2,1,0:T(4,128)S(1)}, f32[5,4,128]{2,1,0:T(4,128)S(1)}, u32[]{:S(2)}, u32[]{:S(2)}) collective-permute-start(f32[5,4,128]{2,1,0:T(4,128)S(1)} %constant_dynamic-update-slice_fusion.40), channel_id=1, source_target_pairs={{0,32},{32,64},{64,96},{96,128},{128,160},{160,192},{192,224},{1,3... | collective-permute-start | bytes 30728 | tf_op jit(solution)/shard_map/ppermute | solution.py:48
  126.2 0.8 broadcast_in_dim.25
  127.0 3.5 %all-to-all-start.2 = ((f32[8,4,4,6,128]{4,2,3,1,0:T(4,128)}), f32[8,4,4,6,128]{4,2,3,1,0:T(4,128)S(1)}, u32[]{:S(2)}, u32[]{:S(2)}) async-start(f32[8,4,4,6,128]{4,2,3,1,0:T(4,128)} %broadcast_in_dim.25), calls=%async_computation.2 | async-start | bytes 786432 | tf_op jit(solution)/shard_map/all_to_all | solution.py:65
  130.8 1.3 collective-permute-start.13
  132.2 1.6 reshape.280.refs_2_
  133.8 1.5 reshape.279.refs_1_
  135.4 2.7 %collective-permute-done.13 = f32[5,4,128]{2,1,0:T(4,128)S(1)} collective-permute-done((f32[5,4,128]{2,1,0:T(4,128)S(1)}, f32[5,4,128]{2,1,0:T(4,128)S(1)}, u32[]{:S(2)}, u32[]{:S(2)}) %collective-permute-start.13) | collective-permute-done | bytes 10272 | tf_op jit(solution)/shard_map/ppermute | solution.py:48
  138.9 3.4 %all-to-all-done.2 = f32[8,4,4,6,128]{4,2,3,1,0:T(4,128)S(1)} async-done(((f32[8,4,4,6,128]{4,2,3,1,0:T(4,128)}), f32[8,4,4,6,128]{4,2,3,1,0:T(4,128)S(1)}, u32[]{:S(2)}, u32[]{:S(2)}) %all-to-all-start.2) | async-done | bytes 393248 | tf_op jit(solution)/shard_map/all_to_all | solution.py:65
  142.4 0.8 copy.486.refs_5_
  143.1 9.3 %shard_map.133.refs_0_ = f32[7,8,4,48,128]{4,3,2,1,0:T(8,128)} custom-call(f32[7,8,4,48,128]{4,3,2,1,0:T(8,128)} %shard_map.132.refs_0_, f32[8,4,48,1]{3,2,1,0:T(8,128)} %reshape.279.refs_1_, f32[8,4,48,1]{3,2,1,0:T(8,128)} %reshape.280.refs_2_, f32[8,48,128]{2,1,0:T(8,128)} %bitcast.829, f32[8,48,128]{2,1,0:T(8,128)} %bitcast.830, ...), custom_call_target="tpu_custom_call" | custom-call | tf_op jit(solution)/shard_map/pallas_call | solution.py:316
  152.4 1.0 fusion.406
  153.5 2.7 %collective-permute-start.14 = (f32[414,128]{1,0:T(8,128)S(1)}, f32[414,128]{1,0:T(8,128)S(1)}, u32[]{:S(2)}, u32[]{:S(2)}) collective-permute-start(f32[414,128]{1,0:T(8,128)S(1)} %pad_maximum_fusion.4), channel_id=1, source_target_pairs={{0,1},{1,2},{2,3},{3,4},{4,5},{5,6},{6,7},{7,8},{8,9},{9,10},{10,1... | collective-permute-start | bytes 635912 | tf_op jit(solution)/shard_map/ppermute | solution.py:54
  156.4 2.1 %slice_reduce_fusion = (f32[8,4,48]{2,1,0:T(4,128)S(1)}, f32[8,4,48]{2,1,0:T(4,128)S(1)}) fusion(f32[7,8,4,48,128]{4,3,2,1,0:T(8,128)} %shard_map.133.refs_0_), kind=kLoop, calls=%fused_computation | loop fusion | bytes 24576 | tf_op jit(solution)/shard_map/slice | solution.py:397
  159.2 4.5 %collective-permute-done.15 = f32[414,128]{1,0:T(8,128)S(1)} collective-permute-done((f32[414,128]{1,0:T(8,128)S(1)}, f32[414,128]{1,0:T(8,128)S(1)}, u32[]{:S(2)}, u32[]{:S(2)}) %collective-permute-start.15) | collective-permute-done | bytes 212000 | tf_op jit(solution)/shard_map/ppermute | solution.py:54
  164.1 1.3 collective-permute-start.17
  166.0 5.5 %collective-permute-start.16 = (f32[1656]{0:T(1024)S(1)}, f32[1656]{0:T(1024)S(1)}, u32[]{:S(2)}, u32[]{:S(2)}) collective-permute-start(f32[1656]{0:T(1024)S(1)} %pad_maximum_fusion.61), channel_id=1, source_target_pairs={{0,16},{1,17},{2,18},{3,19},{4,20},{5,21},{6,22},{7,23},{8,24},{9,... | collective-permute-start | bytes 19880 | tf_op jit(solution)/shard_map/ppermute | solution.py:48
  171.6 0.7 slice.1755
  172.3 0.7 slice.1754
  173.1 1.5 reshape.282.refs_2_
  174.6 1.5 reshape.281.refs_1_
  178.7 0.8 copy.541
  179.5 6.9 %shard_map.134 = f32[8,4,48,128]{3,2,1,0:T(8,128)} custom-call(f32[7,8,4,48,128]{4,3,2,1,0:T(8,128)} %shard_map.133.refs_0_, f32[8,4,48,1]{3,2,1,0:T(8,128)} %reshape.281.refs_1_, f32[8,4,48,1]{3,2,1,0:T(8,128)} %reshape.282.refs_2_, f32[8,48,128]{2,1,0:T(8,128)} %bitcast.840, f32[8,48,128]{2,1,0:T(8,128)} %bitcast.839), custom_call_target="tpu_custom_call" | custom-call | tf_op jit(solution)/shard_map/pallas_call | solution.py:316
  (417 shorter events, 16.6 us)
Async XLA Ops:
  6.2 20.6 %collective-permute-start = (f32[5,4,128]{2,1,0:T(4,128)S(1)}, f32[5,4,128]{2,1,0:T(4,128)S(1)}, u32[]{:S(2)}, u32[]{:S(2)}) collective-permute-start(f32[5,4,128]{2,1,0:T(4,128)S(1)} %constant_dynamic-update-slice_fusion), channel_id=1, source_target_pairs={{0,32},{32,64},{64,96},{96,128},{128,160},{160,192},{192,224},{1,3... | collective-permute-start | bytes 30728 | tf_op jit(solution)/shard_map/ppermute | solution.py:48
  10.7 16.2 %collective-permute-start.1 = (f32[5,4,128]{2,1,0:T(4,128)S(1)}, f32[5,4,128]{2,1,0:T(4,128)S(1)}, u32[]{:S(2)}, u32[]{:S(2)}) collective-permute-start(f32[5,4,128]{2,1,0:T(4,128)S(1)} %constant_dynamic-update-slice_fusion.5), channel_id=1, source_target_pairs={{32,0},{64,32},{96,64},{128,96},{160,128},{192,160},{224,192},{33,... | collective-permute-start | bytes 30728 | tf_op jit(solution)/shard_map/ppermute | solution.py:48
  12.8 22.8 %all-to-all-start = ((f32[8,4,4,6,128]{4,2,3,1,0:T(4,128)}), f32[8,4,4,6,128]{4,2,3,1,0:T(4,128)S(1)}, u32[]{:S(2)}, u32[]{:S(2)}) async-start(f32[8,4,4,6,128]{4,2,3,1,0:T(4,128)} %broadcast_in_dim.21), calls=%async_computation | async-start | bytes 786432 | tf_op jit(solution)/shard_map/all_to_all | solution.py:65
  36.5 29.6 %copy-start.1 = (f32[5]{0:T(128)S(1)}, f32[5]{0:T(128)}, u32[]{:S(2)}) copy-start(f32[5]{0:T(128)} %constant.109.clone) | copy-start | bytes 64
  36.5 30.4 %copy-start = (f32[5]{0:T(128)S(1)}, f32[5]{0:T(128)}, u32[]{:S(2)}) copy-start(f32[5]{0:T(128)} %constant.108.clone) | copy-start | bytes 64
  45.5 6.6 %collective-permute-start.2 = (f32[414,128]{1,0:T(8,128)S(1)}, f32[414,128]{1,0:T(8,128)S(1)}, u32[]{:S(2)}, u32[]{:S(2)}) collective-permute-start(f32[414,128]{1,0:T(8,128)S(1)} %pad_maximum_fusion), channel_id=1, source_target_pairs={{0,1},{1,2},{2,3},{3,4},{4,5},{5,6},{6,7},{7,8},{8,9},{9,10},{10,1... | collective-permute-start | bytes 635912 | tf_op jit(solution)/shard_map/ppermute | solution.py:54
  49.3 7.5 %collective-permute-start.3 = (f32[414,128]{1,0:T(8,128)S(1)}, f32[414,128]{1,0:T(8,128)S(1)}, u32[]{:S(2)}, u32[]{:S(2)}) collective-permute-start(f32[414,128]{1,0:T(8,128)S(1)} %pad_maximum_fusion.1), channel_id=1, source_target_pairs={{0,15},{1,0},{2,1},{3,2},{4,3},{5,4},{6,5},{7,6},{8,7},{9,8},{10,9... | collective-permute-start | bytes 635912 | tf_op jit(solution)/shard_map/ppermute | solution.py:54
  57.2 8.9 %collective-permute-start.5 = (f32[1656]{0:T(1024)S(1)}, f32[1656]{0:T(1024)S(1)}, u32[]{:S(2)}, u32[]{:S(2)}) collective-permute-start(f32[1656]{0:T(1024)S(1)} %pad_maximum_fusion.58), channel_id=1, source_target_pairs={{16,0},{17,1},{18,2},{19,3},{20,4},{21,5},{22,6},{23,7},{24,8},{25... | collective-permute-start | bytes 19880 | tf_op jit(solution)/shard_map/ppermute | solution.py:48
  59.1 7.7 %collective-permute-start.4 = (f32[1656]{0:T(1024)S(1)}, f32[1656]{0:T(1024)S(1)}, u32[]{:S(2)}, u32[]{:S(2)}) collective-permute-start(f32[1656]{0:T(1024)S(1)} %pad_maximum_fusion.57), channel_id=1, source_target_pairs={{0,16},{1,17},{2,18},{3,19},{4,20},{5,21},{6,22},{7,23},{8,24},{9,... | collective-permute-start | bytes 19880 | tf_op jit(solution)/shard_map/ppermute | solution.py:48
  69.2 12.8 %collective-permute-start.6 = (f32[5,4,128]{2,1,0:T(4,128)S(1)}, f32[5,4,128]{2,1,0:T(4,128)S(1)}, u32[]{:S(2)}, u32[]{:S(2)}) collective-permute-start(f32[5,4,128]{2,1,0:T(4,128)S(1)} %constant_dynamic-update-slice_fusion.20), channel_id=1, source_target_pairs={{0,32},{32,64},{64,96},{96,128},{128,160},{160,192},{192,224},{1,3... | collective-permute-start | bytes 30728 | tf_op jit(solution)/shard_map/ppermute | solution.py:48
  71.5 10.5 %collective-permute-start.7 = (f32[5,4,128]{2,1,0:T(4,128)S(1)}, f32[5,4,128]{2,1,0:T(4,128)S(1)}, u32[]{:S(2)}, u32[]{:S(2)}) collective-permute-start(f32[5,4,128]{2,1,0:T(4,128)S(1)} %constant_dynamic-update-slice_fusion.25), channel_id=1, source_target_pairs={{32,0},{64,32},{96,64},{128,96},{160,128},{192,160},{224,192},{33,... | collective-permute-start | bytes 30728 | tf_op jit(solution)/shard_map/ppermute | solution.py:48
  73.6 18.2 %all-to-all-start.1 = ((f32[8,4,4,6,128]{4,2,3,1,0:T(4,128)}), f32[8,4,4,6,128]{4,2,3,1,0:T(4,128)S(1)}, u32[]{:S(2)}, u32[]{:S(2)}) async-start(f32[8,4,4,6,128]{4,2,3,1,0:T(4,128)} %broadcast_in_dim.24), calls=%async_computation.1 | async-start | bytes 786432 | tf_op jit(solution)/shard_map/all_to_all | solution.py:65
  103.0 4.1 %collective-permute-start.8 = (f32[414,128]{1,0:T(8,128)S(1)}, f32[414,128]{1,0:T(8,128)S(1)}, u32[]{:S(2)}, u32[]{:S(2)}) collective-permute-start(f32[414,128]{1,0:T(8,128)S(1)} %pad_maximum_fusion.2), channel_id=1, source_target_pairs={{0,1},{1,2},{2,3},{3,4},{4,5},{5,6},{6,7},{7,8},{8,9},{9,10},{10,1... | collective-permute-start | bytes 635912 | tf_op jit(solution)/shard_map/ppermute | solution.py:54
  104.4 7.5 %collective-permute-start.9 = (f32[414,128]{1,0:T(8,128)S(1)}, f32[414,128]{1,0:T(8,128)S(1)}, u32[]{:S(2)}, u32[]{:S(2)}) collective-permute-start(f32[414,128]{1,0:T(8,128)S(1)} %pad_maximum_fusion.3), channel_id=1, source_target_pairs={{0,15},{1,0},{2,1},{3,2},{4,3},{5,4},{6,5},{7,6},{8,7},{9,8},{10,9... | collective-permute-start | bytes 635912 | tf_op jit(solution)/shard_map/ppermute | solution.py:54
  112.2 9.0 %collective-permute-start.11 = (f32[1656]{0:T(1024)S(1)}, f32[1656]{0:T(1024)S(1)}, u32[]{:S(2)}, u32[]{:S(2)}) collective-permute-start(f32[1656]{0:T(1024)S(1)} %pad_maximum_fusion.60), channel_id=1, source_target_pairs={{16,0},{17,1},{18,2},{19,3},{20,4},{21,5},{22,6},{23,7},{24,8},{25... | collective-permute-start | bytes 19880 | tf_op jit(solution)/shard_map/ppermute | solution.py:48
  114.3 7.7 %collective-permute-start.10 = (f32[1656]{0:T(1024)S(1)}, f32[1656]{0:T(1024)S(1)}, u32[]{:S(2)}, u32[]{:S(2)}) collective-permute-start(f32[1656]{0:T(1024)S(1)} %pad_maximum_fusion.59), channel_id=1, source_target_pairs={{0,16},{1,17},{2,18},{3,19},{4,20},{5,21},{6,22},{7,23},{8,24},{9,... | collective-permute-start | bytes 19880 | tf_op jit(solution)/shard_map/ppermute | solution.py:48
  123.9 11.4 %collective-permute-start.12 = (f32[5,4,128]{2,1,0:T(4,128)S(1)}, f32[5,4,128]{2,1,0:T(4,128)S(1)}, u32[]{:S(2)}, u32[]{:S(2)}) collective-permute-start(f32[5,4,128]{2,1,0:T(4,128)S(1)} %constant_dynamic-update-slice_fusion.40), channel_id=1, source_target_pairs={{0,32},{32,64},{64,96},{96,128},{128,160},{160,192},{192,224},{1,3... | collective-permute-start | bytes 30728 | tf_op jit(solution)/shard_map/ppermute | solution.py:48
  127.0 15.3 %all-to-all-start.2 = ((f32[8,4,4,6,128]{4,2,3,1,0:T(4,128)}), f32[8,4,4,6,128]{4,2,3,1,0:T(4,128)S(1)}, u32[]{:S(2)}, u32[]{:S(2)}) async-start(f32[8,4,4,6,128]{4,2,3,1,0:T(4,128)} %broadcast_in_dim.25), calls=%async_computation.2 | async-start | bytes 786432 | tf_op jit(solution)/shard_map/all_to_all | solution.py:65
  130.8 7.3 %collective-permute-start.13 = (f32[5,4,128]{2,1,0:T(4,128)S(1)}, f32[5,4,128]{2,1,0:T(4,128)S(1)}, u32[]{:S(2)}, u32[]{:S(2)}) collective-permute-start(f32[5,4,128]{2,1,0:T(4,128)S(1)} %constant_dynamic-update-slice_fusion.45), channel_id=1, source_target_pairs={{32,0},{64,32},{96,64},{128,96},{160,128},{192,160},{224,192},{33,... | collective-permute-start | bytes 30728 | tf_op jit(solution)/shard_map/ppermute | solution.py:48
  153.5 5.5 %collective-permute-start.14 = (f32[414,128]{1,0:T(8,128)S(1)}, f32[414,128]{1,0:T(8,128)S(1)}, u32[]{:S(2)}, u32[]{:S(2)}) collective-permute-start(f32[414,128]{1,0:T(8,128)S(1)} %pad_maximum_fusion.4), channel_id=1, source_target_pairs={{0,1},{1,2},{2,3},{3,4},{4,5},{5,6},{6,7},{7,8},{8,9},{9,10},{10,1... | collective-permute-start | bytes 635912 | tf_op jit(solution)/shard_map/ppermute | solution.py:54
  156.3 7.5 %collective-permute-start.15 = (f32[414,128]{1,0:T(8,128)S(1)}, f32[414,128]{1,0:T(8,128)S(1)}, u32[]{:S(2)}, u32[]{:S(2)}) collective-permute-start(f32[414,128]{1,0:T(8,128)S(1)} %pad_maximum_fusion.5), channel_id=1, source_target_pairs={{0,15},{1,0},{2,1},{3,2},{4,3},{5,4},{6,5},{7,6},{8,7},{9,8},{10,9... | collective-permute-start | bytes 635912 | tf_op jit(solution)/shard_map/ppermute | solution.py:54
  164.1 8.9 %collective-permute-start.17 = (f32[1656]{0:T(1024)S(1)}, f32[1656]{0:T(1024)S(1)}, u32[]{:S(2)}, u32[]{:S(2)}) collective-permute-start(f32[1656]{0:T(1024)S(1)} %pad_maximum_fusion.62), channel_id=1, source_target_pairs={{16,0},{17,1},{18,2},{19,3},{20,4},{21,5},{22,6},{23,7},{24,8},{25... | collective-permute-start | bytes 19880 | tf_op jit(solution)/shard_map/ppermute | solution.py:48
  166.0 8.6 %collective-permute-start.16 = (f32[1656]{0:T(1024)S(1)}, f32[1656]{0:T(1024)S(1)}, u32[]{:S(2)}, u32[]{:S(2)}) collective-permute-start(f32[1656]{0:T(1024)S(1)} %pad_maximum_fusion.61), channel_id=1, source_target_pairs={{0,16},{1,17},{2,18},{3,19},{4,20},{5,21},{6,22},{7,23},{8,24},{9,... | collective-permute-start | bytes 19880 | tf_op jit(solution)/shard_map/ppermute | solution.py:48

commit v5 on v4

--- a/solution.py
+++ b/solution.py
@@ -386,7 +386,7 @@
     halos = None
     for time_step in range(STEPS):
         flow, motion = flow_collide(flow, flow_solid)
-        column = gathered_copies(motion, "row", 2)
+        column = lax.all_gather(motion, "row", axis=2, tiled=True)
         mode = "first" if time_step == 0 else "middle"
         scalars = scalar_stage(mode, scalars, halos, column, solid_flag, source)
         from_below = send_vertical(edge_planes(flow, flow_vectors, 2, 1, 1), 1)

time: 188 us -> 233 us (1.24)
  blocking collectives: 0 us -> 69.1 us
  waiting for transfers between devices: 38.1 us -> 20.5 us
  starting transfers between devices: 58.3 us -> 53.7 us
  local copies, waits for them, and re-layouts: 38.8 us -> 36.3 us
    all_gather x0 -> x3, blocking collectives: none -> 69.1 us  [on_device(): column = lax.all_gather(motion, 'row', axis=2, tiled=True)]
    all_to_all x3 -> x0, waiting for transfers between devices: 20.5 us -> none  [copy_for_each(): return lax.all_to_all(copies, axis, split_axis=0, concat_axis=0, tiled=True)]
    all_to_all x3 -> x0, starting transfers between devices: 17.9 us -> none  [copy_for_each(): return lax.all_to_all(copies, axis, split_axis=0, concat_axis=0, tiled=True)]
    ppermute x6, starting transfers between devices: 8.15 us -> 21.3 us  [from_behind(): return lax.ppermute(value, axis, pairs)]
    ppermute x6, waiting for transfers between devices: 14.9 us -> 20.4 us  [from_behind(): return lax.ppermute(value, axis, pairs)]
    ppermute x12, waiting for transfers between devices: 2.77 us -> 0.05 us  [passed_along(): return lax.ppermute(block, axis, route)]
    broadcast_in_dim x3 -> x0, local copies, waits for them, and re-layouts: 2.44 us -> none  [copy_for_each(): copies = jnp.broadcast_to(x, (lax.axis_size(axis), *x.shape))]
    all_gather x0 -> x3, local copies, waits for them, and re-layouts: none -> 2.38 us  [on_device(): column = lax.all_gather(motion, 'row', axis=2, tiled=True)]
  transfers between devices with their start and end apart: 21 -> 18, of which waited for: 10 -> 6; matrix products, arithmetic and copies ran while one was open for 18% -> 16% of each run, Pallas kernels for 0% -> 11%
where the time goes in v5:
time: 233 us; the launch traced here: 231 us
  blocking collectives  69.1 us (30%)
  starting transfers between devices  53.7 us (23%)
  local copies, waits for them, and re-layouts  36.3 us (16%)
  Pallas kernels  33.3 us (14%)
  waiting for transfers between devices  20.5 us (9%)
  other arithmetic  14 us (6%)
    all_gather x3, blocking collectives, on_device(): column = lax.all_gather(motion, 'row', axis=2, tiled=True)  69.1 us
    pallas_call x4, Pallas kernels, scalar_stage(): pl.pallas_call(scalar_kernel(mode, span_y, depth, span_x), grid=(count,),...  33.3 us
    ppermute x12, starting transfers between devices, passed_along(): return lax.ppermute(block, axis, route)  32.4 us
    ppermute x6, starting transfers between devices, from_behind(): return lax.ppermute(value, axis, pairs)  21.3 us
    ppermute x6, waiting for transfers between devices, from_behind(): return lax.ppermute(value, axis, pairs)  20.4 us
    reshape x6, local copies, waits for them, and re-layouts, packed_section(): arrived_scalar[heading] = arrived[split_at:].reshape(scalar_planes.shape)  9.1 us
    select_n x17, other arithmetic, flow_collide(): updated.append(jnp.where(solid, populations[flow_mirror[member]], relaxed))  5.18 us
  transfers between devices with their start and end apart: 18, of which 6 were waited for; matrix products, arithmetic and copies ran while one was open for 16% of the time, Pallas kernels for 11%

profile of v5, /device:TPU:7, one launch (start us, length us, event | category | flops | bytes accessed | tf_op | source)
XLA Modules:
  0.0 231.2 jit_solution(17313768433738089844)
XLA Ops:
  0.6 1.0 fusion.25
  1.6 1.6 fusion.402
  3.3 1.1 bitcast_select_fusion.8
  4.4 0.9 fusion.314
  5.3 0.9 bitcast_select_fusion
  6.2 3.5 %collective-permute-start = (f32[5,4,128]{2,1,0:T(4,128)S(1)}, f32[5,4,128]{2,1,0:T(4,128)S(1)}, u32[]{:S(2)}, u32[]{:S(2)}) collective-permute-start(f32[5,4,128]{2,1,0:T(4,128)S(1)} %constant_dynamic-update-slice_fusion), channel_id=1, source_target_pairs={{0,32},{32,64},{64,96},{96,128},{128,160},{160,192},{192,224},{1,3... | collective-permute-start | bytes 30728 | tf_op jit(solution)/shard_map/ppermute | solution.py:48
  9.8 0.9 fusion.330
  10.7 1.3 collective-permute-start.1
  12.0 23.6 %all_gather.9 = f32[4,4,48,128]{3,1,2,0:T(4,128)S(1)} all-gather(f32[4,4,6,128]{3,1,2,0:T(4,128)S(1)} %pad_maximum_fusion.6), channel_id=1, replica_groups=mesh['row'=8,'gx'=2,'gy'=16] {'row'}, dimensions={2}, use_global_device_ids=true | all-gather | bytes 442368 | tf_op jit(solution)/shard_map/all_gather | solution.py:389
  35.7 0.8 copy.201.refs_1_
  36.5 0.7 broadcast_subtract_fusion
  37.1 0.7 fusion.332
  37.8 2.1 fusion.refs_3_.refs_7_
  39.9 7.9 %shard_map.131.refs_0_ = f32[7,8,4,48,128]{4,3,2,1,0:T(8,128)} custom-call(f32[8,4,48,128]{3,2,1,0:T(8,128)} %refs_0_.1, f32[4,4,48,128]{3,2,1,0:T(8,128)} %copy.201.refs_1_, s32[4,48,128]{2,1,0:T(8,128)} %get-tuple-element.110.refs_2_.refs_6_, f32[8,4,48,128]{3,2,1,0:T(8,128)} %fusion.refs_3_.refs_7_), custom_call_target="tpu_custom_call" | custom-call | tf_op jit(solution)/shard_map/pallas_call | solution.py:316
  47.8 1.0 fusion.408
  49.2 0.8 bitcast_select_fusion.7
  50.0 2.1 slice_reduce_fusion.5
  52.8 8.0 %collective-permute-start.2 = (f32[414,128]{1,0:T(8,128)S(1)}, f32[414,128]{1,0:T(8,128)S(1)}, u32[]{:S(2)}, u32[]{:S(2)}) collective-permute-start(f32[414,128]{1,0:T(8,128)S(1)} %pad_maximum_fusion), channel_id=1, source_target_pairs={{0,1},{1,2},{2,3},{3,4},{4,5},{5,6},{6,7},{7,8},{8,9},{9,10},{10,1... | collective-permute-start | bytes 635912 | tf_op jit(solution)/shard_map/ppermute | solution.py:54
  61.5 2.1 collective-permute-done.2
  63.7 4.6 %collective-permute-done.3 = f32[414,128]{1,0:T(8,128)S(1)} collective-permute-done((f32[414,128]{1,0:T(8,128)S(1)}, f32[414,128]{1,0:T(8,128)S(1)}, u32[]{:S(2)}, u32[]{:S(2)}) %collective-permute-start.3) | collective-permute-done | bytes 212000 | tf_op jit(solution)/shard_map/ppermute | solution.py:54
  68.7 1.3 collective-permute-start.5
  70.6 5.5 %collective-permute-start.4 = (f32[1656]{0:T(1024)S(1)}, f32[1656]{0:T(1024)S(1)}, u32[]{:S(2)}, u32[]{:S(2)}) collective-permute-start(f32[1656]{0:T(1024)S(1)} %pad_maximum_fusion.57), channel_id=1, source_target_pairs={{0,16},{1,17},{2,18},{3,19},{4,20},{5,21},{6,22},{7,23},{8,24},{9,... | collective-permute-start | bytes 19880 | tf_op jit(solution)/shard_map/ppermute | solution.py:48
  76.2 0.7 slice.1589
  76.9 0.7 slice.1588
  79.1 1.0 fusion.252
  80.2 0.3 subtract_select_fusion.37
  80.8 2.7 %collective-permute-start.6 = (f32[5,4,128]{2,1,0:T(4,128)S(1)}, f32[5,4,128]{2,1,0:T(4,128)S(1)}, u32[]{:S(2)}, u32[]{:S(2)}) collective-permute-start(f32[5,4,128]{2,1,0:T(4,128)S(1)} %constant_dynamic-update-slice_fusion.20), channel_id=1, source_target_pairs={{0,32},{32,64},{64,96},{96,128},{128,160},{160,192},{192,224},{1,3... | collective-permute-start | bytes 30728 | tf_op jit(solution)/shard_map/ppermute | solution.py:48
  83.6 1.3 collective-permute-start.7
  84.9 22.5 %all_gather.10 = f32[4,4,48,128]{3,1,2,0:T(4,128)S(1)} all-gather(f32[4,4,6,128]{3,1,2,0:T(4,128)S(1)} %pad_maximum_fusion.7), channel_id=1, replica_groups=mesh['row'=8,'gx'=2,'gy'=16] {'row'}, dimensions={2}, use_global_device_ids=true | all-gather | bytes 442368 | tf_op jit(solution)/shard_map/all_gather | solution.py:389
  107.3 0.8 copy.253.refs_5_
  108.2 1.5 reshape.266.refs_2_
  109.8 1.5 reshape.265.refs_1_
  111.3 9.3 %shard_map.132.refs_0_ = f32[7,8,4,48,128]{4,3,2,1,0:T(8,128)} custom-call(f32[7,8,4,48,128]{4,3,2,1,0:T(8,128)} %shard_map.131.refs_0_, f32[8,4,48,1]{3,2,1,0:T(8,128)} %reshape.265.refs_1_, f32[8,4,48,1]{3,2,1,0:T(8,128)} %reshape.266.refs_2_, f32[8,48,128]{2,1,0:T(8,128)} %bitcast.820, f32[8,48,128]{2,1,0:T(8,128)} %bitcast.819, ...), custom_call_target="tpu_custom_call" | custom-call | tf_op jit(solution)/shard_map/pallas_call | solution.py:316
  120.6 1.0 fusion.407
  122.0 2.1 slice_reduce_fusion.3
  124.9 6.2 %collective-permute-start.8 = (f32[414,128]{1,0:T(8,128)S(1)}, f32[414,128]{1,0:T(8,128)S(1)}, u32[]{:S(2)}, u32[]{:S(2)}) collective-permute-start(f32[414,128]{1,0:T(8,128)S(1)} %pad_maximum_fusion.2), channel_id=1, source_target_pairs={{0,1},{1,2},{2,3},{3,4},{4,5},{5,6},{6,7},{7,8},{8,9},{9,10},{10,1... | collective-permute-start | bytes 635912 | tf_op jit(solution)/shard_map/ppermute | solution.py:54
  131.6 2.2 collective-permute-done.8
  134.0 4.6 %collective-permute-done.9 = f32[414,128]{1,0:T(8,128)S(1)} collective-permute-done((f32[414,128]{1,0:T(8,128)S(1)}, f32[414,128]{1,0:T(8,128)S(1)}, u32[]{:S(2)}, u32[]{:S(2)}) %collective-permute-start.9) | collective-permute-done | bytes 212000 | tf_op jit(solution)/shard_map/ppermute | solution.py:54
  139.0 1.5 collective-permute-start.11
  141.1 5.5 %collective-permute-start.10 = (f32[1656]{0:T(1024)S(1)}, f32[1656]{0:T(1024)S(1)}, u32[]{:S(2)}, u32[]{:S(2)}) collective-permute-start(f32[1656]{0:T(1024)S(1)} %pad_maximum_fusion.59), channel_id=1, source_target_pairs={{0,16},{1,17},{2,18},{3,19},{4,20},{5,21},{6,22},{7,23},{8,24},{9,... | collective-permute-start | bytes 19880 | tf_op jit(solution)/shard_map/ppermute | solution.py:48
  146.6 0.7 slice.1680
  147.3 0.7 slice.1681
  149.5 0.2 fusion.256
  149.9 0.3 divide_subtract_fusion
  150.7 1.8 collective-permute-start.12
  152.6 1.3 collective-permute-start.13
  154.0 23.0 %all_gather.11 = f32[4,4,48,128]{3,1,2,0:T(4,128)S(1)} all-gather(f32[4,4,6,128]{3,1,2,0:T(4,128)S(1)} %pad_maximum_fusion.8), channel_id=1, replica_groups=mesh['row'=8,'gx'=2,'gy'=16] {'row'}, dimensions={2}, use_global_device_ids=true | all-gather | bytes 442368 | tf_op jit(solution)/shard_map/all_gather | solution.py:389
  176.9 0.8 copy.305.refs_5_
  177.8 1.5 reshape.268.refs_2_
  179.4 1.5 reshape.267.refs_1_
  180.9 9.3 %shard_map.133.refs_0_ = f32[7,8,4,48,128]{4,3,2,1,0:T(8,128)} custom-call(f32[7,8,4,48,128]{4,3,2,1,0:T(8,128)} %shard_map.132.refs_0_, f32[8,4,48,1]{3,2,1,0:T(8,128)} %reshape.267.refs_1_, f32[8,4,48,1]{3,2,1,0:T(8,128)} %reshape.268.refs_2_, f32[8,48,128]{2,1,0:T(8,128)} %bitcast.817, f32[8,48,128]{2,1,0:T(8,128)} %bitcast.818, ...), custom_call_target="tpu_custom_call" | custom-call | tf_op jit(solution)/shard_map/pallas_call | solution.py:316
  190.2 1.0 fusion.406
  191.5 2.1 slice_reduce_fusion
  194.2 6.8 %collective-permute-start.14 = (f32[414,128]{1,0:T(8,128)S(1)}, f32[414,128]{1,0:T(8,128)S(1)}, u32[]{:S(2)}, u32[]{:S(2)}) collective-permute-start(f32[414,128]{1,0:T(8,128)S(1)} %pad_maximum_fusion.4), channel_id=1, source_target_pairs={{0,1},{1,2},{2,3},{3,4},{4,5},{5,6},{6,7},{7,8},{8,9},{9,10},{10,1... | collective-permute-start | bytes 635912 | tf_op jit(solution)/shard_map/ppermute | solution.py:54
  201.6 2.2 collective-permute-done.14
  204.0 4.6 %collective-permute-done.15 = f32[414,128]{1,0:T(8,128)S(1)} collective-permute-done((f32[414,128]{1,0:T(8,128)S(1)}, f32[414,128]{1,0:T(8,128)S(1)}, u32[]{:S(2)}, u32[]{:S(2)}) %collective-permute-start.15) | collective-permute-done | bytes 212000 | tf_op jit(solution)/shard_map/ppermute | solution.py:54
  208.9 1.3 collective-permute-start.17
  210.8 5.5 %collective-permute-start.16 = (f32[1656]{0:T(1024)S(1)}, f32[1656]{0:T(1024)S(1)}, u32[]{:S(2)}, u32[]{:S(2)}) collective-permute-start(f32[1656]{0:T(1024)S(1)} %pad_maximum_fusion.61), channel_id=1, source_target_pairs={{0,16},{1,17},{2,18},{3,19},{4,20},{5,21},{6,22},{7,23},{8,24},{9,... | collective-permute-start | bytes 19880 | tf_op jit(solution)/shard_map/ppermute | solution.py:48
  216.5 0.7 slice.1755
  217.1 0.7 slice.1754
  217.9 1.5 reshape.270.refs_2_
  219.5 1.5 reshape.269.refs_1_
  223.6 0.8 copy.360
  224.3 6.9 %shard_map.134 = f32[8,4,48,128]{3,2,1,0:T(8,128)} custom-call(f32[7,8,4,48,128]{4,3,2,1,0:T(8,128)} %shard_map.133.refs_0_, f32[8,4,48,1]{3,2,1,0:T(8,128)} %reshape.269.refs_1_, f32[8,4,48,1]{3,2,1,0:T(8,128)} %reshape.270.refs_2_, f32[8,48,128]{2,1,0:T(8,128)} %bitcast.828, f32[8,48,128]{2,1,0:T(8,128)} %bitcast.827), custom_call_target="tpu_custom_call" | custom-call | tf_op jit(solution)/shard_map/pallas_call | solution.py:316
  (409 shorter events, 14.5 us)
Async XLA Ops:
  6.2 46.3 %collective-permute-start = (f32[5,4,128]{2,1,0:T(4,128)S(1)}, f32[5,4,128]{2,1,0:T(4,128)S(1)}, u32[]{:S(2)}, u32[]{:S(2)}) collective-permute-start(f32[5,4,128]{2,1,0:T(4,128)S(1)} %constant_dynamic-update-slice_fusion), channel_id=1, source_target_pairs={{0,32},{32,64},{64,96},{96,128},{128,160},{160,192},{192,224},{1,3... | collective-permute-start | bytes 30728 | tf_op jit(solution)/shard_map/ppermute | solution.py:48
  10.7 42.0 %collective-permute-start.1 = (f32[5,4,128]{2,1,0:T(4,128)S(1)}, f32[5,4,128]{2,1,0:T(4,128)S(1)}, u32[]{:S(2)}, u32[]{:S(2)}) collective-permute-start(f32[5,4,128]{2,1,0:T(4,128)S(1)} %constant_dynamic-update-slice_fusion.5), channel_id=1, source_target_pairs={{32,0},{64,32},{96,64},{128,96},{160,128},{192,160},{224,192},{33,... | collective-permute-start | bytes 30728 | tf_op jit(solution)/shard_map/ppermute | solution.py:48
  39.9 37.8 %copy-start.1 = (f32[5]{0:T(128)S(1)}, f32[5]{0:T(128)}, u32[]{:S(2)}) copy-start(f32[5]{0:T(128)} %constant.109.clone) | copy-start | bytes 64
  39.9 38.5 %copy-start = (f32[5]{0:T(128)S(1)}, f32[5]{0:T(128)}, u32[]{:S(2)}) copy-start(f32[5]{0:T(128)} %constant.108.clone) | copy-start | bytes 64
  52.8 10.8 %collective-permute-start.2 = (f32[414,128]{1,0:T(8,128)S(1)}, f32[414,128]{1,0:T(8,128)S(1)}, u32[]{:S(2)}, u32[]{:S(2)}) collective-permute-start(f32[414,128]{1,0:T(8,128)S(1)} %pad_maximum_fusion), channel_id=1, source_target_pairs={{0,1},{1,2},{2,3},{3,4},{4,5},{5,6},{6,7},{7,8},{8,9},{9,10},{10,1... | collective-permute-start | bytes 635912 | tf_op jit(solution)/shard_map/ppermute | solution.py:54
  60.9 7.5 %collective-permute-start.3 = (f32[414,128]{1,0:T(8,128)S(1)}, f32[414,128]{1,0:T(8,128)S(1)}, u32[]{:S(2)}, u32[]{:S(2)}) collective-permute-start(f32[414,128]{1,0:T(8,128)S(1)} %pad_maximum_fusion.1), channel_id=1, source_target_pairs={{0,15},{1,0},{2,1},{3,2},{4,3},{5,4},{6,5},{7,6},{8,7},{9,8},{10,9... | collective-permute-start | bytes 635912 | tf_op jit(solution)/shard_map/ppermute | solution.py:54
  68.7 8.9 %collective-permute-start.5 = (f32[1656]{0:T(1024)S(1)}, f32[1656]{0:T(1024)S(1)}, u32[]{:S(2)}, u32[]{:S(2)}) collective-permute-start(f32[1656]{0:T(1024)S(1)} %pad_maximum_fusion.58), channel_id=1, source_target_pairs={{16,0},{17,1},{18,2},{19,3},{20,4},{21,5},{22,6},{23,7},{24,8},{25... | collective-permute-start | bytes 19880 | tf_op jit(solution)/shard_map/ppermute | solution.py:48
  70.6 7.7 %collective-permute-start.4 = (f32[1656]{0:T(1024)S(1)}, f32[1656]{0:T(1024)S(1)}, u32[]{:S(2)}, u32[]{:S(2)}) collective-permute-start(f32[1656]{0:T(1024)S(1)} %pad_maximum_fusion.57), channel_id=1, source_target_pairs={{0,16},{1,17},{2,18},{3,19},{4,20},{5,21},{6,22},{7,23},{8,24},{9,... | collective-permute-start | bytes 19880 | tf_op jit(solution)/shard_map/ppermute | solution.py:48
  80.8 43.7 %collective-permute-start.6 = (f32[5,4,128]{2,1,0:T(4,128)S(1)}, f32[5,4,128]{2,1,0:T(4,128)S(1)}, u32[]{:S(2)}, u32[]{:S(2)}) collective-permute-start(f32[5,4,128]{2,1,0:T(4,128)S(1)} %constant_dynamic-update-slice_fusion.20), channel_id=1, source_target_pairs={{0,32},{32,64},{64,96},{96,128},{128,160},{160,192},{192,224},{1,3... | collective-permute-start | bytes 30728 | tf_op jit(solution)/shard_map/ppermute | solution.py:48
  83.6 41.1 %collective-permute-start.7 = (f32[5,4,128]{2,1,0:T(4,128)S(1)}, f32[5,4,128]{2,1,0:T(4,128)S(1)}, u32[]{:S(2)}, u32[]{:S(2)}) collective-permute-start(f32[5,4,128]{2,1,0:T(4,128)S(1)} %constant_dynamic-update-slice_fusion.25), channel_id=1, source_target_pairs={{32,0},{64,32},{96,64},{128,96},{160,128},{192,160},{224,192},{33,... | collective-permute-start | bytes 30728 | tf_op jit(solution)/shard_map/ppermute | solution.py:48
  124.9 9.0 %collective-permute-start.8 = (f32[414,128]{1,0:T(8,128)S(1)}, f32[414,128]{1,0:T(8,128)S(1)}, u32[]{:S(2)}, u32[]{:S(2)}) collective-permute-start(f32[414,128]{1,0:T(8,128)S(1)} %pad_maximum_fusion.2), channel_id=1, source_target_pairs={{0,1},{1,2},{2,3},{3,4},{4,5},{5,6},{6,7},{7,8},{8,9},{9,10},{10,1... | collective-permute-start | bytes 635912 | tf_op jit(solution)/shard_map/ppermute | solution.py:54
  131.1 7.5 %collective-permute-start.9 = (f32[414,128]{1,0:T(8,128)S(1)}, f32[414,128]{1,0:T(8,128)S(1)}, u32[]{:S(2)}, u32[]{:S(2)}) collective-permute-start(f32[414,128]{1,0:T(8,128)S(1)} %pad_maximum_fusion.3), channel_id=1, source_target_pairs={{0,15},{1,0},{2,1},{3,2},{4,3},{5,4},{6,5},{7,6},{8,7},{9,8},{10,9... | collective-permute-start | bytes 635912 | tf_op jit(solution)/shard_map/ppermute | solution.py:54
  139.0 9.0 %collective-permute-start.11 = (f32[1656]{0:T(1024)S(1)}, f32[1656]{0:T(1024)S(1)}, u32[]{:S(2)}, u32[]{:S(2)}) collective-permute-start(f32[1656]{0:T(1024)S(1)} %pad_maximum_fusion.60), channel_id=1, source_target_pairs={{16,0},{17,1},{18,2},{19,3},{20,4},{21,5},{22,6},{23,7},{24,8},{25... | collective-permute-start | bytes 19880 | tf_op jit(solution)/shard_map/ppermute | solution.py:48
  141.1 7.7 %collective-permute-start.10 = (f32[1656]{0:T(1024)S(1)}, f32[1656]{0:T(1024)S(1)}, u32[]{:S(2)}, u32[]{:S(2)}) collective-permute-start(f32[1656]{0:T(1024)S(1)} %pad_maximum_fusion.59), channel_id=1, source_target_pairs={{0,16},{1,17},{2,18},{3,19},{4,20},{5,21},{6,22},{7,23},{8,24},{9,... | collective-permute-start | bytes 19880 | tf_op jit(solution)/shard_map/ppermute | solution.py:48
  150.7 43.1 %collective-permute-start.12 = (f32[5,4,128]{2,1,0:T(4,128)S(1)}, f32[5,4,128]{2,1,0:T(4,128)S(1)}, u32[]{:S(2)}, u32[]{:S(2)}) collective-permute-start(f32[5,4,128]{2,1,0:T(4,128)S(1)} %constant_dynamic-update-slice_fusion.40), channel_id=1, source_target_pairs={{0,32},{32,64},{64,96},{96,128},{128,160},{160,192},{192,224},{1,3... | collective-permute-start | bytes 30728 | tf_op jit(solution)/shard_map/ppermute | solution.py:48
  152.6 41.3 %collective-permute-start.13 = (f32[5,4,128]{2,1,0:T(4,128)S(1)}, f32[5,4,128]{2,1,0:T(4,128)S(1)}, u32[]{:S(2)}, u32[]{:S(2)}) collective-permute-start(f32[5,4,128]{2,1,0:T(4,128)S(1)} %constant_dynamic-update-slice_fusion.45), channel_id=1, source_target_pairs={{32,0},{64,32},{96,64},{128,96},{160,128},{192,160},{224,192},{33,... | collective-permute-start | bytes 30728 | tf_op jit(solution)/shard_map/ppermute | solution.py:48
  194.2 9.6 %collective-permute-start.14 = (f32[414,128]{1,0:T(8,128)S(1)}, f32[414,128]{1,0:T(8,128)S(1)}, u32[]{:S(2)}, u32[]{:S(2)}) collective-permute-start(f32[414,128]{1,0:T(8,128)S(1)} %pad_maximum_fusion.4), channel_id=1, source_target_pairs={{0,1},{1,2},{2,3},{3,4},{4,5},{5,6},{6,7},{7,8},{8,9},{9,10},{10,1... | collective-permute-start | bytes 635912 | tf_op jit(solution)/shard_map/ppermute | solution.py:54
  201.1 7.5 %collective-permute-start.15 = (f32[414,128]{1,0:T(8,128)S(1)}, f32[414,128]{1,0:T(8,128)S(1)}, u32[]{:S(2)}, u32[]{:S(2)}) collective-permute-start(f32[414,128]{1,0:T(8,128)S(1)} %pad_maximum_fusion.5), channel_id=1, source_target_pairs={{0,15},{1,0},{2,1},{3,2},{4,3},{5,4},{6,5},{7,6},{8,7},{9,8},{10,9... | collective-permute-start | bytes 635912 | tf_op jit(solution)/shard_map/ppermute | solution.py:54
  208.9 8.9 %collective-permute-start.17 = (f32[1656]{0:T(1024)S(1)}, f32[1656]{0:T(1024)S(1)}, u32[]{:S(2)}, u32[]{:S(2)}) collective-permute-start(f32[1656]{0:T(1024)S(1)} %pad_maximum_fusion.62), channel_id=1, source_target_pairs={{16,0},{17,1},{18,2},{19,3},{20,4},{21,5},{22,6},{23,7},{24,8},{25... | collective-permute-start | bytes 19880 | tf_op jit(solution)/shard_map/ppermute | solution.py:48
  210.8 8.6 %collective-permute-start.16 = (f32[1656]{0:T(1024)S(1)}, f32[1656]{0:T(1024)S(1)}, u32[]{:S(2)}, u32[]{:S(2)}) collective-permute-start(f32[1656]{0:T(1024)S(1)} %pad_maximum_fusion.61), channel_id=1, source_target_pairs={{0,16},{1,17},{2,18},{3,19},{4,20},{5,21},{6,22},{7,23},{8,24},{9,... | collective-permute-start | bytes 19880 | tf_op jit(solution)/shard_map/ppermute | solution.py:48

commit v6 on v4

--- a/solution.py
+++ b/solution.py
@@ -384,19 +384,36 @@
     flow = [flow_pops[member] for member in range(19)]
     scalars = concentration
     halos = None
+    leaving = None
     for time_step in range(STEPS):
         flow, motion = flow_collide(flow, flow_solid)
         column = gathered_copies(motion, "row", 2)
-        mode = "first" if time_step == 0 else "middle"
-        scalars = scalar_stage(mode, scalars, halos, column, solid_flag, source)
         from_below = send_vertical(edge_planes(flow, flow_vectors, 2, 1, 1), 1)
         from_above = send_vertical(edge_planes(flow, flow_vectors, 2, 1, -1), -1)
         flow = displace(flow, flow_vectors, 2, 1, from_below, from_above)
-        leaving_y = {1: scalars[3, :, span_y - 1], -1: scalars[4, :, 0]}
-        flow, arrived_y = packed_section(flow, leaving_y, 1, 0, send_spanwise, keep_spanwise, True)
-        leaving_x = {1: scalars[1, :, :, :, span_x - 1 :], -1: scalars[2, :, :, :, :1]}
-        flow, arrived_x = packed_section(flow, leaving_x, 0, 2, send_streamwise, inflow_fill, False)
-        halos = (arrived_x[1], arrived_x[-1], arrived_y[1], arrived_y[-1])
+        if leaving is None:
+            flow = flow_section(flow, 1, 0, send_spanwise, keep_spanwise)
+            flow = flow_section(flow, 0, 2, send_streamwise, inflow_fill)
+            scalars = scalar_stage("first", scalars, None, column, solid_flag, source)
+        else:
+            flow, arrived_y = packed_section(
+                flow, leaving[1], 1, 0, send_spanwise, keep_spanwise, True
+            )
+            flow, arrived_x = packed_section(
+                flow, leaving[0], 0, 2, send_streamwise, inflow_fill, False
+            )
+            halos = (arrived_x[1], arrived_x[-1], arrived_y[1], arrived_y[-1])
+            scalars = scalar_stage("middle", scalars, halos, column, solid_flag, source)
+        leaving = (
+            {1: scalars[1, :, :, :, span_x - 1 :], -1: scalars[2, :, :, :, :1]},
+            {1: scalars[3, :, span_y - 1], -1: scalars[4, :, 0]},
+        )
+    halos = (
+        send_streamwise(leaving[0][1], 1),
+        send_streamwise(leaving[0][-1], -1),
+        send_spanwise(leaving[1][1], 1),
+        send_spanwise(leaving[1][-1], -1),
+    )
     amount = scalar_stage("final", scalars, halos, None, None, None)
     stacked = jnp.stack(flow)
     return (stacked, amount)

time: 188 us -> 189 us (level)
  the two profiles are of different devices: /device:TPU:7 before, /device:TPU:32 now
where the time goes in v6:
time: 189 us; the launch traced here: 187 us
  starting transfers between devices  85.3 us (45%)
  local copies, waits for them, and re-layouts  37.6 us (20%)
  Pallas kernels  33.3 us (18%)
  other arithmetic  14.9 us (8%)
  waiting for transfers between devices  11.4 us (6%)
  between operations  2.31 us (1%)
  matrix products  2.09 us (1%)
    ppermute x14, starting transfers between devices, passed_along(): return lax.ppermute(block, axis, route)  44.9 us
    pallas_call x4, Pallas kernels, scalar_stage(): pl.pallas_call(scalar_kernel(mode, span_y, depth, span_x), grid=(count,),...  33.3 us
    all_to_all x3, starting transfers between devices, copy_for_each(): return lax.all_to_all(copies, axis, split_axis=0, concat_axis=0, tiled=True)  24.5 us
    ppermute x8, starting transfers between devices, from_behind(): return lax.ppermute(value, axis, pairs)  15.9 us
    ppermute x14, waiting for transfers between devices, passed_along(): return lax.ppermute(block, axis, route)  7.02 us
    reshape x4, local copies, waits for them, and re-layouts, packed_section(): arrived_scalar[heading] = arrived[split_at:].reshape(scalar_planes.shape)  6.14 us
    another operation x15, other arithmetic, flow_collide(): jnp.stack([speeds[0] * fluid_part, speeds[1] * fluid_part, speeds[2] * fl...  5.92 us
    ppermute x8, waiting for transfers between devices, from_behind(): return lax.ppermute(value, axis, pairs)  4.36 us
  transfers between devices with their start and end apart: 25, of which 6 were waited for; matrix products, arithmetic and copies ran while one was open for 22% of the time, Pallas kernels for 9%

profile of v6, /device:TPU:32, one launch (start us, length us, event | category | flops | bytes accessed | tf_op | source)
XLA Modules:
  0.0 186.8 jit_solution(17678722254990628385)
XLA Ops:
  0.7 1.6 fusion.387
  2.3 0.9 fusion.248
  3.3 0.9 fusion.249
  4.1 0.9 fusion.250
  5.0 1.1 fusion.251
  6.2 0.8 bitcast_select_fusion.5
  7.0 0.9 fusion.320
  7.9 3.8 %collective-permute-start = (f32[5,4,128]{2,1,0:T(4,128)S(1)}, f32[5,4,128]{2,1,0:T(4,128)S(1)}, u32[]{:S(2)}, u32[]{:S(2)}) collective-permute-start(f32[5,4,128]{2,1,0:T(4,128)S(1)} %constant_dynamic-update-slice_fusion), channel_id=1, source_target_pairs={{0,32},{32,64},{64,96},{96,128},{128,160},{160,192},{192,224},{1,3... | collective-permute-start | bytes 30728 | tf_op jit(solution)/shard_map/ppermute | solution.py:48
  11.8 0.9 bitcast_select_fusion.8
  12.7 0.9 fusion.330
  13.6 2.0 %collective-permute-start.1 = (f32[5,4,128]{2,1,0:T(4,128)S(1)}, f32[5,4,128]{2,1,0:T(4,128)S(1)}, u32[]{:S(2)}, u32[]{:S(2)}) collective-permute-start(f32[5,4,128]{2,1,0:T(4,128)S(1)} %constant_dynamic-update-slice_fusion.5), channel_id=1, source_target_pairs={{32,0},{64,32},{96,64},{128,96},{160,128},{192,160},{224,192},{33,... | collective-permute-start | bytes 30728 | tf_op jit(solution)/shard_map/ppermute | solution.py:48
  15.6 0.8 broadcast_in_dim.21
  16.5 9.8 %all-to-all-start = ((f32[8,4,4,6,128]{4,2,3,1,0:T(4,128)}), f32[8,4,4,6,128]{4,2,3,1,0:T(4,128)S(1)}, u32[]{:S(2)}, u32[]{:S(2)}) async-start(f32[8,4,4,6,128]{4,2,3,1,0:T(4,128)} %broadcast_in_dim.21), calls=%async_computation | async-start | bytes 786432 | tf_op jit(solution)/shard_map/all_to_all | solution.py:65
  26.5 0.7 fusion.332
  27.2 2.1 %fusion.refs_3_.refs_7_ = f32[8,4,48,128]{3,2,1,0:T(8,128)} fusion(f32[96]{0:T(128)} %param.17, s32[96]{0:T(128)S(1)} %get-tuple-element.292, s32[96]{0:T(128)S(1)} %get-tuple-element.291, s32[96]{0:T(128)S(1)} %get-tuple-element.295, s32[96]{0:T(128)S(1)} %get-tuple-element.290), kind=kOutput, calls=%fused_computation.4 | convolution fusion | flops 227389440 | bytes 788352 | tf_op jit(solution)/shard_map/dot_general | solution.py:379
  30.1 3.9 %collective-permute-start.3 = (f32[5,6,128]{2,0,1:T(8,128)S(1)}, f32[5,6,128]{2,0,1:T(8,128)S(1)}, u32[]{:S(2)}, u32[]{:S(2)}) collective-permute-start(f32[5,6,128]{2,0,1:T(8,128)S(1)} %stack.162), channel_id=1, source_target_pairs={{0,15},{1,0},{2,1},{3,2},{4,3},{5,4},{6,5},{7,6},{8,7},{9,8},{10,9... | collective-permute-start | bytes 46088 | tf_op jit(solution)/shard_map/ppermute | solution.py:54
  34.4 1.0 collective-permute-done.2
  35.7 1.3 collective-permute-start.5
  37.4 6.0 %collective-permute-start.4 = (f32[5,4,6]{2,1,0:T(4,128)S(1)}, f32[5,4,6]{2,1,0:T(4,128)S(1)}, u32[]{:S(2)}, u32[]{:S(2)}) collective-permute-start(f32[5,4,6]{2,1,0:T(4,128)S(1)} %constant_dynamic-update-slice_fusion.10), channel_id=1, source_target_pairs={{0,16},{1,17},{2,18},{3,19},{4,20},{5,21},{6,22},{7,23},{8,24},{9,... | collective-permute-start | bytes 1448 | tf_op jit(solution)/shard_map/ppermute | solution.py:48
  44.1 0.7 collective-permute-done.4
  45.5 1.0 fusion.252
  47.1 3.4 %collective-permute-start.6 = (f32[5,4,128]{2,1,0:T(4,128)S(1)}, f32[5,4,128]{2,1,0:T(4,128)S(1)}, u32[]{:S(2)}, u32[]{:S(2)}) collective-permute-start(f32[5,4,128]{2,1,0:T(4,128)S(1)} %constant_dynamic-update-slice_fusion.20), channel_id=1, source_target_pairs={{0,32},{32,64},{64,96},{96,128},{128,160},{160,192},{192,224},{1,3... | collective-permute-start | bytes 30728 | tf_op jit(solution)/shard_map/ppermute | solution.py:48
  50.6 2.5 %collective-permute-start.7 = (f32[5,4,128]{2,1,0:T(4,128)S(1)}, f32[5,4,128]{2,1,0:T(4,128)S(1)}, u32[]{:S(2)}, u32[]{:S(2)}) collective-permute-start(f32[5,4,128]{2,1,0:T(4,128)S(1)} %constant_dynamic-update-slice_fusion.25), channel_id=1, source_target_pairs={{32,0},{64,32},{96,64},{128,96},{160,128},{192,160},{224,192},{33,... | collective-permute-start | bytes 30728 | tf_op jit(solution)/shard_map/ppermute | solution.py:48
  53.7 2.5 %collective-permute-done.7 = f32[5,4,128]{2,1,0:T(4,128)S(1)} collective-permute-done((f32[5,4,128]{2,1,0:T(4,128)S(1)}, f32[5,4,128]{2,1,0:T(4,128)S(1)}, u32[]{:S(2)}, u32[]{:S(2)}) %collective-permute-start.7) | collective-permute-done | bytes 10272 | tf_op jit(solution)/shard_map/ppermute | solution.py:48
  56.8 0.8 broadcast_in_dim.24
  57.6 7.5 %all-to-all-start.1 = ((f32[8,4,4,6,128]{4,2,3,1,0:T(4,128)}), f32[8,4,4,6,128]{4,2,3,1,0:T(4,128)S(1)}, u32[]{:S(2)}, u32[]{:S(2)}) async-start(f32[8,4,4,6,128]{4,2,3,1,0:T(4,128)} %broadcast_in_dim.24), calls=%async_computation.1 | async-start | bytes 786432 | tf_op jit(solution)/shard_map/all_to_all | solution.py:65
  65.3 0.8 copy.409.refs_1_
  66.1 7.9 %shard_map.131.refs_0_ = f32[7,8,4,48,128]{4,3,2,1,0:T(8,128)} custom-call(f32[8,4,48,128]{3,2,1,0:T(8,128)} %refs_0_.1, f32[4,4,48,128]{3,2,1,0:T(8,128)} %copy.409.refs_1_, s32[4,48,128]{2,1,0:T(8,128)} %get-tuple-element.90.refs_2_.refs_6_, f32[8,4,48,128]{3,2,1,0:T(8,128)} %fusion.refs_3_.refs_7_), custom_call_target="tpu_custom_call" | custom-call | tf_op jit(solution)/shard_map/pallas_call | solution.py:316
  74.0 1.0 fusion.411
  75.2 3.9 %collective-permute-start.9 = (f32[414,128]{1,0:T(8,128)S(1)}, f32[414,128]{1,0:T(8,128)S(1)}, u32[]{:S(2)}, u32[]{:S(2)}) collective-permute-start(f32[414,128]{1,0:T(8,128)S(1)} %pad_maximum_fusion.1), channel_id=1, source_target_pairs={{0,15},{1,0},{2,1},{3,2},{4,3},{5,4},{6,5},{7,6},{8,7},{9,8},{10,9... | collective-permute-start | bytes 635912 | tf_op jit(solution)/shard_map/ppermute | solution.py:54
  79.1 2.1 %slice_reduce_fusion.3 = (f32[8,4,48]{2,1,0:T(4,128)S(1)}, f32[8,4,48]{2,1,0:T(4,128)S(1)}) fusion(f32[7,8,4,48,128]{4,3,2,1,0:T(8,128)} %shard_map.131.refs_0_), kind=kLoop, calls=%fused_computation.3 | loop fusion | bytes 24576 | tf_op jit(solution)/shard_map/slice | solution.py:408
  81.4 0.8 copy.462.refs_5_
  83.0 1.3 collective-permute-start.11
  84.9 6.0 %collective-permute-start.10 = (f32[1656]{0:T(1024)S(1)}, f32[1656]{0:T(1024)S(1)}, u32[]{:S(2)}, u32[]{:S(2)}) collective-permute-start(f32[1656]{0:T(1024)S(1)} %pad_maximum_fusion.55), channel_id=1, source_target_pairs={{0,16},{1,17},{2,18},{3,19},{4,20},{5,21},{6,22},{7,23},{8,24},{9,... | collective-permute-start | bytes 19880 | tf_op jit(solution)/shard_map/ppermute | solution.py:48
  91.1 0.7 slice.1578
  95.0 0.8 broadcast_in_dim.25
  95.8 7.2 %all-to-all-start.2 = ((f32[8,4,4,6,128]{4,2,3,1,0:T(4,128)}), f32[8,4,4,6,128]{4,2,3,1,0:T(4,128)S(1)}, u32[]{:S(2)}, u32[]{:S(2)}) async-start(f32[8,4,4,6,128]{4,2,3,1,0:T(4,128)} %broadcast_in_dim.25), calls=%async_computation.2 | async-start | bytes 786432 | tf_op jit(solution)/shard_map/all_to_all | solution.py:65
  103.1 3.4 %collective-permute-start.12 = (f32[5,4,128]{2,1,0:T(4,128)S(1)}, f32[5,4,128]{2,1,0:T(4,128)S(1)}, u32[]{:S(2)}, u32[]{:S(2)}) collective-permute-start(f32[5,4,128]{2,1,0:T(4,128)S(1)} %constant_dynamic-update-slice_fusion.40), channel_id=1, source_target_pairs={{0,32},{32,64},{64,96},{96,128},{128,160},{160,192},{192,224},{1,3... | collective-permute-start | bytes 30728 | tf_op jit(solution)/shard_map/ppermute | solution.py:48
  106.6 2.6 %collective-permute-start.13 = (f32[5,4,128]{2,1,0:T(4,128)S(1)}, f32[5,4,128]{2,1,0:T(4,128)S(1)}, u32[]{:S(2)}, u32[]{:S(2)}) collective-permute-start(f32[5,4,128]{2,1,0:T(4,128)S(1)} %constant_dynamic-update-slice_fusion.45), channel_id=1, source_target_pairs={{32,0},{64,32},{96,64},{128,96},{160,128},{192,160},{224,192},{33,... | collective-permute-start | bytes 30728 | tf_op jit(solution)/shard_map/ppermute | solution.py:48
  109.3 1.6 reshape.210.refs_2_
  110.9 1.5 reshape.209.refs_1_
  112.5 9.3 %shard_map.132.refs_0_ = f32[7,8,4,48,128]{4,3,2,1,0:T(8,128)} custom-call(f32[7,8,4,48,128]{4,3,2,1,0:T(8,128)} %shard_map.131.refs_0_, f32[8,4,48,1]{3,2,1,0:T(8,128)} %reshape.209.refs_1_, f32[8,4,48,1]{3,2,1,0:T(8,128)} %reshape.210.refs_2_, f32[8,48,128]{2,1,0:T(8,128)} %bitcast.847, f32[8,48,128]{2,1,0:T(8,128)} %bitcast.848, ...), custom_call_target="tpu_custom_call" | custom-call | tf_op jit(solution)/shard_map/pallas_call | solution.py:316
  121.8 1.0 fusion.410
  123.0 2.1 %slice_reduce_fusion = (f32[8,4,48]{2,1,0:T(4,128)S(1)}, f32[8,4,48]{2,1,0:T(4,128)S(1)}) fusion(f32[7,8,4,48,128]{4,3,2,1,0:T(8,128)} %shard_map.132.refs_0_), kind=kLoop, calls=%fused_computation | loop fusion | bytes 24576 | tf_op jit(solution)/shard_map/slice | solution.py:408
  126.0 3.9 %collective-permute-start.15 = (f32[414,128]{1,0:T(8,128)S(1)}, f32[414,128]{1,0:T(8,128)S(1)}, u32[]{:S(2)}, u32[]{:S(2)}) collective-permute-start(f32[414,128]{1,0:T(8,128)S(1)} %pad_maximum_fusion.3), channel_id=1, source_target_pairs={{0,15},{1,0},{2,1},{3,2},{4,3},{5,4},{6,5},{7,6},{8,7},{9,8},{10,9... | collective-permute-start | bytes 635912 | tf_op jit(solution)/shard_map/ppermute | solution.py:54
  130.3 3.0 %collective-permute-done.14 = f32[414,128]{1,0:T(8,128)S(1)} collective-permute-done((f32[414,128]{1,0:T(8,128)S(1)}, f32[414,128]{1,0:T(8,128)S(1)}, u32[]{:S(2)}, u32[]{:S(2)}) %collective-permute-start.14) | collective-permute-done | bytes 212000 | tf_op jit(solution)/shard_map/ppermute | solution.py:54
  133.8 1.3 collective-permute-start.17
  135.7 6.0 %collective-permute-start.16 = (f32[1656]{0:T(1024)S(1)}, f32[1656]{0:T(1024)S(1)}, u32[]{:S(2)}, u32[]{:S(2)}) collective-permute-start(f32[1656]{0:T(1024)S(1)} %pad_maximum_fusion.57), channel_id=1, source_target_pairs={{0,16},{1,17},{2,18},{3,19},{4,20},{5,21},{6,22},{7,23},{8,24},{9,... | collective-permute-start | bytes 19880 | tf_op jit(solution)/shard_map/ppermute | solution.py:48
  141.9 0.7 slice.1653
  142.6 0.7 slice.1652
  143.3 1.6 reshape.212.refs_2_
  144.9 1.5 reshape.211.refs_1_
  149.0 0.8 copy.518.refs_5_
  149.8 9.2 %shard_map.133.refs_0_ = f32[7,8,4,48,128]{4,3,2,1,0:T(8,128)} custom-call(f32[7,8,4,48,128]{4,3,2,1,0:T(8,128)} %shard_map.132.refs_0_, f32[8,4,48,1]{3,2,1,0:T(8,128)} %reshape.211.refs_1_, f32[8,4,48,1]{3,2,1,0:T(8,128)} %reshape.212.refs_2_, f32[8,48,128]{2,1,0:T(8,128)} %bitcast.850, f32[8,48,128]{2,1,0:T(8,128)} %bitcast.849, ...), custom_call_target="tpu_custom_call" | custom-call | tf_op jit(solution)/shard_map/pallas_call | solution.py:316
  159.0 1.0 slice_bitcast_fusion
  160.2 3.8 %collective-permute-start.21 = (f32[8,48,128]{2,1,0:T(8,128)S(1)}, f32[8,48,128]{2,1,0:T(8,128)S(1)}, u32[]{:S(2)}, u32[]{:S(2)}) collective-permute-start(f32[8,48,128]{2,1,0:T(8,128)S(1)} %get-tuple-element.121), channel_id=1, source_target_pairs={{0,15},{1,0},{2,1},{3,2},{4,3},{5,4},{6,5},{7,6},{8,7},{9,8},{10,9... | collective-permute-start | bytes 589832 | tf_op jit(solution)/shard_map/ppermute | solution.py:54
  164.0 1.6 fusion.409
  166.0 3.9 %collective-permute-start.18 = (f32[8,4,48,1]{2,0,3,1:T(8,128)S(1)}, f32[8,4,48,1]{2,0,3,1:T(8,128)S(1)}, u32[]{:S(2)}, u32[]{:S(2)}) collective-permute-start(f32[8,4,48,1]{2,0,3,1:T(8,128)S(1)} %bitcast.944), channel_id=1, source_target_pairs={{0,16},{1,17},{2,18},{3,19},{4,20},{5,21},{6,22},{7,23},{8,24},{9,... | collective-permute-start | bytes 18440 | tf_op jit(solution)/shard_map/ppermute | solution.py:48
  170.2 1.3 collective-permute-start.19
  171.5 0.8 copy.525
  172.3 1.3 copy.523.refs_1_
  173.5 3.8 %collective-permute-done.19 = f32[8,4,48,1]{2,0,3,1:T(8,128)S(1)} collective-permute-done((f32[8,4,48,1]{2,0,3,1:T(8,128)S(1)}, f32[8,4,48,1]{2,0,3,1:T(8,128)S(1)}, u32[]{:S(2)}, u32[]{:S(2)}) %collective-permute-start.19) | collective-permute-done | bytes 6176 | tf_op jit(solution)/shard_map/ppermute | solution.py:48
  177.3 1.2 copy.524.refs_2_
  179.9 6.9 %shard_map.134 = f32[8,4,48,128]{3,2,1,0:T(8,128)} custom-call(f32[7,8,4,48,128]{4,3,2,1,0:T(8,128)} %shard_map.133.refs_0_, f32[8,4,48,1]{3,2,1,0:T(8,128)} %copy.523.refs_1_, f32[8,4,48,1]{3,2,1,0:T(8,128)} %copy.524.refs_2_, f32[8,48,128]{2,1,0:T(8,128)} %copy-done, f32[8,48,128]{2,1,0:T(8,128)} %copy-done.1), custom_call_target="tpu_custom_call" | custom-call | tf_op jit(solution)/shard_map/pallas_call | solution.py:316
  (401 shorter events, 17.4 us)
Async XLA Ops:
  0.6 42.9 %copy-start.3 = (f32[5]{0:T(128)S(1)}, f32[5]{0:T(128)}, u32[]{:S(2)}) copy-start(f32[5]{0:T(128)} %constant.109.clone) | copy-start | bytes 64
  0.6 44.2 %copy-start.2 = (f32[5]{0:T(128)S(1)}, f32[5]{0:T(128)}, u32[]{:S(2)}) copy-start(f32[5]{0:T(128)} %constant.108.clone) | copy-start | bytes 64
  7.9 21.7 %collective-permute-start = (f32[5,4,128]{2,1,0:T(4,128)S(1)}, f32[5,4,128]{2,1,0:T(4,128)S(1)}, u32[]{:S(2)}, u32[]{:S(2)}) collective-permute-start(f32[5,4,128]{2,1,0:T(4,128)S(1)} %constant_dynamic-update-slice_fusion), channel_id=1, source_target_pairs={{0,32},{32,64},{64,96},{96,128},{128,160},{160,192},{192,224},{1,3... | collective-permute-start | bytes 30728 | tf_op jit(solution)/shard_map/ppermute | solution.py:48
  13.6 16.2 %collective-permute-start.1 = (f32[5,4,128]{2,1,0:T(4,128)S(1)}, f32[5,4,128]{2,1,0:T(4,128)S(1)}, u32[]{:S(2)}, u32[]{:S(2)}) collective-permute-start(f32[5,4,128]{2,1,0:T(4,128)S(1)} %constant_dynamic-update-slice_fusion.5), channel_id=1, source_target_pairs={{32,0},{64,32},{96,64},{128,96},{160,128},{192,160},{224,192},{33,... | collective-permute-start | bytes 30728 | tf_op jit(solution)/shard_map/ppermute | solution.py:48
  16.5 40.3 %all-to-all-start = ((f32[8,4,4,6,128]{4,2,3,1,0:T(4,128)}), f32[8,4,4,6,128]{4,2,3,1,0:T(4,128)S(1)}, u32[]{:S(2)}, u32[]{:S(2)}) async-start(f32[8,4,4,6,128]{4,2,3,1,0:T(4,128)} %broadcast_in_dim.21), calls=%async_computation | async-start | bytes 786432 | tf_op jit(solution)/shard_map/all_to_all | solution.py:65
  29.9 5.4 %collective-permute-start.2 = (f32[5,6,128]{2,0,1:T(8,128)S(1)}, f32[5,6,128]{2,0,1:T(8,128)S(1)}, u32[]{:S(2)}, u32[]{:S(2)}) collective-permute-start(f32[5,6,128]{2,0,1:T(8,128)S(1)} %stack.161), channel_id=1, source_target_pairs={{0,1},{1,2},{2,3},{3,4},{4,5},{5,6},{6,7},{7,8},{8,9},{9,10},{10,1... | collective-permute-start | bytes 46088 | tf_op jit(solution)/shard_map/ppermute | solution.py:54
  30.1 5.4 %collective-permute-start.3 = (f32[5,6,128]{2,0,1:T(8,128)S(1)}, f32[5,6,128]{2,0,1:T(8,128)S(1)}, u32[]{:S(2)}, u32[]{:S(2)}) collective-permute-start(f32[5,6,128]{2,0,1:T(8,128)S(1)} %stack.162), channel_id=1, source_target_pairs={{0,15},{1,0},{2,1},{3,2},{4,3},{5,4},{6,5},{7,6},{8,7},{9,8},{10,9... | collective-permute-start | bytes 46088 | tf_op jit(solution)/shard_map/ppermute | solution.py:54
  35.7 7.8 %collective-permute-start.5 = (f32[5,4,6]{2,1,0:T(4,128)S(1)}, f32[5,4,6]{2,1,0:T(4,128)S(1)}, u32[]{:S(2)}, u32[]{:S(2)}) collective-permute-start(f32[5,4,6]{2,1,0:T(4,128)S(1)} %constant_dynamic-update-slice_fusion.15), channel_id=1, source_target_pairs={{16,0},{17,1},{18,2},{19,3},{20,4},{21,5},{22,6},{23,7},{24,8},{25... | collective-permute-start | bytes 1448 | tf_op jit(solution)/shard_map/ppermute | solution.py:48
  37.4 7.4 %collective-permute-start.4 = (f32[5,4,6]{2,1,0:T(4,128)S(1)}, f32[5,4,6]{2,1,0:T(4,128)S(1)}, u32[]{:S(2)}, u32[]{:S(2)}) collective-permute-start(f32[5,4,6]{2,1,0:T(4,128)S(1)} %constant_dynamic-update-slice_fusion.10), channel_id=1, source_target_pairs={{0,16},{1,17},{2,18},{3,19},{4,20},{5,21},{6,22},{7,23},{8,24},{9,... | collective-permute-start | bytes 1448 | tf_op jit(solution)/shard_map/ppermute | solution.py:48
  47.1 6.5 %collective-permute-start.6 = (f32[5,4,128]{2,1,0:T(4,128)S(1)}, f32[5,4,128]{2,1,0:T(4,128)S(1)}, u32[]{:S(2)}, u32[]{:S(2)}) collective-permute-start(f32[5,4,128]{2,1,0:T(4,128)S(1)} %constant_dynamic-update-slice_fusion.20), channel_id=1, source_target_pairs={{0,32},{32,64},{64,96},{96,128},{128,160},{160,192},{192,224},{1,3... | collective-permute-start | bytes 30728 | tf_op jit(solution)/shard_map/ppermute | solution.py:48
  50.6 5.6 %collective-permute-start.7 = (f32[5,4,128]{2,1,0:T(4,128)S(1)}, f32[5,4,128]{2,1,0:T(4,128)S(1)}, u32[]{:S(2)}, u32[]{:S(2)}) collective-permute-start(f32[5,4,128]{2,1,0:T(4,128)S(1)} %constant_dynamic-update-slice_fusion.25), channel_id=1, source_target_pairs={{32,0},{64,32},{96,64},{128,96},{160,128},{192,160},{224,192},{33,... | collective-permute-start | bytes 30728 | tf_op jit(solution)/shard_map/ppermute | solution.py:48
  57.6 23.8 %all-to-all-start.1 = ((f32[8,4,4,6,128]{4,2,3,1,0:T(4,128)}), f32[8,4,4,6,128]{4,2,3,1,0:T(4,128)S(1)}, u32[]{:S(2)}, u32[]{:S(2)}) async-start(f32[8,4,4,6,128]{4,2,3,1,0:T(4,128)} %broadcast_in_dim.24), calls=%async_computation.1 | async-start | bytes 786432 | tf_op jit(solution)/shard_map/all_to_all | solution.py:65
  75.1 7.5 %collective-permute-start.8 = (f32[414,128]{1,0:T(8,128)S(1)}, f32[414,128]{1,0:T(8,128)S(1)}, u32[]{:S(2)}, u32[]{:S(2)}) collective-permute-start(f32[414,128]{1,0:T(8,128)S(1)} %pad_maximum_fusion), channel_id=1, source_target_pairs={{0,1},{1,2},{2,3},{3,4},{4,5},{5,6},{6,7},{7,8},{8,9},{9,10},{10,1... | collective-permute-start | bytes 635912 | tf_op jit(solution)/shard_map/ppermute | solution.py:54
  75.2 7.5 %collective-permute-start.9 = (f32[414,128]{1,0:T(8,128)S(1)}, f32[414,128]{1,0:T(8,128)S(1)}, u32[]{:S(2)}, u32[]{:S(2)}) collective-permute-start(f32[414,128]{1,0:T(8,128)S(1)} %pad_maximum_fusion.1), channel_id=1, source_target_pairs={{0,15},{1,0},{2,1},{3,2},{4,3},{5,4},{6,5},{7,6},{8,7},{9,8},{10,9... | collective-permute-start | bytes 635912 | tf_op jit(solution)/shard_map/ppermute | solution.py:54
  83.0 9.4 %collective-permute-start.11 = (f32[1656]{0:T(1024)S(1)}, f32[1656]{0:T(1024)S(1)}, u32[]{:S(2)}, u32[]{:S(2)}) collective-permute-start(f32[1656]{0:T(1024)S(1)} %pad_maximum_fusion.56), channel_id=1, source_target_pairs={{16,0},{17,1},{18,2},{19,3},{20,4},{21,5},{22,6},{23,7},{24,8},{25... | collective-permute-start | bytes 19880 | tf_op jit(solution)/shard_map/ppermute | solution.py:48
  84.9 8.2 %collective-permute-start.10 = (f32[1656]{0:T(1024)S(1)}, f32[1656]{0:T(1024)S(1)}, u32[]{:S(2)}, u32[]{:S(2)}) collective-permute-start(f32[1656]{0:T(1024)S(1)} %pad_maximum_fusion.55), channel_id=1, source_target_pairs={{0,16},{1,17},{2,18},{3,19},{4,20},{5,21},{6,22},{7,23},{8,24},{9,... | collective-permute-start | bytes 19880 | tf_op jit(solution)/shard_map/ppermute | solution.py:48
  95.8 53.2 %all-to-all-start.2 = ((f32[8,4,4,6,128]{4,2,3,1,0:T(4,128)}), f32[8,4,4,6,128]{4,2,3,1,0:T(4,128)S(1)}, u32[]{:S(2)}, u32[]{:S(2)}) async-start(f32[8,4,4,6,128]{4,2,3,1,0:T(4,128)} %broadcast_in_dim.25), calls=%async_computation.2 | async-start | bytes 786432 | tf_op jit(solution)/shard_map/all_to_all | solution.py:65
  103.1 22.3 %collective-permute-start.12 = (f32[5,4,128]{2,1,0:T(4,128)S(1)}, f32[5,4,128]{2,1,0:T(4,128)S(1)}, u32[]{:S(2)}, u32[]{:S(2)}) collective-permute-start(f32[5,4,128]{2,1,0:T(4,128)S(1)} %constant_dynamic-update-slice_fusion.40), channel_id=1, source_target_pairs={{0,32},{32,64},{64,96},{96,128},{128,160},{160,192},{192,224},{1,3... | collective-permute-start | bytes 30728 | tf_op jit(solution)/shard_map/ppermute | solution.py:48
  106.6 19.0 %collective-permute-start.13 = (f32[5,4,128]{2,1,0:T(4,128)S(1)}, f32[5,4,128]{2,1,0:T(4,128)S(1)}, u32[]{:S(2)}, u32[]{:S(2)}) collective-permute-start(f32[5,4,128]{2,1,0:T(4,128)S(1)} %constant_dynamic-update-slice_fusion.45), channel_id=1, source_target_pairs={{32,0},{64,32},{96,64},{128,96},{160,128},{192,160},{224,192},{33,... | collective-permute-start | bytes 30728 | tf_op jit(solution)/shard_map/ppermute | solution.py:48
  125.8 7.5 %collective-permute-start.14 = (f32[414,128]{1,0:T(8,128)S(1)}, f32[414,128]{1,0:T(8,128)S(1)}, u32[]{:S(2)}, u32[]{:S(2)}) collective-permute-start(f32[414,128]{1,0:T(8,128)S(1)} %pad_maximum_fusion.2), channel_id=1, source_target_pairs={{0,1},{1,2},{2,3},{3,4},{4,5},{5,6},{6,7},{7,8},{8,9},{9,10},{10,1... | collective-permute-start | bytes 635912 | tf_op jit(solution)/shard_map/ppermute | solution.py:54
  126.0 7.4 %collective-permute-start.15 = (f32[414,128]{1,0:T(8,128)S(1)}, f32[414,128]{1,0:T(8,128)S(1)}, u32[]{:S(2)}, u32[]{:S(2)}) collective-permute-start(f32[414,128]{1,0:T(8,128)S(1)} %pad_maximum_fusion.3), channel_id=1, source_target_pairs={{0,15},{1,0},{2,1},{3,2},{4,3},{5,4},{6,5},{7,6},{8,7},{9,8},{10,9... | collective-permute-start | bytes 635912 | tf_op jit(solution)/shard_map/ppermute | solution.py:54
  133.8 9.5 %collective-permute-start.17 = (f32[1656]{0:T(1024)S(1)}, f32[1656]{0:T(1024)S(1)}, u32[]{:S(2)}, u32[]{:S(2)}) collective-permute-start(f32[1656]{0:T(1024)S(1)} %pad_maximum_fusion.58), channel_id=1, source_target_pairs={{16,0},{17,1},{18,2},{19,3},{20,4},{21,5},{22,6},{23,7},{24,8},{25... | collective-permute-start | bytes 19880 | tf_op jit(solution)/shard_map/ppermute | solution.py:48
  135.7 9.2 %collective-permute-start.16 = (f32[1656]{0:T(1024)S(1)}, f32[1656]{0:T(1024)S(1)}, u32[]{:S(2)}, u32[]{:S(2)}) collective-permute-start(f32[1656]{0:T(1024)S(1)} %pad_maximum_fusion.57), channel_id=1, source_target_pairs={{0,16},{1,17},{2,18},{3,19},{4,20},{5,21},{6,22},{7,23},{8,24},{9,... | collective-permute-start | bytes 19880 | tf_op jit(solution)/shard_map/ppermute | solution.py:48
  160.1 18.5 %collective-permute-start.20 = (f32[8,48,128]{2,1,0:T(8,128)S(1)}, f32[8,48,128]{2,1,0:T(8,128)S(1)}, u32[]{:S(2)}, u32[]{:S(2)}) collective-permute-start(f32[8,48,128]{2,1,0:T(8,128)S(1)} %get-tuple-element.122), channel_id=1, source_target_pairs={{0,1},{1,2},{2,3},{3,4},{4,5},{5,6},{6,7},{7,8},{8,9},{9,10},{10,1... | collective-permute-start | bytes 589832 | tf_op jit(solution)/shard_map/ppermute | solution.py:54
  160.2 18.4 %collective-permute-start.21 = (f32[8,48,128]{2,1,0:T(8,128)S(1)}, f32[8,48,128]{2,1,0:T(8,128)S(1)}, u32[]{:S(2)}, u32[]{:S(2)}) collective-permute-start(f32[8,48,128]{2,1,0:T(8,128)S(1)} %get-tuple-element.121), channel_id=1, source_target_pairs={{0,15},{1,0},{2,1},{3,2},{4,3},{5,4},{6,5},{7,6},{8,7},{9,8},{10,9... | collective-permute-start | bytes 589832 | tf_op jit(solution)/shard_map/ppermute | solution.py:54
  166.0 6.3 %collective-permute-start.18 = (f32[8,4,48,1]{2,0,3,1:T(8,128)S(1)}, f32[8,4,48,1]{2,0,3,1:T(8,128)S(1)}, u32[]{:S(2)}, u32[]{:S(2)}) collective-permute-start(f32[8,4,48,1]{2,0,3,1:T(8,128)S(1)} %bitcast.944), channel_id=1, source_target_pairs={{0,16},{1,17},{2,18},{3,19},{4,20},{5,21},{6,22},{7,23},{8,24},{9,... | collective-permute-start | bytes 18440 | tf_op jit(solution)/shard_map/ppermute | solution.py:48
  170.2 7.1 %collective-permute-start.19 = (f32[8,4,48,1]{2,0,3,1:T(8,128)S(1)}, f32[8,4,48,1]{2,0,3,1:T(8,128)S(1)}, u32[]{:S(2)}, u32[]{:S(2)}) collective-permute-start(f32[8,4,48,1]{2,0,3,1:T(8,128)S(1)} %bitcast.945), channel_id=1, source_target_pairs={{16,0},{17,1},{18,2},{19,3},{20,4},{21,5},{22,6},{23,7},{24,8},{25... | collective-permute-start | bytes 18440 | tf_op jit(solution)/shard_map/ppermute | solution.py:48
  178.6 0.7 copy-start
  179.2 0.7 copy-start.1

commit v7 on v5

--- a/solution.py
+++ b/solution.py
@@ -344,6 +344,32 @@
     return (flow, arrived_scalar)
 
 
+def swapped_section(flow, scalar_out, sender, edge_fill):
+    first = lax.axis_index("gx") == 0
+    leaving = {}
+    for heading in (1, -1):
+        flow_planes = edge_planes(flow, flow_vectors, 0, 2, heading)
+        leaving[heading] = (flow_planes, scalar_out[heading])
+    split_at = leaving[1][0].size
+    packed = {
+        heading: jnp.concatenate([part.reshape(-1) for part in leaving[heading]], 0)
+        for heading in (1, -1)
+    }
+    arrived = lax.ppermute(jnp.where(first, packed[1], packed[-1]), "gx", [(0, 1), (1, 0)])
+    outside = jnp.zeros_like(arrived)
+    incoming = {1: jnp.where(first, outside, arrived), -1: jnp.where(first, arrived, outside)}
+    arrived_flow = {}
+    arrived_scalar = {}
+    for heading in (1, -1):
+        flow_planes, scalar_planes = leaving[heading]
+        arrived_flow[heading] = edge_fill(
+            incoming[heading][:split_at].reshape(flow_planes.shape), heading
+        )
+        arrived_scalar[heading] = incoming[heading][split_at:].reshape(scalar_planes.shape)
+    flow = displace(flow, flow_vectors, 0, 2, arrived_flow[1], arrived_flow[-1])
+    return (flow, arrived_scalar)
+
+
 def flow_section(flow, component, flow_dim, sender, edge_fill):
     arrived = {}
     for heading in (1, -1):
@@ -381,21 +407,37 @@
     ).reshape(concentration.shape)
     solid_flag = solid.astype(jnp.int32)
     flow_solid = lax.dynamic_slice_in_dim(solid, row_index * slab_depth, slab_depth, 1)
+    rows = lax.axis_size("row")
     flow = [flow_pops[member] for member in range(19)]
     scalars = concentration
     halos = None
     for time_step in range(STEPS):
         flow, motion = flow_collide(flow, flow_solid)
-        column = lax.all_gather(motion, "row", axis=2, tiled=True)
+        rising = edge_planes(flow, flow_vectors, 2, 1, 1)
+        sinking = edge_planes(flow, flow_vectors, 2, 1, -1)
+        payload = jnp.concatenate([motion.reshape(-1), rising.reshape(-1), sinking.reshape(-1)], 0)
+        everyone = copy_for_each(payload, "row")
+        column = in_order(everyone[:, : motion.size].reshape((rows,) + motion.shape), 2)
+        below = lax.dynamic_index_in_dim(everyone, jnp.maximum(row_index - 1, 0), 0, False)
+        above = lax.dynamic_index_in_dim(everyone, jnp.minimum(row_index + 1, rows - 1), 0, False)
+        from_below = jnp.where(
+            row_index == 0, 0.0, below[motion.size : motion.size + rising.size]
+        ).reshape(rising.shape)
+        from_above = jnp.where(
+            row_index == rows - 1, 0.0, above[motion.size + rising.size :]
+        ).reshape(sinking.shape)
         mode = "first" if time_step == 0 else "middle"
         scalars = scalar_stage(mode, scalars, halos, column, solid_flag, source)
-        from_below = send_vertical(edge_planes(flow, flow_vectors, 2, 1, 1), 1)
-        from_above = send_vertical(edge_planes(flow, flow_vectors, 2, 1, -1), -1)
         flow = displace(flow, flow_vectors, 2, 1, from_below, from_above)
         leaving_y = {1: scalars[3, :, span_y - 1], -1: scalars[4, :, 0]}
         flow, arrived_y = packed_section(flow, leaving_y, 1, 0, send_spanwise, keep_spanwise, True)
         leaving_x = {1: scalars[1, :, :, :, span_x - 1 :], -1: scalars[2, :, :, :, :1]}
-        flow, arrived_x = packed_section(flow, leaving_x, 0, 2, send_streamwise, inflow_fill, False)
+        if lax.axis_size("gx") == 2:
+            flow, arrived_x = swapped_section(flow, leaving_x, send_streamwise, inflow_fill)
+        else:
+            flow, arrived_x = packed_section(
+                flow, leaving_x, 0, 2, send_streamwise, inflow_fill, False
+            )
         halos = (arrived_x[1], arrived_x[-1], arrived_y[1], arrived_y[-1])
     amount = scalar_stage("final", scalars, halos, None, None, None)
     stacked = jnp.stack(flow)

time: 233 us -> 177 us (0.76)
  blocking collectives: 69.1 us -> 0 us
  waiting for transfers between devices: 20.5 us -> 54.3 us
  starting transfers between devices: 53.7 us -> 29.4 us
  local copies, waits for them, and re-layouts: 36.3 us -> 40.6 us
    all_gather x3 -> x0, blocking collectives: 69.1 us -> none  [on_device(): column = lax.all_gather(motion, 'row', axis=2, tiled=True)]
    all_to_all x0 -> x3, waiting for transfers between devices: none -> 42.3 us  [copy_for_each(): return lax.all_to_all(copies, axis, split_axis=0, concat_axis=0, tiled=True)]
    ppermute x12 -> x3, starting transfers between devices: 32.4 us -> 8.63 us  [swapped_section(): lax.ppermute(jnp.where(first, packed[1], packed[-1]), 'gx', [(0, 1), (1,...]
    ppermute x6, starting transfers between devices: 21.3 us -> 5.5 us  [from_behind(): return lax.ppermute(value, axis, pairs)]
    all_to_all x0 -> x3, starting transfers between devices: none -> 15.3 us  [copy_for_each(): return lax.all_to_all(copies, axis, split_axis=0, concat_axis=0, tiled=True)]
    ppermute x6, waiting for transfers between devices: 20.4 us -> 11.1 us  [from_behind(): return lax.ppermute(value, axis, pairs)]
    slice x1 -> x3, local copies, waits for them, and re-layouts: 2.08 us -> 6.24 us  [on_device(): scalars[2, :, :, :, :1]]
    broadcast_in_dim x0 -> x3, local copies, waits for them, and re-layouts: none -> 3.32 us  [copy_for_each(): copies = jnp.broadcast_to(x, (lax.axis_size(axis), *x.shape))]
  transfers between devices with their start and end apart: 18 -> 12, of which waited for: 6 -> 8; matrix products, arithmetic and copies ran while one was open for 16% -> 13% of each run, Pallas kernels for 11% -> 0%
where the time goes in v7:
time: 177 us; the launch traced here: 175 us
  waiting for transfers between devices  54.3 us (31%)
  local copies, waits for them, and re-layouts  40.6 us (23%)
  Pallas kernels  33.4 us (19%)
  starting transfers between devices  29.4 us (17%)
  other arithmetic  13.2 us (7%)
  between operations  2.37 us (1%)
  matrix products  2.09 us (1%)
    all_to_all x3, waiting for transfers between devices, copy_for_each(): return lax.all_to_all(copies, axis, split_axis=0, concat_axis=0, tiled=True)  42.3 us
    pallas_call x4, Pallas kernels, scalar_stage(): pl.pallas_call(scalar_kernel(mode, span_y, depth, span_x), grid=(count,),...  33.4 us
    all_to_all x3, starting transfers between devices, copy_for_each(): return lax.all_to_all(copies, axis, split_axis=0, concat_axis=0, tiled=True)  15.3 us
    ppermute x6, waiting for transfers between devices, from_behind(): return lax.ppermute(value, axis, pairs)  11.1 us
    reshape x6, local copies, waits for them, and re-layouts, swapped_section(): incoming[heading][split_at:].reshape(scalar_planes.shape)  9.13 us
    ppermute x3, starting transfers between devices, swapped_section(): lax.ppermute(jnp.where(first, packed[1], packed[-1]), 'gx', [(0, 1), (1,...  8.63 us
    slice x3, local copies, waits for them, and re-layouts, on_device(): scalars[2, :, :, :, :1]  6.24 us
    ppermute x6, starting transfers between devices, from_behind(): return lax.ppermute(value, axis, pairs)  5.5 us
  transfers between devices with their start and end apart: 12, of which 8 were waited for; matrix products, arithmetic and copies ran while one was open for 13% of the time, Pallas kernels for 0%

profile of v7, /device:TPU:7, one launch (start us, length us, event | category | flops | bytes accessed | tf_op | source)
XLA Modules:
  0.0 175.3 jit_solution(5202720370544031460)
XLA Ops:
  0.6 1.0 fusion.29
  1.6 1.6 fusion.403
  3.3 1.1 fusion.330
  4.4 0.9 bitcast_select_fusion.4
  5.3 0.9 fusion.320
  6.2 0.9 bitcast_select_fusion.7
  7.3 1.1 broadcast_in_dim.31
  8.4 8.2 %all-to-all-start = ((f32[8,1,17408]{2,1,0:T(1,128)}), f32[8,1,17408]{2,1,0:T(1,128)S(1)}, u32[]{:S(2)}, u32[]{:S(2)}) async-start(f32[8,1,17408]{2,1,0:T(1,128)} %broadcast_in_dim.31), calls=%async_computation | async-start | bytes 1114112 | tf_op jit(solution)/shard_map/all_to_all | solution.py:65
  16.6 0.8 bitcast_select_fusion.5
  17.9 0.7 fusion.332
  18.6 2.1 %fusion.refs_3_.refs_7_ = f32[8,4,48,128]{3,2,1,0:T(8,128)} fusion(f32[96]{0:T(128)} %param.17, s32[96]{0:T(128)S(1)} %get-tuple-element.306, s32[96]{0:T(128)S(1)} %get-tuple-element.305, s32[96]{0:T(128)S(1)} %get-tuple-element.309, s32[96]{0:T(128)S(1)} %get-tuple-element.304), kind=kOutput, calls=%fused_computation.6 | convolution fusion | flops 227389440 | bytes 788352 | tf_op jit(solution)/shard_map/dot_general | solution.py:405
  20.7 14.6 %all-to-all-done = f32[8,1,17408]{2,1,0:T(1,128)S(1)} async-done(((f32[8,1,17408]{2,1,0:T(1,128)}), f32[8,1,17408]{2,1,0:T(1,128)S(1)}, u32[]{:S(2)}, u32[]{:S(2)}) %all-to-all-start) | async-done | bytes 557088 | tf_op jit(solution)/shard_map/all_to_all | solution.py:65
  35.4 0.2 copy.380
  35.5 0.8 copy.381.refs_1_
  36.3 7.9 %shard_map.131.refs_0_ = f32[7,8,4,48,128]{4,3,2,1,0:T(8,128)} custom-call(f32[8,4,48,128]{3,2,1,0:T(8,128)} %refs_0_.1, f32[4,4,48,128]{3,2,1,0:T(8,128)} %copy.381.refs_1_, s32[4,48,128]{2,1,0:T(8,128)} %get-tuple-element.113.refs_2_.refs_6_, f32[8,4,48,128]{3,2,1,0:T(8,128)} %fusion.refs_3_.refs_7_), custom_call_target="tpu_custom_call" | custom-call | tf_op jit(solution)/shard_map/pallas_call | solution.py:316
  44.3 1.0 fusion.409
  45.5 0.6 collective-permute-start.1
  46.2 3.4 %collective-permute-start = (f32[414,128]{1,0:T(8,128)S(1)}, f32[414,128]{1,0:T(8,128)S(1)}, u32[]{:S(2)}, u32[]{:S(2)}) collective-permute-start(f32[414,128]{1,0:T(8,128)S(1)} %pad_maximum_fusion), channel_id=1, source_target_pairs={{0,1},{1,2},{2,3},{3,4},{4,5},{5,6},{6,7},{7,8},{8,9},{9,10},{10,1... | collective-permute-start | bytes 635912 | tf_op jit(solution)/shard_map/ppermute | solution.py:54
  50.3 2.1 %slice_reduce_fusion.4 = (f32[8,4,48]{2,1,0:T(4,128)S(1)}, f32[8,4,48]{2,1,0:T(4,128)S(1)}) fusion(f32[7,8,4,48,128]{4,3,2,1,0:T(8,128)} %shard_map.131.refs_0_), kind=kLoop, calls=%fused_computation.4 | loop fusion | bytes 24576 | tf_op jit(solution)/shard_map/slice | solution.py:434
  52.5 0.5 collective-permute-done.1
  54.0 2.9 %collective-permute-start.2 = (f32[1656]{0:T(1024)S(1)}, f32[1656]{0:T(1024)S(1)}, u32[]{:S(2)}, u32[]{:S(2)}) collective-permute-start(f32[1656]{0:T(1024)S(1)} %maximum_select_fusion), channel_id=1, source_target_pairs={{0,16},{16,0},{1,17},{17,1},{2,18},{18,2},{3,19},{19,3},{4,20},{20... | collective-permute-start | bytes 19880 | tf_op jit(solution)/shard_map/ppermute | solution.py:358
  57.2 0.9 collective-permute-done.2
  59.6 1.0 fusion.252
  60.7 0.3 subtract_select_fusion.19
  61.4 1.1 broadcast_in_dim.34
  62.5 3.5 %all-to-all-start.1 = ((f32[8,1,17408]{2,1,0:T(1,128)}), f32[8,1,17408]{2,1,0:T(1,128)S(1)}, u32[]{:S(2)}, u32[]{:S(2)}) async-start(f32[8,1,17408]{2,1,0:T(1,128)} %broadcast_in_dim.34), calls=%async_computation.1 | async-start | bytes 1114112 | tf_op jit(solution)/shard_map/all_to_all | solution.py:65
  66.0 0.7 slice.1834
  66.7 0.7 slice.1833
  67.7 1.5 reshape.559.refs_1_
  69.2 1.6 reshape.560.refs_2_
  71.1 13.6 %all-to-all-done.1 = f32[8,1,17408]{2,1,0:T(1,128)S(1)} async-done(((f32[8,1,17408]{2,1,0:T(1,128)}), f32[8,1,17408]{2,1,0:T(1,128)S(1)}, u32[]{:S(2)}, u32[]{:S(2)}) %all-to-all-start.1) | async-done | bytes 557088 | tf_op jit(solution)/shard_map/all_to_all | solution.py:65
  85.3 0.2 copy.432
  85.4 0.8 copy.435.refs_5_
  86.2 9.3 %shard_map.132.refs_0_ = f32[7,8,4,48,128]{4,3,2,1,0:T(8,128)} custom-call(f32[7,8,4,48,128]{4,3,2,1,0:T(8,128)} %shard_map.131.refs_0_, f32[8,4,48,1]{3,2,1,0:T(8,128)} %reshape.559.refs_1_, f32[8,4,48,1]{3,2,1,0:T(8,128)} %reshape.560.refs_2_, f32[8,48,128]{2,1,0:T(8,128)} %bitcast.843, f32[8,48,128]{2,1,0:T(8,128)} %bitcast.842, ...), custom_call_target="tpu_custom_call" | custom-call | tf_op jit(solution)/shard_map/pallas_call | solution.py:316
  95.5 1.0 fusion.408
  96.6 0.4 collective-permute-start.3
  97.1 0.4 collective-permute-start.4
  97.9 2.1 %slice_reduce_fusion.2 = (f32[8,4,48]{2,1,0:T(4,128)S(1)}, f32[8,4,48]{2,1,0:T(4,128)S(1)}) fusion(f32[7,8,4,48,128]{4,3,2,1,0:T(8,128)} %shard_map.132.refs_0_), kind=kLoop, calls=%fused_computation.2 | loop fusion | bytes 24576 | tf_op jit(solution)/shard_map/slice | solution.py:434
  100.3 4.4 %collective-permute-done.4 = f32[414,128]{1,0:T(8,128)S(1)} collective-permute-done((f32[414,128]{1,0:T(8,128)S(1)}, f32[414,128]{1,0:T(8,128)S(1)}, u32[]{:S(2)}, u32[]{:S(2)}) %collective-permute-start.4) | collective-permute-done | bytes 212000 | tf_op jit(solution)/shard_map/ppermute | solution.py:54
  105.6 2.7 %collective-permute-start.5 = (f32[1656]{0:T(1024)S(1)}, f32[1656]{0:T(1024)S(1)}, u32[]{:S(2)}, u32[]{:S(2)}) collective-permute-start(f32[1656]{0:T(1024)S(1)} %maximum_select_fusion.1), channel_id=1, source_target_pairs={{0,16},{16,0},{1,17},{17,1},{2,18},{18,2},{3,19},{19,3},{4,20},{20... | collective-permute-start | bytes 19880 | tf_op jit(solution)/shard_map/ppermute | solution.py:358
  108.4 0.7 slice.1928
  109.1 0.7 slice.1929
  111.3 0.2 fusion.256
  111.7 0.3 divide_subtract_fusion
  112.4 1.1 broadcast_in_dim.35
  113.5 3.5 %all-to-all-start.2 = ((f32[8,1,17408]{2,1,0:T(1,128)}), f32[8,1,17408]{2,1,0:T(1,128)S(1)}, u32[]{:S(2)}, u32[]{:S(2)}) async-start(f32[8,1,17408]{2,1,0:T(1,128)} %broadcast_in_dim.35), calls=%async_computation.2 | async-start | bytes 1114112 | tf_op jit(solution)/shard_map/all_to_all | solution.py:65
  117.7 1.5 reshape.561.refs_1_
  119.2 1.6 reshape.562.refs_2_
  120.8 14.1 %all-to-all-done.2 = f32[8,1,17408]{2,1,0:T(1,128)S(1)} async-done(((f32[8,1,17408]{2,1,0:T(1,128)}), f32[8,1,17408]{2,1,0:T(1,128)S(1)}, u32[]{:S(2)}, u32[]{:S(2)}) %all-to-all-start.2) | async-done | bytes 557088 | tf_op jit(solution)/shard_map/all_to_all | solution.py:65
  135.1 0.2 copy.487
  135.2 0.8 copy.490.refs_5_
  136.0 9.3 %shard_map.133.refs_0_ = f32[7,8,4,48,128]{4,3,2,1,0:T(8,128)} custom-call(f32[7,8,4,48,128]{4,3,2,1,0:T(8,128)} %shard_map.132.refs_0_, f32[8,4,48,1]{3,2,1,0:T(8,128)} %reshape.561.refs_1_, f32[8,4,48,1]{3,2,1,0:T(8,128)} %reshape.562.refs_2_, f32[8,48,128]{2,1,0:T(8,128)} %bitcast.840, f32[8,48,128]{2,1,0:T(8,128)} %bitcast.841, ...), custom_call_target="tpu_custom_call" | custom-call | tf_op jit(solution)/shard_map/pallas_call | solution.py:316
  145.3 1.0 fusion.407
  146.4 2.1 %slice_reduce_fusion = (f32[8,4,48]{2,1,0:T(4,128)S(1)}, f32[8,4,48]{2,1,0:T(4,128)S(1)}) fusion(f32[7,8,4,48,128]{4,3,2,1,0:T(8,128)} %shard_map.133.refs_0_), kind=kLoop, calls=%fused_computation | loop fusion | bytes 24576 | tf_op jit(solution)/shard_map/slice | solution.py:434
  149.1 0.6 collective-permute-start.7
  150.2 1.6 collective-permute-done.6
  151.9 4.6 %collective-permute-done.7 = f32[414,128]{1,0:T(8,128)S(1)} collective-permute-done((f32[414,128]{1,0:T(8,128)S(1)}, f32[414,128]{1,0:T(8,128)S(1)}, u32[]{:S(2)}, u32[]{:S(2)}) %collective-permute-start.7) | collective-permute-done | bytes 212000 | tf_op jit(solution)/shard_map/ppermute | solution.py:54
  157.4 3.0 %collective-permute-start.8 = (f32[1656]{0:T(1024)S(1)}, f32[1656]{0:T(1024)S(1)}, u32[]{:S(2)}, u32[]{:S(2)}) collective-permute-start(f32[1656]{0:T(1024)S(1)} %maximum_select_fusion.2), channel_id=1, source_target_pairs={{0,16},{16,0},{1,17},{17,1},{2,18},{18,2},{3,19},{19,3},{4,20},{20... | collective-permute-start | bytes 19880 | tf_op jit(solution)/shard_map/ppermute | solution.py:358
  160.6 0.7 slice.2004
  161.3 0.7 slice.2003
  162.1 1.5 reshape.563.refs_1_
  163.6 1.5 reshape.564.refs_2_
  167.7 0.8 copy.543
  168.4 6.9 %shard_map.134 = f32[8,4,48,128]{3,2,1,0:T(8,128)} custom-call(f32[7,8,4,48,128]{4,3,2,1,0:T(8,128)} %shard_map.133.refs_0_, f32[8,4,48,1]{3,2,1,0:T(8,128)} %reshape.563.refs_1_, f32[8,4,48,1]{3,2,1,0:T(8,128)} %reshape.564.refs_2_, f32[8,48,128]{2,1,0:T(8,128)} %bitcast.851, f32[8,48,128]{2,1,0:T(8,128)} %bitcast.850), custom_call_target="tpu_custom_call" | custom-call | tf_op jit(solution)/shard_map/pallas_call | solution.py:316
  (429 shorter events, 14.7 us)
Async XLA Ops:
  8.4 26.8 %all-to-all-start = ((f32[8,1,17408]{2,1,0:T(1,128)}), f32[8,1,17408]{2,1,0:T(1,128)S(1)}, u32[]{:S(2)}, u32[]{:S(2)}) async-start(f32[8,1,17408]{2,1,0:T(1,128)} %broadcast_in_dim.31), calls=%async_computation | async-start | bytes 1114112 | tf_op jit(solution)/shard_map/all_to_all | solution.py:65
  36.3 21.9 %copy-start = (f32[5]{0:T(128)S(1)}, f32[5]{0:T(128)}, u32[]{:S(2)}) copy-start(f32[5]{0:T(128)} %constant.133.clone) | copy-start | bytes 64
  36.3 22.2 %copy-start.1 = (f32[5]{0:T(128)S(1)}, f32[5]{0:T(128)}, u32[]{:S(2)}) copy-start(f32[5]{0:T(128)} %constant.134.clone) | copy-start | bytes 64
  45.5 7.5 %collective-permute-start.1 = (f32[414,128]{1,0:T(8,128)S(1)}, f32[414,128]{1,0:T(8,128)S(1)}, u32[]{:S(2)}, u32[]{:S(2)}) collective-permute-start(f32[414,128]{1,0:T(8,128)S(1)} %pad_maximum_fusion.1), channel_id=1, source_target_pairs={{0,15},{1,0},{2,1},{3,2},{4,3},{5,4},{6,5},{7,6},{8,7},{9,8},{10,9... | collective-permute-start | bytes 635912 | tf_op jit(solution)/shard_map/ppermute | solution.py:54
  46.2 6.9 %collective-permute-start = (f32[414,128]{1,0:T(8,128)S(1)}, f32[414,128]{1,0:T(8,128)S(1)}, u32[]{:S(2)}, u32[]{:S(2)}) collective-permute-start(f32[414,128]{1,0:T(8,128)S(1)} %pad_maximum_fusion), channel_id=1, source_target_pairs={{0,1},{1,2},{2,3},{3,4},{4,5},{5,6},{6,7},{7,8},{8,9},{9,10},{10,1... | collective-permute-start | bytes 635912 | tf_op jit(solution)/shard_map/ppermute | solution.py:54
  54.0 4.0 %collective-permute-start.2 = (f32[1656]{0:T(1024)S(1)}, f32[1656]{0:T(1024)S(1)}, u32[]{:S(2)}, u32[]{:S(2)}) collective-permute-start(f32[1656]{0:T(1024)S(1)} %maximum_select_fusion), channel_id=1, source_target_pairs={{0,16},{16,0},{1,17},{17,1},{2,18},{18,2},{3,19},{19,3},{4,20},{20... | collective-permute-start | bytes 19880 | tf_op jit(solution)/shard_map/ppermute | solution.py:358
  62.5 22.2 %all-to-all-start.1 = ((f32[8,1,17408]{2,1,0:T(1,128)}), f32[8,1,17408]{2,1,0:T(1,128)S(1)}, u32[]{:S(2)}, u32[]{:S(2)}) async-start(f32[8,1,17408]{2,1,0:T(1,128)} %broadcast_in_dim.34), calls=%async_computation.1 | async-start | bytes 1114112 | tf_op jit(solution)/shard_map/all_to_all | solution.py:65
  96.6 3.6 %collective-permute-start.3 = (f32[414,128]{1,0:T(8,128)S(1)}, f32[414,128]{1,0:T(8,128)S(1)}, u32[]{:S(2)}, u32[]{:S(2)}) collective-permute-start(f32[414,128]{1,0:T(8,128)S(1)} %pad_maximum_fusion.2), channel_id=1, source_target_pairs={{0,1},{1,2},{2,3},{3,4},{4,5},{5,6},{6,7},{7,8},{8,9},{9,10},{10,1... | collective-permute-start | bytes 635912 | tf_op jit(solution)/shard_map/ppermute | solution.py:54
  97.1 7.6 %collective-permute-start.4 = (f32[414,128]{1,0:T(8,128)S(1)}, f32[414,128]{1,0:T(8,128)S(1)}, u32[]{:S(2)}, u32[]{:S(2)}) collective-permute-start(f32[414,128]{1,0:T(8,128)S(1)} %pad_maximum_fusion.3), channel_id=1, source_target_pairs={{0,15},{1,0},{2,1},{3,2},{4,3},{5,4},{6,5},{7,6},{8,7},{9,8},{10,9... | collective-permute-start | bytes 635912 | tf_op jit(solution)/shard_map/ppermute | solution.py:54
  105.6 4.2 %collective-permute-start.5 = (f32[1656]{0:T(1024)S(1)}, f32[1656]{0:T(1024)S(1)}, u32[]{:S(2)}, u32[]{:S(2)}) collective-permute-start(f32[1656]{0:T(1024)S(1)} %maximum_select_fusion.1), channel_id=1, source_target_pairs={{0,16},{16,0},{1,17},{17,1},{2,18},{18,2},{3,19},{19,3},{4,20},{20... | collective-permute-start | bytes 19880 | tf_op jit(solution)/shard_map/ppermute | solution.py:358
  113.5 21.5 %all-to-all-start.2 = ((f32[8,1,17408]{2,1,0:T(1,128)}), f32[8,1,17408]{2,1,0:T(1,128)S(1)}, u32[]{:S(2)}, u32[]{:S(2)}) async-start(f32[8,1,17408]{2,1,0:T(1,128)} %broadcast_in_dim.35), calls=%async_computation.2 | async-start | bytes 1114112 | tf_op jit(solution)/shard_map/all_to_all | solution.py:65
  148.9 2.9 %collective-permute-start.6 = (f32[414,128]{1,0:T(8,128)S(1)}, f32[414,128]{1,0:T(8,128)S(1)}, u32[]{:S(2)}, u32[]{:S(2)}) collective-permute-start(f32[414,128]{1,0:T(8,128)S(1)} %pad_maximum_fusion.4), channel_id=1, source_target_pairs={{0,1},{1,2},{2,3},{3,4},{4,5},{5,6},{6,7},{7,8},{8,9},{9,10},{10,1... | collective-permute-start | bytes 635912 | tf_op jit(solution)/shard_map/ppermute | solution.py:54
  149.1 7.5 %collective-permute-start.7 = (f32[414,128]{1,0:T(8,128)S(1)}, f32[414,128]{1,0:T(8,128)S(1)}, u32[]{:S(2)}, u32[]{:S(2)}) collective-permute-start(f32[414,128]{1,0:T(8,128)S(1)} %pad_maximum_fusion.5), channel_id=1, source_target_pairs={{0,15},{1,0},{2,1},{3,2},{4,3},{5,4},{6,5},{7,6},{8,7},{9,8},{10,9... | collective-permute-start | bytes 635912 | tf_op jit(solution)/shard_map/ppermute | solution.py:54
  157.4 4.5 %collective-permute-start.8 = (f32[1656]{0:T(1024)S(1)}, f32[1656]{0:T(1024)S(1)}, u32[]{:S(2)}, u32[]{:S(2)}) collective-permute-start(f32[1656]{0:T(1024)S(1)} %maximum_select_fusion.2), channel_id=1, source_target_pairs={{0,16},{16,0},{1,17},{17,1},{2,18},{18,2},{3,19},{19,3},{4,20},{20... | collective-permute-start | bytes 19880 | tf_op jit(solution)/shard_map/ppermute | solution.py:358

commit v8 on v7

--- a/solution.py
+++ b/solution.py
@@ -410,7 +410,7 @@
     rows = lax.axis_size("row")
     flow = [flow_pops[member] for member in range(19)]
     scalars = concentration
-    halos = None
+    leaving = None
     for time_step in range(STEPS):
         flow, motion = flow_collide(flow, flow_solid)
         rising = edge_planes(flow, flow_vectors, 2, 1, 1)
@@ -426,19 +426,33 @@
         from_above = jnp.where(
             row_index == rows - 1, 0.0, above[motion.size + rising.size :]
         ).reshape(sinking.shape)
-        mode = "first" if time_step == 0 else "middle"
-        scalars = scalar_stage(mode, scalars, halos, column, solid_flag, source)
         flow = displace(flow, flow_vectors, 2, 1, from_below, from_above)
-        leaving_y = {1: scalars[3, :, span_y - 1], -1: scalars[4, :, 0]}
-        flow, arrived_y = packed_section(flow, leaving_y, 1, 0, send_spanwise, keep_spanwise, True)
-        leaving_x = {1: scalars[1, :, :, :, span_x - 1 :], -1: scalars[2, :, :, :, :1]}
-        if lax.axis_size("gx") == 2:
-            flow, arrived_x = swapped_section(flow, leaving_x, send_streamwise, inflow_fill)
+        if leaving is None:
+            flow = flow_section(flow, 1, 0, send_spanwise, keep_spanwise)
+            flow = flow_section(flow, 0, 2, send_streamwise, inflow_fill)
+            scalars = scalar_stage("first", scalars, None, column, solid_flag, source)
         else:
-            flow, arrived_x = packed_section(
-                flow, leaving_x, 0, 2, send_streamwise, inflow_fill, False
+            flow, arrived_y = packed_section(
+                flow, leaving[1], 1, 0, send_spanwise, keep_spanwise, True
             )
-        halos = (arrived_x[1], arrived_x[-1], arrived_y[1], arrived_y[-1])
+            if lax.axis_size("gx") == 2:
+                flow, arrived_x = swapped_section(flow, leaving[0], send_streamwise, inflow_fill)
+            else:
+                flow, arrived_x = packed_section(
+                    flow, leaving[0], 0, 2, send_streamwise, inflow_fill, False
+                )
+            halos = (arrived_x[1], arrived_x[-1], arrived_y[1], arrived_y[-1])
+            scalars = scalar_stage("middle", scalars, halos, column, solid_flag, source)
+        leaving = (
+            {1: scalars[1, :, :, :, span_x - 1 :], -1: scalars[2, :, :, :, :1]},
+            {1: scalars[3, :, span_y - 1], -1: scalars[4, :, 0]},
+        )
+    halos = (
+        send_streamwise(leaving[0][1], 1),
+        send_streamwise(leaving[0][-1], -1),
+        send_spanwise(leaving[1][1], 1),
+        send_spanwise(leaving[1][-1], -1),
+    )
     amount = scalar_stage("final", scalars, halos, None, None, None)
     stacked = jnp.stack(flow)
     return (stacked, amount)

time: 177 us -> 183 us (1.034)
  starting transfers between devices: 29.4 us -> 37.1 us
  local copies, waits for them, and re-layouts: 40.6 us -> 38.7 us
    ppermute x0 -> x4, starting transfers between devices: none -> 10.6 us  [passed_along(): return lax.ppermute(block, axis, route)]
    all_to_all x3, waiting for transfers between devices: 42.3 us -> 34.7 us  [copy_for_each(): return lax.all_to_all(copies, axis, split_axis=0, concat_axis=0, tiled=True)]
    ppermute x3 -> x2, starting transfers between devices: 8.63 us -> 1.57 us  [swapped_section(): lax.ppermute(jnp.where(first, packed[1], packed[-1]), 'gx', [(0, 1), (1,...]
    ppermute x0 -> x4, waiting for transfers between devices: none -> 5.76 us  [passed_along(): return lax.ppermute(block, axis, route)]
    ppermute x6 -> x8, starting transfers between devices: 5.5 us -> 9.68 us  [from_behind(): return lax.ppermute(value, axis, pairs)]
    reshape x6 -> x4, local copies, waits for them, and re-layouts: 9.13 us -> 6.14 us  [swapped_section(): incoming[heading][split_at:].reshape(scalar_planes.shape)]
    ppermute x0 -> x2, local copies, waits for them, and re-layouts: none -> 2.47 us  [passed_along(): return lax.ppermute(block, axis, route)]
    slice x6 -> x4, local copies, waits for them, and re-layouts: 4.12 us -> 2.76 us  [packed_section(): arrived_scalar[heading] = arrived[split_at:].reshape(scalar_planes.shape)]
  transfers between devices with their start and end apart: 12 -> 17, of which waited for: 8 -> 12; matrix products, arithmetic and copies ran while one was open for 13% -> 13% of each run, Pallas kernels for 0% -> 10%
where the time goes in v8:
time: 183 us; the launch traced here: 180 us
  waiting for transfers between devices  53 us (29%)
  local copies, waits for them, and re-layouts  38.7 us (21%)
  starting transfers between devices  37.1 us (20%)
  Pallas kernels  33.2 us (18%)
  other arithmetic  13.1 us (7%)
  between operations  2.35 us (1%)
  matrix products  2.09 us (1%)
    all_to_all x3, waiting for transfers between devices, copy_for_each(): return lax.all_to_all(copies, axis, split_axis=0, concat_axis=0, tiled=True)  34.7 us
    pallas_call x4, Pallas kernels, scalar_stage(): pl.pallas_call(scalar_kernel(mode, span_y, depth, span_x), grid=(count,),...  33.2 us
    all_to_all x3, starting transfers between devices, copy_for_each(): return lax.all_to_all(copies, axis, split_axis=0, concat_axis=0, tiled=True)  15.3 us
    ppermute x4, starting transfers between devices, passed_along(): return lax.ppermute(block, axis, route)  10.6 us
    ppermute x8, waiting for transfers between devices, from_behind(): return lax.ppermute(value, axis, pairs)  10 us
    ppermute x8, starting transfers between devices, from_behind(): return lax.ppermute(value, axis, pairs)  9.68 us
    reshape x4, local copies, waits for them, and re-layouts, swapped_section(): incoming[heading][split_at:].reshape(scalar_planes.shape)  6.14 us
    slice x4, local copies, waits for them, and re-layouts, on_device(): scalars[2, :, :, :, :1]  6.1 us
  transfers between devices with their start and end apart: 17, of which 12 were waited for; matrix products, arithmetic and copies ran while one was open for 13% of the time, Pallas kernels for 10%

profile of v8, /device:TPU:7, one launch (start us, length us, event | category | flops | bytes accessed | tf_op | source)
XLA Modules:
  0.0 179.5 jit_solution(11952912041203969278)
XLA Ops:
  0.6 1.0 fusion.25
  1.6 1.6 fusion.378
  3.3 1.1 bitcast_select_fusion.8
  4.4 0.9 fusion.320
  5.3 0.9 fusion.330
  6.3 0.8 bitcast_select_fusion.7
  7.0 0.9 bitcast_select_fusion.5
  8.1 1.1 broadcast_in_dim.31
  9.2 8.2 %all-to-all-start = ((f32[8,1,17408]{2,1,0:T(1,128)}), f32[8,1,17408]{2,1,0:T(1,128)S(1)}, u32[]{:S(2)}, u32[]{:S(2)}) async-start(f32[8,1,17408]{2,1,0:T(1,128)} %broadcast_in_dim.31), calls=%async_computation | async-start | bytes 1114112 | tf_op jit(solution)/shard_map/all_to_all | solution.py:65
  18.0 0.7 fusion.332
  18.7 2.1 %fusion.refs_3_.refs_7_ = f32[8,4,48,128]{3,2,1,0:T(8,128)} fusion(f32[96]{0:T(128)} %param.17, s32[96]{0:T(128)S(1)} %get-tuple-element.304, s32[96]{0:T(128)S(1)} %get-tuple-element.303, s32[96]{0:T(128)S(1)} %get-tuple-element.307, s32[96]{0:T(128)S(1)} %get-tuple-element.302), kind=kOutput, calls=%fused_computation.4 | convolution fusion | flops 227389440 | bytes 788352 | tf_op jit(solution)/shard_map/dot_general | solution.py:405
  20.8 15.2 %all-to-all-done = f32[8,1,17408]{2,1,0:T(1,128)S(1)} async-done(((f32[8,1,17408]{2,1,0:T(1,128)}), f32[8,1,17408]{2,1,0:T(1,128)S(1)}, u32[]{:S(2)}, u32[]{:S(2)}) %all-to-all-start) | async-done | bytes 557088 | tf_op jit(solution)/shard_map/all_to_all | solution.py:65
  36.2 0.6 collective-permute-start.1
  36.8 3.4 %collective-permute-start = (f32[5,6,128]{2,0,1:T(8,128)S(1)}, f32[5,6,128]{2,0,1:T(8,128)S(1)}, u32[]{:S(2)}, u32[]{:S(2)}) collective-permute-start(f32[5,6,128]{2,0,1:T(8,128)S(1)} %stack.166), channel_id=1, source_target_pairs={{0,1},{1,2},{2,3},{3,4},{4,5},{5,6},{6,7},{7,8},{8,9},{9,10},{10,1... | collective-permute-start | bytes 46088 | tf_op jit(solution)/shard_map/ppermute | solution.py:54
  40.7 0.8 copy.411.refs_1_
  42.0 7.8 %shard_map.131.refs_0_ = f32[7,8,4,48,128]{4,3,2,1,0:T(8,128)} custom-call(f32[8,4,48,128]{3,2,1,0:T(8,128)} %refs_0_.1, f32[4,4,48,128]{3,2,1,0:T(8,128)} %copy.411.refs_1_, s32[4,48,128]{2,1,0:T(8,128)} %get-tuple-element.71.refs_2_.refs_6_, f32[8,4,48,128]{3,2,1,0:T(8,128)} %fusion.refs_3_.refs_7_), custom_call_target="tpu_custom_call" | custom-call | tf_op jit(solution)/shard_map/pallas_call | solution.py:316
  50.3 4.8 %collective-permute-start.2 = (f32[5,4,6]{2,1,0:T(4,128)S(1)}, f32[5,4,6]{2,1,0:T(4,128)S(1)}, u32[]{:S(2)}, u32[]{:S(2)}) collective-permute-start(f32[5,4,6]{2,1,0:T(4,128)S(1)} %constant_dynamic-update-slice_fusion.10), channel_id=1, source_target_pairs={{0,16},{1,17},{2,18},{3,19},{4,20},{5,21},{6,22},{7,23},{8,24},{9,... | collective-permute-start | bytes 1448 | tf_op jit(solution)/shard_map/ppermute | solution.py:48
  55.4 1.3 collective-permute-start.3
  56.9 4.4 %collective-permute-done.3 = f32[5,4,6]{2,1,0:T(4,128)S(1)} collective-permute-done((f32[5,4,6]{2,1,0:T(4,128)S(1)}, f32[5,4,6]{2,1,0:T(4,128)S(1)}, u32[]{:S(2)}, u32[]{:S(2)}) %collective-permute-start.3) | collective-permute-done | bytes 512 | tf_op jit(solution)/shard_map/ppermute | solution.py:48
  62.4 1.0 fusion.252
  64.2 1.1 broadcast_in_dim.32
  65.3 3.5 %all-to-all-start.1 = ((f32[8,1,17408]{2,1,0:T(1,128)}), f32[8,1,17408]{2,1,0:T(1,128)S(1)}, u32[]{:S(2)}, u32[]{:S(2)}) async-start(f32[8,1,17408]{2,1,0:T(1,128)} %broadcast_in_dim.32), calls=%async_computation.1 | async-start | bytes 1114112 | tf_op jit(solution)/shard_map/all_to_all | solution.py:65
  68.8 2.1 %slice_reduce_fusion.2 = (f32[8,4,48]{2,1,0:T(4,128)S(1)}, f32[8,4,48]{2,1,0:T(4,128)S(1)}) fusion(f32[7,8,4,48,128]{4,3,2,1,0:T(8,128)} %shard_map.131.refs_0_), kind=kLoop, calls=%fused_computation.2 | loop fusion | bytes 24576 | tf_op jit(solution)/shard_map/slice | solution.py:447
  71.0 1.1 fusion.409
  72.6 13.8 %all-to-all-done.1 = f32[8,1,17408]{2,1,0:T(1,128)S(1)} async-done(((f32[8,1,17408]{2,1,0:T(1,128)}), f32[8,1,17408]{2,1,0:T(1,128)S(1)}, u32[]{:S(2)}, u32[]{:S(2)}) %all-to-all-start.1) | async-done | bytes 557088 | tf_op jit(solution)/shard_map/all_to_all | solution.py:65
  86.6 0.5 collective-permute-start.5
  87.2 3.5 %collective-permute-start.4 = (f32[414,128]{1,0:T(8,128)S(1)}, f32[414,128]{1,0:T(8,128)S(1)}, u32[]{:S(2)}, u32[]{:S(2)}) collective-permute-start(f32[414,128]{1,0:T(8,128)S(1)} %pad_maximum_fusion), channel_id=1, source_target_pairs={{0,1},{1,2},{2,3},{3,4},{4,5},{5,6},{6,7},{7,8},{8,9},{9,10},{10,1... | collective-permute-start | bytes 635912 | tf_op jit(solution)/shard_map/ppermute | solution.py:54
  91.4 2.2 %collective-permute-done.4 = f32[414,128]{1,0:T(8,128)S(1)} collective-permute-done((f32[414,128]{1,0:T(8,128)S(1)}, f32[414,128]{1,0:T(8,128)S(1)}, u32[]{:S(2)}, u32[]{:S(2)}) %collective-permute-start.4) | collective-permute-done | bytes 212000 | tf_op jit(solution)/shard_map/ppermute | solution.py:54
  93.7 0.3 collective-permute-done.5
  95.5 0.8 copy.466.refs_5_
  96.4 0.7 slice.1819
  97.1 0.7 slice.1820
  97.8 1.4 collective-permute-done.6
  100.8 1.5 reshape.497.refs_1_
  102.3 1.6 reshape.498.refs_2_
  105.1 1.1 broadcast_in_dim.35
  106.2 3.5 %all-to-all-start.2 = ((f32[8,1,17408]{2,1,0:T(1,128)}), f32[8,1,17408]{2,1,0:T(1,128)S(1)}, u32[]{:S(2)}, u32[]{:S(2)}) async-start(f32[8,1,17408]{2,1,0:T(1,128)} %broadcast_in_dim.35), calls=%async_computation.2 | async-start | bytes 1114112 | tf_op jit(solution)/shard_map/all_to_all | solution.py:65
  109.8 9.3 %shard_map.132.refs_0_ = f32[7,8,4,48,128]{4,3,2,1,0:T(8,128)} custom-call(f32[7,8,4,48,128]{4,3,2,1,0:T(8,128)} %shard_map.131.refs_0_, f32[8,4,48,1]{3,2,1,0:T(8,128)} %reshape.497.refs_1_, f32[8,4,48,1]{3,2,1,0:T(8,128)} %reshape.498.refs_2_, f32[8,48,128]{2,1,0:T(8,128)} %bitcast.830, f32[8,48,128]{2,1,0:T(8,128)} %bitcast.831, ...), custom_call_target="tpu_custom_call" | custom-call | tf_op jit(solution)/shard_map/pallas_call | solution.py:316
  119.1 2.1 %slice_reduce_fusion = (f32[8,4,48]{2,1,0:T(4,128)S(1)}, f32[8,4,48]{2,1,0:T(4,128)S(1)}) fusion(f32[7,8,4,48,128]{4,3,2,1,0:T(8,128)} %shard_map.132.refs_0_), kind=kLoop, calls=%fused_computation | loop fusion | bytes 24576 | tf_op jit(solution)/shard_map/slice | solution.py:447
  121.7 1.1 fusion.408
  122.7 5.6 %all-to-all-done.2 = f32[8,1,17408]{2,1,0:T(1,128)S(1)} async-done(((f32[8,1,17408]{2,1,0:T(1,128)}), f32[8,1,17408]{2,1,0:T(1,128)S(1)}, u32[]{:S(2)}, u32[]{:S(2)}) %all-to-all-start.2) | async-done | bytes 557088 | tf_op jit(solution)/shard_map/all_to_all | solution.py:65
  128.6 0.4 collective-permute-start.7
  130.2 0.8 copy.520.refs_5_
  131.0 0.7 collective-permute-done.7
  131.9 4.5 %collective-permute-done.8 = f32[414,128]{1,0:T(8,128)S(1)} collective-permute-done((f32[414,128]{1,0:T(8,128)S(1)}, f32[414,128]{1,0:T(8,128)S(1)}, u32[]{:S(2)}, u32[]{:S(2)}) %collective-permute-start.8) | collective-permute-done | bytes 212000 | tf_op jit(solution)/shard_map/ppermute | solution.py:54
  137.3 1.4 collective-permute-start.9
  138.7 0.7 slice.1894
  139.4 0.7 slice.1895
  140.1 1.2 collective-permute-done.9
  141.5 1.5 reshape.499.refs_1_
  143.0 1.6 reshape.500.refs_2_
  144.5 9.2 %shard_map.133.refs_0_ = f32[7,8,4,48,128]{4,3,2,1,0:T(8,128)} custom-call(f32[7,8,4,48,128]{4,3,2,1,0:T(8,128)} %shard_map.132.refs_0_, f32[8,4,48,1]{3,2,1,0:T(8,128)} %reshape.499.refs_1_, f32[8,4,48,1]{3,2,1,0:T(8,128)} %reshape.500.refs_2_, f32[8,48,128]{2,1,0:T(8,128)} %bitcast.832, f32[8,48,128]{2,1,0:T(8,128)} %bitcast.833, ...), custom_call_target="tpu_custom_call" | custom-call | tf_op jit(solution)/shard_map/pallas_call | solution.py:316
  153.7 1.6 fusion.407
  155.4 1.1 slice_bitcast_fusion
  158.9 3.2 %collective-permute-start.10 = (f32[8,4,48,1]{2,0,3,1:T(8,128)S(1)}, f32[8,4,48,1]{2,0,3,1:T(8,128)S(1)}, u32[]{:S(2)}, u32[]{:S(2)}) collective-permute-start(f32[8,4,48,1]{2,0,3,1:T(8,128)S(1)} %bitcast.983), channel_id=1, source_target_pairs={{0,16},{1,17},{2,18},{3,19},{4,20},{5,21},{6,22},{7,23},{8,24},{9,... | collective-permute-start | bytes 18440 | tf_op jit(solution)/shard_map/ppermute | solution.py:48
  162.5 1.3 collective-permute-start.11
  163.8 1.0 collective-permute-start.12
  165.1 0.8 copy.527
  165.9 1.2 copy.525.refs_1_
  167.1 1.3 collective-permute-done.11
  168.5 1.2 copy.526.refs_2_
  169.7 2.3 %collective-permute-done.13.refs_4_ = f32[8,48,128]{2,1,0:T(8,128)S(1)} collective-permute-done((f32[8,48,128]{2,1,0:T(8,128)S(1)}, f32[8,48,128]{2,1,0:T(8,128)S(1)}, u32[]{:S(2)}, u32[]{:S(2)}) %collective-permute-start.13) | collective-permute-done | bytes 196640 | tf_op jit(solution)/shard_map/ppermute | solution.py:54
  172.0 0.7 copy-done.1
  172.7 6.9 %shard_map.134 = f32[8,4,48,128]{3,2,1,0:T(8,128)} custom-call(f32[7,8,4,48,128]{4,3,2,1,0:T(8,128)} %shard_map.133.refs_0_, f32[8,4,48,1]{3,2,1,0:T(8,128)} %copy.525.refs_1_, f32[8,4,48,1]{3,2,1,0:T(8,128)} %copy.526.refs_2_, f32[8,48,128]{2,1,0:T(8,128)} %copy-done, f32[8,48,128]{2,1,0:T(8,128)} %copy-done.1), custom_call_target="tpu_custom_call" | custom-call | tf_op jit(solution)/shard_map/pallas_call | solution.py:316
  (415 shorter events, 16.1 us)
Async XLA Ops:
  9.2 26.8 %all-to-all-start = ((f32[8,1,17408]{2,1,0:T(1,128)}), f32[8,1,17408]{2,1,0:T(1,128)S(1)}, u32[]{:S(2)}, u32[]{:S(2)}) async-start(f32[8,1,17408]{2,1,0:T(1,128)} %broadcast_in_dim.31), calls=%async_computation | async-start | bytes 1114112 | tf_op jit(solution)/shard_map/all_to_all | solution.py:65
  36.2 13.8 %collective-permute-start.1 = (f32[5,6,128]{2,0,1:T(8,128)S(1)}, f32[5,6,128]{2,0,1:T(8,128)S(1)}, u32[]{:S(2)}, u32[]{:S(2)}) collective-permute-start(f32[5,6,128]{2,0,1:T(8,128)S(1)} %stack.167), channel_id=1, source_target_pairs={{0,15},{1,0},{2,1},{3,2},{4,3},{5,4},{6,5},{7,6},{8,7},{9,8},{10,9... | collective-permute-start | bytes 46088 | tf_op jit(solution)/shard_map/ppermute | solution.py:54
  36.8 13.0 %collective-permute-start = (f32[5,6,128]{2,0,1:T(8,128)S(1)}, f32[5,6,128]{2,0,1:T(8,128)S(1)}, u32[]{:S(2)}, u32[]{:S(2)}) collective-permute-start(f32[5,6,128]{2,0,1:T(8,128)S(1)} %stack.166), channel_id=1, source_target_pairs={{0,1},{1,2},{2,3},{3,4},{4,5},{5,6},{6,7},{7,8},{8,9},{9,10},{10,1... | collective-permute-start | bytes 46088 | tf_op jit(solution)/shard_map/ppermute | solution.py:54
  40.4 16.3 %copy-start.3 = (f32[5]{0:T(128)S(1)}, f32[5]{0:T(128)}, u32[]{:S(2)}) copy-start(f32[5]{0:T(128)} %constant.133.clone) | copy-start | bytes 64
  40.4 20.9 %copy-start.2 = (f32[5]{0:T(128)S(1)}, f32[5]{0:T(128)}, u32[]{:S(2)}) copy-start(f32[5]{0:T(128)} %constant.134.clone) | copy-start | bytes 64
  50.3 6.4 %collective-permute-start.2 = (f32[5,4,6]{2,1,0:T(4,128)S(1)}, f32[5,4,6]{2,1,0:T(4,128)S(1)}, u32[]{:S(2)}, u32[]{:S(2)}) collective-permute-start(f32[5,4,6]{2,1,0:T(4,128)S(1)} %constant_dynamic-update-slice_fusion.10), channel_id=1, source_target_pairs={{0,16},{1,17},{2,18},{3,19},{4,20},{5,21},{6,22},{7,23},{8,24},{9,... | collective-permute-start | bytes 1448 | tf_op jit(solution)/shard_map/ppermute | solution.py:48
  55.4 5.9 %collective-permute-start.3 = (f32[5,4,6]{2,1,0:T(4,128)S(1)}, f32[5,4,6]{2,1,0:T(4,128)S(1)}, u32[]{:S(2)}, u32[]{:S(2)}) collective-permute-start(f32[5,4,6]{2,1,0:T(4,128)S(1)} %constant_dynamic-update-slice_fusion.15), channel_id=1, source_target_pairs={{16,0},{17,1},{18,2},{19,3},{20,4},{21,5},{22,6},{23,7},{24,8},{25... | collective-permute-start | bytes 1448 | tf_op jit(solution)/shard_map/ppermute | solution.py:48
  65.3 21.2 %all-to-all-start.1 = ((f32[8,1,17408]{2,1,0:T(1,128)}), f32[8,1,17408]{2,1,0:T(1,128)S(1)}, u32[]{:S(2)}, u32[]{:S(2)}) async-start(f32[8,1,17408]{2,1,0:T(1,128)} %broadcast_in_dim.32), calls=%async_computation.1 | async-start | bytes 1114112 | tf_op jit(solution)/shard_map/all_to_all | solution.py:65
  86.6 7.5 %collective-permute-start.5 = (f32[414,128]{1,0:T(8,128)S(1)}, f32[414,128]{1,0:T(8,128)S(1)}, u32[]{:S(2)}, u32[]{:S(2)}) collective-permute-start(f32[414,128]{1,0:T(8,128)S(1)} %pad_maximum_fusion.1), channel_id=1, source_target_pairs={{0,15},{1,0},{2,1},{3,2},{4,3},{5,4},{6,5},{7,6},{8,7},{9,8},{10,9... | collective-permute-start | bytes 635912 | tf_op jit(solution)/shard_map/ppermute | solution.py:54
  87.2 6.3 %collective-permute-start.4 = (f32[414,128]{1,0:T(8,128)S(1)}, f32[414,128]{1,0:T(8,128)S(1)}, u32[]{:S(2)}, u32[]{:S(2)}) collective-permute-start(f32[414,128]{1,0:T(8,128)S(1)} %pad_maximum_fusion), channel_id=1, source_target_pairs={{0,1},{1,2},{2,3},{3,4},{4,5},{5,6},{6,7},{7,8},{8,9},{9,10},{10,1... | collective-permute-start | bytes 635912 | tf_op jit(solution)/shard_map/ppermute | solution.py:54
  94.9 4.2 %collective-permute-start.6 = (f32[1656]{0:T(1024)S(1)}, f32[1656]{0:T(1024)S(1)}, u32[]{:S(2)}, u32[]{:S(2)}) collective-permute-start(f32[1656]{0:T(1024)S(1)} %maximum_select_fusion), channel_id=1, source_target_pairs={{0,16},{16,0},{1,17},{17,1},{2,18},{18,2},{3,19},{19,3},{4,20},{20... | collective-permute-start | bytes 19880 | tf_op jit(solution)/shard_map/ppermute | solution.py:358
  106.2 22.2 %all-to-all-start.2 = ((f32[8,1,17408]{2,1,0:T(1,128)}), f32[8,1,17408]{2,1,0:T(1,128)S(1)}, u32[]{:S(2)}, u32[]{:S(2)}) async-start(f32[8,1,17408]{2,1,0:T(1,128)} %broadcast_in_dim.35), calls=%async_computation.2 | async-start | bytes 1114112 | tf_op jit(solution)/shard_map/all_to_all | solution.py:65
  128.6 3.1 %collective-permute-start.7 = (f32[414,128]{1,0:T(8,128)S(1)}, f32[414,128]{1,0:T(8,128)S(1)}, u32[]{:S(2)}, u32[]{:S(2)}) collective-permute-start(f32[414,128]{1,0:T(8,128)S(1)} %pad_maximum_fusion.2), channel_id=1, source_target_pairs={{0,1},{1,2},{2,3},{3,4},{4,5},{5,6},{6,7},{7,8},{8,9},{9,10},{10,1... | collective-permute-start | bytes 635912 | tf_op jit(solution)/shard_map/ppermute | solution.py:54
  129.0 7.5 %collective-permute-start.8 = (f32[414,128]{1,0:T(8,128)S(1)}, f32[414,128]{1,0:T(8,128)S(1)}, u32[]{:S(2)}, u32[]{:S(2)}) collective-permute-start(f32[414,128]{1,0:T(8,128)S(1)} %pad_maximum_fusion.3), channel_id=1, source_target_pairs={{0,15},{1,0},{2,1},{3,2},{4,3},{5,4},{6,5},{7,6},{8,7},{9,8},{10,9... | collective-permute-start | bytes 635912 | tf_op jit(solution)/shard_map/ppermute | solution.py:54
  137.3 4.0 %collective-permute-start.9 = (f32[1656]{0:T(1024)S(1)}, f32[1656]{0:T(1024)S(1)}, u32[]{:S(2)}, u32[]{:S(2)}) collective-permute-start(f32[1656]{0:T(1024)S(1)} %maximum_select_fusion.1), channel_id=1, source_target_pairs={{0,16},{16,0},{1,17},{17,1},{2,18},{18,2},{3,19},{19,3},{4,20},{20... | collective-permute-start | bytes 19880 | tf_op jit(solution)/shard_map/ppermute | solution.py:358
  158.9 6.9 %collective-permute-start.10 = (f32[8,4,48,1]{2,0,3,1:T(8,128)S(1)}, f32[8,4,48,1]{2,0,3,1:T(8,128)S(1)}, u32[]{:S(2)}, u32[]{:S(2)}) collective-permute-start(f32[8,4,48,1]{2,0,3,1:T(8,128)S(1)} %bitcast.983), channel_id=1, source_target_pairs={{0,16},{1,17},{2,18},{3,19},{4,20},{5,21},{6,22},{7,23},{8,24},{9,... | collective-permute-start | bytes 18440 | tf_op jit(solution)/shard_map/ppermute | solution.py:48
  162.5 6.0 %collective-permute-start.11 = (f32[8,4,48,1]{2,0,3,1:T(8,128)S(1)}, f32[8,4,48,1]{2,0,3,1:T(8,128)S(1)}, u32[]{:S(2)}, u32[]{:S(2)}) collective-permute-start(f32[8,4,48,1]{2,0,3,1:T(8,128)S(1)} %bitcast.984), channel_id=1, source_target_pairs={{16,0},{17,1},{18,2},{19,3},{20,4},{21,5},{22,6},{23,7},{24,8},{25... | collective-permute-start | bytes 18440 | tf_op jit(solution)/shard_map/ppermute | solution.py:48
  163.8 5.9 %collective-permute-start.12 = (f32[8,48,128]{2,1,0:T(8,128)S(1)}, f32[8,48,128]{2,1,0:T(8,128)S(1)}, u32[]{:S(2)}, u32[]{:S(2)}) collective-permute-start(f32[8,48,128]{2,1,0:T(8,128)S(1)} %get-tuple-element.120), channel_id=1, source_target_pairs={{0,1},{1,2},{2,3},{3,4},{4,5},{5,6},{6,7},{7,8},{8,9},{9,10},{10,1... | collective-permute-start | bytes 589832 | tf_op jit(solution)/shard_map/ppermute | solution.py:54
  164.8 7.2 %collective-permute-start.13 = (f32[8,48,128]{2,1,0:T(8,128)S(1)}, f32[8,48,128]{2,1,0:T(8,128)S(1)}, u32[]{:S(2)}, u32[]{:S(2)}) collective-permute-start(f32[8,48,128]{2,1,0:T(8,128)S(1)} %get-tuple-element.119), channel_id=1, source_target_pairs={{0,15},{1,0},{2,1},{3,2},{4,3},{5,4},{6,5},{7,6},{8,7},{9,8},{10,9... | collective-permute-start | bytes 589832 | tf_op jit(solution)/shard_map/ppermute | solution.py:54
  169.7 2.3 %copy-start = (f32[8,48,128]{2,1,0:T(8,128)}, f32[8,48,128]{2,1,0:T(8,128)S(1)}, u32[]{:S(2)}) copy-start(f32[8,48,128]{2,1,0:T(8,128)S(1)} %collective-permute-done.12.refs_3_) | copy-start | bytes 589828
  172.0 0.7 copy-start.1

commit v9 on v7

--- a/solution.py
+++ b/solution.py
@@ -239,29 +239,47 @@
 
 
 def scalar_kernel(mode, span_y, depth, span_x):
+    exact = lax.Precision.HIGHEST
+
     def body(*refs):
         if mode == "first":
-            conc_ref, motion_ref, solid_ref, source_ref, out_ref = refs
+            conc_ref, motion_ref, solid_ref, source_ref, out_ref, edge_ref = refs
         elif mode == "middle":
-            (g_ref, lo_x_ref, hi_x_ref, lo_y_ref, hi_y_ref,
-             motion_ref, solid_ref, source_ref, out_ref) = refs
+            (g_ref, side_ref, lo_y_ref, hi_y_ref,
+             motion_ref, solid_ref, source_ref, out_ref, edge_ref) = refs
         else:
-            g_ref, lo_x_ref, hi_x_ref, lo_y_ref, hi_y_ref, out_ref = refs
+            g_ref, side_ref, lo_y_ref, hi_y_ref, out_ref = refs
         lane = lax.broadcasted_iota(jnp.int32, (depth, span_x), 1)
         level = lax.broadcasted_iota(jnp.int32, (depth, span_x), 0)
+        diagonal = lax.broadcasted_iota(jnp.int32, (depth, depth), 0) == lax.broadcasted_iota(
+            jnp.int32, (depth, depth), 1
+        )
+        at_low = (lane == 0).astype(jnp.float32)
+        at_high = (lane == span_x - 1).astype(jnp.float32)
+        pick_lane = lax.broadcasted_iota(jnp.int32, (8, span_x), 1)
+        pick_high = (pick_lane == span_x - 1).astype(jnp.float32)
+        pick_low = (pick_lane == 0).astype(jnp.float32)
+        edge_row = lax.broadcasted_iota(jnp.int32, (2, depth), 0)
+        by_lanes = (((1,), (1,)), ((), ()))
         for y in range(span_y):
             if mode == "first":
                 block = conc_ref[0, y]
                 scalar = [scalar_weights[member] * block for member in range(7)]
             else:
+                side = side_ref[0, y]
+                spread_low = jnp.where(diagonal, side[0:1, :], 0.0)
+                spread_high = jnp.where(diagonal, side[1:2, :], 0.0)
+                column = jnp.dot(spread_low, at_low, precision=exact) + jnp.dot(
+                    spread_high, at_high, precision=exact
+                )
                 moved_x = pltpu.roll(g_ref[1, 0, y], 1, 1)
                 back_x = pltpu.roll(g_ref[2, 0, y], span_x - 1, 1)
                 moved_z = pltpu.roll(g_ref[5, 0, y], 1, 0)
                 back_z = pltpu.roll(g_ref[6, 0, y], depth - 1, 0)
                 scalar = [
                     g_ref[0, 0, y],
-                    jnp.where(lane == 0, lo_x_ref[0, y], moved_x),
-                    jnp.where(lane == span_x - 1, hi_x_ref[0, y], back_x),
+                    jnp.where(lane == 0, column, moved_x),
+                    jnp.where(lane == span_x - 1, column, back_x),
                     g_ref[3, 0, y - 1] if y > 0 else lo_y_ref[0],
                     g_ref[4, 0, y + 1] if y < span_y - 1 else hi_y_ref[0],
                     jnp.where(level == 0, 0.0, moved_z),
@@ -277,6 +295,7 @@
             relaxation = tau_scalar_base + 4.0 * motion_ref[3, y] / schmidt_turb
             solid = solid_ref[y] != 0
             source = source_ref[0, y]
+            post = []
             for member in range(7):
                 vector = flow_vectors[member]
                 project = vector[0] * speeds[0] + vector[1] * speeds[1] + vector[2] * speeds[2]
@@ -286,7 +305,11 @@
                     - (scalar[member] - equilibrium) / relaxation
                     + scalar_weights[member] * source
                 )
-                out_ref[member, 0, y] = jnp.where(solid, scalar[flow_mirror[member]], relaxed)
+                post.append(jnp.where(solid, scalar[flow_mirror[member]], relaxed))
+                out_ref[member, 0, y] = post[member]
+            leaving_high = lax.dot_general(pick_high, post[1], by_lanes, precision=exact)
+            leaving_low = lax.dot_general(pick_low, post[2], by_lanes, precision=exact)
+            edge_ref[0, y] = jnp.where(edge_row == 0, leaving_high[0:2], leaving_low[0:2])
 
     return body
 
@@ -297,7 +320,7 @@
     one = lambda shape: pl.BlockSpec(shape, lambda s: (s,) + (0,) * (len(shape) - 1))
     stacked = pl.BlockSpec((7, 1, span_y, depth, span_x), lambda s: (0, s, 0, 0, 0))
     cells = (span_y, depth, span_x)
-    edge_specs = [one((1, span_y, depth, 1))] * 2 + [one((1, depth, span_x))] * 2
+    edge_specs = [one((1, span_y, 2, depth))] + [one((1, depth, span_x))] * 2
     if mode == "first":
         operands = [scalars, motion, solid, source]
         specs = [one((1,) + cells), whole((4,) + cells), whole(cells), one((1,) + cells)]
@@ -311,8 +334,11 @@
         out_spec = one((1,) + cells)
         out_shape = jax.ShapeDtypeStruct((count,) + cells, jnp.float32)
     else:
-        out_spec = stacked
-        out_shape = jax.ShapeDtypeStruct((7, count) + cells, jnp.float32)
+        out_spec = [stacked, one((1, span_y, 2, depth))]
+        out_shape = [
+            jax.ShapeDtypeStruct((7, count) + cells, jnp.float32),
+            jax.ShapeDtypeStruct((count, span_y, 2, depth), jnp.float32),
+        ]
     return pl.pallas_call(
         scalar_kernel(mode, span_y, depth, span_x),
         grid=(count,),
@@ -427,18 +453,18 @@
             row_index == rows - 1, 0.0, above[motion.size + rising.size :]
         ).reshape(sinking.shape)
         mode = "first" if time_step == 0 else "middle"
-        scalars = scalar_stage(mode, scalars, halos, column, solid_flag, source)
+        scalars, sides = scalar_stage(mode, scalars, halos, column, solid_flag, source)
         flow = displace(flow, flow_vectors, 2, 1, from_below, from_above)
         leaving_y = {1: scalars[3, :, span_y - 1], -1: scalars[4, :, 0]}
         flow, arrived_y = packed_section(flow, leaving_y, 1, 0, send_spanwise, keep_spanwise, True)
-        leaving_x = {1: scalars[1, :, :, :, span_x - 1 :], -1: scalars[2, :, :, :, :1]}
+        leaving_x = {1: sides[:, :, 0], -1: sides[:, :, 1]}
         if lax.axis_size("gx") == 2:
             flow, arrived_x = swapped_section(flow, leaving_x, send_streamwise, inflow_fill)
         else:
             flow, arrived_x = packed_section(
                 flow, leaving_x, 0, 2, send_streamwise, inflow_fill, False
             )
-        halos = (arrived_x[1], arrived_x[-1], arrived_y[1], arrived_y[-1])
+        halos = (jnp.stack([arrived_x[1], arrived_x[-1]], 2), arrived_y[1], arrived_y[-1])
     amount = scalar_stage("final", scalars, halos, None, None, None)
     stacked = jnp.stack(flow)
     return (stacked, amount)

time: 177 us -> 184 us (1.040)
  local copies, waits for them, and re-layouts: 40.6 us -> 28.6 us
  Pallas kernels: 33.4 us -> 43.8 us
  waiting for transfers between devices: 54.3 us -> 60.4 us
  other arithmetic: 13.2 us -> 15.2 us
    pallas_call x4, Pallas kernels: 33.4 us -> 43.8 us  [scalar_stage(): pl.pallas_call(scalar_kernel(mode, span_y, depth, span_x), grid=(count,),...]
    reshape x6 -> x0, local copies, waits for them, and re-layouts: 9.13 us -> none  [swapped_section(): incoming[heading][split_at:].reshape(scalar_planes.shape)]
    all_to_all x3, waiting for transfers between devices: 42.3 us -> 47 us  [copy_for_each(): return lax.all_to_all(copies, axis, split_axis=0, concat_axis=0, tiled=True)]
    slice x3, local copies, waits for them, and re-layouts: 6.24 us -> 2.82 us  [on_device(): leaving_x = {1: sides[:, :, 0], -1: sides[:, :, 1]}]
    another operation x0 -> x3, other arithmetic: none -> 1.98 us  [on_device(): jnp.stack([arrived_x[1], arrived_x[-1]], 2)]
  transfers between devices with their start and end apart: 12 -> 12, of which waited for: 8 -> 9; matrix products, arithmetic and copies ran while one was open for 13% -> 9% of each run, Pallas kernels for 0% -> 0%
where the time goes in v9:
time: 184 us; the launch traced here: 182 us
  waiting for transfers between devices  60.4 us (33%)
  Pallas kernels  43.8 us (24%)
  starting transfers between devices  29.4 us (16%)
  local copies, waits for them, and re-layouts  28.6 us (16%)
  other arithmetic  15.2 us (8%)
  between operations  2.43 us (1%)
  matrix products  2.09 us (1%)
    all_to_all x3, waiting for transfers between devices, copy_for_each(): return lax.all_to_all(copies, axis, split_axis=0, concat_axis=0, tiled=True)  47 us
    pallas_call x4, Pallas kernels, scalar_stage(): pl.pallas_call(scalar_kernel(mode, span_y, depth, span_x), grid=(count,),...  43.8 us
    all_to_all x3, starting transfers between devices, copy_for_each(): return lax.all_to_all(copies, axis, split_axis=0, concat_axis=0, tiled=True)  15.3 us
    ppermute x6, waiting for transfers between devices, from_behind(): return lax.ppermute(value, axis, pairs)  12.4 us
    ppermute x3, starting transfers between devices, swapped_section(): lax.ppermute(jnp.where(first, packed[1], packed[-1]), 'gx', [(0, 1), (1,...  8.64 us
    ppermute x6, starting transfers between devices, from_behind(): return lax.ppermute(value, axis, pairs)  5.5 us
    select_n x16, other arithmetic, flow_collide(): updated.append(jnp.where(solid, populations[flow_mirror[member]], relaxed))  5.18 us
    slice x6, local copies, waits for them, and re-layouts, packed_section(): arrived_scalar[heading] = arrived[split_at:].reshape(scalar_planes.shape)  4.18 us
  transfers between devices with their start and end apart: 12, of which 9 were waited for; matrix products, arithmetic and copies ran while one was open for 9% of the time, Pallas kernels for 0%

profile of v9, /device:TPU:7, one launch (start us, length us, event | category | flops | bytes accessed | tf_op | source)
XLA Modules:
  0.0 182.0 jit_solution(654110151496063293)
XLA Ops:
  0.6 1.0 fusion.29
  1.6 1.6 fusion.403
  3.3 1.1 fusion.330
  4.4 0.9 bitcast_select_fusion.4
  5.3 0.9 fusion.320
  6.3 0.9 bitcast_select_fusion.7
  7.3 1.1 broadcast_in_dim.31
  8.4 8.2 %all-to-all-start = ((f32[8,1,17408]{2,1,0:T(1,128)}), f32[8,1,17408]{2,1,0:T(1,128)S(1)}, u32[]{:S(2)}, u32[]{:S(2)}) async-start(f32[8,1,17408]{2,1,0:T(1,128)} %broadcast_in_dim.31), calls=%async_computation | async-start | bytes 1114112 | tf_op jit(solution)/shard_map/all_to_all | solution.py:65
  16.6 0.8 bitcast_select_fusion.5
  17.9 0.7 fusion.332
  18.6 2.1 %fusion.refs_3_.refs_6_ = f32[8,4,48,128]{3,2,1,0:T(8,128)} fusion(f32[96]{0:T(128)} %param.17, s32[96]{0:T(128)S(1)} %get-tuple-element.318, s32[96]{0:T(128)S(1)} %get-tuple-element.317, s32[96]{0:T(128)S(1)} %get-tuple-element.321, s32[96]{0:T(128)S(1)} %get-tuple-element.316), kind=kOutput, calls=%fused_computation | convolution fusion | flops 227389440 | bytes 788352 | tf_op jit(solution)/shard_map/dot_general | solution.py:431
  20.7 14.5 %all-to-all-done = f32[8,1,17408]{2,1,0:T(1,128)S(1)} async-done(((f32[8,1,17408]{2,1,0:T(1,128)}), f32[8,1,17408]{2,1,0:T(1,128)S(1)}, u32[]{:S(2)}, u32[]{:S(2)}) %all-to-all-start) | async-done | bytes 557088 | tf_op jit(solution)/shard_map/all_to_all | solution.py:65
  35.4 0.2 copy.374
  35.6 0.8 copy.375.refs_1_
  36.4 8.6 %shard_map.131 = (f32[7,8,4,48,128]{4,3,2,1,0:T(8,128)}, f32[8,4,2,48]{3,2,1,0:T(2,128)}) custom-call(f32[8,4,48,128]{3,2,1,0:T(8,128)} %refs_0_.1, f32[4,4,48,128]{3,2,1,0:T(8,128)} %copy.375.refs_1_, s32[4,48,128]{2,1,0:T(8,128)} %get-tuple-element.125.refs_2_.refs_5_, f32[8,4,48,128]{3,2,1,0:T(8,128)} %fusion.refs_3_.refs_6_), custom_call_target="tpu_custom_call" | custom-call | tf_op jit(solution)/shard_map/pallas_call | solution.py:342
  44.9 1.0 fusion.409
  46.2 0.6 collective-permute-start.1
  46.9 3.4 %collective-permute-start = (f32[414,128]{1,0:T(8,128)S(1)}, f32[414,128]{1,0:T(8,128)S(1)}, u32[]{:S(2)}, u32[]{:S(2)}) collective-permute-start(f32[414,128]{1,0:T(8,128)S(1)} %pad_maximum_fusion), channel_id=1, source_target_pairs={{0,1},{1,2},{2,3},{3,4},{4,5},{5,6},{6,7},{7,8},{8,9},{9,10},{10,1... | collective-permute-start | bytes 635912 | tf_op jit(solution)/shard_map/ppermute | solution.py:54
  50.3 0.1 copy.390
  50.9 0.9 slice_reduce_fusion.5
  52.0 1.6 collective-permute-done.1
  54.7 2.9 %collective-permute-start.2 = (f32[1656]{0:T(1024)S(1)}, f32[1656]{0:T(1024)S(1)}, u32[]{:S(2)}, u32[]{:S(2)}) collective-permute-start(f32[1656]{0:T(1024)S(1)} %maximum_select_fusion), channel_id=1, source_target_pairs={{0,16},{16,0},{1,17},{17,1},{2,18},{18,2},{3,19},{19,3},{4,20},{20... | collective-permute-start | bytes 19880 | tf_op jit(solution)/shard_map/ppermute | solution.py:384
  57.8 0.9 collective-permute-done.2
  60.3 1.0 fusion.252
  61.4 0.3 subtract_select_fusion.19
  62.0 1.1 broadcast_in_dim.34
  63.2 3.5 %all-to-all-start.1 = ((f32[8,1,17408]{2,1,0:T(1,128)}), f32[8,1,17408]{2,1,0:T(1,128)S(1)}, u32[]{:S(2)}, u32[]{:S(2)}) async-start(f32[8,1,17408]{2,1,0:T(1,128)} %broadcast_in_dim.34), calls=%async_computation.1 | async-start | bytes 1114112 | tf_op jit(solution)/shard_map/all_to_all | solution.py:65
  66.7 0.7 slice.1830
  67.4 0.7 slice.1829
  68.9 0.7 pad_maximum_fusion.12.refs_1_
  69.6 15.8 %all-to-all-done.1 = f32[8,1,17408]{2,1,0:T(1,128)S(1)} async-done(((f32[8,1,17408]{2,1,0:T(1,128)}), f32[8,1,17408]{2,1,0:T(1,128)S(1)}, u32[]{:S(2)}, u32[]{:S(2)}) %all-to-all-start.1) | async-done | bytes 557088 | tf_op jit(solution)/shard_map/all_to_all | solution.py:65
  85.9 0.2 copy.426
  86.1 0.8 copy.427.refs_4_
  86.9 14.0 %shard_map.132 = (f32[7,8,4,48,128]{4,3,2,1,0:T(8,128)}, f32[8,4,2,48]{3,2,1,0:T(2,128)}) custom-call(f32[7,8,4,48,128]{4,3,2,1,0:T(8,128)} %get-tuple-element.8.refs_0_, f32[8,4,2,48]{3,2,1,0:T(2,128)} %pad_maximum_fusion.12.refs_1_, f32[8,48,128]{2,1,0:T(8,128)} %bitcast.843, f32[8,48,128]{2,1,0:T(8,128)} %bitcast.842, f32[4,4,48,128]{3,2,1,0:T(8,128)} %copy.427.refs_4_, ...), custom_call_target="tpu_custom_call" | custom-call | tf_op jit(solution)/shard_map/pallas_call | solution.py:342
  100.8 1.1 fusion.408
  101.9 0.4 collective-permute-start.3
  102.4 0.4 collective-permute-start.4
  103.2 0.9 slice_reduce_fusion.3
  104.3 0.8 collective-permute-done.3
  105.2 4.8 %collective-permute-done.4 = f32[414,128]{1,0:T(8,128)S(1)} collective-permute-done((f32[414,128]{1,0:T(8,128)S(1)}, f32[414,128]{1,0:T(8,128)S(1)}, u32[]{:S(2)}, u32[]{:S(2)}) %collective-permute-start.4) | collective-permute-done | bytes 212000 | tf_op jit(solution)/shard_map/ppermute | solution.py:54
  111.0 2.7 %collective-permute-start.5 = (f32[1656]{0:T(1024)S(1)}, f32[1656]{0:T(1024)S(1)}, u32[]{:S(2)}, u32[]{:S(2)}) collective-permute-start(f32[1656]{0:T(1024)S(1)} %maximum_select_fusion.1), channel_id=1, source_target_pairs={{0,16},{16,0},{1,17},{17,1},{2,18},{18,2},{3,19},{19,3},{4,20},{20... | collective-permute-start | bytes 19880 | tf_op jit(solution)/shard_map/ppermute | solution.py:384
  113.8 0.7 slice.1920
  114.5 0.7 slice.1921
  116.8 0.2 fusion.256
  117.2 0.3 divide_subtract_fusion
  118.2 1.1 broadcast_in_dim.35
  119.3 3.5 %all-to-all-start.2 = ((f32[8,1,17408]{2,1,0:T(1,128)}), f32[8,1,17408]{2,1,0:T(1,128)S(1)}, u32[]{:S(2)}, u32[]{:S(2)}) async-start(f32[8,1,17408]{2,1,0:T(1,128)} %broadcast_in_dim.35), calls=%async_computation.2 | async-start | bytes 1114112 | tf_op jit(solution)/shard_map/all_to_all | solution.py:65
  123.3 0.7 pad_maximum_fusion.13.refs_1_
  124.0 16.7 %all-to-all-done.2 = f32[8,1,17408]{2,1,0:T(1,128)S(1)} async-done(((f32[8,1,17408]{2,1,0:T(1,128)}), f32[8,1,17408]{2,1,0:T(1,128)S(1)}, u32[]{:S(2)}, u32[]{:S(2)}) %all-to-all-start.2) | async-done | bytes 557088 | tf_op jit(solution)/shard_map/all_to_all | solution.py:65
  141.3 0.2 copy.479
  141.5 0.8 copy.480.refs_4_
  142.2 14.0 %shard_map.133 = (f32[7,8,4,48,128]{4,3,2,1,0:T(8,128)}, f32[8,4,2,48]{3,2,1,0:T(2,128)}) custom-call(f32[7,8,4,48,128]{4,3,2,1,0:T(8,128)} %get-tuple-element.10.refs_0_, f32[8,4,2,48]{3,2,1,0:T(2,128)} %pad_maximum_fusion.13.refs_1_, f32[8,48,128]{2,1,0:T(8,128)} %bitcast.840, f32[8,48,128]{2,1,0:T(8,128)} %bitcast.841, f32[4,4,48,128]{3,2,1,0:T(8,128)} %copy.480.refs_4_, ...), custom_call_target="tpu_custom_call" | custom-call | tf_op jit(solution)/shard_map/pallas_call | solution.py:342
  156.2 1.1 fusion.407
  157.4 0.6 collective-permute-start.7
  158.4 0.9 slice_reduce_fusion.1
  159.5 0.6 collective-permute-done.6
  160.3 4.6 %collective-permute-done.7 = f32[414,128]{1,0:T(8,128)S(1)} collective-permute-done((f32[414,128]{1,0:T(8,128)S(1)}, f32[414,128]{1,0:T(8,128)S(1)}, u32[]{:S(2)}, u32[]{:S(2)}) %collective-permute-start.7) | collective-permute-done | bytes 212000 | tf_op jit(solution)/shard_map/ppermute | solution.py:54
  165.8 3.0 %collective-permute-start.8 = (f32[1656]{0:T(1024)S(1)}, f32[1656]{0:T(1024)S(1)}, u32[]{:S(2)}, u32[]{:S(2)}) collective-permute-start(f32[1656]{0:T(1024)S(1)} %maximum_select_fusion.2), channel_id=1, source_target_pairs={{0,16},{16,0},{1,17},{17,1},{2,18},{18,2},{3,19},{19,3},{4,20},{20... | collective-permute-start | bytes 19880 | tf_op jit(solution)/shard_map/ppermute | solution.py:384
  169.0 0.7 slice.1992
  169.7 0.7 slice.1991
  171.7 0.1 copy.510
  173.2 0.8 copy.531
  174.0 0.7 pad_maximum_fusion.14.refs_1_
  174.6 7.3 %shard_map.134 = f32[8,4,48,128]{3,2,1,0:T(8,128)} custom-call(f32[7,8,4,48,128]{4,3,2,1,0:T(8,128)} %get-tuple-element.12.refs_0_, f32[8,4,2,48]{3,2,1,0:T(2,128)} %pad_maximum_fusion.14.refs_1_, f32[8,48,128]{2,1,0:T(8,128)} %bitcast.845, f32[8,48,128]{2,1,0:T(8,128)} %bitcast.844), custom_call_target="tpu_custom_call" | custom-call | tf_op jit(solution)/shard_map/pallas_call | solution.py:342
  (432 shorter events, 15.0 us)
Async XLA Ops:
  8.4 26.8 %all-to-all-start = ((f32[8,1,17408]{2,1,0:T(1,128)}), f32[8,1,17408]{2,1,0:T(1,128)S(1)}, u32[]{:S(2)}, u32[]{:S(2)}) async-start(f32[8,1,17408]{2,1,0:T(1,128)} %broadcast_in_dim.31), calls=%async_computation | async-start | bytes 1114112 | tf_op jit(solution)/shard_map/all_to_all | solution.py:65
  16.6 42.2 %copy-start = (f32[5]{0:T(128)S(1)}, f32[5]{0:T(128)}, u32[]{:S(2)}) copy-start(f32[5]{0:T(128)} %constant.133.clone) | copy-start | bytes 64
  16.6 42.5 %copy-start.1 = (f32[5]{0:T(128)S(1)}, f32[5]{0:T(128)}, u32[]{:S(2)}) copy-start(f32[5]{0:T(128)} %constant.134.clone) | copy-start | bytes 64
  46.2 7.5 %collective-permute-start.1 = (f32[414,128]{1,0:T(8,128)S(1)}, f32[414,128]{1,0:T(8,128)S(1)}, u32[]{:S(2)}, u32[]{:S(2)}) collective-permute-start(f32[414,128]{1,0:T(8,128)S(1)} %pad_maximum_fusion.1), channel_id=1, source_target_pairs={{0,15},{1,0},{2,1},{3,2},{4,3},{5,4},{6,5},{7,6},{8,7},{9,8},{10,9... | collective-permute-start | bytes 635912 | tf_op jit(solution)/shard_map/ppermute | solution.py:54
  46.9 6.9 %collective-permute-start = (f32[414,128]{1,0:T(8,128)S(1)}, f32[414,128]{1,0:T(8,128)S(1)}, u32[]{:S(2)}, u32[]{:S(2)}) collective-permute-start(f32[414,128]{1,0:T(8,128)S(1)} %pad_maximum_fusion), channel_id=1, source_target_pairs={{0,1},{1,2},{2,3},{3,4},{4,5},{5,6},{6,7},{7,8},{8,9},{9,10},{10,1... | collective-permute-start | bytes 635912 | tf_op jit(solution)/shard_map/ppermute | solution.py:54
  54.7 4.0 %collective-permute-start.2 = (f32[1656]{0:T(1024)S(1)}, f32[1656]{0:T(1024)S(1)}, u32[]{:S(2)}, u32[]{:S(2)}) collective-permute-start(f32[1656]{0:T(1024)S(1)} %maximum_select_fusion), channel_id=1, source_target_pairs={{0,16},{16,0},{1,17},{17,1},{2,18},{18,2},{3,19},{19,3},{4,20},{20... | collective-permute-start | bytes 19880 | tf_op jit(solution)/shard_map/ppermute | solution.py:384
  63.2 22.2 %all-to-all-start.1 = ((f32[8,1,17408]{2,1,0:T(1,128)}), f32[8,1,17408]{2,1,0:T(1,128)S(1)}, u32[]{:S(2)}, u32[]{:S(2)}) async-start(f32[8,1,17408]{2,1,0:T(1,128)} %broadcast_in_dim.34), calls=%async_computation.1 | async-start | bytes 1114112 | tf_op jit(solution)/shard_map/all_to_all | solution.py:65
  101.9 3.2 %collective-permute-start.3 = (f32[414,128]{1,0:T(8,128)S(1)}, f32[414,128]{1,0:T(8,128)S(1)}, u32[]{:S(2)}, u32[]{:S(2)}) collective-permute-start(f32[414,128]{1,0:T(8,128)S(1)} %pad_maximum_fusion.2), channel_id=1, source_target_pairs={{0,1},{1,2},{2,3},{3,4},{4,5},{5,6},{6,7},{7,8},{8,9},{9,10},{10,1... | collective-permute-start | bytes 635912 | tf_op jit(solution)/shard_map/ppermute | solution.py:54
  102.4 7.6 %collective-permute-start.4 = (f32[414,128]{1,0:T(8,128)S(1)}, f32[414,128]{1,0:T(8,128)S(1)}, u32[]{:S(2)}, u32[]{:S(2)}) collective-permute-start(f32[414,128]{1,0:T(8,128)S(1)} %pad_maximum_fusion.3), channel_id=1, source_target_pairs={{0,15},{1,0},{2,1},{3,2},{4,3},{5,4},{6,5},{7,6},{8,7},{9,8},{10,9... | collective-permute-start | bytes 635912 | tf_op jit(solution)/shard_map/ppermute | solution.py:54
  111.0 4.2 %collective-permute-start.5 = (f32[1656]{0:T(1024)S(1)}, f32[1656]{0:T(1024)S(1)}, u32[]{:S(2)}, u32[]{:S(2)}) collective-permute-start(f32[1656]{0:T(1024)S(1)} %maximum_select_fusion.1), channel_id=1, source_target_pairs={{0,16},{16,0},{1,17},{17,1},{2,18},{18,2},{3,19},{19,3},{4,20},{20... | collective-permute-start | bytes 19880 | tf_op jit(solution)/shard_map/ppermute | solution.py:384
  119.3 21.4 %all-to-all-start.2 = ((f32[8,1,17408]{2,1,0:T(1,128)}), f32[8,1,17408]{2,1,0:T(1,128)S(1)}, u32[]{:S(2)}, u32[]{:S(2)}) async-start(f32[8,1,17408]{2,1,0:T(1,128)} %broadcast_in_dim.35), calls=%async_computation.2 | async-start | bytes 1114112 | tf_op jit(solution)/shard_map/all_to_all | solution.py:65
  157.3 2.9 %collective-permute-start.6 = (f32[414,128]{1,0:T(8,128)S(1)}, f32[414,128]{1,0:T(8,128)S(1)}, u32[]{:S(2)}, u32[]{:S(2)}) collective-permute-start(f32[414,128]{1,0:T(8,128)S(1)} %pad_maximum_fusion.4), channel_id=1, source_target_pairs={{0,1},{1,2},{2,3},{3,4},{4,5},{5,6},{6,7},{7,8},{8,9},{9,10},{10,1... | collective-permute-start | bytes 635912 | tf_op jit(solution)/shard_map/ppermute | solution.py:54
  157.4 7.5 %collective-permute-start.7 = (f32[414,128]{1,0:T(8,128)S(1)}, f32[414,128]{1,0:T(8,128)S(1)}, u32[]{:S(2)}, u32[]{:S(2)}) collective-permute-start(f32[414,128]{1,0:T(8,128)S(1)} %pad_maximum_fusion.5), channel_id=1, source_target_pairs={{0,15},{1,0},{2,1},{3,2},{4,3},{5,4},{6,5},{7,6},{8,7},{9,8},{10,9... | collective-permute-start | bytes 635912 | tf_op jit(solution)/shard_map/ppermute | solution.py:54
  165.8 4.5 %collective-permute-start.8 = (f32[1656]{0:T(1024)S(1)}, f32[1656]{0:T(1024)S(1)}, u32[]{:S(2)}, u32[]{:S(2)}) collective-permute-start(f32[1656]{0:T(1024)S(1)} %maximum_select_fusion.2), channel_id=1, source_target_pairs={{0,16},{16,0},{1,17},{17,1},{2,18},{18,2},{3,19},{19,3},{4,20},{20... | collective-permute-start | bytes 19880 | tf_op jit(solution)/shard_map/ppermute | solution.py:384

commit v10 on v9

--- a/solution.py
+++ b/solution.py
@@ -251,11 +251,6 @@
             g_ref, side_ref, lo_y_ref, hi_y_ref, out_ref = refs
         lane = lax.broadcasted_iota(jnp.int32, (depth, span_x), 1)
         level = lax.broadcasted_iota(jnp.int32, (depth, span_x), 0)
-        diagonal = lax.broadcasted_iota(jnp.int32, (depth, depth), 0) == lax.broadcasted_iota(
-            jnp.int32, (depth, depth), 1
-        )
-        at_low = (lane == 0).astype(jnp.float32)
-        at_high = (lane == span_x - 1).astype(jnp.float32)
         pick_lane = lax.broadcasted_iota(jnp.int32, (8, span_x), 1)
         pick_high = (pick_lane == span_x - 1).astype(jnp.float32)
         pick_low = (pick_lane == 0).astype(jnp.float32)
@@ -266,12 +261,8 @@
                 block = conc_ref[0, y]
                 scalar = [scalar_weights[member] * block for member in range(7)]
             else:
-                side = side_ref[0, y]
-                spread_low = jnp.where(diagonal, side[0:1, :], 0.0)
-                spread_high = jnp.where(diagonal, side[1:2, :], 0.0)
-                column = jnp.dot(spread_low, at_low, precision=exact) + jnp.dot(
-                    spread_high, at_high, precision=exact
-                )
+                side = jnp.transpose(side_ref[0, y])[0:depth]
+                column = jnp.where(lane == 0, side[:, 0:1], side[:, 1:2])
                 moved_x = pltpu.roll(g_ref[1, 0, y], 1, 1)
                 back_x = pltpu.roll(g_ref[2, 0, y], span_x - 1, 1)
                 moved_z = pltpu.roll(g_ref[5, 0, y], 1, 0)
@@ -320,7 +311,7 @@
     one = lambda shape: pl.BlockSpec(shape, lambda s: (s,) + (0,) * (len(shape) - 1))
     stacked = pl.BlockSpec((7, 1, span_y, depth, span_x), lambda s: (0, s, 0, 0, 0))
     cells = (span_y, depth, span_x)
-    edge_specs = [one((1, span_y, 2, depth))] + [one((1, depth, span_x))] * 2
+    edge_specs = [one((1, span_y, 8, span_x))] + [one((1, depth, span_x))] * 2
     if mode == "first":
         operands = [scalars, motion, solid, source]
         specs = [one((1,) + cells), whole((4,) + cells), whole(cells), one((1,) + cells)]
@@ -464,7 +455,9 @@
             flow, arrived_x = packed_section(
                 flow, leaving_x, 0, 2, send_streamwise, inflow_fill, False
             )
-        halos = (jnp.stack([arrived_x[1], arrived_x[-1]], 2), arrived_y[1], arrived_y[-1])
+        sides = jnp.stack([arrived_x[1], arrived_x[-1]], 2)
+        sides = jnp.pad(sides, ((0, 0), (0, 0), (0, 6), (0, span_x - depth)))
+        halos = (sides, arrived_y[1], arrived_y[-1])
     amount = scalar_stage("final", scalars, halos, None, None, None)
     stacked = jnp.stack(flow)
     return (stacked, amount)

time: 184 us -> 177 us (0.962)
  Pallas kernels: 43.8 us -> 36.8 us
    pallas_call x4, Pallas kernels: 43.8 us -> 36.8 us  [scalar_stage(): pl.pallas_call(scalar_kernel(mode, span_y, depth, span_x), grid=(count,),...]
where the time goes in v10:
time: 177 us; the launch traced here: 175 us
  waiting for transfers between devices  60.5 us (34%)
  Pallas kernels  36.8 us (21%)
  starting transfers between devices  29.4 us (17%)
  local copies, waits for them, and re-layouts  28.6 us (16%)
  other arithmetic  15.3 us (9%)
  between operations  2.43 us (1%)
  matrix products  2.09 us (1%)
    all_to_all x3, waiting for transfers between devices, copy_for_each(): return lax.all_to_all(copies, axis, split_axis=0, concat_axis=0, tiled=True)  47.1 us
    pallas_call x4, Pallas kernels, scalar_stage(): pl.pallas_call(scalar_kernel(mode, span_y, depth, span_x), grid=(count,),...  36.8 us
    all_to_all x3, starting transfers between devices, copy_for_each(): return lax.all_to_all(copies, axis, split_axis=0, concat_axis=0, tiled=True)  15.3 us
    ppermute x6, waiting for transfers between devices, from_behind(): return lax.ppermute(value, axis, pairs)  12.4 us
    ppermute x3, starting transfers between devices, swapped_section(): lax.ppermute(jnp.where(first, packed[1], packed[-1]), 'gx', [(0, 1), (1,...  8.82 us
    ppermute x6, starting transfers between devices, from_behind(): return lax.ppermute(value, axis, pairs)  5.32 us
    select_n x16, other arithmetic, flow_collide(): updated.append(jnp.where(solid, populations[flow_mirror[member]], relaxed))  5.18 us
    slice x6, local copies, waits for them, and re-layouts, packed_section(): arrived_scalar[heading] = arrived[split_at:].reshape(scalar_planes.shape)  4.18 us
  transfers between devices with their start and end apart: 12, of which 9 were waited for; matrix products, arithmetic and copies ran while one was open for 9% of the time, Pallas kernels for 0%

profile of v10, /device:TPU:7, one launch (start us, length us, event | category | flops | bytes accessed | tf_op | source)
XLA Modules:
  0.0 175.2 jit_solution(13864626780189104767)
XLA Ops:
  0.6 1.0 fusion.30
  1.6 1.6 fusion.404
  3.3 1.1 fusion.331
  4.4 0.9 bitcast_select_fusion.4
  5.3 0.9 fusion.321
  6.2 0.9 bitcast_select_fusion.7
  7.3 1.1 broadcast_in_dim.31
  8.4 8.2 %all-to-all-start = ((f32[8,1,17408]{2,1,0:T(1,128)}), f32[8,1,17408]{2,1,0:T(1,128)S(1)}, u32[]{:S(2)}, u32[]{:S(2)}) async-start(f32[8,1,17408]{2,1,0:T(1,128)} %broadcast_in_dim.31), calls=%async_computation | async-start | bytes 1114112 | tf_op jit(solution)/shard_map/all_to_all | solution.py:65
  16.6 0.8 bitcast_select_fusion.5
  17.9 0.7 fusion.333
  18.6 2.1 %fusion.refs_3_.refs_6_ = f32[8,4,48,128]{3,2,1,0:T(8,128)} fusion(f32[96]{0:T(128)} %param.17, s32[96]{0:T(128)S(1)} %get-tuple-element.318, s32[96]{0:T(128)S(1)} %get-tuple-element.317, s32[96]{0:T(128)S(1)} %get-tuple-element.321, s32[96]{0:T(128)S(1)} %get-tuple-element.316), kind=kOutput, calls=%fused_computation | convolution fusion | flops 227389440 | bytes 788352 | tf_op jit(solution)/shard_map/dot_general | solution.py:422
  20.7 14.5 %all-to-all-done = f32[8,1,17408]{2,1,0:T(1,128)S(1)} async-done(((f32[8,1,17408]{2,1,0:T(1,128)}), f32[8,1,17408]{2,1,0:T(1,128)S(1)}, u32[]{:S(2)}, u32[]{:S(2)}) %all-to-all-start) | async-done | bytes 557088 | tf_op jit(solution)/shard_map/all_to_all | solution.py:65
  35.4 0.2 copy.374
  35.6 0.8 copy.375.refs_1_
  36.4 8.6 %shard_map.131 = (f32[7,8,4,48,128]{4,3,2,1,0:T(8,128)}, f32[8,4,2,48]{3,2,1,0:T(2,128)}) custom-call(f32[8,4,48,128]{3,2,1,0:T(8,128)} %refs_0_.1, f32[4,4,48,128]{3,2,1,0:T(8,128)} %copy.375.refs_1_, s32[4,48,128]{2,1,0:T(8,128)} %get-tuple-element.125.refs_2_.refs_5_, f32[8,4,48,128]{3,2,1,0:T(8,128)} %fusion.refs_3_.refs_6_), custom_call_target="tpu_custom_call" | custom-call | tf_op jit(solution)/shard_map/pallas_call | solution.py:333
  44.9 1.0 fusion.410
  46.2 0.6 collective-permute-start.1
  46.9 3.4 %collective-permute-start = (f32[414,128]{1,0:T(8,128)S(1)}, f32[414,128]{1,0:T(8,128)S(1)}, u32[]{:S(2)}, u32[]{:S(2)}) collective-permute-start(f32[414,128]{1,0:T(8,128)S(1)} %pad_maximum_fusion), channel_id=1, source_target_pairs={{0,1},{1,2},{2,3},{3,4},{4,5},{5,6},{6,7},{7,8},{8,9},{9,10},{10,1... | collective-permute-start | bytes 635912 | tf_op jit(solution)/shard_map/ppermute | solution.py:54
  50.9 0.9 slice_reduce_fusion.5
  52.0 1.6 collective-permute-done.1
  54.2 0.1 copy.382
  54.7 2.9 %collective-permute-start.2 = (f32[1656]{0:T(1024)S(1)}, f32[1656]{0:T(1024)S(1)}, u32[]{:S(2)}, u32[]{:S(2)}) collective-permute-start(f32[1656]{0:T(1024)S(1)} %maximum_select_fusion), channel_id=1, source_target_pairs={{0,16},{16,0},{1,17},{17,1},{2,18},{18,2},{3,19},{19,3},{4,20},{20... | collective-permute-start | bytes 19880 | tf_op jit(solution)/shard_map/ppermute | solution.py:375
  57.8 0.9 collective-permute-done.2
  60.2 1.0 fusion.253
  61.4 0.3 subtract_select_fusion.19
  62.0 1.1 broadcast_in_dim.34
  63.1 3.5 %all-to-all-start.1 = ((f32[8,1,17408]{2,1,0:T(1,128)}), f32[8,1,17408]{2,1,0:T(1,128)S(1)}, u32[]{:S(2)}, u32[]{:S(2)}) async-start(f32[8,1,17408]{2,1,0:T(1,128)} %broadcast_in_dim.34), calls=%async_computation.1 | async-start | bytes 1114112 | tf_op jit(solution)/shard_map/all_to_all | solution.py:65
  66.7 0.7 slice.1830
  67.4 0.7 slice.1829
  68.9 0.7 select_maximum_fusion.2.refs_1_
  69.6 15.7 %all-to-all-done.1 = f32[8,1,17408]{2,1,0:T(1,128)S(1)} async-done(((f32[8,1,17408]{2,1,0:T(1,128)}), f32[8,1,17408]{2,1,0:T(1,128)S(1)}, u32[]{:S(2)}, u32[]{:S(2)}) %all-to-all-start.1) | async-done | bytes 557088 | tf_op jit(solution)/shard_map/all_to_all | solution.py:65
  85.9 0.2 copy.426
  86.1 0.8 copy.427.refs_4_
  86.9 10.6 %shard_map.132 = (f32[7,8,4,48,128]{4,3,2,1,0:T(8,128)}, f32[8,4,2,48]{3,2,1,0:T(2,128)}) custom-call(f32[7,8,4,48,128]{4,3,2,1,0:T(8,128)} %get-tuple-element.8.refs_0_, f32[8,4,8,128]{3,2,1,0:T(8,128)} %select_maximum_fusion.2.refs_1_, f32[8,48,128]{2,1,0:T(8,128)} %bitcast.851, f32[8,48,128]{2,1,0:T(8,128)} %bitcast.850, ...), custom_call_target="tpu_custom_call" | custom-call | tf_op jit(solution)/shard_map/pallas_call | solution.py:333
  97.4 1.1 fusion.409
  98.5 0.4 collective-permute-start.3
  99.0 0.3 collective-permute-start.4
  99.7 0.9 slice_reduce_fusion.3
  100.8 0.9 collective-permute-done.3
  101.8 4.6 %collective-permute-done.4 = f32[414,128]{1,0:T(8,128)S(1)} collective-permute-done((f32[414,128]{1,0:T(8,128)S(1)}, f32[414,128]{1,0:T(8,128)S(1)}, u32[]{:S(2)}, u32[]{:S(2)}) %collective-permute-start.4) | collective-permute-done | bytes 212000 | tf_op jit(solution)/shard_map/ppermute | solution.py:54
  107.4 2.8 %collective-permute-start.5 = (f32[1656]{0:T(1024)S(1)}, f32[1656]{0:T(1024)S(1)}, u32[]{:S(2)}, u32[]{:S(2)}) collective-permute-start(f32[1656]{0:T(1024)S(1)} %maximum_select_fusion.1), channel_id=1, source_target_pairs={{0,16},{16,0},{1,17},{17,1},{2,18},{18,2},{3,19},{19,3},{4,20},{20... | collective-permute-start | bytes 19880 | tf_op jit(solution)/shard_map/ppermute | solution.py:375
  110.4 0.7 slice.1920
  111.1 0.7 slice.1921
  113.4 0.2 fusion.257
  113.8 0.3 divide_subtract_fusion
  114.8 1.1 broadcast_in_dim.35
  115.9 3.5 %all-to-all-start.2 = ((f32[8,1,17408]{2,1,0:T(1,128)}), f32[8,1,17408]{2,1,0:T(1,128)S(1)}, u32[]{:S(2)}, u32[]{:S(2)}) async-start(f32[8,1,17408]{2,1,0:T(1,128)} %broadcast_in_dim.35), calls=%async_computation.2 | async-start | bytes 1114112 | tf_op jit(solution)/shard_map/all_to_all | solution.py:65
  119.9 0.7 select_maximum_fusion.1.refs_1_
  120.7 16.8 %all-to-all-done.2 = f32[8,1,17408]{2,1,0:T(1,128)S(1)} async-done(((f32[8,1,17408]{2,1,0:T(1,128)}), f32[8,1,17408]{2,1,0:T(1,128)S(1)}, u32[]{:S(2)}, u32[]{:S(2)}) %all-to-all-start.2) | async-done | bytes 557088 | tf_op jit(solution)/shard_map/all_to_all | solution.py:65
  138.1 0.2 copy.479
  138.2 0.8 copy.480.refs_4_
  139.0 10.6 %shard_map.133 = (f32[7,8,4,48,128]{4,3,2,1,0:T(8,128)}, f32[8,4,2,48]{3,2,1,0:T(2,128)}) custom-call(f32[7,8,4,48,128]{4,3,2,1,0:T(8,128)} %get-tuple-element.10.refs_0_, f32[8,4,8,128]{3,2,1,0:T(8,128)} %select_maximum_fusion.1.refs_1_, f32[8,48,128]{2,1,0:T(8,128)} %bitcast.846, f32[8,48,128]{2,1,0:T(8,128)} %bitcast.847, ...), custom_call_target="tpu_custom_call" | custom-call | tf_op jit(solution)/shard_map/pallas_call | solution.py:333
  149.6 1.1 fusion.408
  150.8 0.6 collective-permute-start.7
  151.7 0.9 slice_reduce_fusion.1
  152.9 0.6 collective-permute-done.6
  153.6 4.6 %collective-permute-done.7 = f32[414,128]{1,0:T(8,128)S(1)} collective-permute-done((f32[414,128]{1,0:T(8,128)S(1)}, f32[414,128]{1,0:T(8,128)S(1)}, u32[]{:S(2)}, u32[]{:S(2)}) %collective-permute-start.7) | collective-permute-done | bytes 212000 | tf_op jit(solution)/shard_map/ppermute | solution.py:54
  159.2 3.0 %collective-permute-start.8 = (f32[1656]{0:T(1024)S(1)}, f32[1656]{0:T(1024)S(1)}, u32[]{:S(2)}, u32[]{:S(2)}) collective-permute-start(f32[1656]{0:T(1024)S(1)} %maximum_select_fusion.2), channel_id=1, source_target_pairs={{0,16},{16,0},{1,17},{17,1},{2,18},{18,2},{3,19},{19,3},{4,20},{20... | collective-permute-start | bytes 19880 | tf_op jit(solution)/shard_map/ppermute | solution.py:375
  162.3 0.7 slice.1992
  163.0 0.7 slice.1991
  165.0 0.1 copy.510
  166.6 0.8 copy.531
  167.3 0.7 select_maximum_fusion.refs_1_
  168.0 7.1 %shard_map.134 = f32[8,4,48,128]{3,2,1,0:T(8,128)} custom-call(f32[7,8,4,48,128]{4,3,2,1,0:T(8,128)} %get-tuple-element.12.refs_0_, f32[8,4,8,128]{3,2,1,0:T(8,128)} %select_maximum_fusion.refs_1_, f32[8,48,128]{2,1,0:T(8,128)} %bitcast.849, f32[8,48,128]{2,1,0:T(8,128)} %bitcast.848), custom_call_target="tpu_custom_call" | custom-call | tf_op jit(solution)/shard_map/pallas_call | solution.py:333
  (432 shorter events, 15.0 us)
Async XLA Ops:
  8.4 26.8 %all-to-all-start = ((f32[8,1,17408]{2,1,0:T(1,128)}), f32[8,1,17408]{2,1,0:T(1,128)S(1)}, u32[]{:S(2)}, u32[]{:S(2)}) async-start(f32[8,1,17408]{2,1,0:T(1,128)} %broadcast_in_dim.31), calls=%async_computation | async-start | bytes 1114112 | tf_op jit(solution)/shard_map/all_to_all | solution.py:65
  16.6 42.2 %copy-start = (f32[5]{0:T(128)S(1)}, f32[5]{0:T(128)}, u32[]{:S(2)}) copy-start(f32[5]{0:T(128)} %constant.134.clone) | copy-start | bytes 64
  16.6 42.5 %copy-start.1 = (f32[5]{0:T(128)S(1)}, f32[5]{0:T(128)}, u32[]{:S(2)}) copy-start(f32[5]{0:T(128)} %constant.135.clone) | copy-start | bytes 64
  46.2 7.5 %collective-permute-start.1 = (f32[414,128]{1,0:T(8,128)S(1)}, f32[414,128]{1,0:T(8,128)S(1)}, u32[]{:S(2)}, u32[]{:S(2)}) collective-permute-start(f32[414,128]{1,0:T(8,128)S(1)} %pad_maximum_fusion.1), channel_id=1, source_target_pairs={{0,15},{1,0},{2,1},{3,2},{4,3},{5,4},{6,5},{7,6},{8,7},{9,8},{10,9... | collective-permute-start | bytes 635912 | tf_op jit(solution)/shard_map/ppermute | solution.py:54
  46.9 6.9 %collective-permute-start = (f32[414,128]{1,0:T(8,128)S(1)}, f32[414,128]{1,0:T(8,128)S(1)}, u32[]{:S(2)}, u32[]{:S(2)}) collective-permute-start(f32[414,128]{1,0:T(8,128)S(1)} %pad_maximum_fusion), channel_id=1, source_target_pairs={{0,1},{1,2},{2,3},{3,4},{4,5},{5,6},{6,7},{7,8},{8,9},{9,10},{10,1... | collective-permute-start | bytes 635912 | tf_op jit(solution)/shard_map/ppermute | solution.py:54
  54.7 4.0 %collective-permute-start.2 = (f32[1656]{0:T(1024)S(1)}, f32[1656]{0:T(1024)S(1)}, u32[]{:S(2)}, u32[]{:S(2)}) collective-permute-start(f32[1656]{0:T(1024)S(1)} %maximum_select_fusion), channel_id=1, source_target_pairs={{0,16},{16,0},{1,17},{17,1},{2,18},{18,2},{3,19},{19,3},{4,20},{20... | collective-permute-start | bytes 19880 | tf_op jit(solution)/shard_map/ppermute | solution.py:375
  63.1 22.2 %all-to-all-start.1 = ((f32[8,1,17408]{2,1,0:T(1,128)}), f32[8,1,17408]{2,1,0:T(1,128)S(1)}, u32[]{:S(2)}, u32[]{:S(2)}) async-start(f32[8,1,17408]{2,1,0:T(1,128)} %broadcast_in_dim.34), calls=%async_computation.1 | async-start | bytes 1114112 | tf_op jit(solution)/shard_map/all_to_all | solution.py:65
  98.5 3.2 %collective-permute-start.3 = (f32[414,128]{1,0:T(8,128)S(1)}, f32[414,128]{1,0:T(8,128)S(1)}, u32[]{:S(2)}, u32[]{:S(2)}) collective-permute-start(f32[414,128]{1,0:T(8,128)S(1)} %pad_maximum_fusion.2), channel_id=1, source_target_pairs={{0,1},{1,2},{2,3},{3,4},{4,5},{5,6},{6,7},{7,8},{8,9},{9,10},{10,1... | collective-permute-start | bytes 635912 | tf_op jit(solution)/shard_map/ppermute | solution.py:54
  99.0 7.5 %collective-permute-start.4 = (f32[414,128]{1,0:T(8,128)S(1)}, f32[414,128]{1,0:T(8,128)S(1)}, u32[]{:S(2)}, u32[]{:S(2)}) collective-permute-start(f32[414,128]{1,0:T(8,128)S(1)} %pad_maximum_fusion.3), channel_id=1, source_target_pairs={{0,15},{1,0},{2,1},{3,2},{4,3},{5,4},{6,5},{7,6},{8,7},{9,8},{10,9... | collective-permute-start | bytes 635912 | tf_op jit(solution)/shard_map/ppermute | solution.py:54
  107.4 4.4 %collective-permute-start.5 = (f32[1656]{0:T(1024)S(1)}, f32[1656]{0:T(1024)S(1)}, u32[]{:S(2)}, u32[]{:S(2)}) collective-permute-start(f32[1656]{0:T(1024)S(1)} %maximum_select_fusion.1), channel_id=1, source_target_pairs={{0,16},{16,0},{1,17},{17,1},{2,18},{18,2},{3,19},{19,3},{4,20},{20... | collective-permute-start | bytes 19880 | tf_op jit(solution)/shard_map/ppermute | solution.py:375
  115.9 21.6 %all-to-all-start.2 = ((f32[8,1,17408]{2,1,0:T(1,128)}), f32[8,1,17408]{2,1,0:T(1,128)S(1)}, u32[]{:S(2)}, u32[]{:S(2)}) async-start(f32[8,1,17408]{2,1,0:T(1,128)} %broadcast_in_dim.35), calls=%async_computation.2 | async-start | bytes 1114112 | tf_op jit(solution)/shard_map/all_to_all | solution.py:65
  150.6 2.9 %collective-permute-start.6 = (f32[414,128]{1,0:T(8,128)S(1)}, f32[414,128]{1,0:T(8,128)S(1)}, u32[]{:S(2)}, u32[]{:S(2)}) collective-permute-start(f32[414,128]{1,0:T(8,128)S(1)} %pad_maximum_fusion.4), channel_id=1, source_target_pairs={{0,1},{1,2},{2,3},{3,4},{4,5},{5,6},{6,7},{7,8},{8,9},{9,10},{10,1... | collective-permute-start | bytes 635912 | tf_op jit(solution)/shard_map/ppermute | solution.py:54
  150.8 7.5 %collective-permute-start.7 = (f32[414,128]{1,0:T(8,128)S(1)}, f32[414,128]{1,0:T(8,128)S(1)}, u32[]{:S(2)}, u32[]{:S(2)}) collective-permute-start(f32[414,128]{1,0:T(8,128)S(1)} %pad_maximum_fusion.5), channel_id=1, source_target_pairs={{0,15},{1,0},{2,1},{3,2},{4,3},{5,4},{6,5},{7,6},{8,7},{9,8},{10,9... | collective-permute-start | bytes 635912 | tf_op jit(solution)/shard_map/ppermute | solution.py:54
  159.2 4.5 %collective-permute-start.8 = (f32[1656]{0:T(1024)S(1)}, f32[1656]{0:T(1024)S(1)}, u32[]{:S(2)}, u32[]{:S(2)}) collective-permute-start(f32[1656]{0:T(1024)S(1)} %maximum_select_fusion.2), channel_id=1, source_target_pairs={{0,16},{16,0},{1,17},{17,1},{2,18},{18,2},{3,19},{19,3},{4,20},{20... | collective-permute-start | bytes 19880 | tf_op jit(solution)/shard_map/ppermute | solution.py:375

commit v11 on v7

--- a/solution.py
+++ b/solution.py
@@ -415,17 +415,23 @@
         flow, motion = flow_collide(flow, flow_solid)
         rising = edge_planes(flow, flow_vectors, 2, 1, 1)
         sinking = edge_planes(flow, flow_vectors, 2, 1, -1)
-        payload = jnp.concatenate([motion.reshape(-1), rising.reshape(-1), sinking.reshape(-1)], 0)
-        everyone = copy_for_each(payload, "row")
+        target = lax.broadcasted_iota(jnp.int32, (rows, 1), 0)
+        planes = jnp.where(
+            target == row_index + 1,
+            rising.reshape(1, -1),
+            jnp.where(target == row_index - 1, sinking.reshape(1, -1), 0.0),
+        )
+        spread = jnp.broadcast_to(motion.reshape(1, -1), (rows, motion.size))
+        everyone = lax.all_to_all(
+            jnp.concatenate([spread, planes], 1), "row", split_axis=0, concat_axis=0, tiled=True
+        )
         column = in_order(everyone[:, : motion.size].reshape((rows,) + motion.shape), 2)
         below = lax.dynamic_index_in_dim(everyone, jnp.maximum(row_index - 1, 0), 0, False)
         above = lax.dynamic_index_in_dim(everyone, jnp.minimum(row_index + 1, rows - 1), 0, False)
-        from_below = jnp.where(
-            row_index == 0, 0.0, below[motion.size : motion.size + rising.size]
-        ).reshape(rising.shape)
-        from_above = jnp.where(
-            row_index == rows - 1, 0.0, above[motion.size + rising.size :]
-        ).reshape(sinking.shape)
+        from_below = jnp.where(row_index == 0, 0.0, below[motion.size :]).reshape(rising.shape)
+        from_above = jnp.where(row_index == rows - 1, 0.0, above[motion.size :]).reshape(
+            sinking.shape
+        )
         mode = "first" if time_step == 0 else "middle"
         scalars = scalar_stage(mode, scalars, halos, column, solid_flag, source)
         flow = displace(flow, flow_vectors, 2, 1, from_below, from_above)

time: 177 us -> 172 us (0.972)
  waiting for transfers between devices: 54.3 us -> 49.8 us
    all_to_all x3, waiting for transfers between devices: 42.3 us -> 37.7 us  [on_device(): lax.all_to_all(jnp.concatenate([spread, planes], 1), 'row', split_axis=0,...]
    all_to_all x0 -> x3, local copies, waits for them, and re-layouts: none -> 3.36 us  [on_device(): lax.all_to_all(jnp.concatenate([spread, planes], 1), 'row', split_axis=0,...]
    broadcast_in_dim x3 -> x9, local copies, waits for them, and re-layouts: 3.32 us -> 0.08 us  [the longest x3 0.03 us: on_device(): jnp.where(target == row_index - 1, sinking.reshape(1, -1), 0.0)]
  transfers between devices with their start and end apart: 12 -> 12, of which waited for: 8 -> 8; matrix products, arithmetic and copies ran while one was open for 13% -> 12% of each run, Pallas kernels for 0% -> 0%
where the time goes in v11:
time: 172 us; the launch traced here: 170 us
  waiting for transfers between devices  49.8 us (29%)
  local copies, waits for them, and re-layouts  40.4 us (23%)
  Pallas kernels  33.3 us (19%)
  starting transfers between devices  29.9 us (17%)
  other arithmetic  12.9 us (8%)
  between operations  2.47 us (1%)
    all_to_all x3, waiting for transfers between devices, on_device(): lax.all_to_all(jnp.concatenate([spread, planes], 1), 'row', split_axis=0,...  37.7 us
    pallas_call x4, Pallas kernels, scalar_stage(): pl.pallas_call(scalar_kernel(mode, span_y, depth, span_x), grid=(count,),...  33.3 us
    all_to_all x3, starting transfers between devices, on_device(): lax.all_to_all(jnp.concatenate([spread, planes], 1), 'row', split_axis=0,...  15.1 us
    ppermute x6, waiting for transfers between devices, from_behind(): return lax.ppermute(value, axis, pairs)  11.2 us
    reshape x6, local copies, waits for them, and re-layouts, swapped_section(): incoming[heading][split_at:].reshape(scalar_planes.shape)  9.11 us
    ppermute x3, starting transfers between devices, swapped_section(): lax.ppermute(jnp.where(first, packed[1], packed[-1]), 'gx', [(0, 1), (1,...  8.98 us
    slice x3, local copies, waits for them, and re-layouts, on_device(): scalars[2, :, :, :, :1]  6.24 us
    ppermute x6, starting transfers between devices, from_behind(): return lax.ppermute(value, axis, pairs)  5.8 us
  transfers between devices with their start and end apart: 12, of which 8 were waited for; matrix products, arithmetic and copies ran while one was open for 12% of the time, Pallas kernels for 0%

profile of v11, /device:TPU:7, one launch (start us, length us, event | category | flops | bytes accessed | tf_op | source)
XLA Modules:
  0.0 170.1 jit_solution(7247750213732990002)
XLA Ops:
  0.7 1.0 fusion.29
  1.7 1.6 fusion.403
  3.3 1.1 fusion.330
  4.4 0.9 bitcast_select_fusion.4
  5.3 0.9 fusion.320
  6.3 0.9 bitcast_select_fusion.7
  7.5 1.1 all_to_all.24
  8.6 8.2 %all-to-all-start = ((f32[8,1,14848]{2,1,0:T(1,128)}), f32[8,1,14848]{2,1,0:T(1,128)S(1)}, u32[]{:S(2)}, u32[]{:S(2)}) async-start(f32[8,1,14848]{2,1,0:T(1,128)} %all_to_all.24), calls=%async_computation | async-start | bytes 950272 | tf_op jit(solution)/shard_map/all_to_all | solution.py:425
  17.0 0.8 bitcast_select_fusion.5
  18.1 1.4 fusion.refs_3_.refs_7_
  19.5 14.1 %all-to-all-done = f32[8,1,14848]{2,1,0:T(1,128)S(1)} async-done(((f32[8,1,14848]{2,1,0:T(1,128)}), f32[8,1,14848]{2,1,0:T(1,128)S(1)}, u32[]{:S(2)}, u32[]{:S(2)}) %all-to-all-start) | async-done | bytes 475168 | tf_op jit(solution)/shard_map/all_to_all | solution.py:425
  33.7 0.2 copy.380
  33.9 0.8 copy.381.refs_1_
  34.6 7.9 %shard_map.131.refs_0_ = f32[7,8,4,48,128]{4,3,2,1,0:T(8,128)} custom-call(f32[8,4,48,128]{3,2,1,0:T(8,128)} %refs_0_.1, f32[4,4,48,128]{3,2,1,0:T(8,128)} %copy.381.refs_1_, s32[4,48,128]{2,1,0:T(8,128)} %get-tuple-element.113.refs_2_.refs_6_, f32[8,4,48,128]{3,2,1,0:T(8,128)} %fusion.refs_3_.refs_7_), custom_call_target="tpu_custom_call" | custom-call | tf_op jit(solution)/shard_map/pallas_call | solution.py:316
  42.5 1.0 fusion.409
  43.8 0.6 collective-permute-start.1
  44.5 3.4 %collective-permute-start = (f32[414,128]{1,0:T(8,128)S(1)}, f32[414,128]{1,0:T(8,128)S(1)}, u32[]{:S(2)}, u32[]{:S(2)}) collective-permute-start(f32[414,128]{1,0:T(8,128)S(1)} %pad_maximum_fusion.3), channel_id=1, source_target_pairs={{0,1},{1,2},{2,3},{3,4},{4,5},{5,6},{6,7},{7,8},{8,9},{9,10},{10,1... | collective-permute-start | bytes 635912 | tf_op jit(solution)/shard_map/ppermute | solution.py:54
  48.5 2.1 %slice_reduce_fusion.4 = (f32[8,4,48]{2,1,0:T(4,128)S(1)}, f32[8,4,48]{2,1,0:T(4,128)S(1)}) fusion(f32[7,8,4,48,128]{4,3,2,1,0:T(8,128)} %shard_map.131.refs_0_), kind=kLoop, calls=%fused_computation.4 | loop fusion | bytes 24576 | tf_op jit(solution)/shard_map/slice | solution.py:440
  50.8 0.5 collective-permute-done.1
  52.3 2.9 %collective-permute-start.2 = (f32[1656]{0:T(1024)S(1)}, f32[1656]{0:T(1024)S(1)}, u32[]{:S(2)}, u32[]{:S(2)}) collective-permute-start(f32[1656]{0:T(1024)S(1)} %maximum_select_fusion), channel_id=1, source_target_pairs={{0,16},{16,0},{1,17},{17,1},{2,18},{18,2},{3,19},{19,3},{4,20},{20... | collective-permute-start | bytes 19880 | tf_op jit(solution)/shard_map/ppermute | solution.py:358
  55.4 0.9 collective-permute-done.2
  57.8 1.0 fusion.252
  59.0 0.3 subtract_select_fusion.19
  59.8 1.1 all_to_all.27
  60.9 3.5 %all-to-all-start.1 = ((f32[8,1,14848]{2,1,0:T(1,128)}), f32[8,1,14848]{2,1,0:T(1,128)S(1)}, u32[]{:S(2)}, u32[]{:S(2)}) async-start(f32[8,1,14848]{2,1,0:T(1,128)} %all_to_all.27), calls=%async_computation.1 | async-start | bytes 950272 | tf_op jit(solution)/shard_map/all_to_all | solution.py:425
  64.4 0.7 slice.1834
  65.0 0.7 slice.1833
  66.0 1.5 reshape.545.refs_1_
  67.6 1.5 reshape.546.refs_2_
  69.4 11.9 %all-to-all-done.1 = f32[8,1,14848]{2,1,0:T(1,128)S(1)} async-done(((f32[8,1,14848]{2,1,0:T(1,128)}), f32[8,1,14848]{2,1,0:T(1,128)S(1)}, u32[]{:S(2)}, u32[]{:S(2)}) %all-to-all-start.1) | async-done | bytes 475168 | tf_op jit(solution)/shard_map/all_to_all | solution.py:425
  81.8 0.2 copy.432
  81.9 0.8 copy.435.refs_5_
  82.7 9.3 %shard_map.132.refs_0_ = f32[7,8,4,48,128]{4,3,2,1,0:T(8,128)} custom-call(f32[7,8,4,48,128]{4,3,2,1,0:T(8,128)} %shard_map.131.refs_0_, f32[8,4,48,1]{3,2,1,0:T(8,128)} %reshape.545.refs_1_, f32[8,4,48,1]{3,2,1,0:T(8,128)} %reshape.546.refs_2_, f32[8,48,128]{2,1,0:T(8,128)} %bitcast.843, f32[8,48,128]{2,1,0:T(8,128)} %bitcast.842, ...), custom_call_target="tpu_custom_call" | custom-call | tf_op jit(solution)/shard_map/pallas_call | solution.py:316
  92.0 1.0 fusion.408
  93.0 0.9 collective-permute-start.3
  94.0 0.3 collective-permute-start.4
  94.7 2.1 %slice_reduce_fusion.2 = (f32[8,4,48]{2,1,0:T(4,128)S(1)}, f32[8,4,48]{2,1,0:T(4,128)S(1)}) fusion(f32[7,8,4,48,128]{4,3,2,1,0:T(8,128)} %shard_map.132.refs_0_), kind=kLoop, calls=%fused_computation.2 | loop fusion | bytes 24576 | tf_op jit(solution)/shard_map/slice | solution.py:440
  97.1 4.6 %collective-permute-done.4 = f32[414,128]{1,0:T(8,128)S(1)} collective-permute-done((f32[414,128]{1,0:T(8,128)S(1)}, f32[414,128]{1,0:T(8,128)S(1)}, u32[]{:S(2)}, u32[]{:S(2)}) %collective-permute-start.4) | collective-permute-done | bytes 212000 | tf_op jit(solution)/shard_map/ppermute | solution.py:54
  102.6 3.0 %collective-permute-start.5 = (f32[1656]{0:T(1024)S(1)}, f32[1656]{0:T(1024)S(1)}, u32[]{:S(2)}, u32[]{:S(2)}) collective-permute-start(f32[1656]{0:T(1024)S(1)} %maximum_select_fusion.1), channel_id=1, source_target_pairs={{0,16},{16,0},{1,17},{17,1},{2,18},{18,2},{3,19},{19,3},{4,20},{20... | collective-permute-start | bytes 19880 | tf_op jit(solution)/shard_map/ppermute | solution.py:358
  105.8 0.7 slice.1928
  106.4 0.7 slice.1929
  108.8 0.2 fusion.256
  109.1 0.3 divide_subtract_fusion
  110.3 1.1 all_to_all.30
  111.4 3.5 %all-to-all-start.2 = ((f32[8,1,14848]{2,1,0:T(1,128)}), f32[8,1,14848]{2,1,0:T(1,128)S(1)}, u32[]{:S(2)}, u32[]{:S(2)}) async-start(f32[8,1,14848]{2,1,0:T(1,128)} %all_to_all.30), calls=%async_computation.2 | async-start | bytes 950272 | tf_op jit(solution)/shard_map/all_to_all | solution.py:425
  115.0 1.5 reshape.547.refs_1_
  116.5 1.5 reshape.548.refs_2_
  118.3 11.7 %all-to-all-done.2 = f32[8,1,14848]{2,1,0:T(1,128)S(1)} async-done(((f32[8,1,14848]{2,1,0:T(1,128)}), f32[8,1,14848]{2,1,0:T(1,128)S(1)}, u32[]{:S(2)}, u32[]{:S(2)}) %all-to-all-start.2) | async-done | bytes 475168 | tf_op jit(solution)/shard_map/all_to_all | solution.py:425
  130.1 0.2 copy.487
  130.2 0.8 copy.490.refs_5_
  131.0 9.2 %shard_map.133.refs_0_ = f32[7,8,4,48,128]{4,3,2,1,0:T(8,128)} custom-call(f32[7,8,4,48,128]{4,3,2,1,0:T(8,128)} %shard_map.132.refs_0_, f32[8,4,48,1]{3,2,1,0:T(8,128)} %reshape.547.refs_1_, f32[8,4,48,1]{3,2,1,0:T(8,128)} %reshape.548.refs_2_, f32[8,48,128]{2,1,0:T(8,128)} %bitcast.840, f32[8,48,128]{2,1,0:T(8,128)} %bitcast.841, ...), custom_call_target="tpu_custom_call" | custom-call | tf_op jit(solution)/shard_map/pallas_call | solution.py:316
  140.2 1.0 fusion.407
  141.3 2.1 %slice_reduce_fusion = (f32[8,4,48]{2,1,0:T(4,128)S(1)}, f32[8,4,48]{2,1,0:T(4,128)S(1)}) fusion(f32[7,8,4,48,128]{4,3,2,1,0:T(8,128)} %shard_map.133.refs_0_), kind=kLoop, calls=%fused_computation | loop fusion | bytes 24576 | tf_op jit(solution)/shard_map/slice | solution.py:440
  144.0 0.6 collective-permute-start.7
  145.1 1.6 collective-permute-done.6
  146.8 4.6 %collective-permute-done.7 = f32[414,128]{1,0:T(8,128)S(1)} collective-permute-done((f32[414,128]{1,0:T(8,128)S(1)}, f32[414,128]{1,0:T(8,128)S(1)}, u32[]{:S(2)}, u32[]{:S(2)}) %collective-permute-start.7) | collective-permute-done | bytes 212000 | tf_op jit(solution)/shard_map/ppermute | solution.py:54
  152.3 3.0 %collective-permute-start.8 = (f32[1656]{0:T(1024)S(1)}, f32[1656]{0:T(1024)S(1)}, u32[]{:S(2)}, u32[]{:S(2)}) collective-permute-start(f32[1656]{0:T(1024)S(1)} %maximum_select_fusion.2), channel_id=1, source_target_pairs={{0,16},{16,0},{1,17},{17,1},{2,18},{18,2},{3,19},{19,3},{4,20},{20... | collective-permute-start | bytes 19880 | tf_op jit(solution)/shard_map/ppermute | solution.py:358
  155.5 0.7 slice.2004
  156.1 0.7 slice.2003
  157.0 1.5 reshape.549.refs_1_
  158.5 1.5 reshape.550.refs_2_
  160.9 0.1 copy.520
  162.5 0.8 copy.543
  163.3 6.9 %shard_map.134 = f32[8,4,48,128]{3,2,1,0:T(8,128)} custom-call(f32[7,8,4,48,128]{4,3,2,1,0:T(8,128)} %shard_map.133.refs_0_, f32[8,4,48,1]{3,2,1,0:T(8,128)} %reshape.549.refs_1_, f32[8,4,48,1]{3,2,1,0:T(8,128)} %reshape.550.refs_2_, f32[8,48,128]{2,1,0:T(8,128)} %bitcast.851, f32[8,48,128]{2,1,0:T(8,128)} %bitcast.850), custom_call_target="tpu_custom_call" | custom-call | tf_op jit(solution)/shard_map/pallas_call | solution.py:316
  (442 shorter events, 14.8 us)
Async XLA Ops:
  0.6 17.4 %copy-start.2 = (s32[96]{0:T(128)S(1)}, s32[96]{0:T(128)}, u32[]{:S(2)}) copy-start(s32[96]{0:T(128)} %param.15) | copy-start | bytes 1156
  0.6 17.4 %copy-start.3 = (s32[96]{0:T(128)S(1)}, s32[96]{0:T(128)}, u32[]{:S(2)}) copy-start(s32[96]{0:T(128)} %param.16) | copy-start | bytes 1156
  0.7 17.4 %copy-start.4 = (f32[96]{0:T(128)S(1)}, f32[96]{0:T(128)}, u32[]{:S(2)}) copy-start(f32[96]{0:T(128)} %param.17) | copy-start | bytes 1156
  8.6 25.0 %all-to-all-start = ((f32[8,1,14848]{2,1,0:T(1,128)}), f32[8,1,14848]{2,1,0:T(1,128)S(1)}, u32[]{:S(2)}, u32[]{:S(2)}) async-start(f32[8,1,14848]{2,1,0:T(1,128)} %all_to_all.24), calls=%async_computation | async-start | bytes 950272 | tf_op jit(solution)/shard_map/all_to_all | solution.py:425
  34.6 21.8 %copy-start = (f32[5]{0:T(128)S(1)}, f32[5]{0:T(128)}, u32[]{:S(2)}) copy-start(f32[5]{0:T(128)} %constant.133.clone) | copy-start | bytes 64
  34.6 22.1 %copy-start.1 = (f32[5]{0:T(128)S(1)}, f32[5]{0:T(128)}, u32[]{:S(2)}) copy-start(f32[5]{0:T(128)} %constant.134.clone) | copy-start | bytes 64
  43.8 7.5 %collective-permute-start.1 = (f32[414,128]{1,0:T(8,128)S(1)}, f32[414,128]{1,0:T(8,128)S(1)}, u32[]{:S(2)}, u32[]{:S(2)}) collective-permute-start(f32[414,128]{1,0:T(8,128)S(1)} %pad_maximum_fusion.4), channel_id=1, source_target_pairs={{0,15},{1,0},{2,1},{3,2},{4,3},{5,4},{6,5},{7,6},{8,7},{9,8},{10,9... | collective-permute-start | bytes 635912 | tf_op jit(solution)/shard_map/ppermute | solution.py:54
  44.5 6.9 %collective-permute-start = (f32[414,128]{1,0:T(8,128)S(1)}, f32[414,128]{1,0:T(8,128)S(1)}, u32[]{:S(2)}, u32[]{:S(2)}) collective-permute-start(f32[414,128]{1,0:T(8,128)S(1)} %pad_maximum_fusion.3), channel_id=1, source_target_pairs={{0,1},{1,2},{2,3},{3,4},{4,5},{5,6},{6,7},{7,8},{8,9},{9,10},{10,1... | collective-permute-start | bytes 635912 | tf_op jit(solution)/shard_map/ppermute | solution.py:54
  52.3 4.0 %collective-permute-start.2 = (f32[1656]{0:T(1024)S(1)}, f32[1656]{0:T(1024)S(1)}, u32[]{:S(2)}, u32[]{:S(2)}) collective-permute-start(f32[1656]{0:T(1024)S(1)} %maximum_select_fusion), channel_id=1, source_target_pairs={{0,16},{16,0},{1,17},{17,1},{2,18},{18,2},{3,19},{19,3},{4,20},{20... | collective-permute-start | bytes 19880 | tf_op jit(solution)/shard_map/ppermute | solution.py:358
  60.9 20.4 %all-to-all-start.1 = ((f32[8,1,14848]{2,1,0:T(1,128)}), f32[8,1,14848]{2,1,0:T(1,128)S(1)}, u32[]{:S(2)}, u32[]{:S(2)}) async-start(f32[8,1,14848]{2,1,0:T(1,128)} %all_to_all.27), calls=%async_computation.1 | async-start | bytes 950272 | tf_op jit(solution)/shard_map/all_to_all | solution.py:425
  93.0 3.9 %collective-permute-start.3 = (f32[414,128]{1,0:T(8,128)S(1)}, f32[414,128]{1,0:T(8,128)S(1)}, u32[]{:S(2)}, u32[]{:S(2)}) collective-permute-start(f32[414,128]{1,0:T(8,128)S(1)} %pad_maximum_fusion.5), channel_id=1, source_target_pairs={{0,1},{1,2},{2,3},{3,4},{4,5},{5,6},{6,7},{7,8},{8,9},{9,10},{10,1... | collective-permute-start | bytes 635912 | tf_op jit(solution)/shard_map/ppermute | solution.py:54
  94.0 7.6 %collective-permute-start.4 = (f32[414,128]{1,0:T(8,128)S(1)}, f32[414,128]{1,0:T(8,128)S(1)}, u32[]{:S(2)}, u32[]{:S(2)}) collective-permute-start(f32[414,128]{1,0:T(8,128)S(1)} %pad_maximum_fusion.6), channel_id=1, source_target_pairs={{0,15},{1,0},{2,1},{3,2},{4,3},{5,4},{6,5},{7,6},{8,7},{9,8},{10,9... | collective-permute-start | bytes 635912 | tf_op jit(solution)/shard_map/ppermute | solution.py:54
  102.6 4.6 %collective-permute-start.5 = (f32[1656]{0:T(1024)S(1)}, f32[1656]{0:T(1024)S(1)}, u32[]{:S(2)}, u32[]{:S(2)}) collective-permute-start(f32[1656]{0:T(1024)S(1)} %maximum_select_fusion.1), channel_id=1, source_target_pairs={{0,16},{16,0},{1,17},{17,1},{2,18},{18,2},{3,19},{19,3},{4,20},{20... | collective-permute-start | bytes 19880 | tf_op jit(solution)/shard_map/ppermute | solution.py:358
  111.4 18.5 %all-to-all-start.2 = ((f32[8,1,14848]{2,1,0:T(1,128)}), f32[8,1,14848]{2,1,0:T(1,128)S(1)}, u32[]{:S(2)}, u32[]{:S(2)}) async-start(f32[8,1,14848]{2,1,0:T(1,128)} %all_to_all.30), calls=%async_computation.2 | async-start | bytes 950272 | tf_op jit(solution)/shard_map/all_to_all | solution.py:425
  143.8 2.9 %collective-permute-start.6 = (f32[414,128]{1,0:T(8,128)S(1)}, f32[414,128]{1,0:T(8,128)S(1)}, u32[]{:S(2)}, u32[]{:S(2)}) collective-permute-start(f32[414,128]{1,0:T(8,128)S(1)} %pad_maximum_fusion.7), channel_id=1, source_target_pairs={{0,1},{1,2},{2,3},{3,4},{4,5},{5,6},{6,7},{7,8},{8,9},{9,10},{10,1... | collective-permute-start | bytes 635912 | tf_op jit(solution)/shard_map/ppermute | solution.py:54
  144.0 7.5 %collective-permute-start.7 = (f32[414,128]{1,0:T(8,128)S(1)}, f32[414,128]{1,0:T(8,128)S(1)}, u32[]{:S(2)}, u32[]{:S(2)}) collective-permute-start(f32[414,128]{1,0:T(8,128)S(1)} %pad_maximum_fusion.8), channel_id=1, source_target_pairs={{0,15},{1,0},{2,1},{3,2},{4,3},{5,4},{6,5},{7,6},{8,7},{9,8},{10,9... | collective-permute-start | bytes 635912 | tf_op jit(solution)/shard_map/ppermute | solution.py:54
  152.3 4.5 %collective-permute-start.8 = (f32[1656]{0:T(1024)S(1)}, f32[1656]{0:T(1024)S(1)}, u32[]{:S(2)}, u32[]{:S(2)}) collective-permute-start(f32[1656]{0:T(1024)S(1)} %maximum_select_fusion.2), channel_id=1, source_target_pairs={{0,16},{16,0},{1,17},{17,1},{2,18},{18,2},{3,19},{19,3},{4,20},{20... | collective-permute-start | bytes 19880 | tf_op jit(solution)/shard_map/ppermute | solution.py:358

commit v12 on v10

--- a/solution.py
+++ b/solution.py
@@ -432,17 +432,23 @@
         flow, motion = flow_collide(flow, flow_solid)
         rising = edge_planes(flow, flow_vectors, 2, 1, 1)
         sinking = edge_planes(flow, flow_vectors, 2, 1, -1)
-        payload = jnp.concatenate([motion.reshape(-1), rising.reshape(-1), sinking.reshape(-1)], 0)
-        everyone = copy_for_each(payload, "row")
+        target = lax.broadcasted_iota(jnp.int32, (rows, 1), 0)
+        planes = jnp.where(
+            target == row_index + 1,
+            rising.reshape(1, -1),
+            jnp.where(target == row_index - 1, sinking.reshape(1, -1), 0.0),
+        )
+        spread = jnp.broadcast_to(motion.reshape(1, -1), (rows, motion.size))
+        everyone = lax.all_to_all(
+            jnp.concatenate([spread, planes], 1), "row", split_axis=0, concat_axis=0, tiled=True
+        )
         column = in_order(everyone[:, : motion.size].reshape((rows,) + motion.shape), 2)
         below = lax.dynamic_index_in_dim(everyone, jnp.maximum(row_index - 1, 0), 0, False)
         above = lax.dynamic_index_in_dim(everyone, jnp.minimum(row_index + 1, rows - 1), 0, False)
-        from_below = jnp.where(
-            row_index == 0, 0.0, below[motion.size : motion.size + rising.size]
-        ).reshape(rising.shape)
-        from_above = jnp.where(
-            row_index == rows - 1, 0.0, above[motion.size + rising.size :]
-        ).reshape(sinking.shape)
+        from_below = jnp.where(row_index == 0, 0.0, below[motion.size :]).reshape(rising.shape)
+        from_above = jnp.where(row_index == rows - 1, 0.0, above[motion.size :]).reshape(
+            sinking.shape
+        )
         mode = "first" if time_step == 0 else "middle"
         scalars, sides = scalar_stage(mode, scalars, halos, column, solid_flag, source)
         flow = displace(flow, flow_vectors, 2, 1, from_below, from_above)

time: 177 us -> 171 us (0.966)
  waiting for transfers between devices: 60.5 us -> 55.2 us
    all_to_all x3, waiting for transfers between devices: 47.1 us -> 41.6 us  [on_device(): lax.all_to_all(jnp.concatenate([spread, planes], 1), 'row', split_axis=0,...]
    all_to_all x0 -> x3, local copies, waits for them, and re-layouts: none -> 3.34 us  [on_device(): lax.all_to_all(jnp.concatenate([spread, planes], 1), 'row', split_axis=0,...]
    broadcast_in_dim x3 -> x9, local copies, waits for them, and re-layouts: 3.35 us -> 0.08 us  [the longest x3 0.03 us: on_device(): jnp.where(target == row_index - 1, sinking.reshape(1, -1), 0.0)]
where the time goes in v12:
time: 171 us; the launch traced here: 169 us
  waiting for transfers between devices  55.2 us (32%)
  Pallas kernels  36.8 us (22%)
  starting transfers between devices  30.2 us (18%)
  local copies, waits for them, and re-layouts  28.4 us (17%)
  other arithmetic  15 us (9%)
  between operations  2.45 us (1%)
    all_to_all x3, waiting for transfers between devices, on_device(): lax.all_to_all(jnp.concatenate([spread, planes], 1), 'row', split_axis=0,...  41.6 us
    pallas_call x4, Pallas kernels, scalar_stage(): pl.pallas_call(scalar_kernel(mode, span_y, depth, span_x), grid=(count,),...  36.8 us
    all_to_all x3, starting transfers between devices, on_device(): lax.all_to_all(jnp.concatenate([spread, planes], 1), 'row', split_axis=0,...  15.3 us
    ppermute x6, waiting for transfers between devices, from_behind(): return lax.ppermute(value, axis, pairs)  12.6 us
    ppermute x3, starting transfers between devices, swapped_section(): lax.ppermute(jnp.where(first, packed[1], packed[-1]), 'gx', [(0, 1), (1,...  9.29 us
    ppermute x6, starting transfers between devices, from_behind(): return lax.ppermute(value, axis, pairs)  5.62 us
    select_n x16, other arithmetic, flow_collide(): updated.append(jnp.where(solid, populations[flow_mirror[member]], relaxed))  5.17 us
    slice x6, local copies, waits for them, and re-layouts, packed_section(): arrived_scalar[heading] = arrived[split_at:].reshape(scalar_planes.shape)  4.16 us
  transfers between devices with their start and end apart: 12, of which 9 were waited for; matrix products, arithmetic and copies ran while one was open for 9% of the time, Pallas kernels for 0%

profile of v12, /device:TPU:7, one launch (start us, length us, event | category | flops | bytes accessed | tf_op | source)
XLA Modules:
  0.0 169.4 jit_solution(3077144032778540425)
XLA Ops:
  0.7 1.0 fusion.30
  1.7 1.6 fusion.404
  3.3 1.1 fusion.331
  4.4 0.9 bitcast_select_fusion.4
  5.3 0.9 fusion.321
  6.3 0.9 bitcast_select_fusion.7
  7.5 1.1 all_to_all.24
  8.6 8.3 %all-to-all-start = ((f32[8,1,14848]{2,1,0:T(1,128)}), f32[8,1,14848]{2,1,0:T(1,128)S(1)}, u32[]{:S(2)}, u32[]{:S(2)}) async-start(f32[8,1,14848]{2,1,0:T(1,128)} %all_to_all.24), calls=%async_computation | async-start | bytes 950272 | tf_op jit(solution)/shard_map/all_to_all | solution.py:442
  17.2 0.8 bitcast_select_fusion.5
  18.2 1.4 fusion.refs_3_.refs_6_
  19.7 14.1 %all-to-all-done = f32[8,1,14848]{2,1,0:T(1,128)S(1)} async-done(((f32[8,1,14848]{2,1,0:T(1,128)}), f32[8,1,14848]{2,1,0:T(1,128)S(1)}, u32[]{:S(2)}, u32[]{:S(2)}) %all-to-all-start) | async-done | bytes 475168 | tf_op jit(solution)/shard_map/all_to_all | solution.py:442
  33.8 0.2 copy.374
  34.0 0.8 copy.375.refs_1_
  34.8 8.5 %shard_map.131 = (f32[7,8,4,48,128]{4,3,2,1,0:T(8,128)}, f32[8,4,2,48]{3,2,1,0:T(2,128)}) custom-call(f32[8,4,48,128]{3,2,1,0:T(8,128)} %refs_0_.1, f32[4,4,48,128]{3,2,1,0:T(8,128)} %copy.375.refs_1_, s32[4,48,128]{2,1,0:T(8,128)} %get-tuple-element.125.refs_2_.refs_5_, f32[8,4,48,128]{3,2,1,0:T(8,128)} %fusion.refs_3_.refs_6_), custom_call_target="tpu_custom_call" | custom-call | tf_op jit(solution)/shard_map/pallas_call | solution.py:333
  43.3 1.0 fusion.410
  44.6 0.6 collective-permute-start.1
  45.3 3.4 %collective-permute-start = (f32[414,128]{1,0:T(8,128)S(1)}, f32[414,128]{1,0:T(8,128)S(1)}, u32[]{:S(2)}, u32[]{:S(2)}) collective-permute-start(f32[414,128]{1,0:T(8,128)S(1)} %pad_maximum_fusion.3), channel_id=1, source_target_pairs={{0,1},{1,2},{2,3},{3,4},{4,5},{5,6},{6,7},{7,8},{8,9},{9,10},{10,1... | collective-permute-start | bytes 635912 | tf_op jit(solution)/shard_map/ppermute | solution.py:54
  49.3 0.9 slice_reduce_fusion.5
  50.4 1.6 collective-permute-done.1
  53.1 2.9 %collective-permute-start.2 = (f32[1656]{0:T(1024)S(1)}, f32[1656]{0:T(1024)S(1)}, u32[]{:S(2)}, u32[]{:S(2)}) collective-permute-start(f32[1656]{0:T(1024)S(1)} %maximum_select_fusion), channel_id=1, source_target_pairs={{0,16},{16,0},{1,17},{17,1},{2,18},{18,2},{3,19},{19,3},{4,20},{20... | collective-permute-start | bytes 19880 | tf_op jit(solution)/shard_map/ppermute | solution.py:375
  56.2 0.9 collective-permute-done.2
  57.3 0.1 copy.392
  58.6 1.0 fusion.253
  59.8 0.3 subtract_select_fusion.19
  60.6 1.1 all_to_all.27
  61.7 3.5 %all-to-all-start.1 = ((f32[8,1,14848]{2,1,0:T(1,128)}), f32[8,1,14848]{2,1,0:T(1,128)S(1)}, u32[]{:S(2)}, u32[]{:S(2)}) async-start(f32[8,1,14848]{2,1,0:T(1,128)} %all_to_all.27), calls=%async_computation.1 | async-start | bytes 950272 | tf_op jit(solution)/shard_map/all_to_all | solution.py:442
  65.2 0.7 slice.1830
  65.8 0.7 slice.1829
  67.3 0.7 select_maximum_fusion.2.refs_1_
  68.1 14.0 %all-to-all-done.1 = f32[8,1,14848]{2,1,0:T(1,128)S(1)} async-done(((f32[8,1,14848]{2,1,0:T(1,128)}), f32[8,1,14848]{2,1,0:T(1,128)S(1)}, u32[]{:S(2)}, u32[]{:S(2)}) %all-to-all-start.1) | async-done | bytes 475168 | tf_op jit(solution)/shard_map/all_to_all | solution.py:442
  82.6 0.2 copy.426
  82.7 0.8 copy.427.refs_4_
  83.5 10.6 %shard_map.132 = (f32[7,8,4,48,128]{4,3,2,1,0:T(8,128)}, f32[8,4,2,48]{3,2,1,0:T(2,128)}) custom-call(f32[7,8,4,48,128]{4,3,2,1,0:T(8,128)} %get-tuple-element.8.refs_0_, f32[8,4,8,128]{3,2,1,0:T(8,128)} %select_maximum_fusion.2.refs_1_, f32[8,48,128]{2,1,0:T(8,128)} %bitcast.851, f32[8,48,128]{2,1,0:T(8,128)} %bitcast.850, ...), custom_call_target="tpu_custom_call" | custom-call | tf_op jit(solution)/shard_map/pallas_call | solution.py:333
  94.1 1.0 fusion.409
  95.2 0.9 collective-permute-start.3
  96.6 0.9 slice_reduce_fusion.3
  97.7 1.1 collective-permute-done.3
  99.0 4.6 %collective-permute-done.4 = f32[414,128]{1,0:T(8,128)S(1)} collective-permute-done((f32[414,128]{1,0:T(8,128)S(1)}, f32[414,128]{1,0:T(8,128)S(1)}, u32[]{:S(2)}, u32[]{:S(2)}) %collective-permute-start.4) | collective-permute-done | bytes 212000 | tf_op jit(solution)/shard_map/ppermute | solution.py:54
  104.5 3.2 %collective-permute-start.5 = (f32[1656]{0:T(1024)S(1)}, f32[1656]{0:T(1024)S(1)}, u32[]{:S(2)}, u32[]{:S(2)}) collective-permute-start(f32[1656]{0:T(1024)S(1)} %maximum_select_fusion.1), channel_id=1, source_target_pairs={{0,16},{16,0},{1,17},{17,1},{2,18},{18,2},{3,19},{19,3},{4,20},{20... | collective-permute-start | bytes 19880 | tf_op jit(solution)/shard_map/ppermute | solution.py:375
  107.9 0.7 slice.1920
  108.6 0.7 slice.1921
  109.5 0.1 copy.445
  110.2 0.1 copy.444
  110.8 0.2 fusion.257
  111.1 0.3 divide_subtract_fusion
  112.0 1.1 all_to_all.30
  113.1 3.5 %all-to-all-start.2 = ((f32[8,1,14848]{2,1,0:T(1,128)}), f32[8,1,14848]{2,1,0:T(1,128)S(1)}, u32[]{:S(2)}, u32[]{:S(2)}) async-start(f32[8,1,14848]{2,1,0:T(1,128)} %all_to_all.30), calls=%async_computation.2 | async-start | bytes 950272 | tf_op jit(solution)/shard_map/all_to_all | solution.py:442
  117.5 0.7 select_maximum_fusion.1.refs_1_
  118.2 13.5 %all-to-all-done.2 = f32[8,1,14848]{2,1,0:T(1,128)S(1)} async-done(((f32[8,1,14848]{2,1,0:T(1,128)}), f32[8,1,14848]{2,1,0:T(1,128)S(1)}, u32[]{:S(2)}, u32[]{:S(2)}) %all-to-all-start.2) | async-done | bytes 475168 | tf_op jit(solution)/shard_map/all_to_all | solution.py:442
  132.2 0.2 copy.479
  132.4 0.8 copy.480.refs_4_
  133.2 10.6 %shard_map.133 = (f32[7,8,4,48,128]{4,3,2,1,0:T(8,128)}, f32[8,4,2,48]{3,2,1,0:T(2,128)}) custom-call(f32[7,8,4,48,128]{4,3,2,1,0:T(8,128)} %get-tuple-element.10.refs_0_, f32[8,4,8,128]{3,2,1,0:T(8,128)} %select_maximum_fusion.1.refs_1_, f32[8,48,128]{2,1,0:T(8,128)} %bitcast.846, f32[8,48,128]{2,1,0:T(8,128)} %bitcast.847, ...), custom_call_target="tpu_custom_call" | custom-call | tf_op jit(solution)/shard_map/pallas_call | solution.py:333
  143.7 1.1 fusion.408
  145.0 0.6 collective-permute-start.7
  145.9 0.9 slice_reduce_fusion.1
  147.0 0.6 collective-permute-done.6
  147.8 4.6 %collective-permute-done.7 = f32[414,128]{1,0:T(8,128)S(1)} collective-permute-done((f32[414,128]{1,0:T(8,128)S(1)}, f32[414,128]{1,0:T(8,128)S(1)}, u32[]{:S(2)}, u32[]{:S(2)}) %collective-permute-start.7) | collective-permute-done | bytes 212000 | tf_op jit(solution)/shard_map/ppermute | solution.py:54
  153.3 3.1 %collective-permute-start.8 = (f32[1656]{0:T(1024)S(1)}, f32[1656]{0:T(1024)S(1)}, u32[]{:S(2)}, u32[]{:S(2)}) collective-permute-start(f32[1656]{0:T(1024)S(1)} %maximum_select_fusion.2), channel_id=1, source_target_pairs={{0,16},{16,0},{1,17},{17,1},{2,18},{18,2},{3,19},{19,3},{4,20},{20... | collective-permute-start | bytes 19880 | tf_op jit(solution)/shard_map/ppermute | solution.py:375
  156.6 0.7 slice.1992
  157.3 0.7 slice.1991
  159.3 0.1 copy.510
  160.8 0.8 copy.531
  161.6 0.7 select_maximum_fusion.refs_1_
  162.3 7.1 %shard_map.134 = f32[8,4,48,128]{3,2,1,0:T(8,128)} custom-call(f32[7,8,4,48,128]{4,3,2,1,0:T(8,128)} %get-tuple-element.12.refs_0_, f32[8,4,8,128]{3,2,1,0:T(8,128)} %select_maximum_fusion.refs_1_, f32[8,48,128]{2,1,0:T(8,128)} %bitcast.849, f32[8,48,128]{2,1,0:T(8,128)} %bitcast.848), custom_call_target="tpu_custom_call" | custom-call | tf_op jit(solution)/shard_map/pallas_call | solution.py:333
  (445 shorter events, 15.0 us)
Async XLA Ops:
  0.6 17.5 %copy-start.2 = (s32[96]{0:T(128)S(1)}, s32[96]{0:T(128)}, u32[]{:S(2)}) copy-start(s32[96]{0:T(128)} %param.15) | copy-start | bytes 1156
  0.6 17.5 %copy-start.3 = (s32[96]{0:T(128)S(1)}, s32[96]{0:T(128)}, u32[]{:S(2)}) copy-start(s32[96]{0:T(128)} %param.16) | copy-start | bytes 1156
  0.7 17.6 %copy-start.4 = (f32[96]{0:T(128)S(1)}, f32[96]{0:T(128)}, u32[]{:S(2)}) copy-start(f32[96]{0:T(128)} %param.17) | copy-start | bytes 1156
  8.6 48.7 %copy-start = (f32[5]{0:T(128)S(1)}, f32[5]{0:T(128)}, u32[]{:S(2)}) copy-start(f32[5]{0:T(128)} %constant.134.clone) | copy-start | bytes 64
  8.6 49.0 %copy-start.1 = (f32[5]{0:T(128)S(1)}, f32[5]{0:T(128)}, u32[]{:S(2)}) copy-start(f32[5]{0:T(128)} %constant.135.clone) | copy-start | bytes 64
  8.6 25.2 %all-to-all-start = ((f32[8,1,14848]{2,1,0:T(1,128)}), f32[8,1,14848]{2,1,0:T(1,128)S(1)}, u32[]{:S(2)}, u32[]{:S(2)}) async-start(f32[8,1,14848]{2,1,0:T(1,128)} %all_to_all.24), calls=%async_computation | async-start | bytes 950272 | tf_op jit(solution)/shard_map/all_to_all | solution.py:442
  44.6 7.5 %collective-permute-start.1 = (f32[414,128]{1,0:T(8,128)S(1)}, f32[414,128]{1,0:T(8,128)S(1)}, u32[]{:S(2)}, u32[]{:S(2)}) collective-permute-start(f32[414,128]{1,0:T(8,128)S(1)} %pad_maximum_fusion.4), channel_id=1, source_target_pairs={{0,15},{1,0},{2,1},{3,2},{4,3},{5,4},{6,5},{7,6},{8,7},{9,8},{10,9... | collective-permute-start | bytes 635912 | tf_op jit(solution)/shard_map/ppermute | solution.py:54
  45.3 6.9 %collective-permute-start = (f32[414,128]{1,0:T(8,128)S(1)}, f32[414,128]{1,0:T(8,128)S(1)}, u32[]{:S(2)}, u32[]{:S(2)}) collective-permute-start(f32[414,128]{1,0:T(8,128)S(1)} %pad_maximum_fusion.3), channel_id=1, source_target_pairs={{0,1},{1,2},{2,3},{3,4},{4,5},{5,6},{6,7},{7,8},{8,9},{9,10},{10,1... | collective-permute-start | bytes 635912 | tf_op jit(solution)/shard_map/ppermute | solution.py:54
  53.1 4.0 %collective-permute-start.2 = (f32[1656]{0:T(1024)S(1)}, f32[1656]{0:T(1024)S(1)}, u32[]{:S(2)}, u32[]{:S(2)}) collective-permute-start(f32[1656]{0:T(1024)S(1)} %maximum_select_fusion), channel_id=1, source_target_pairs={{0,16},{16,0},{1,17},{17,1},{2,18},{18,2},{3,19},{19,3},{4,20},{20... | collective-permute-start | bytes 19880 | tf_op jit(solution)/shard_map/ppermute | solution.py:375
  61.7 20.4 %all-to-all-start.1 = ((f32[8,1,14848]{2,1,0:T(1,128)}), f32[8,1,14848]{2,1,0:T(1,128)S(1)}, u32[]{:S(2)}, u32[]{:S(2)}) async-start(f32[8,1,14848]{2,1,0:T(1,128)} %all_to_all.27), calls=%async_computation.1 | async-start | bytes 950272 | tf_op jit(solution)/shard_map/all_to_all | solution.py:442
  95.2 3.7 %collective-permute-start.3 = (f32[414,128]{1,0:T(8,128)S(1)}, f32[414,128]{1,0:T(8,128)S(1)}, u32[]{:S(2)}, u32[]{:S(2)}) collective-permute-start(f32[414,128]{1,0:T(8,128)S(1)} %pad_maximum_fusion.5), channel_id=1, source_target_pairs={{0,1},{1,2},{2,3},{3,4},{4,5},{5,6},{6,7},{7,8},{8,9},{9,10},{10,1... | collective-permute-start | bytes 635912 | tf_op jit(solution)/shard_map/ppermute | solution.py:54
  96.1 7.5 %collective-permute-start.4 = (f32[414,128]{1,0:T(8,128)S(1)}, f32[414,128]{1,0:T(8,128)S(1)}, u32[]{:S(2)}, u32[]{:S(2)}) collective-permute-start(f32[414,128]{1,0:T(8,128)S(1)} %pad_maximum_fusion.6), channel_id=1, source_target_pairs={{0,15},{1,0},{2,1},{3,2},{4,3},{5,4},{6,5},{7,6},{8,7},{9,8},{10,9... | collective-permute-start | bytes 635912 | tf_op jit(solution)/shard_map/ppermute | solution.py:54
  104.5 4.8 %collective-permute-start.5 = (f32[1656]{0:T(1024)S(1)}, f32[1656]{0:T(1024)S(1)}, u32[]{:S(2)}, u32[]{:S(2)}) collective-permute-start(f32[1656]{0:T(1024)S(1)} %maximum_select_fusion.1), channel_id=1, source_target_pairs={{0,16},{16,0},{1,17},{17,1},{2,18},{18,2},{3,19},{19,3},{4,20},{20... | collective-permute-start | bytes 19880 | tf_op jit(solution)/shard_map/ppermute | solution.py:375
  113.1 18.7 %all-to-all-start.2 = ((f32[8,1,14848]{2,1,0:T(1,128)}), f32[8,1,14848]{2,1,0:T(1,128)S(1)}, u32[]{:S(2)}, u32[]{:S(2)}) async-start(f32[8,1,14848]{2,1,0:T(1,128)} %all_to_all.30), calls=%async_computation.2 | async-start | bytes 950272 | tf_op jit(solution)/shard_map/all_to_all | solution.py:442
  144.8 2.9 %collective-permute-start.6 = (f32[414,128]{1,0:T(8,128)S(1)}, f32[414,128]{1,0:T(8,128)S(1)}, u32[]{:S(2)}, u32[]{:S(2)}) collective-permute-start(f32[414,128]{1,0:T(8,128)S(1)} %pad_maximum_fusion.7), channel_id=1, source_target_pairs={{0,1},{1,2},{2,3},{3,4},{4,5},{5,6},{6,7},{7,8},{8,9},{9,10},{10,1... | collective-permute-start | bytes 635912 | tf_op jit(solution)/shard_map/ppermute | solution.py:54
  145.0 7.5 %collective-permute-start.7 = (f32[414,128]{1,0:T(8,128)S(1)}, f32[414,128]{1,0:T(8,128)S(1)}, u32[]{:S(2)}, u32[]{:S(2)}) collective-permute-start(f32[414,128]{1,0:T(8,128)S(1)} %pad_maximum_fusion.8), channel_id=1, source_target_pairs={{0,15},{1,0},{2,1},{3,2},{4,3},{5,4},{6,5},{7,6},{8,7},{9,8},{10,9... | collective-permute-start | bytes 635912 | tf_op jit(solution)/shard_map/ppermute | solution.py:54
  153.3 4.6 %collective-permute-start.8 = (f32[1656]{0:T(1024)S(1)}, f32[1656]{0:T(1024)S(1)}, u32[]{:S(2)}, u32[]{:S(2)}) collective-permute-start(f32[1656]{0:T(1024)S(1)} %maximum_select_fusion.2), channel_id=1, source_target_pairs={{0,16},{16,0},{1,17},{17,1},{2,18},{18,2},{3,19},{19,3},{4,20},{20... | collective-permute-start | bytes 19880 | tf_op jit(solution)/shard_map/ppermute | solution.py:375
